TPU v7x, 32 devices: a whole 2x2x4 slice. The times are simulated.
32 devices in a mesh: gx: 4 (over x, core), gy: 8 (over z, y).
Axes of the slice: x: 2, y: 2, z: 4, core: 2. Of those that a mesh axis runs over, the one named last changes fastest.
Arguments:
- right_side: float32 [4, 1024, 2048], P(None, 'gx', 'gy')
- prior_weight: float32 [4, 1024, 2048], P(None, 'gx', 'gy'), may hold values from 0.5 to 4
- jacobi_inverse: float32 [4, 1024, 2048], P(None, 'gx', 'gy'), may hold values from 0.1 to 0.5
- interaction: float32 [2, 4, 128, 128], replicated, may hold values from -0.5 to 0.5
- footprint: int32 [2, 16, 16, 4], P(None, 'gx', 'gy'), may hold values from 0 to 255, as said below
Outputs:
- solution: float32 [4, 1024, 2048], P(None, 'gx', 'gy')
- residual: float32 [4, 1024, 2048], P(None, 'gx', 'gy')
Inputs may be any that keep to these rules, and one draw needn't show every extreme that they name: `footprint`: each entry is bx * 16 + by of a block of the same 4 block rows along the first dimension as its ray block's tile. Of the 64 entries of one tile's ray blocks, between 7 and 9 fall in each tile of the same strip along the second dimension, exactly 9 in some; one tile of the second dimension receives exactly 9 entries from every tile of the strip.
All inputs are finite; a program needn't handle non-finite values.
Results may differ from a plain program's by a relative error of at most 0.0003.
Values sent between devices are 32-bit elements; how exact they have to be, the bound alone decides.
No kernel may reach another device: no remote copies, remote signals or barrier semaphores. Data moves between devices by JAX's collectives and lax.ppermute only.
A program may use at most 128 MiB of HBM per device.

v0:
```python
import jax
import jax.numpy as jnp
from jax import lax
from jax.sharding import PartitionSpec as P

ITERS = 4


DAUB_LOW = (
    0.3326705529509569,
    0.8068915093133388,
    0.4598775021193313,
    -0.13501102001039084,
    -0.08544127388224149,
    0.035226291882100656,
)
DAUB_HIGH = tuple(((-1.0) ** tap_index * DAUB_LOW[5 - tap_index] for tap_index in range(6)))


def extended(block, sides, width):
    for axis, dim in sides:
        count = lax.axis_size(axis)
        forward = [(i, i + 1) for i in range(count - 1)]
        backward = [(target, source) for source, target in forward]
        low = lax.ppermute(
            lax.slice_in_dim(block, block.shape[dim] - width, None, axis=dim), axis, forward
        )
        high = lax.ppermute(lax.slice_in_dim(block, 0, width, axis=dim), axis, backward)
        block = jnp.concatenate([low, block, high], axis=dim)
    return block


def synth_table(length):
    inputs = jnp.arange(length + 8, dtype=jnp.int32)[:, None]
    outputs = jnp.arange(length, dtype=jnp.int32)[None, :]
    half = outputs // 2
    phase = outputs % 2
    table = jnp.zeros((length + 8, length), jnp.float32)
    for tap_num in range(3):
        low_coef = jnp.where(phase == 0, DAUB_LOW[2 * tap_num], DAUB_LOW[2 * tap_num + 1])
        high_coef = jnp.where(phase == 0, DAUB_HIGH[2 * tap_num], DAUB_HIGH[2 * tap_num + 1])
        table = table + jnp.where(inputs == 2 * (half - tap_num) + 4, low_coef, 0.0)
        table = table + jnp.where(inputs == 2 * (half - tap_num) + 5, high_coef, 0.0)
    return table


def analysis_table(length):
    inputs = jnp.arange(length + 8, dtype=jnp.int32)[:, None]
    outputs = jnp.arange(length, dtype=jnp.int32)[None, :]
    half = outputs // 2
    phase = outputs % 2
    table = jnp.zeros((length + 8, length), jnp.float32)
    for tap_num in range(3):
        for offset in (0, 1):
            coef = jnp.where(
                phase == 0, DAUB_LOW[2 * tap_num + offset], DAUB_HIGH[2 * tap_num + offset]
            )
            table = table + jnp.where(inputs == 2 * (half + tap_num) + offset + 4, coef, 0.0)
    return table


def with_rim(field):
    return extended(field, (("gx", 1), ("gy", 2)), 4)


def shards(right_side, prior_weight, jacobi_inverse, interaction, footprint):
    highest = lax.Precision.HIGHEST
    layers, tile_rows, tile_cols = right_side.shape
    sensors, rows_blocks, cols_blocks = (footprint.shape[0], footprint.shape[1], footprint.shape[2])
    block_rows = tile_rows // rows_blocks
    block_cols = tile_cols // cols_blocks
    owners = lax.axis_size("gy")
    layer_blocks_cols = cols_blocks * owners
    requests = sensors * rows_blocks * cols_blocks * layers
    capacity = requests // owners + 1
    own_blocks = layers * rows_blocks * cols_blocks
    synth_rows = synth_table(tile_rows)
    synth_cols = synth_table(tile_cols)
    analysis_rows = analysis_table(tile_rows)
    analysis_cols = analysis_table(tile_cols)
    flat_ids = footprint.reshape(requests)
    request_num = jnp.arange(requests, dtype=jnp.int32)
    layer_of = request_num % layers
    sensor_of = request_num // (requests // sensors)
    target = flat_ids % layer_blocks_cols // cols_blocks
    owned_index = (
        layer_of * (rows_blocks * cols_blocks)
        + flat_ids // layer_blocks_cols % rows_blocks * cols_blocks
        + flat_ids % layer_blocks_cols % cols_blocks
    )
    picks = (target[:, None] == jnp.arange(owners, dtype=jnp.int32)[None, :]).astype(jnp.int32)
    slot = jnp.sum(picks * (jnp.cumsum(picks, axis=0) - 1), axis=1)
    send_ids = jnp.full((owners, capacity), own_blocks, jnp.int32).at[target, slot].set(owned_index)
    send_pairs = (
        jnp.zeros((owners, capacity), jnp.int32).at[target, slot].set(sensor_of * layers + layer_of)
    )
    wanted_ids, wanted_pairs = (
        lax.all_to_all(send_ids, "gy", split_axis=0, concat_axis=0, tiled=True),
        lax.all_to_all(send_pairs, "gy", split_axis=0, concat_axis=0, tiled=True),
    )
    slot_source = (
        jnp.full((owners, capacity), requests, jnp.int32).at[target, slot].set(request_num)
    )
    landing = (
        wanted_ids.reshape(-1)[None, :] == jnp.arange(own_blocks, dtype=jnp.int32)[:, None]
    ).astype(jnp.float32)
    solution = jnp.zeros_like(right_side)
    residual = right_side
    precond_res = jacobi_inverse * residual

    def global_sum(local_value):
        return lax.psum(local_value, ("gx", "gy"))

    direction = precond_res
    rho_now = global_sum(jnp.sum(residual * precond_res))
    for step in range(ITERS):
        synthesize_padded = with_rim(direction)
        along_rows = jnp.einsum("lab,ac->lcb", synthesize_padded, synth_rows, precision=highest)
        blocks = (
            jnp.einsum("lab,bc->lac", along_rows, synth_cols, precision=highest)
            .reshape(layers, rows_blocks, block_rows, cols_blocks, block_cols)
            .transpose(0, 1, 3, 2, 4)
            .reshape(own_blocks, block_rows, block_cols)
        )
        outgoing = jnp.take(blocks, wanted_ids, axis=0, mode="fill", fill_value=0.0)
        arrived = lax.all_to_all(outgoing, "gy", split_axis=0, concat_axis=0, tiled=True)
        seen = arrived[target, slot].reshape(
            sensors, rows_blocks * cols_blocks, layers, block_rows, block_cols
        )
        slopes = jnp.einsum("sklxy,slyz->skxz", seen, interaction, precision=highest)
        back = jnp.einsum("skxz,slyz->sklxy", slopes, interaction, precision=highest).reshape(
            requests, block_rows, block_cols
        )
        returning = jnp.take(back, slot_source, axis=0, mode="fill", fill_value=0.0)
        landed = lax.all_to_all(returning, "gy", split_axis=0, concat_axis=0, tiled=True)
        summed = jnp.dot(
            landing, landed.reshape(owners * capacity, block_rows * block_cols), precision=highest
        )
        padded = with_rim(
            summed.reshape(layers, rows_blocks, cols_blocks, block_rows, block_cols)
            .transpose(0, 1, 3, 2, 4)
            .reshape(layers, tile_rows, tile_cols)
        )
        along_cols = jnp.einsum("lab,bc->lac", padded, analysis_cols, precision=highest)
        image = (
            jnp.einsum("lab,ac->lcb", along_cols, analysis_rows, precision=highest)
            + prior_weight * direction
        )
        step_size = rho_now / global_sum(jnp.sum(direction * image))
        solution = solution + step_size * direction
        residual = residual - step_size * image
        if step + 1 < ITERS:
            precond_res = jacobi_inverse * residual
            rho_next = global_sum(jnp.sum(residual * precond_res))
            direction = precond_res + rho_next / rho_now * direction
            rho_now = rho_next
    return (solution, residual)


def solution(mesh):
    return jax.shard_map(
        shards,
        mesh=mesh,
        in_specs=(
            P(None, "gx", "gy"),
            P(None, "gx", "gy"),
            P(None, "gx", "gy"),
            P(),
            P(None, "gx", "gy", None),
        ),
        out_specs=(P(None, "gx", "gy"), P(None, "gx", "gy")),
        check_vma=False,
    )
```

profile of v0, /device:TPU:10, one launch (start us, length us, event | category | flops | bytes accessed | tf_op | source)
XLA Modules:
  0.0 1153.5 jit_solution(17234243243100346092)
XLA Ops:
  3.4 10.1 scatter_fusion
  13.5 6.3 all-to-all-start
  31.2 4.9 collective-permute-done
  60.4 6.3 all-to-all-start.1
  70.3 40.1 %all-to-all-done.1 = f32[8,9,64,128]{3,2,1,0:T(8,128)} async-done(((f32[8,9,64,128]{3,2,1,0:T(8,128)}), f32[8,9,64,128]{3,2,1,0:T(8,128)}, u32[]{:S(2)}, u32[]{:S(2)}) %all-to-all-start.1) | async-done | bytes 2359328 | tf_op jit(solution)/shard_map/all_to_all | solution.py:126
  127.7 7.1 all-to-all-start.2
  136.2 45.8 %all-to-all-done.2 = f32[8,9,64,128]{3,2,1,0:T(8,128)} async-done(((f32[8,9,64,128]{3,2,1,0:T(8,128)}), f32[8,9,64,128]{3,2,1,0:T(8,128)}, u32[]{:S(2)}, u32[]{:S(2)}) %all-to-all-start.2) | async-done | bytes 2359328 | tf_op jit(solution)/shard_map/all_to_all | solution.py:135
  193.9 10.9 collective-permute-start.5
  208.6 5.3 collective-permute-start.7
  221.8 3.8 fusion.18
  225.6 4.6 multiply_reduce_fusion.6
  230.2 38.9 %all-reduce = (f32[]{:T(128)}, f32[]{:T(128)}) all-reduce(f32[]{:T(128)} %get-tuple-element.7, f32[]{:T(128)} %get-tuple-element.6), channel_id=1, replica_groups=mesh['gx'=4,'gy'=8] {'gx','gy'}, use_global_device_ids=true, to_apply=%region_1.2 | all-reduce | flops 2 | bytes 16 | tf_op jit(solution)/shard_map/psum | solution.py:112
  270.4 4.0 multiply_reduce_fusion.5
  274.4 41.8 %psum.58 = f32[]{:T(128)} all-reduce(f32[]{:T(128)} %get-tuple-element.16), channel_id=1, replica_groups=mesh['gx'=4,'gy'=8] {'gx','gy'}, use_global_device_ids=true, to_apply=%region_9.12 | all-reduce | flops 1 | bytes 8 | tf_op jit(solution)/shard_map/psum | solution.py:112
  324.5 4.9 collective-permute-done.8
  333.6 4.6 collective-permute-start.11
  341.9 3.8 fusion.199
  356.0 50.4 %all_to_all.52 = f32[8,9,64,128]{3,2,1,0:T(8,128)} all-to-all(f32[8,9,64,128]{3,2,1,0:T(8,128)S(1)} %broadcast_select_fusion.5), channel_id=1, replica_groups=mesh['gx'=4,'gy'=8] {'gy'}, dimensions={0} | all-to-all | bytes 4718592 | tf_op jit(solution)/shard_map/all_to_all | solution.py:126
  422.3 54.3 %all_to_all.53 = f32[8,9,64,128]{3,2,1,0:T(8,128)S(1)} all-to-all(f32[8,9,64,128]{3,2,1,0:T(8,128)S(1)} %broadcast_select_fusion.4), channel_id=1, replica_groups=mesh['gx'=4,'gy'=8] {'gy'}, dimensions={0} | all-to-all | bytes 4718592 | tf_op jit(solution)/shard_map/all_to_all | solution.py:135
  488.6 8.5 collective-permute-start.13
  504.4 5.2 collective-permute-start.15
  511.8 3.8 fusion.38
  515.6 4.5 multiply_reduce_fusion.4
  520.0 41.9 %psum.59 = f32[]{:T(128)} all-reduce(f32[]{:T(128)} %get-tuple-element.57), channel_id=1, replica_groups=mesh['gx'=4,'gy'=8] {'gx','gy'}, use_global_device_ids=true, to_apply=%region_11.14 | all-reduce | flops 1 | bytes 8 | tf_op jit(solution)/shard_map/psum | solution.py:112
  563.3 4.1 multiply_reduce_fusion.3
  567.4 39.4 %psum.60 = f32[]{:T(128)} all-reduce(f32[]{:T(128)} %get-tuple-element.13), channel_id=1, replica_groups=mesh['gx'=4,'gy'=8] {'gx','gy'}, use_global_device_ids=true, to_apply=%region_13.16 | all-reduce | flops 1 | bytes 8 | tf_op jit(solution)/shard_map/psum | solution.py:112
  615.3 4.9 collective-permute-done.16
  622.1 4.0 collective-permute-start.18
  634.2 3.8 fusion.196
  648.2 50.1 %all_to_all.54 = f32[8,9,64,128]{3,2,1,0:T(8,128)} all-to-all(f32[8,9,64,128]{3,2,1,0:T(8,128)S(1)} %broadcast_select_fusion.3), channel_id=1, replica_groups=mesh['gx'=4,'gy'=8] {'gy'}, dimensions={0} | all-to-all | bytes 4718592 | tf_op jit(solution)/shard_map/all_to_all | solution.py:126
  714.2 54.8 %all_to_all.55 = f32[8,9,64,128]{3,2,1,0:T(8,128)S(1)} all-to-all(f32[8,9,64,128]{3,2,1,0:T(8,128)S(1)} %broadcast_select_fusion.2), channel_id=1, replica_groups=mesh['gx'=4,'gy'=8] {'gy'}, dimensions={0} | all-to-all | bytes 4718592 | tf_op jit(solution)/shard_map/all_to_all | solution.py:135
  781.0 7.8 collective-permute-start.21
  796.1 5.2 collective-permute-start.23
  803.5 3.9 fusion.58
  807.4 4.5 multiply_reduce_fusion.2
  811.9 41.9 %psum.61 = f32[]{:T(128)} all-reduce(f32[]{:T(128)} %get-tuple-element.59), channel_id=1, replica_groups=mesh['gx'=4,'gy'=8] {'gx','gy'}, use_global_device_ids=true, to_apply=%region_15.18 | all-reduce | flops 1 | bytes 8 | tf_op jit(solution)/shard_map/psum | solution.py:112
  855.2 4.1 multiply_reduce_fusion.1
  859.3 39.4 %psum.62 = f32[]{:T(128)} all-reduce(f32[]{:T(128)} %get-tuple-element.10), channel_id=1, replica_groups=mesh['gx'=4,'gy'=8] {'gx','gy'}, use_global_device_ids=true, to_apply=%region_17.20 | all-reduce | flops 1 | bytes 8 | tf_op jit(solution)/shard_map/psum | solution.py:112
  907.3 4.9 collective-permute-done.24
  914.1 3.9 collective-permute-start.26
  926.1 3.8 fusion.193
  940.2 50.1 %all_to_all.56 = f32[8,9,64,128]{3,2,1,0:T(8,128)} all-to-all(f32[8,9,64,128]{3,2,1,0:T(8,128)S(1)} %broadcast_select_fusion.1), channel_id=1, replica_groups=mesh['gx'=4,'gy'=8] {'gy'}, dimensions={0} | all-to-all | bytes 4718592 | tf_op jit(solution)/shard_map/all_to_all | solution.py:126
  1006.3 54.8 %all_to_all.57 = f32[8,9,64,128]{3,2,1,0:T(8,128)S(1)} all-to-all(f32[8,9,64,128]{3,2,1,0:T(8,128)S(1)} %broadcast_select_fusion), channel_id=1, replica_groups=mesh['gx'=4,'gy'=8] {'gy'}, dimensions={0} | all-to-all | bytes 4718592 | tf_op jit(solution)/shard_map/all_to_all | solution.py:135
  1073.1 8.0 collective-permute-start.29
  1088.4 5.1 collective-permute-start.31
  1095.7 3.9 fusion.78
  1099.6 4.5 multiply_reduce_fusion
  1104.2 41.9 %psum.63 = f32[]{:T(128)} all-reduce(f32[]{:T(128)} %get-tuple-element.61), channel_id=1, replica_groups=mesh['gx'=4,'gy'=8] {'gx','gy'}, use_global_device_ids=true, to_apply=%region_19.22 | all-reduce | flops 1 | bytes 8 | tf_op jit(solution)/shard_map/psum | solution.py:112
  (225 shorter events, 282.0 us)
Async XLA Ops:
  0.6 113.4 %copy-start = (f32[2,4,128,128]{3,2,1,0:T(8,128)S(1)}, f32[2,4,128,128]{3,2,1,0:T(8,128)}, u32[]{:S(2)}) copy-start(f32[2,4,128,128]{3,2,1,0:T(8,128)} %param.12) | copy-start | bytes 1572868
  0.6 19.1 %copy-start.15 = (f32[4,256,256]{2,1,0:T(8,128)S(1)}, f32[4,256,256]{2,1,0:T(8,128)}, u32[]{:S(2)}) copy-start(f32[4,256,256]{2,1,0:T(8,128)} %param.11) | copy-start | bytes 3145732
  13.5 17.6 %all-to-all-start = ((s32[8,1,9]{2,1,0:T(1,128)}), s32[8,1,9]{2,1,0:T(1,128)S(1)}, u32[]{:S(2)}, u32[]{:S(2)}) async-start(s32[8,1,9]{2,1,0:T(1,128)} %bitcast.4), calls=%async_computation | async-start | bytes 8192 | tf_op jit(solution)/shard_map/all_to_all | solution.py:98
  20.1 4.3 copy-start.9
  25.5 10.7 collective-permute-start
  27.4 10.3 collective-permute-start.1
  37.8 6.8 collective-permute-start.2
  41.2 5.7 collective-permute-start.3
  60.4 49.9 %all-to-all-start.1 = ((f32[8,9,64,128]{3,2,1,0:T(8,128)}), f32[8,9,64,128]{3,2,1,0:T(8,128)}, u32[]{:S(2)}, u32[]{:S(2)}) async-start(f32[8,9,64,128]{3,2,1,0:T(8,128)} %broadcast_select_fusion.7), calls=%async_computation.1 | async-start | bytes 4718592 | tf_op jit(solution)/shard_map/all_to_all | solution.py:126
  127.7 54.2 %all-to-all-start.2 = ((f32[8,9,64,128]{3,2,1,0:T(8,128)}), f32[8,9,64,128]{3,2,1,0:T(8,128)}, u32[]{:S(2)}, u32[]{:S(2)}) async-start(f32[8,9,64,128]{3,2,1,0:T(8,128)} %broadcast_select_fusion.6), calls=%async_computation.2 | async-start | bytes 4718592 | tf_op jit(solution)/shard_map/all_to_all | solution.py:135
  192.0 15.1 %copy-start.11 = (f32[4,256,256]{2,1,0:T(8,128)}, f32[4,256,256]{2,1,0:T(8,128)S(1)}, u32[]{:S(2)}) copy-start(f32[4,256,256]{2,1,0:T(8,128)S(1)} %reshape.422) | copy-start | bytes 3145732
  192.0 12.9 %collective-permute-start.4 = (f32[4,4,256]{2,1,0:T(4,128)S(1)}, f32[4,4,256]{2,1,0:T(4,128)S(1)}, u32[]{:S(2)}, u32[]{:S(2)}) collective-permute-start(f32[4,4,256]{2,1,0:T(4,128)S(1)} %get-tuple-element.52), channel_id=1, source_target_pairs={{0,8},{8,16},{16,24},{1,9},{9,17},{17,25},{2,10},{10,18},{18,26},{... | collective-permute-start | bytes 49160 | tf_op jit(solution)/shard_map/ppermute | solution.py:25
  193.9 12.0 %collective-permute-start.5 = (f32[4,4,256]{2,1,0:T(4,128)S(1)}, f32[4,4,256]{2,1,0:T(4,128)S(1)}, u32[]{:S(2)}, u32[]{:S(2)}) collective-permute-start(f32[4,4,256]{2,1,0:T(4,128)S(1)} %get-tuple-element.53), channel_id=1, source_target_pairs={{8,0},{16,8},{24,16},{9,1},{17,9},{25,17},{10,2},{18,10},{26,18},{... | collective-permute-start | bytes 49160 | tf_op jit(solution)/shard_map/ppermute | solution.py:28
  208.6 12.2 %collective-permute-start.7 = (f32[4,264,4]{1,2,0:T(4,128)S(1)}, f32[4,264,4]{1,2,0:T(4,128)S(1)}, u32[]{:S(2)}, u32[]{:S(2)}) collective-permute-start(f32[4,264,4]{1,2,0:T(4,128)S(1)} %copy.27), channel_id=1, source_target_pairs={{1,0},{2,1},{3,2},{4,3},{5,4},{6,5},{7,6},{9,8},{10,9},{11,10},{12... | collective-permute-start | bytes 50696 | tf_op jit(solution)/shard_map/ppermute | solution.py:28
  213.9 6.6 collective-permute-start.6
  217.4 8.2 copy-start.3
  221.8 3.8 copy-start.10
  318.9 10.5 collective-permute-start.8
  320.9 10.3 collective-permute-start.9
  331.3 6.9 collective-permute-start.10
  333.6 6.0 collective-permute-start.11
  486.7 10.4 collective-permute-start.12
  488.6 9.9 collective-permute-start.13
  502.2 7.4 collective-permute-start.14
  504.4 6.3 collective-permute-start.15
  511.7 3.8 copy-start.4
  609.5 22.3 %copy-start.1 = (f32[4,256,256]{1,2,0:T(8,128)}, f32[4,256,256]{1,2,0:T(8,128)S(1)}, u32[]{:S(2)}) copy-start(f32[4,256,256]{1,2,0:T(8,128)S(1)} %multiply_add_fusion.2) | copy-start | bytes 3145732
  609.7 10.5 collective-permute-start.16
  611.7 10.3 collective-permute-start.17
  622.1 6.9 collective-permute-start.18
  626.1 5.7 collective-permute-start.19
  779.1 9.8 collective-permute-start.20
  781.0 9.3 collective-permute-start.21
  793.9 7.4 collective-permute-start.22
  796.1 6.3 collective-permute-start.23
  803.5 3.9 copy-start.2
  803.5 3.9 copy-start.5
  901.6 22.2 %copy-start.7 = (f32[4,256,256]{1,2,0:T(8,128)}, f32[4,256,256]{1,2,0:T(8,128)S(1)}, u32[]{:S(2)}) copy-start(f32[4,256,256]{1,2,0:T(8,128)S(1)} %multiply_add_fusion.1) | copy-start | bytes 3145732
  901.8 10.5 collective-permute-start.24
  903.7 10.3 collective-permute-start.25
  914.1 6.9 collective-permute-start.26
  918.0 5.7 collective-permute-start.27
  1071.2 9.9 collective-permute-start.28
  1073.1 9.4 collective-permute-start.29
  1086.2 7.3 collective-permute-start.30
  1088.4 6.3 collective-permute-start.31
  1095.7 3.9 copy-start.6
  1095.7 3.9 copy-start.8
  (3 other events, 7.4 us)
where the time goes:
time: 1170 us; the launch traced here: 1150 us
  blocking collectives  600 us (51%)
  starting transfers between devices  141 us (12%)
  waiting for transfers between devices  133 us (11%)
  local copies, waits for them, and re-layouts  131 us (11%)
  matrix products  94.2 us (8%)
  other arithmetic  44.8 us (4%)
    psum x7, blocking collectives, global_sum(): return lax.psum(local_value, ('gx', 'gy'))  285 us
    all_to_all x3, blocking collectives, shards(): lax.all_to_all(returning, 'gy', split_axis=0, concat_axis=0, tiled=True)  164 us
    all_to_all x3, blocking collectives, shards(): lax.all_to_all(outgoing, 'gy', split_axis=0, concat_axis=0, tiled=True)  151 us
    ppermute x16, starting transfers between devices, extended(): lax.ppermute(lax.slice_in_dim(block, 0, width, axis=dim), axis, backward)  84.6 us
    all_to_all x1, waiting for transfers between devices, shards(): lax.all_to_all(returning, 'gy', split_axis=0, concat_axis=0, tiled=True)  45.8 us
    all_to_all x1, waiting for transfers between devices, shards(): lax.all_to_all(outgoing, 'gy', split_axis=0, concat_axis=0, tiled=True)  40.1 us
    ppermute x16, starting transfers between devices, extended(): lax.ppermute(lax.slice_in_dim(block, block.shape[dim] - width, None, axis...  36.5 us
    ppermute x16, waiting for transfers between devices, extended(): lax.ppermute(lax.slice_in_dim(block, 0, width, axis=dim), axis, backward)  23.8 us
  transfers between devices with their start and end apart: 35, of which 22 were waited for; matrix products, arithmetic and copies ran while one was open for 1% of the time, Pallas kernels for 0%

commit v1 on v0

--- a/solution.py
+++ b/solution.py
@@ -59,6 +59,21 @@
     return table
 
 
+def butterfly_sum(value, axis):
+    count = lax.axis_size(axis)
+    if count & (count - 1):
+        return lax.psum(value, axis)
+    stride = 1
+    while stride < count:
+        value = value + lax.ppermute(value, axis, [(i, i ^ stride) for i in range(count)])
+        stride *= 2
+    return value
+
+
+def global_sum(local_value):
+    return butterfly_sum(butterfly_sum(local_value, "gx"), "gy")
+
+
 def with_rim(field):
     return extended(field, (("gx", 1), ("gy", 2)), 4)
 
@@ -104,16 +119,7 @@
     landing = (
         wanted_ids.reshape(-1)[None, :] == jnp.arange(own_blocks, dtype=jnp.int32)[:, None]
     ).astype(jnp.float32)
-    solution = jnp.zeros_like(right_side)
-    residual = right_side
-    precond_res = jacobi_inverse * residual
-
-    def global_sum(local_value):
-        return lax.psum(local_value, ("gx", "gy"))
-
-    direction = precond_res
-    rho_now = global_sum(jnp.sum(residual * precond_res))
-    for step in range(ITERS):
+    def apply_op(direction):
         synthesize_padded = with_rim(direction)
         along_rows = jnp.einsum("lab,ac->lcb", synthesize_padded, synth_rows, precision=highest)
         blocks = (
@@ -142,17 +148,28 @@
             .reshape(layers, tile_rows, tile_cols)
         )
         along_cols = jnp.einsum("lab,bc->lac", padded, analysis_cols, precision=highest)
-        image = (
+        return (
             jnp.einsum("lab,ac->lcb", along_cols, analysis_rows, precision=highest)
             + prior_weight * direction
         )
+
+    solution = jnp.zeros_like(right_side)
+    residual = right_side
+    precond_res = jacobi_inverse * residual
+    direction = precond_res
+    rho_now = global_sum(jnp.sum(residual * precond_res))
+    image = apply_op(direction)
+    for step in range(ITERS):
         step_size = rho_now / global_sum(jnp.sum(direction * image))
         solution = solution + step_size * direction
         residual = residual - step_size * image
         if step + 1 < ITERS:
             precond_res = jacobi_inverse * residual
             rho_next = global_sum(jnp.sum(residual * precond_res))
-            direction = precond_res + rho_next / rho_now * direction
+            applied = apply_op(precond_res)
+            ratio = rho_next / rho_now
+            direction = precond_res + ratio * direction
+            image = applied + ratio * image
             rho_now = rho_next
     return (solution, residual)
 

time: 1170 us -> 1020 us (0.87)
  blocking collectives: 600 us -> 316 us
  starting transfers between devices: 141 us -> 207 us
  waiting for transfers between devices: 133 us -> 183 us
  between operations: 10.9 us -> 31.6 us
    psum x7 -> x0, blocking collectives: 285 us -> none  [global_sum(): return lax.psum(local_value, ('gx', 'gy'))]
    ppermute x0 -> x40, starting transfers between devices: none -> 65.2 us  [butterfly_sum(): lax.ppermute(value, axis, [(i, i ^ stride) for i in range(count)])]
    ppermute x0 -> x40, waiting for transfers between devices: none -> 56.3 us  [butterfly_sum(): lax.ppermute(value, axis, [(i, i ^ stride) for i in range(count)])]
  transfers between devices with their start and end apart: 35 -> 75, of which waited for: 22 -> 50; matrix products, arithmetic and copies ran while one was open for 1% -> 1% of each run, Pallas kernels for 0% -> 0%
where the time goes in v1:
time: 1020 us; the launch traced here: 1000 us
  blocking collectives  316 us (31%)
  starting transfers between devices  207 us (20%)
  waiting for transfers between devices  183 us (18%)
  local copies, waits for them, and re-layouts  130 us (13%)
  matrix products  95 us (9%)
  other arithmetic  39.3 us (4%)
  between operations  31.6 us (3%)
    all_to_all x3, blocking collectives, apply_op(): lax.all_to_all(returning, 'gy', split_axis=0, concat_axis=0, tiled=True)  163 us
    all_to_all x3, blocking collectives, apply_op(): lax.all_to_all(outgoing, 'gy', split_axis=0, concat_axis=0, tiled=True)  153 us
    ppermute x16, starting transfers between devices, extended(): lax.ppermute(lax.slice_in_dim(block, 0, width, axis=dim), axis, backward)  89 us
    ppermute x40, starting transfers between devices, butterfly_sum(): lax.ppermute(value, axis, [(i, i ^ stride) for i in range(count)])  65.2 us
    ppermute x40, waiting for transfers between devices, butterfly_sum(): lax.ppermute(value, axis, [(i, i ^ stride) for i in range(count)])  56.3 us
    all_to_all x1, waiting for transfers between devices, apply_op(): lax.all_to_all(returning, 'gy', split_axis=0, concat_axis=0, tiled=True)  45.8 us
    all_to_all x1, waiting for transfers between devices, apply_op(): lax.all_to_all(outgoing, 'gy', split_axis=0, concat_axis=0, tiled=True)  40.1 us
    ppermute x16, starting transfers between devices, extended(): lax.ppermute(lax.slice_in_dim(block, block.shape[dim] - width, None, axis...  32.9 us
  transfers between devices with their start and end apart: 75, of which 50 were waited for; matrix products, arithmetic and copies ran while one was open for 1% of the time, Pallas kernels for 0%

profile of v1, /device:TPU:10, one launch (start us, length us, event | category | flops | bytes accessed | tf_op | source)
XLA Modules:
  0.0 1003.2 jit_solution(15432480952967989075)
XLA Ops:
  3.4 10.1 %scatter_fusion = s32[8,9]{1,0:T(8,128)} fusion(s32[8,9]{1,0:T(8,128)} %broadcast_in_dim.425, s32[64]{0:T(128)S(1)} %fusion.183, s32[64]{0:T(128)S(1)} %get-tuple-element.21), kind=kCustom, calls=%fused_computation.12 | custom fusion | bytes 1280 | tf_op jit(solution)/shard_map/scatter | solution.py:108
  13.5 6.3 all-to-all-start
  31.3 4.9 collective-permute-done.5
  60.4 6.6 all-to-all-start.1
  70.6 40.1 %all-to-all-done.1 = f32[8,9,64,128]{3,2,1,0:T(8,128)} async-done(((f32[8,9,64,128]{3,2,1,0:T(8,128)}), f32[8,9,64,128]{3,2,1,0:T(8,128)}, u32[]{:S(2)}, u32[]{:S(2)}) %all-to-all-start.1) | async-done | bytes 2359328 | tf_op jit(solution)/shard_map/all_to_all | solution.py:132
  110.6 3.7 gather_fusion
  121.0 3.7 gather_fusion.5
  127.9 7.1 all-to-all-start.2
  136.3 45.8 %all-to-all-done.2 = f32[8,9,64,128]{3,2,1,0:T(8,128)} async-done(((f32[8,9,64,128]{3,2,1,0:T(8,128)}), f32[8,9,64,128]{3,2,1,0:T(8,128)}, u32[]{:S(2)}, u32[]{:S(2)}) %all-to-all-start.2) | async-done | bytes 2359328 | tf_op jit(solution)/shard_map/all_to_all | solution.py:141
  194.1 10.7 %collective-permute-start.10 = (f32[4,4,256]{2,1,0:T(4,128)S(1)}, f32[4,4,256]{2,1,0:T(4,128)S(1)}, u32[]{:S(2)}, u32[]{:S(2)}) collective-permute-start(f32[4,4,256]{2,1,0:T(4,128)S(1)} %get-tuple-element.53), channel_id=1, source_target_pairs={{8,0},{16,8},{24,16},{9,1},{17,9},{25,17},{10,2},{18,10},{26,18},{... | collective-permute-start | bytes 49160 | tf_op jit(solution)/shard_map/ppermute | solution.py:28
  208.8 5.3 collective-permute-start.12
  222.0 3.8 fusion.18
  225.8 4.5 multiply_reduce_fusion.6
  253.5 4.3 collective-permute-start.4
  268.5 4.9 collective-permute-done.23
  277.9 4.3 collective-permute-start.26
  286.0 3.8 fusion.199
  300.1 52.1 %all_to_all.52 = f32[8,9,64,128]{3,2,1,0:T(8,128)} all-to-all(f32[8,9,64,128]{3,2,1,0:T(8,128)S(1)} %broadcast_select_fusion.5), channel_id=1, replica_groups=mesh['gx'=4,'gy'=8] {'gy'}, dimensions={0} | all-to-all | bytes 4718592 | tf_op jit(solution)/shard_map/all_to_all | solution.py:132
  352.2 3.7 gather_fusion.1
  362.5 3.7 gather_fusion.7
  368.1 54.9 %all_to_all.53 = f32[8,9,64,128]{3,2,1,0:T(8,128)S(1)} all-to-all(f32[8,9,64,128]{3,2,1,0:T(8,128)S(1)} %broadcast_select_fusion.4), channel_id=1, replica_groups=mesh['gx'=4,'gy'=8] {'gy'}, dimensions={0} | all-to-all | bytes 4718592 | tf_op jit(solution)/shard_map/all_to_all | solution.py:141
  435.0 8.1 collective-permute-start.28
  450.4 5.3 collective-permute-start.30
  477.7 3.8 fusion.38
  481.5 4.6 multiply_reduce_fusion.4
  506.3 3.7 multiply_reduce_fusion.3
  515.8 4.9 collective-permute-done.41
  524.5 5.0 collective-permute-start.44
  533.2 3.8 fusion.196
  547.3 50.5 %all_to_all.54 = f32[8,9,64,128]{3,2,1,0:T(8,128)} all-to-all(f32[8,9,64,128]{3,2,1,0:T(8,128)S(1)} %broadcast_select_fusion.3), channel_id=1, replica_groups=mesh['gx'=4,'gy'=8] {'gy'}, dimensions={0} | all-to-all | bytes 4718592 | tf_op jit(solution)/shard_map/all_to_all | solution.py:132
  597.7 3.7 gather_fusion.2
  608.1 3.7 gather_fusion.9
  613.7 54.3 %all_to_all.55 = f32[8,9,64,128]{3,2,1,0:T(8,128)S(1)} all-to-all(f32[8,9,64,128]{3,2,1,0:T(8,128)S(1)} %broadcast_select_fusion.2), channel_id=1, replica_groups=mesh['gx'=4,'gy'=8] {'gy'}, dimensions={0} | all-to-all | bytes 4718592 | tf_op jit(solution)/shard_map/all_to_all | solution.py:141
  680.0 8.5 collective-permute-start.46
  695.8 5.1 collective-permute-start.48
  722.8 3.9 fusion.58
  726.7 5.2 multiply_reduce_fusion.2
  752.0 3.7 multiply_reduce_fusion.1
  761.5 4.9 collective-permute-done.59
  770.2 5.3 collective-permute-start.62
  778.9 3.8 fusion.193
  793.0 50.5 %all_to_all.56 = f32[8,9,64,128]{3,2,1,0:T(8,128)} all-to-all(f32[8,9,64,128]{3,2,1,0:T(8,128)S(1)} %broadcast_select_fusion.1), channel_id=1, replica_groups=mesh['gx'=4,'gy'=8] {'gy'}, dimensions={0} | all-to-all | bytes 4718592 | tf_op jit(solution)/shard_map/all_to_all | solution.py:132
  843.5 3.7 gather_fusion.3
  859.4 54.2 %all_to_all.57 = f32[8,9,64,128]{3,2,1,0:T(8,128)S(1)} all-to-all(f32[8,9,64,128]{3,2,1,0:T(8,128)S(1)} %broadcast_select_fusion), channel_id=1, replica_groups=mesh['gx'=4,'gy'=8] {'gy'}, dimensions={0} | all-to-all | bytes 4718592 | tf_op jit(solution)/shard_map/all_to_all | solution.py:141
  925.7 8.5 collective-permute-start.64
  941.4 5.0 collective-permute-start.66
  968.4 3.9 fusion.78
  972.3 4.6 multiply_reduce_fusion
  (303 shorter events, 365.2 us)
Async XLA Ops:
  13.5 17.6 %all-to-all-start = ((s32[8,1,9]{2,1,0:T(1,128)}), s32[8,1,9]{2,1,0:T(1,128)S(1)}, u32[]{:S(2)}, u32[]{:S(2)}) async-start(s32[8,1,9]{2,1,0:T(1,128)} %bitcast.4), calls=%async_computation | async-start | bytes 8192 | tf_op jit(solution)/shard_map/all_to_all | solution.py:113
  25.5 10.7 %collective-permute-start.5 = (f32[4,4,256]{1,2,0:T(8,128)}, f32[4,4,256]{1,2,0:T(8,128)S(1)}, u32[]{:S(2)}, u32[]{:S(2)}) collective-permute-start(f32[4,4,256]{1,2,0:T(8,128)} %get-tuple-element.54), channel_id=1, source_target_pairs={{0,8},{8,16},{16,24},{1,9},{9,17},{17,25},{2,10},{10,18},{18,26},{... | collective-permute-start | bytes 49160 | tf_op jit(solution)/shard_map/ppermute | solution.py:25
  27.4 10.3 %collective-permute-start.6 = (f32[4,4,256]{1,2,0:T(8,128)S(1)}, f32[4,4,256]{1,2,0:T(8,128)S(1)}, u32[]{:S(2)}, u32[]{:S(2)}) collective-permute-start(f32[4,4,256]{1,2,0:T(8,128)S(1)} %get-tuple-element.55), channel_id=1, source_target_pairs={{8,0},{16,8},{24,16},{9,1},{17,9},{25,17},{10,2},{18,10},{26,18},{... | collective-permute-start | bytes 49160 | tf_op jit(solution)/shard_map/ppermute | solution.py:28
  37.9 6.8 collective-permute-start.7
  41.2 5.7 collective-permute-start.8
  60.4 50.3 %all-to-all-start.1 = ((f32[8,9,64,128]{3,2,1,0:T(8,128)}), f32[8,9,64,128]{3,2,1,0:T(8,128)}, u32[]{:S(2)}, u32[]{:S(2)}) async-start(f32[8,9,64,128]{3,2,1,0:T(8,128)} %broadcast_select_fusion.7), calls=%async_computation.1 | async-start | bytes 4718592 | tf_op jit(solution)/shard_map/all_to_all | solution.py:132
  127.9 54.2 %all-to-all-start.2 = ((f32[8,9,64,128]{3,2,1,0:T(8,128)}), f32[8,9,64,128]{3,2,1,0:T(8,128)}, u32[]{:S(2)}, u32[]{:S(2)}) async-start(f32[8,9,64,128]{3,2,1,0:T(8,128)} %broadcast_select_fusion.6), calls=%async_computation.2 | async-start | bytes 4718592 | tf_op jit(solution)/shard_map/all_to_all | solution.py:141
  192.2 12.6 %collective-permute-start.9 = (f32[4,4,256]{2,1,0:T(4,128)S(1)}, f32[4,4,256]{2,1,0:T(4,128)S(1)}, u32[]{:S(2)}, u32[]{:S(2)}) collective-permute-start(f32[4,4,256]{2,1,0:T(4,128)S(1)} %get-tuple-element.52), channel_id=1, source_target_pairs={{0,8},{8,16},{16,24},{1,9},{9,17},{17,25},{2,10},{10,18},{18,26},{... | collective-permute-start | bytes 49160 | tf_op jit(solution)/shard_map/ppermute | solution.py:25
  194.1 12.0 %collective-permute-start.10 = (f32[4,4,256]{2,1,0:T(4,128)S(1)}, f32[4,4,256]{2,1,0:T(4,128)S(1)}, u32[]{:S(2)}, u32[]{:S(2)}) collective-permute-start(f32[4,4,256]{2,1,0:T(4,128)S(1)} %get-tuple-element.53), channel_id=1, source_target_pairs={{8,0},{16,8},{24,16},{9,1},{17,9},{25,17},{10,2},{18,10},{26,18},{... | collective-permute-start | bytes 49160 | tf_op jit(solution)/shard_map/ppermute | solution.py:28
  208.8 12.1 %collective-permute-start.12 = (f32[4,264,4]{1,2,0:T(4,128)S(1)}, f32[4,264,4]{1,2,0:T(4,128)S(1)}, u32[]{:S(2)}, u32[]{:S(2)}) collective-permute-start(f32[4,264,4]{1,2,0:T(4,128)S(1)} %copy.27), channel_id=1, source_target_pairs={{1,0},{2,1},{3,2},{4,3},{5,4},{6,5},{7,6},{9,8},{10,9},{11,10},{12... | collective-permute-start | bytes 50696 | tf_op jit(solution)/shard_map/ppermute | solution.py:28
  214.0 6.6 collective-permute-start.11
  233.0 5.9 collective-permute-start.14
  235.9 5.1 collective-permute-start.1
  239.6 5.4 collective-permute-start.15
  241.6 5.3 collective-permute-start.2
  245.5 5.4 collective-permute-start.16
  247.6 5.3 collective-permute-start.3
  251.5 6.3 collective-permute-start.17
  253.5 4.8 collective-permute-start.4
  262.9 10.5 %collective-permute-start.23 = (f32[4,4,256]{1,2,0:T(8,128)S(1)}, f32[4,4,256]{1,2,0:T(8,128)S(1)}, u32[]{:S(2)}, u32[]{:S(2)}) collective-permute-start(f32[4,4,256]{1,2,0:T(8,128)S(1)} %get-tuple-element.50), channel_id=1, source_target_pairs={{0,8},{8,16},{16,24},{1,9},{9,17},{17,25},{2,10},{10,18},{18,26},{... | collective-permute-start | bytes 49160 | tf_op jit(solution)/shard_map/ppermute | solution.py:25
  264.8 10.3 %collective-permute-start.24 = (f32[4,4,256]{1,2,0:T(8,128)S(1)}, f32[4,4,256]{1,2,0:T(8,128)S(1)}, u32[]{:S(2)}, u32[]{:S(2)}) collective-permute-start(f32[4,4,256]{1,2,0:T(8,128)S(1)} %get-tuple-element.51), channel_id=1, source_target_pairs={{8,0},{16,8},{24,16},{9,1},{17,9},{25,17},{10,2},{18,10},{26,18},{... | collective-permute-start | bytes 49160 | tf_op jit(solution)/shard_map/ppermute | solution.py:28
  275.3 7.0 collective-permute-start.25
  277.9 5.7 collective-permute-start.26
  433.1 10.0 collective-permute-start.27
  435.0 9.5 collective-permute-start.28
  448.2 28.2 %collective-permute-start.29 = (f32[4,264,4]{1,2,0:T(4,128)S(1)}, f32[4,264,4]{1,2,0:T(4,128)S(1)}, u32[]{:S(2)}, u32[]{:S(2)}) collective-permute-start(f32[4,264,4]{1,2,0:T(4,128)S(1)} %copy.37), channel_id=1, source_target_pairs={{0,1},{1,2},{2,3},{3,4},{4,5},{5,6},{6,7},{8,9},{9,10},{10,11},{11... | collective-permute-start | bytes 50696 | tf_op jit(solution)/shard_map/ppermute | solution.py:25
  450.4 26.3 %collective-permute-start.30 = (f32[4,264,4]{1,2,0:T(4,128)S(1)}, f32[4,264,4]{1,2,0:T(4,128)S(1)}, u32[]{:S(2)}, u32[]{:S(2)}) collective-permute-start(f32[4,264,4]{1,2,0:T(4,128)S(1)} %copy.38), channel_id=1, source_target_pairs={{1,0},{2,1},{3,2},{4,3},{5,4},{6,5},{7,6},{9,8},{10,9},{11,10},{12... | collective-permute-start | bytes 50696 | tf_op jit(solution)/shard_map/ppermute | solution.py:28
  471.1 4.6 collective-permute-start.22
  501.2 4.5 collective-permute-start.35
  510.2 10.5 %collective-permute-start.41 = (f32[4,4,256]{1,2,0:T(8,128)S(1)}, f32[4,4,256]{1,2,0:T(8,128)S(1)}, u32[]{:S(2)}, u32[]{:S(2)}) collective-permute-start(f32[4,4,256]{1,2,0:T(8,128)S(1)} %get-tuple-element.46), channel_id=1, source_target_pairs={{0,8},{8,16},{16,24},{1,9},{9,17},{17,25},{2,10},{10,18},{18,26},{... | collective-permute-start | bytes 49160 | tf_op jit(solution)/shard_map/ppermute | solution.py:25
  512.1 10.3 %collective-permute-start.42 = (f32[4,4,256]{1,2,0:T(8,128)S(1)}, f32[4,4,256]{1,2,0:T(8,128)S(1)}, u32[]{:S(2)}, u32[]{:S(2)}) collective-permute-start(f32[4,4,256]{1,2,0:T(8,128)S(1)} %get-tuple-element.47), channel_id=1, source_target_pairs={{8,0},{16,8},{24,16},{9,1},{17,9},{25,17},{10,2},{18,10},{26,18},{... | collective-permute-start | bytes 49160 | tf_op jit(solution)/shard_map/ppermute | solution.py:28
  522.6 6.9 collective-permute-start.43
  524.5 6.3 collective-permute-start.44
  678.0 10.4 %collective-permute-start.45 = (f32[4,4,256]{2,1,0:T(4,128)S(1)}, f32[4,4,256]{2,1,0:T(4,128)S(1)}, u32[]{:S(2)}, u32[]{:S(2)}) collective-permute-start(f32[4,4,256]{2,1,0:T(4,128)S(1)} %get-tuple-element.44), channel_id=1, source_target_pairs={{0,8},{8,16},{16,24},{1,9},{9,17},{17,25},{2,10},{10,18},{18,26},{... | collective-permute-start | bytes 49160 | tf_op jit(solution)/shard_map/ppermute | solution.py:25
  680.0 9.9 collective-permute-start.46
  693.6 27.9 %collective-permute-start.47 = (f32[4,264,4]{1,2,0:T(4,128)S(1)}, f32[4,264,4]{1,2,0:T(4,128)S(1)}, u32[]{:S(2)}, u32[]{:S(2)}) collective-permute-start(f32[4,264,4]{1,2,0:T(4,128)S(1)} %copy.47), channel_id=1, source_target_pairs={{0,1},{1,2},{2,3},{3,4},{4,5},{5,6},{6,7},{8,9},{9,10},{10,11},{11... | collective-permute-start | bytes 50696 | tf_op jit(solution)/shard_map/ppermute | solution.py:25
  695.8 25.9 %collective-permute-start.48 = (f32[4,264,4]{1,2,0:T(4,128)S(1)}, f32[4,264,4]{1,2,0:T(4,128)S(1)}, u32[]{:S(2)}, u32[]{:S(2)}) collective-permute-start(f32[4,264,4]{1,2,0:T(4,128)S(1)} %copy.48), channel_id=1, source_target_pairs={{1,0},{2,1},{3,2},{4,3},{5,4},{6,5},{7,6},{9,8},{10,9},{11,10},{12... | collective-permute-start | bytes 50696 | tf_op jit(solution)/shard_map/ppermute | solution.py:28
  716.2 4.6 collective-permute-start.40
  746.9 4.5 collective-permute-start.53
  755.9 10.5 %collective-permute-start.59 = (f32[4,4,256]{1,2,0:T(8,128)S(1)}, f32[4,4,256]{1,2,0:T(8,128)S(1)}, u32[]{:S(2)}, u32[]{:S(2)}) collective-permute-start(f32[4,4,256]{1,2,0:T(8,128)S(1)} %get-tuple-element.42), channel_id=1, source_target_pairs={{0,8},{8,16},{16,24},{1,9},{9,17},{17,25},{2,10},{10,18},{18,26},{... | collective-permute-start | bytes 49160 | tf_op jit(solution)/shard_map/ppermute | solution.py:25
  757.9 10.3 %collective-permute-start.60 = (f32[4,4,256]{1,2,0:T(8,128)S(1)}, f32[4,4,256]{1,2,0:T(8,128)S(1)}, u32[]{:S(2)}, u32[]{:S(2)}) collective-permute-start(f32[4,4,256]{1,2,0:T(8,128)S(1)} %get-tuple-element.43), channel_id=1, source_target_pairs={{8,0},{16,8},{24,16},{9,1},{17,9},{25,17},{10,2},{18,10},{26,18},{... | collective-permute-start | bytes 49160 | tf_op jit(solution)/shard_map/ppermute | solution.py:28
  768.3 7.2 collective-permute-start.61
  770.2 6.3 collective-permute-start.62
  923.7 10.4 %collective-permute-start.63 = (f32[4,4,256]{2,1,0:T(4,128)S(1)}, f32[4,4,256]{2,1,0:T(4,128)S(1)}, u32[]{:S(2)}, u32[]{:S(2)}) collective-permute-start(f32[4,4,256]{2,1,0:T(4,128)S(1)} %get-tuple-element.40), channel_id=1, source_target_pairs={{0,8},{8,16},{16,24},{1,9},{9,17},{17,25},{2,10},{10,18},{18,26},{... | collective-permute-start | bytes 49160 | tf_op jit(solution)/shard_map/ppermute | solution.py:25
  925.7 9.9 collective-permute-start.64
  939.3 27.8 %collective-permute-start.65 = (f32[4,264,4]{1,2,0:T(4,128)S(1)}, f32[4,264,4]{1,2,0:T(4,128)S(1)}, u32[]{:S(2)}, u32[]{:S(2)}) collective-permute-start(f32[4,264,4]{1,2,0:T(4,128)S(1)} %copy.57), channel_id=1, source_target_pairs={{0,1},{1,2},{2,3},{3,4},{4,5},{5,6},{6,7},{8,9},{9,10},{10,11},{11... | collective-permute-start | bytes 50696 | tf_op jit(solution)/shard_map/ppermute | solution.py:25
  941.4 25.9 %collective-permute-start.66 = (f32[4,264,4]{1,2,0:T(4,128)S(1)}, f32[4,264,4]{1,2,0:T(4,128)S(1)}, u32[]{:S(2)}, u32[]{:S(2)}) collective-permute-start(f32[4,264,4]{1,2,0:T(4,128)S(1)} %copy.58), channel_id=1, source_target_pairs={{1,0},{2,1},{3,2},{4,3},{5,4},{6,5},{7,6},{9,8},{10,9},{11,10},{12... | collective-permute-start | bytes 50696 | tf_op jit(solution)/shard_map/ppermute | solution.py:28
  961.9 4.6 collective-permute-start.58
  (47 other events, 331.8 us)

commit v2 on v1

--- a/solution.py
+++ b/solution.py
@@ -70,8 +70,41 @@
     return value
 
 
+def sum_steps(axes):
+    steps = []
+    for axis in axes:
+        count = lax.axis_size(axis)
+        if count & (count - 1):
+            steps.append(lambda value, axis=axis: lax.psum(value, axis))
+            continue
+        stride = 1
+        while stride < count:
+            pairs = [(i, i ^ stride) for i in range(count)]
+            steps.append(lambda value, axis=axis, pairs=pairs: value + lax.ppermute(value, axis, pairs))
+            stride *= 2
+    return steps
+
+
 def global_sum(local_value):
-    return butterfly_sum(butterfly_sum(local_value, "gx"), "gy")
+    for step in sum_steps(("gx", "gy")):
+        local_value = step(local_value)
+    return local_value
+
+
+def advance(carry, value):
+    total, steps = carry
+    if steps:
+        total = steps[0](total)
+        steps = steps[1:]
+    total, value = lax.optimization_barrier((total, value))
+    return (total, steps), value
+
+
+def finish(carry):
+    total, steps = carry
+    for step in steps:
+        total = step(total)
+    return total
 
 
 def with_rim(field):
@@ -119,8 +152,9 @@
     landing = (
         wanted_ids.reshape(-1)[None, :] == jnp.arange(own_blocks, dtype=jnp.int32)[:, None]
     ).astype(jnp.float32)
-    def apply_op(direction):
+    def apply_op(direction, carry):
         synthesize_padded = with_rim(direction)
+        carry, synthesize_padded = advance(carry, synthesize_padded)
         along_rows = jnp.einsum("lab,ac->lcb", synthesize_padded, synth_rows, precision=highest)
         blocks = (
             jnp.einsum("lab,bc->lac", along_rows, synth_cols, precision=highest)
@@ -129,7 +163,9 @@
             .reshape(own_blocks, block_rows, block_cols)
         )
         outgoing = jnp.take(blocks, wanted_ids, axis=0, mode="fill", fill_value=0.0)
+        carry, outgoing = advance(carry, outgoing)
         arrived = lax.all_to_all(outgoing, "gy", split_axis=0, concat_axis=0, tiled=True)
+        carry, arrived = advance(carry, arrived)
         seen = arrived[target, slot].reshape(
             sensors, rows_blocks * cols_blocks, layers, block_rows, block_cols
         )
@@ -138,7 +174,9 @@
             requests, block_rows, block_cols
         )
         returning = jnp.take(back, slot_source, axis=0, mode="fill", fill_value=0.0)
+        carry, returning = advance(carry, returning)
         landed = lax.all_to_all(returning, "gy", split_axis=0, concat_axis=0, tiled=True)
+        carry, landed = advance(carry, landed)
         summed = jnp.dot(
             landing, landed.reshape(owners * capacity, block_rows * block_cols), precision=highest
         )
@@ -151,22 +189,22 @@
         return (
             jnp.einsum("lab,ac->lcb", along_cols, analysis_rows, precision=highest)
             + prior_weight * direction
-        )
+        ), finish(carry)
 
     solution = jnp.zeros_like(right_side)
     residual = right_side
     precond_res = jacobi_inverse * residual
     direction = precond_res
-    rho_now = global_sum(jnp.sum(residual * precond_res))
-    image = apply_op(direction)
+    image, rho_now = apply_op(direction, (jnp.sum(residual * precond_res), sum_steps(("gx", "gy"))))
     for step in range(ITERS):
         step_size = rho_now / global_sum(jnp.sum(direction * image))
         solution = solution + step_size * direction
         residual = residual - step_size * image
         if step + 1 < ITERS:
             precond_res = jacobi_inverse * residual
-            rho_next = global_sum(jnp.sum(residual * precond_res))
-            applied = apply_op(precond_res)
+            applied, rho_next = apply_op(
+                precond_res, (jnp.sum(residual * precond_res), sum_steps(("gx", "gy")))
+            )
             ratio = rho_next / rho_now
             direction = precond_res + ratio * direction
             image = applied + ratio * image

time: 1020 us -> 1010 us (level)
  blocking collectives: 316 us -> 0 us
  starting transfers between devices: 207 us -> 499 us
  other arithmetic: 39.3 us -> 56.1 us
    all_to_all x6 -> x0, blocking collectives: 316 us -> none  [the longest x3 163 us: apply_op(): lax.all_to_all(returning, 'gy', split_axis=0, concat_axis=0, tiled=True)]
    ppermute x40, starting transfers between devices: 65.2 us -> 342 us  [sum_steps(): lax.ppermute(value, axis, pairs)]
    all_to_all x1 -> x4, waiting for transfers between devices: 40.1 us -> 126 us  [apply_op(): lax.all_to_all(outgoing, 'gy', split_axis=0, concat_axis=0, tiled=True)]
    all_to_all x1 -> x4, waiting for transfers between devices: 45.8 us -> 0.01 us  [apply_op(): lax.all_to_all(returning, 'gy', split_axis=0, concat_axis=0, tiled=True)]
    ppermute x40, waiting for transfers between devices: 56.3 us -> 29.4 us  [sum_steps(): lax.ppermute(value, axis, pairs)]
    all_to_all x1 -> x4, starting transfers between devices: 6.57 us -> 21.9 us  [apply_op(): lax.all_to_all(outgoing, 'gy', split_axis=0, concat_axis=0, tiled=True)]
    ppermute x16, starting transfers between devices: 89 us -> 73.8 us  [extended(): lax.ppermute(lax.slice_in_dim(block, 0, width, axis=dim), axis, backward)]
    ppermute x16, waiting for transfers between devices: 22.8 us -> 8.84 us  [extended(): lax.ppermute(lax.slice_in_dim(block, block.shape[dim] - width, None, axis...]
  transfers between devices with their start and end apart: 75 -> 81, of which waited for: 50 -> 38; matrix products, arithmetic and copies ran while one was open for 1% -> 8% of each run, Pallas kernels for 0% -> 0%
where the time goes in v2:
time: 1010 us; the launch traced here: 999 us
  starting transfers between devices  499 us (49%)
  waiting for transfers between devices  176 us (17%)
  local copies, waits for them, and re-layouts  139 us (14%)
  matrix products  96.7 us (10%)
  other arithmetic  56.1 us (6%)
  between operations  31.2 us (3%)
    ppermute x40, starting transfers between devices, sum_steps(): lax.ppermute(value, axis, pairs)  342 us
    all_to_all x4, waiting for transfers between devices, apply_op(): lax.all_to_all(outgoing, 'gy', split_axis=0, concat_axis=0, tiled=True)  126 us
    ppermute x16, starting transfers between devices, extended(): lax.ppermute(lax.slice_in_dim(block, 0, width, axis=dim), axis, backward)  73.8 us
    ppermute x16, starting transfers between devices, extended(): lax.ppermute(lax.slice_in_dim(block, block.shape[dim] - width, None, axis...  37.5 us
    ppermute x40, waiting for transfers between devices, sum_steps(): lax.ppermute(value, axis, pairs)  29.4 us
    all_to_all x4, starting transfers between devices, apply_op(): lax.all_to_all(outgoing, 'gy', split_axis=0, concat_axis=0, tiled=True)  21.9 us
  transfers between devices with their start and end apart: 81, of which 38 were waited for; matrix products, arithmetic and copies ran while one was open for 8% of the time, Pallas kernels for 0%

profile of v2, /device:TPU:10, one launch (start us, length us, event | category | flops | bytes accessed | tf_op | source)
XLA Modules:
  0.0 998.6 jit_solution(14570596201897019970)
XLA Ops:
  3.4 10.2 %scatter_fusion = s32[8,9]{1,0:T(8,128)} fusion(s32[8,9]{1,0:T(8,128)} %broadcast_in_dim.425, s32[64]{0:T(128)S(1)} %fusion.134, s32[64]{0:T(128)S(1)} %get-tuple-element.97), kind=kCustom, calls=%fused_computation.12 | custom fusion | bytes 1280 | tf_op jit(solution)/shard_map/scatter | solution.py:141
  13.6 6.3 all-to-all-start
  35.7 4.1 collective-permute-done.3
  57.7 5.4 all-to-all-start.1
  66.7 15.3 %collective-permute-start.6 = (f32[]{:T(128)}, f32[]{:T(128)}, u32[]{:S(2)}, u32[]{:S(2)}) collective-permute-start(f32[]{:T(128)} %add.909), channel_id=1, source_target_pairs={{0,1},{1,0},{2,3},{3,2},{4,5},{5,4},{6,7},{7,6},{8,9},{9,8},{10,11... | collective-permute-start | bytes 20 | tf_op jit(solution)/shard_map/ppermute | solution.py:83
  82.7 31.8 %all-to-all-done.1 = f32[8,9,64,128]{3,2,1,0:T(8,128)} async-done(((f32[8,9,64,128]{3,2,1,0:T(8,128)}), f32[8,9,64,128]{3,2,1,0:T(8,128)}, u32[]{:S(2)}, u32[]{:S(2)}) %all-to-all-start.1) | async-done | bytes 2359328 | tf_op jit(solution)/shard_map/all_to_all | solution.py:167
  114.4 3.9 collective-permute-start.7
  136.2 4.3 all-to-all-start.2
  141.9 49.3 %collective-permute-start.8 = (f32[]{:T(128)}, f32[]{:T(128)}, u32[]{:S(2)}, u32[]{:S(2)}) collective-permute-start(f32[]{:T(128)} %add.932), channel_id=1, source_target_pairs={{0,4},{1,5},{2,6},{3,7},{4,0},{5,1},{6,2},{7,3},{8,12},{9,13},{10,... | collective-permute-start | bytes 20 | tf_op jit(solution)/shard_map/ppermute | solution.py:83
  203.8 14.3 %collective-permute-start.10 = (f32[4,4,256]{2,1,0:T(4,128)S(1)}, f32[4,4,256]{2,1,0:T(4,128)S(1)}, u32[]{:S(2)}, u32[]{:S(2)}) collective-permute-start(f32[4,4,256]{2,1,0:T(4,128)S(1)} %get-tuple-element.131), channel_id=1, source_target_pairs={{8,0},{16,8},{24,16},{9,1},{17,9},{25,17},{10,2},{18,10},{26,18},{... | collective-permute-start | bytes 49160 | tf_op jit(solution)/shard_map/ppermute | solution.py:28
  220.8 5.4 collective-permute-start.12
  228.2 4.7 collective-permute-done.11
  234.2 3.8 fusion.8
  277.7 4.8 collective-permute-start.22
  291.8 3.8 fusion.154
  310.4 4.7 all-to-all-start.3
  315.2 18.5 %collective-permute-start.24 = (f32[]{:T(128)}, f32[]{:T(128)}, u32[]{:S(2)}, u32[]{:S(2)}) collective-permute-start(f32[]{:T(128)} %add.952), channel_id=1, source_target_pairs={{0,1},{1,0},{2,3},{3,2},{4,5},{5,4},{6,7},{7,6},{8,9},{9,8},{10,11... | collective-permute-start | bytes 20 | tf_op jit(solution)/shard_map/ppermute | solution.py:83
  334.4 31.0 %all-to-all-done.3 = f32[8,9,64,128]{3,2,1,0:T(8,128)} async-done(((f32[8,9,64,128]{3,2,1,0:T(8,128)}), f32[8,9,64,128]{3,2,1,0:T(8,128)}, u32[]{:S(2)}, u32[]{:S(2)}) %all-to-all-start.3) | async-done | bytes 2359328 | tf_op jit(solution)/shard_map/all_to_all | solution.py:167
  372.6 3.8 collective-permute-start.25
  387.1 4.3 all-to-all-start.4
  391.5 50.6 %collective-permute-start.26 = (f32[]{:T(128)}, f32[]{:T(128)}, u32[]{:S(2)}, u32[]{:S(2)}) collective-permute-start(f32[]{:T(128)} %add.954), channel_id=1, source_target_pairs={{0,4},{1,5},{2,6},{3,7},{4,0},{5,1},{6,2},{7,3},{8,12},{9,13},{10,... | collective-permute-start | bytes 20 | tf_op jit(solution)/shard_map/ppermute | solution.py:83
  468.0 4.9 collective-permute-start.30
  475.3 3.8 fusion.18
  479.2 3.8 multiply_reduce_fusion.4
  489.9 4.1 collective-permute-start.33
  518.0 3.8 collective-permute-start.39
  534.6 3.8 fusion.151
  553.1 6.0 all-to-all-start.5
  559.2 18.5 %collective-permute-start.42 = (f32[]{:T(128)}, f32[]{:T(128)}, u32[]{:S(2)}, u32[]{:S(2)}) collective-permute-start(f32[]{:T(128)} %add.966), channel_id=1, source_target_pairs={{0,1},{1,0},{2,3},{3,2},{4,5},{5,4},{6,7},{7,6},{8,9},{9,8},{10,11... | collective-permute-start | bytes 20 | tf_op jit(solution)/shard_map/ppermute | solution.py:83
  578.3 31.8 %all-to-all-done.5 = f32[8,9,64,128]{3,2,1,0:T(8,128)} async-done(((f32[8,9,64,128]{3,2,1,0:T(8,128)}), f32[8,9,64,128]{3,2,1,0:T(8,128)}, u32[]{:S(2)}, u32[]{:S(2)}) %all-to-all-start.5) | async-done | bytes 2359328 | tf_op jit(solution)/shard_map/all_to_all | solution.py:167
  617.3 4.1 collective-permute-start.43
  632.0 4.3 all-to-all-start.6
  636.4 50.4 %collective-permute-start.44 = (f32[]{:T(128)}, f32[]{:T(128)}, u32[]{:S(2)}, u32[]{:S(2)}) collective-permute-start(f32[]{:T(128)} %add.968), channel_id=1, source_target_pairs={{0,4},{1,5},{2,6},{3,7},{4,0},{5,1},{6,2},{7,3},{8,12},{9,13},{10,... | collective-permute-start | bytes 20 | tf_op jit(solution)/shard_map/ppermute | solution.py:83
  712.7 5.0 collective-permute-start.48
  720.0 3.9 fusion.28
  724.0 4.3 multiply_reduce_fusion.2
  735.0 4.0 collective-permute-start.51
  749.6 3.8 multiply_reduce_fusion.1
  779.4 3.8 fusion.148
  798.0 5.7 all-to-all-start.7
  803.8 18.5 %collective-permute-start.60 = (f32[]{:T(128)}, f32[]{:T(128)}, u32[]{:S(2)}, u32[]{:S(2)}) collective-permute-start(f32[]{:T(128)} %add.980), channel_id=1, source_target_pairs={{0,1},{1,0},{2,3},{3,2},{4,5},{5,4},{6,7},{7,6},{8,9},{9,8},{10,11... | collective-permute-start | bytes 20 | tf_op jit(solution)/shard_map/ppermute | solution.py:83
  822.9 31.8 %all-to-all-done.7 = f32[8,9,64,128]{3,2,1,0:T(8,128)} async-done(((f32[8,9,64,128]{3,2,1,0:T(8,128)}), f32[8,9,64,128]{3,2,1,0:T(8,128)}, u32[]{:S(2)}, u32[]{:S(2)}) %all-to-all-start.7) | async-done | bytes 2359328 | tf_op jit(solution)/shard_map/all_to_all | solution.py:167
  861.9 4.1 collective-permute-start.61
  876.6 4.3 all-to-all-start.8
  881.0 50.4 %collective-permute-start.62 = (f32[]{:T(128)}, f32[]{:T(128)}, u32[]{:S(2)}, u32[]{:S(2)}) collective-permute-start(f32[]{:T(128)} %add.982), channel_id=1, source_target_pairs={{0,4},{1,5},{2,6},{3,7},{4,0},{5,1},{6,2},{7,3},{8,12},{9,13},{10,... | collective-permute-start | bytes 20 | tf_op jit(solution)/shard_map/ppermute | solution.py:83
  957.3 5.0 collective-permute-start.66
  964.7 3.9 fusion.38
  979.2 4.0 collective-permute-start.69
  (322 shorter events, 394.9 us)
Async XLA Ops:
  13.6 15.3 %all-to-all-start = ((s32[8,1,9]{2,1,0:T(1,128)}), s32[8,1,9]{2,1,0:T(1,128)S(1)}, u32[]{:S(2)}, u32[]{:S(2)}) async-start(s32[8,1,9]{2,1,0:T(1,128)} %bitcast.3), calls=%async_computation | async-start | bytes 8192 | tf_op jit(solution)/shard_map/all_to_all | solution.py:146
  22.0 5.7 collective-permute-start
  22.0 7.0 collective-permute-start.1
  29.9 10.2 %collective-permute-start.4 = (f32[4,264,4]{1,2,0:T(4,128)S(1)}, f32[4,264,4]{1,2,0:T(4,128)S(1)}, u32[]{:S(2)}, u32[]{:S(2)}) collective-permute-start(f32[4,264,4]{1,2,0:T(4,128)S(1)} %copy.20), channel_id=1, source_target_pairs={{1,0},{2,1},{3,2},{4,3},{5,4},{6,5},{7,6},{9,8},{10,9},{11,10},{12... | collective-permute-start | bytes 50696 | tf_op jit(solution)/shard_map/ppermute | solution.py:28
  33.2 6.6 collective-permute-start.3
  50.3 6.7 collective-permute-start.5
  57.7 56.7 %all-to-all-start.1 = ((f32[8,9,64,128]{3,2,1,0:T(8,128)}), f32[8,9,64,128]{3,2,1,0:T(8,128)}, u32[]{:S(2)}, u32[]{:S(2)}) async-start(f32[8,9,64,128]{3,2,1,0:T(8,128)} %broadcast_select_fusion.7), calls=%async_computation.1 | async-start | bytes 4718592 | tf_op jit(solution)/shard_map/all_to_all | solution.py:167
  66.7 15.3 %collective-permute-start.6 = (f32[]{:T(128)}, f32[]{:T(128)}, u32[]{:S(2)}, u32[]{:S(2)}) collective-permute-start(f32[]{:T(128)} %add.909), channel_id=1, source_target_pairs={{0,1},{1,0},{2,3},{3,2},{4,5},{5,4},{6,7},{7,6},{8,9},{9,8},{10,11... | collective-permute-start | bytes 20 | tf_op jit(solution)/shard_map/ppermute | solution.py:83
  114.4 21.2 %collective-permute-start.7 = (f32[]{:T(128)}, f32[]{:T(128)}, u32[]{:S(2)}, u32[]{:S(2)}) collective-permute-start(f32[]{:T(128)} %add.931), channel_id=1, source_target_pairs={{0,2},{1,3},{2,0},{3,1},{4,6},{5,7},{6,4},{7,5},{8,10},{9,11},{10,... | collective-permute-start | bytes 20 | tf_op jit(solution)/shard_map/ppermute | solution.py:83
  136.2 55.6 %all-to-all-start.2 = ((f32[8,9,64,128]{3,2,1,0:T(8,128)}), f32[8,9,64,128]{3,2,1,0:T(8,128)}, u32[]{:S(2)}, u32[]{:S(2)}) async-start(f32[8,9,64,128]{3,2,1,0:T(8,128)} %broadcast_select_fusion.6), calls=%async_computation.2 | async-start | bytes 4718592 | tf_op jit(solution)/shard_map/all_to_all | solution.py:178
  141.9 49.3 %collective-permute-start.8 = (f32[]{:T(128)}, f32[]{:T(128)}, u32[]{:S(2)}, u32[]{:S(2)}) collective-permute-start(f32[]{:T(128)} %add.932), channel_id=1, source_target_pairs={{0,4},{1,5},{2,6},{3,7},{4,0},{5,1},{6,2},{7,3},{8,12},{9,13},{10,... | collective-permute-start | bytes 20 | tf_op jit(solution)/shard_map/ppermute | solution.py:83
  201.9 16.2 %collective-permute-start.9 = (f32[4,4,256]{2,1,0:T(4,128)S(1)}, f32[4,4,256]{2,1,0:T(4,128)S(1)}, u32[]{:S(2)}, u32[]{:S(2)}) collective-permute-start(f32[4,4,256]{2,1,0:T(4,128)S(1)} %get-tuple-element.130), channel_id=1, source_target_pairs={{0,8},{8,16},{16,24},{1,9},{9,17},{17,25},{2,10},{10,18},{18,26},{... | collective-permute-start | bytes 49160 | tf_op jit(solution)/shard_map/ppermute | solution.py:25
  203.8 14.3 %collective-permute-start.10 = (f32[4,4,256]{2,1,0:T(4,128)S(1)}, f32[4,4,256]{2,1,0:T(4,128)S(1)}, u32[]{:S(2)}, u32[]{:S(2)}) collective-permute-start(f32[4,4,256]{2,1,0:T(4,128)S(1)} %get-tuple-element.131), channel_id=1, source_target_pairs={{8,0},{16,8},{24,16},{9,1},{17,9},{25,17},{10,2},{18,10},{26,18},{... | collective-permute-start | bytes 49160 | tf_op jit(solution)/shard_map/ppermute | solution.py:28
  220.8 12.3 %collective-permute-start.12 = (f32[4,264,4]{1,2,0:T(4,128)S(1)}, f32[4,264,4]{1,2,0:T(4,128)S(1)}, u32[]{:S(2)}, u32[]{:S(2)}) collective-permute-start(f32[4,264,4]{1,2,0:T(4,128)S(1)} %copy.29), channel_id=1, source_target_pairs={{1,0},{2,1},{3,2},{4,3},{5,4},{6,5},{7,6},{9,8},{10,9},{11,10},{12... | collective-permute-start | bytes 50696 | tf_op jit(solution)/shard_map/ppermute | solution.py:28
  226.3 6.6 collective-permute-start.11
  275.5 9.6 collective-permute-start.21
  277.7 7.7 collective-permute-start.22
  300.6 9.2 collective-permute-start.23
  310.4 54.9 %all-to-all-start.3 = ((f32[8,9,64,128]{3,2,1,0:T(8,128)}), f32[8,9,64,128]{3,2,1,0:T(8,128)}, u32[]{:S(2)}, u32[]{:S(2)}) async-start(f32[8,9,64,128]{3,2,1,0:T(8,128)} %broadcast_select_fusion.5), calls=%async_computation.3 | async-start | bytes 4718592 | tf_op jit(solution)/shard_map/all_to_all | solution.py:167
  315.2 18.5 %collective-permute-start.24 = (f32[]{:T(128)}, f32[]{:T(128)}, u32[]{:S(2)}, u32[]{:S(2)}) collective-permute-start(f32[]{:T(128)} %add.952), channel_id=1, source_target_pairs={{0,1},{1,0},{2,3},{3,2},{4,5},{5,4},{6,7},{7,6},{8,9},{9,8},{10,11... | collective-permute-start | bytes 20 | tf_op jit(solution)/shard_map/ppermute | solution.py:83
  372.6 13.9 %collective-permute-start.25 = (f32[]{:T(128)}, f32[]{:T(128)}, u32[]{:S(2)}, u32[]{:S(2)}) collective-permute-start(f32[]{:T(128)} %add.953), channel_id=1, source_target_pairs={{0,2},{1,3},{2,0},{3,1},{4,6},{5,7},{6,4},{7,5},{8,10},{9,11},{10,... | collective-permute-start | bytes 20 | tf_op jit(solution)/shard_map/ppermute | solution.py:83
  387.1 55.6 %all-to-all-start.4 = ((f32[8,9,64,128]{3,2,1,0:T(8,128)}), f32[8,9,64,128]{3,2,1,0:T(8,128)}, u32[]{:S(2)}, u32[]{:S(2)}) async-start(f32[8,9,64,128]{3,2,1,0:T(8,128)} %broadcast_select_fusion.4), calls=%async_computation.4 | async-start | bytes 4718592 | tf_op jit(solution)/shard_map/all_to_all | solution.py:178
  391.5 50.6 %collective-permute-start.26 = (f32[]{:T(128)}, f32[]{:T(128)}, u32[]{:S(2)}, u32[]{:S(2)}) collective-permute-start(f32[]{:T(128)} %add.954), channel_id=1, source_target_pairs={{0,4},{1,5},{2,6},{3,7},{4,0},{5,1},{6,2},{7,3},{8,12},{9,13},{10,... | collective-permute-start | bytes 20 | tf_op jit(solution)/shard_map/ppermute | solution.py:83
  465.2 7.8 collective-permute-start.29
  468.0 6.2 collective-permute-start.30
  508.5 5.6 collective-permute-start.37
  518.0 9.6 collective-permute-start.39
  522.1 5.8 collective-permute-start.40
  543.4 9.2 collective-permute-start.41
  553.1 57.0 %all-to-all-start.5 = ((f32[8,9,64,128]{3,2,1,0:T(8,128)}), f32[8,9,64,128]{3,2,1,0:T(8,128)}, u32[]{:S(2)}, u32[]{:S(2)}) async-start(f32[8,9,64,128]{3,2,1,0:T(8,128)} %broadcast_select_fusion.3), calls=%async_computation.5 | async-start | bytes 4718592 | tf_op jit(solution)/shard_map/all_to_all | solution.py:167
  559.2 18.5 %collective-permute-start.42 = (f32[]{:T(128)}, f32[]{:T(128)}, u32[]{:S(2)}, u32[]{:S(2)}) collective-permute-start(f32[]{:T(128)} %add.966), channel_id=1, source_target_pairs={{0,1},{1,0},{2,3},{3,2},{4,5},{5,4},{6,7},{7,6},{8,9},{9,8},{10,11... | collective-permute-start | bytes 20 | tf_op jit(solution)/shard_map/ppermute | solution.py:83
  617.3 14.2 %collective-permute-start.43 = (f32[]{:T(128)}, f32[]{:T(128)}, u32[]{:S(2)}, u32[]{:S(2)}) collective-permute-start(f32[]{:T(128)} %add.967), channel_id=1, source_target_pairs={{0,2},{1,3},{2,0},{3,1},{4,6},{5,7},{6,4},{7,5},{8,10},{9,11},{10,... | collective-permute-start | bytes 20 | tf_op jit(solution)/shard_map/ppermute | solution.py:83
  632.0 55.3 %all-to-all-start.6 = ((f32[8,9,64,128]{3,2,1,0:T(8,128)}), f32[8,9,64,128]{3,2,1,0:T(8,128)}, u32[]{:S(2)}, u32[]{:S(2)}) async-start(f32[8,9,64,128]{3,2,1,0:T(8,128)} %broadcast_select_fusion.2), calls=%async_computation.6 | async-start | bytes 4718592 | tf_op jit(solution)/shard_map/all_to_all | solution.py:178
  636.4 50.4 %collective-permute-start.44 = (f32[]{:T(128)}, f32[]{:T(128)}, u32[]{:S(2)}, u32[]{:S(2)}) collective-permute-start(f32[]{:T(128)} %add.968), channel_id=1, source_target_pairs={{0,4},{1,5},{2,6},{3,7},{4,0},{5,1},{6,2},{7,3},{8,12},{9,13},{10,... | collective-permute-start | bytes 20 | tf_op jit(solution)/shard_map/ppermute | solution.py:83
  709.7 8.0 collective-permute-start.47
  712.7 6.3 collective-permute-start.48
  753.4 5.6 collective-permute-start.55
  762.8 9.6 collective-permute-start.57
  766.7 5.9 collective-permute-start.58
  788.3 9.2 collective-permute-start.59
  798.0 56.7 %all-to-all-start.7 = ((f32[8,9,64,128]{3,2,1,0:T(8,128)}), f32[8,9,64,128]{3,2,1,0:T(8,128)}, u32[]{:S(2)}, u32[]{:S(2)}) async-start(f32[8,9,64,128]{3,2,1,0:T(8,128)} %broadcast_select_fusion.1), calls=%async_computation.7 | async-start | bytes 4718592 | tf_op jit(solution)/shard_map/all_to_all | solution.py:167
  803.8 18.5 %collective-permute-start.60 = (f32[]{:T(128)}, f32[]{:T(128)}, u32[]{:S(2)}, u32[]{:S(2)}) collective-permute-start(f32[]{:T(128)} %add.980), channel_id=1, source_target_pairs={{0,1},{1,0},{2,3},{3,2},{4,5},{5,4},{6,7},{7,6},{8,9},{9,8},{10,11... | collective-permute-start | bytes 20 | tf_op jit(solution)/shard_map/ppermute | solution.py:83
  861.9 14.2 %collective-permute-start.61 = (f32[]{:T(128)}, f32[]{:T(128)}, u32[]{:S(2)}, u32[]{:S(2)}) collective-permute-start(f32[]{:T(128)} %add.981), channel_id=1, source_target_pairs={{0,2},{1,3},{2,0},{3,1},{4,6},{5,7},{6,4},{7,5},{8,10},{9,11},{10,... | collective-permute-start | bytes 20 | tf_op jit(solution)/shard_map/ppermute | solution.py:83
  876.6 55.3 %all-to-all-start.8 = ((f32[8,9,64,128]{3,2,1,0:T(8,128)}), f32[8,9,64,128]{3,2,1,0:T(8,128)}, u32[]{:S(2)}, u32[]{:S(2)}) async-start(f32[8,9,64,128]{3,2,1,0:T(8,128)} %broadcast_select_fusion), calls=%async_computation.8 | async-start | bytes 4718592 | tf_op jit(solution)/shard_map/all_to_all | solution.py:178
  881.0 50.4 %collective-permute-start.62 = (f32[]{:T(128)}, f32[]{:T(128)}, u32[]{:S(2)}, u32[]{:S(2)}) collective-permute-start(f32[]{:T(128)} %add.982), channel_id=1, source_target_pairs={{0,4},{1,5},{2,6},{3,7},{4,0},{5,1},{6,2},{7,3},{8,12},{9,13},{10,... | collective-permute-start | bytes 20 | tf_op jit(solution)/shard_map/ppermute | solution.py:83
  943.7 5.6 collective-permute-start.63
  954.4 8.0 collective-permute-start.65
  957.3 6.3 collective-permute-start.66
  (50 other events, 346.1 us)

commit v3 on v2

--- a/solution.py
+++ b/solution.py
@@ -91,9 +91,9 @@
     return local_value
 
 
-def advance(carry, value):
+def advance(carry, value, step=True):
     total, steps = carry
-    if steps:
+    if step and steps:
         total = steps[0](total)
         steps = steps[1:]
     total, value = lax.optimization_barrier((total, value))
@@ -162,10 +162,11 @@
             .transpose(0, 1, 3, 2, 4)
             .reshape(own_blocks, block_rows, block_cols)
         )
-        outgoing = jnp.take(blocks, wanted_ids, axis=0, mode="fill", fill_value=0.0)
+        blocks = jnp.concatenate([blocks, jnp.zeros((1, block_rows, block_cols), blocks.dtype)])
+        outgoing = jnp.take(blocks, wanted_ids, axis=0, mode="clip")
         carry, outgoing = advance(carry, outgoing)
         arrived = lax.all_to_all(outgoing, "gy", split_axis=0, concat_axis=0, tiled=True)
-        carry, arrived = advance(carry, arrived)
+        carry, arrived = advance(carry, arrived, step=False)
         seen = arrived[target, slot].reshape(
             sensors, rows_blocks * cols_blocks, layers, block_rows, block_cols
         )
@@ -173,10 +174,11 @@
         back = jnp.einsum("skxz,slyz->sklxy", slopes, interaction, precision=highest).reshape(
             requests, block_rows, block_cols
         )
-        returning = jnp.take(back, slot_source, axis=0, mode="fill", fill_value=0.0)
+        back = jnp.concatenate([back, jnp.zeros((1, block_rows, block_cols), back.dtype)])
+        returning = jnp.take(back, slot_source, axis=0, mode="clip")
         carry, returning = advance(carry, returning)
         landed = lax.all_to_all(returning, "gy", split_axis=0, concat_axis=0, tiled=True)
-        carry, landed = advance(carry, landed)
+        carry, landed = advance(carry, landed, step=False)
         summed = jnp.dot(
             landing, landed.reshape(owners * capacity, block_rows * block_cols), precision=highest
         )
@@ -185,6 +187,7 @@
             .transpose(0, 1, 3, 2, 4)
             .reshape(layers, tile_rows, tile_cols)
         )
+        carry, padded = advance(carry, padded)
         along_cols = jnp.einsum("lab,bc->lac", padded, analysis_cols, precision=highest)
         return (
             jnp.einsum("lab,ac->lcb", along_cols, analysis_rows, precision=highest)

time: 1010 us -> 1010 us (level)
  blocking collectives: 0 us -> 341 us
  starting transfers between devices: 499 us -> 178 us
  other arithmetic: 56.1 us -> 37.7 us
    all_to_all x0 -> x6, blocking collectives: none -> 341 us  [the longest x3 171 us: apply_op(): lax.all_to_all(returning, 'gy', split_axis=0, concat_axis=0, tiled=True)]
    ppermute x40, starting transfers between devices: 342 us -> 58.4 us  [sum_steps(): lax.ppermute(value, axis, pairs)]
    all_to_all x4 -> x1, waiting for transfers between devices: 126 us -> 45.9 us  [apply_op(): lax.all_to_all(outgoing, 'gy', split_axis=0, concat_axis=0, tiled=True)]
    all_to_all x4 -> x1, waiting for transfers between devices: 0.01 us -> 49.3 us  [apply_op(): lax.all_to_all(returning, 'gy', split_axis=0, concat_axis=0, tiled=True)]
    ppermute x40, waiting for transfers between devices: 29.4 us -> 58.8 us  [sum_steps(): lax.ppermute(value, axis, pairs)]
    select_n x10 -> x0, other arithmetic: 26.2 us -> none  [the longest x5 13.1 us: apply_op(): outgoing = jnp.take(blocks, wanted_ids, axis=0, mode='fill', fill_value=0.0)]
    all_to_all x4 -> x1, starting transfers between devices: 21.9 us -> 5.34 us  [apply_op(): lax.all_to_all(outgoing, 'gy', split_axis=0, concat_axis=0, tiled=True)]
    concatenate x0 -> x8, local copies, waits for them, and re-layouts: none -> 10.4 us  [the longest x4 5.99 us: apply_op(): jnp.concatenate([back, jnp.zeros((1, block_rows, block_cols), back.dtype)])]
  transfers between devices with their start and end apart: 81 -> 75, of which waited for: 38 -> 40; matrix products, arithmetic and copies ran while one was open for 8% -> 6% of each run, Pallas kernels for 0% -> 0%
where the time goes in v3:
time: 1010 us; the launch traced here: 993 us
  blocking collectives  341 us (34%)
  starting transfers between devices  178 us (18%)
  waiting for transfers between devices  168 us (17%)
  local copies, waits for them, and re-layouts  143 us (14%)
  matrix products  93.5 us (9%)
  other arithmetic  37.7 us (4%)
  between operations  31.2 us (3%)
    all_to_all x3, blocking collectives, apply_op(): lax.all_to_all(returning, 'gy', split_axis=0, concat_axis=0, tiled=True)  171 us
    all_to_all x3, blocking collectives, apply_op(): lax.all_to_all(outgoing, 'gy', split_axis=0, concat_axis=0, tiled=True)  170 us
    ppermute x16, starting transfers between devices, extended(): lax.ppermute(lax.slice_in_dim(block, 0, width, axis=dim), axis, backward)  67.9 us
    ppermute x40, waiting for transfers between devices, sum_steps(): lax.ppermute(value, axis, pairs)  58.8 us
    ppermute x40, starting transfers between devices, sum_steps(): lax.ppermute(value, axis, pairs)  58.4 us
    all_to_all x1, waiting for transfers between devices, apply_op(): lax.all_to_all(returning, 'gy', split_axis=0, concat_axis=0, tiled=True)  49.3 us
    all_to_all x1, waiting for transfers between devices, apply_op(): lax.all_to_all(outgoing, 'gy', split_axis=0, concat_axis=0, tiled=True)  45.9 us
    ppermute x16, starting transfers between devices, extended(): lax.ppermute(lax.slice_in_dim(block, block.shape[dim] - width, None, axis...  32.8 us
  transfers between devices with their start and end apart: 75, of which 40 were waited for; matrix products, arithmetic and copies ran while one was open for 6% of the time, Pallas kernels for 0%

profile of v3, /device:TPU:10, one launch (start us, length us, event | category | flops | bytes accessed | tf_op | source)
XLA Modules:
  0.0 993.2 jit_solution(14670828173016475252)
XLA Ops:
  3.4 10.2 %scatter_fusion = s32[8,9]{1,0:T(8,128)} fusion(s32[8,9]{1,0:T(8,128)} %broadcast_in_dim.421, s32[64]{0:T(128)S(1)} %fusion.91, s32[64]{0:T(128)S(1)} %get-tuple-element.111), kind=kCustom, calls=%fused_computation.12 | custom fusion | bytes 1280 | tf_op jit(solution)/shard_map/scatter | solution.py:141
  13.6 6.3 all-to-all-start
  37.0 4.1 collective-permute-done.3
  42.3 3.6 convolution_bitcast_fusion.3
  58.0 5.3 all-to-all-start.1
  66.9 45.9 %all-to-all-done.1 = f32[8,9,64,128]{3,2,1,0:T(8,128)} async-done(((f32[8,9,64,128]{3,2,1,0:T(8,128)}), f32[8,9,64,128]{3,2,1,0:T(8,128)}, u32[]{:S(2)}, u32[]{:S(2)}) %all-to-all-start.1) | async-done | bytes 2359328 | tf_op jit(solution)/shard_map/all_to_all | solution.py:168
  115.4 3.7 gather_fusion.1
  125.9 3.7 gather_fusion.2
  130.2 7.6 all-to-all-start.2
  137.8 49.3 %all-to-all-done.2 = f32[8,9,64,128]{3,2,1,0:T(8,128)} async-done(((f32[8,9,64,128]{3,2,1,0:T(8,128)}), f32[8,9,64,128]{3,2,1,0:T(8,128)}, u32[]{:S(2)}, u32[]{:S(2)}) %all-to-all-start.2) | async-done | bytes 2359328 | tf_op jit(solution)/shard_map/all_to_all | solution.py:180
  199.1 3.6 collective-permute-start.9
  206.8 6.5 collective-permute-start.11
  225.1 3.7 multiply_reduce_fusion.6
  249.9 3.7 multiply_reduce_fusion.5
  255.6 3.6 collective-permute-start.20
  265.7 4.4 collective-permute-start.22
  279.4 3.8 fusion.111
  294.9 57.8 %all_to_all.49 = f32[8,9,64,128]{3,2,1,0:T(8,128)} all-to-all(f32[8,9,64,128]{3,2,1,0:T(8,128)} %bitcast.255), channel_id=1, replica_groups=mesh['gx'=4,'gy'=8] {'gy'}, dimensions={0} | all-to-all | bytes 4718592 | tf_op jit(solution)/shard_map/all_to_all | solution.py:168
  352.8 3.7 gather_fusion.4
  364.8 3.7 gather_fusion.5
  369.1 56.8 %all_to_all.50 = f32[8,9,64,128]{3,2,1,0:T(8,128)S(1)} all-to-all(f32[8,9,64,128]{3,2,1,0:T(8,128)} %bitcast.256), channel_id=1, replica_groups=mesh['gx'=4,'gy'=8] {'gy'}, dimensions={0} | all-to-all | bytes 4718592 | tf_op jit(solution)/shard_map/all_to_all | solution.py:180
  437.9 3.6 collective-permute-start.27
  449.0 4.8 collective-permute-start.29
  469.8 5.6 multiply_reduce_fusion.4
  496.1 3.8 multiply_reduce_fusion.3
  501.8 3.6 collective-permute-start.38
  511.5 5.2 collective-permute-start.40
  522.7 3.6 convolution_bitcast_fusion.1
  526.4 3.8 fusion.108
  541.9 56.3 %all_to_all.51 = f32[8,9,64,128]{3,2,1,0:T(8,128)} all-to-all(f32[8,9,64,128]{3,2,1,0:T(8,128)} %bitcast.257), channel_id=1, replica_groups=mesh['gx'=4,'gy'=8] {'gy'}, dimensions={0} | all-to-all | bytes 4718592 | tf_op jit(solution)/shard_map/all_to_all | solution.py:168
  598.2 3.7 gather_fusion.7
  610.3 3.7 gather_fusion.8
  614.6 57.4 %all_to_all.52 = f32[8,9,64,128]{3,2,1,0:T(8,128)S(1)} all-to-all(f32[8,9,64,128]{3,2,1,0:T(8,128)} %bitcast.258), channel_id=1, replica_groups=mesh['gx'=4,'gy'=8] {'gy'}, dimensions={0} | all-to-all | bytes 4718592 | tf_op jit(solution)/shard_map/all_to_all | solution.py:180
  684.0 3.6 collective-permute-start.45
  695.1 4.8 collective-permute-start.47
  715.7 6.4 multiply_reduce_fusion.2
  742.7 3.7 multiply_reduce_fusion.1
  748.4 3.6 collective-permute-start.56
  758.1 5.2 collective-permute-start.58
  769.4 3.6 convolution_bitcast_fusion
  773.0 3.8 fusion.105
  788.5 56.2 %all_to_all.53 = f32[8,9,64,128]{3,2,1,0:T(8,128)} all-to-all(f32[8,9,64,128]{3,2,1,0:T(8,128)} %bitcast.253), channel_id=1, replica_groups=mesh['gx'=4,'gy'=8] {'gy'}, dimensions={0} | all-to-all | bytes 4718592 | tf_op jit(solution)/shard_map/all_to_all | solution.py:168
  844.7 3.7 gather_fusion.10
  856.8 3.7 gather_fusion.11
  861.0 56.9 %all_to_all.54 = f32[8,9,64,128]{3,2,1,0:T(8,128)S(1)} all-to-all(f32[8,9,64,128]{3,2,1,0:T(8,128)} %bitcast.254), channel_id=1, replica_groups=mesh['gx'=4,'gy'=8] {'gy'}, dimensions={0} | all-to-all | bytes 4718592 | tf_op jit(solution)/shard_map/all_to_all | solution.py:180
  930.0 3.6 collective-permute-start.63
  941.1 4.8 collective-permute-start.65
  961.8 6.3 multiply_reduce_fusion
  (295 shorter events, 345.6 us)
Async XLA Ops:
  13.6 15.4 %all-to-all-start = ((s32[8,1,9]{2,1,0:T(1,128)}), s32[8,1,9]{2,1,0:T(1,128)S(1)}, u32[]{:S(2)}, u32[]{:S(2)}) async-start(s32[8,1,9]{2,1,0:T(1,128)} %bitcast.7), calls=%async_computation | async-start | bytes 8192 | tf_op jit(solution)/shard_map/all_to_all | solution.py:146
  22.0 5.7 collective-permute-start
  22.0 8.2 collective-permute-start.1
  24.4 5.8 collective-permute-start.2
  31.1 10.2 %collective-permute-start.4 = (f32[4,264,4]{1,2,0:T(4,128)S(1)}, f32[4,264,4]{1,2,0:T(4,128)S(1)}, u32[]{:S(2)}, u32[]{:S(2)}) collective-permute-start(f32[4,264,4]{1,2,0:T(4,128)S(1)} %copy.20), channel_id=1, source_target_pairs={{1,0},{2,1},{3,2},{4,3},{5,4},{6,5},{7,6},{9,8},{10,9},{11,10},{12... | collective-permute-start | bytes 50696 | tf_op jit(solution)/shard_map/ppermute | solution.py:28
  34.5 6.6 collective-permute-start.3
  51.5 5.8 collective-permute-start.5
  58.0 54.8 %all-to-all-start.1 = ((f32[8,9,64,128]{3,2,1,0:T(8,128)}), f32[8,9,64,128]{3,2,1,0:T(8,128)}, u32[]{:S(2)}, u32[]{:S(2)}) async-start(f32[8,9,64,128]{3,2,1,0:T(8,128)} %bitcast.251), calls=%async_computation.1 | async-start | bytes 4718592 | tf_op jit(solution)/shard_map/all_to_all | solution.py:168
  112.8 16.8 %collective-permute-start.6 = (f32[]{:T(128)}, f32[]{:T(128)}, u32[]{:S(2)}, u32[]{:S(2)}) collective-permute-start(f32[]{:T(128)} %add.913), channel_id=1, source_target_pairs={{0,1},{1,0},{2,3},{3,2},{4,5},{5,4},{6,7},{7,6},{8,9},{9,8},{10,11... | collective-permute-start | bytes 20 | tf_op jit(solution)/shard_map/ppermute | solution.py:83
  130.2 57.0 %all-to-all-start.2 = ((f32[8,9,64,128]{3,2,1,0:T(8,128)}), f32[8,9,64,128]{3,2,1,0:T(8,128)}, u32[]{:S(2)}, u32[]{:S(2)}) async-start(f32[8,9,64,128]{3,2,1,0:T(8,128)} %bitcast.252), calls=%async_computation.2 | async-start | bytes 4718592 | tf_op jit(solution)/shard_map/all_to_all | solution.py:180
  197.1 5.6 collective-permute-start.8
  199.1 5.1 collective-permute-start.9
  206.8 13.4 %collective-permute-start.11 = (f32[4,264,4]{1,2,0:T(4,128)S(1)}, f32[4,264,4]{1,2,0:T(4,128)S(1)}, u32[]{:S(2)}, u32[]{:S(2)}) collective-permute-start(f32[4,264,4]{1,2,0:T(4,128)S(1)} %copy.29), channel_id=1, source_target_pairs={{1,0},{2,1},{3,2},{4,3},{5,4},{6,5},{7,6},{9,8},{10,9},{11,10},{12... | collective-permute-start | bytes 50696 | tf_op jit(solution)/shard_map/ppermute | solution.py:28
  213.4 6.6 collective-permute-start.10
  228.8 5.0 collective-permute-start.12
  253.6 5.6 collective-permute-start.19
  255.6 5.1 collective-permute-start.20
  263.1 9.7 collective-permute-start.21
  265.7 7.3 collective-permute-start.22
  287.2 7.1 collective-permute-start.23
  360.0 8.5 collective-permute-start.24
  436.0 5.6 collective-permute-start.26
  437.9 5.1 collective-permute-start.27
  446.7 11.5 %collective-permute-start.28 = (f32[4,264,4]{1,2,0:T(4,128)S(1)}, f32[4,264,4]{1,2,0:T(4,128)S(1)}, u32[]{:S(2)}, u32[]{:S(2)}) collective-permute-start(f32[4,264,4]{1,2,0:T(4,128)S(1)} %copy.40), channel_id=1, source_target_pairs={{0,1},{1,2},{2,3},{3,4},{4,5},{5,6},{6,7},{8,9},{9,10},{10,11},{11... | collective-permute-start | bytes 50696 | tf_op jit(solution)/shard_map/ppermute | solution.py:25
  449.0 9.4 collective-permute-start.29
  490.9 4.6 collective-permute-start.35
  499.8 5.6 collective-permute-start.37
  501.8 5.1 collective-permute-start.38
  509.3 10.1 %collective-permute-start.39 = (f32[4,264,4]{1,2,0:T(4,128)S(1)}, f32[4,264,4]{1,2,0:T(4,128)S(1)}, u32[]{:S(2)}, u32[]{:S(2)}) collective-permute-start(f32[4,264,4]{1,2,0:T(4,128)S(1)} %copy.44), channel_id=1, source_target_pairs={{0,1},{1,2},{2,3},{3,4},{4,5},{5,6},{6,7},{8,9},{9,10},{10,11},{11... | collective-permute-start | bytes 50696 | tf_op jit(solution)/shard_map/ppermute | solution.py:25
  511.5 8.1 collective-permute-start.40
  534.2 7.0 collective-permute-start.41
  605.4 8.6 collective-permute-start.42
  682.0 5.6 collective-permute-start.44
  684.0 5.1 collective-permute-start.45
  692.7 11.5 %collective-permute-start.46 = (f32[4,264,4]{1,2,0:T(4,128)S(1)}, f32[4,264,4]{1,2,0:T(4,128)S(1)}, u32[]{:S(2)}, u32[]{:S(2)}) collective-permute-start(f32[4,264,4]{1,2,0:T(4,128)S(1)} %copy.52), channel_id=1, source_target_pairs={{0,1},{1,2},{2,3},{3,4},{4,5},{5,6},{6,7},{8,9},{9,10},{10,11},{11... | collective-permute-start | bytes 50696 | tf_op jit(solution)/shard_map/ppermute | solution.py:25
  695.1 9.4 collective-permute-start.47
  737.5 4.6 collective-permute-start.53
  746.4 5.6 collective-permute-start.55
  748.4 5.1 collective-permute-start.56
  755.9 10.1 %collective-permute-start.57 = (f32[4,264,4]{1,2,0:T(4,128)S(1)}, f32[4,264,4]{1,2,0:T(4,128)S(1)}, u32[]{:S(2)}, u32[]{:S(2)}) collective-permute-start(f32[4,264,4]{1,2,0:T(4,128)S(1)} %copy.56), channel_id=1, source_target_pairs={{0,1},{1,2},{2,3},{3,4},{4,5},{5,6},{6,7},{8,9},{9,10},{10,11},{11... | collective-permute-start | bytes 50696 | tf_op jit(solution)/shard_map/ppermute | solution.py:25
  758.1 8.1 collective-permute-start.58
  780.8 7.1 collective-permute-start.59
  851.8 8.6 collective-permute-start.60
  928.1 5.6 collective-permute-start.62
  930.0 5.1 collective-permute-start.63
  938.7 11.5 %collective-permute-start.64 = (f32[4,264,4]{1,2,0:T(4,128)S(1)}, f32[4,264,4]{1,2,0:T(4,128)S(1)}, u32[]{:S(2)}, u32[]{:S(2)}) collective-permute-start(f32[4,264,4]{1,2,0:T(4,128)S(1)} %copy.64), channel_id=1, source_target_pairs={{0,1},{1,2},{2,3},{3,4},{4,5},{5,6},{6,7},{8,9},{9,10},{10,11},{11... | collective-permute-start | bytes 50696 | tf_op jit(solution)/shard_map/ppermute | solution.py:25
  941.1 9.4 collective-permute-start.65
  983.5 4.6 collective-permute-start.71
  (34 other events, 249.6 us)

commit v4 on v3

--- a/solution.py
+++ b/solution.py
@@ -107,8 +107,12 @@
     return total
 
 
-def with_rim(field):
-    return extended(field, (("gx", 1), ("gy", 2)), 4)
+def with_rim(field, width=4):
+    return extended(field, (("gx", 1), ("gy", 2)), width)
+
+
+def interior(field):
+    return field[:, 4:-4, 4:-4]
 
 
 def shards(right_side, prior_weight, jacobi_inverse, interaction, footprint):
@@ -124,8 +128,8 @@
     own_blocks = layers * rows_blocks * cols_blocks
     synth_rows = synth_table(tile_rows)
     synth_cols = synth_table(tile_cols)
-    analysis_rows = analysis_table(tile_rows)
-    analysis_cols = analysis_table(tile_cols)
+    analysis_rows = analysis_table(tile_rows + 8)
+    analysis_cols = analysis_table(tile_cols + 8)
     flat_ids = footprint.reshape(requests)
     request_num = jnp.arange(requests, dtype=jnp.int32)
     layer_of = request_num % layers
@@ -153,8 +157,7 @@
         wanted_ids.reshape(-1)[None, :] == jnp.arange(own_blocks, dtype=jnp.int32)[:, None]
     ).astype(jnp.float32)
     def apply_op(direction, carry):
-        synthesize_padded = with_rim(direction)
-        carry, synthesize_padded = advance(carry, synthesize_padded)
+        carry, synthesize_padded = advance(carry, direction)
         along_rows = jnp.einsum("lab,ac->lcb", synthesize_padded, synth_rows, precision=highest)
         blocks = (
             jnp.einsum("lab,bc->lac", along_rows, synth_cols, precision=highest)
@@ -185,7 +188,8 @@
         padded = with_rim(
             summed.reshape(layers, rows_blocks, cols_blocks, block_rows, block_cols)
             .transpose(0, 1, 3, 2, 4)
-            .reshape(layers, tile_rows, tile_cols)
+            .reshape(layers, tile_rows, tile_cols),
+            8,
         )
         carry, padded = advance(carry, padded)
         along_cols = jnp.einsum("lab,bc->lac", padded, analysis_cols, precision=highest)
@@ -194,24 +198,33 @@
             + prior_weight * direction
         ), finish(carry)
 
+    rims = with_rim(jnp.concatenate([right_side, jacobi_inverse, prior_weight]))
+    residual, jacobi_inverse, prior_weight = jnp.split(rims, 3)
     solution = jnp.zeros_like(right_side)
-    residual = right_side
     precond_res = jacobi_inverse * residual
-    direction = precond_res
-    image, rho_now = apply_op(direction, (jnp.sum(residual * precond_res), sum_steps(("gx", "gy"))))
+    direction = interior(precond_res)
+    image, rho_now = apply_op(
+        precond_res,
+        (jnp.sum(interior(residual) * direction), sum_steps(("gx", "gy"))),
+    )
     for step in range(ITERS):
-        step_size = rho_now / global_sum(jnp.sum(direction * image))
+        step_size = rho_now / global_sum(jnp.sum(direction * interior(image)))
         solution = solution + step_size * direction
         residual = residual - step_size * image
         if step + 1 < ITERS:
             precond_res = jacobi_inverse * residual
             applied, rho_next = apply_op(
-                precond_res, (jnp.sum(residual * precond_res), sum_steps(("gx", "gy")))
+                precond_res,
+                (
+                    jnp.sum(interior(residual) * interior(precond_res)),
+                    sum_steps(("gx", "gy")),
+                ),
             )
             ratio = rho_next / rho_now
-            direction = precond_res + ratio * direction
+            direction = interior(precond_res) + ratio * direction
             image = applied + ratio * image
             rho_now = rho_next
+    residual = interior(residual)
     return (solution, residual)
 
 

time: 1010 us -> 990 us (0.980)
  blocking collectives: 341 us -> 405 us
  waiting for transfers between devices: 168 us -> 110 us
  starting transfers between devices: 178 us -> 133 us
  local copies, waits for them, and re-layouts: 143 us -> 156 us
  matrix products: 93.5 us -> 106 us
    all_to_all x3 -> x4, blocking collectives: 170 us -> 233 us  [apply_op(): lax.all_to_all(outgoing, 'gy', split_axis=0, concat_axis=0, tiled=True)]
    all_to_all x1 -> x0, waiting for transfers between devices: 45.9 us -> none  [apply_op(): lax.all_to_all(outgoing, 'gy', split_axis=0, concat_axis=0, tiled=True)]
    ppermute x16 -> x10, starting transfers between devices: 67.9 us -> 42.3 us  [extended(): lax.ppermute(lax.slice_in_dim(block, 0, width, axis=dim), axis, backward)]
    unnamed x22 -> x70, local copies, waits for them, and re-layouts: 8.87 us -> 24.1 us
    ppermute x16 -> x10, starting transfers between devices: 32.8 us -> 20.7 us  [extended(): lax.ppermute(lax.slice_in_dim(block, block.shape[dim] - width, None, axis...]
  transfers between devices with their start and end apart: 75 -> 62, of which waited for: 40 -> 37; matrix products, arithmetic and copies ran while one was open for 6% -> 12% of each run, Pallas kernels for 0% -> 0%
where the time goes in v4:
time: 990 us; the launch traced here: 982 us
  blocking collectives  405 us (41%)
  local copies, waits for them, and re-layouts  156 us (16%)
  starting transfers between devices  133 us (13%)
  waiting for transfers between devices  110 us (11%)
  matrix products  106 us (11%)
  other arithmetic  40.1 us (4%)
  between operations  32.4 us (3%)
    all_to_all x4, blocking collectives, apply_op(): lax.all_to_all(outgoing, 'gy', split_axis=0, concat_axis=0, tiled=True)  233 us
    all_to_all x3, blocking collectives, apply_op(): lax.all_to_all(returning, 'gy', split_axis=0, concat_axis=0, tiled=True)  171 us
    ppermute x40, starting transfers between devices, sum_steps(): lax.ppermute(value, axis, pairs)  57.5 us
    ppermute x40, waiting for transfers between devices, sum_steps(): lax.ppermute(value, axis, pairs)  54.8 us
    all_to_all x1, waiting for transfers between devices, apply_op(): lax.all_to_all(returning, 'gy', split_axis=0, concat_axis=0, tiled=True)  48.5 us
    ppermute x10, starting transfers between devices, extended(): lax.ppermute(lax.slice_in_dim(block, 0, width, axis=dim), axis, backward)  42.3 us
    dot_general x4, matrix products, apply_op(): jnp.einsum('lab,ac->lcb', along_cols, analysis_rows, precision=highest)  25.8 us
    unnamed x70, local copies, waits for them, and re-layouts  24.1 us
  transfers between devices with their start and end apart: 62, of which 37 were waited for; matrix products, arithmetic and copies ran while one was open for 12% of the time, Pallas kernels for 0%

profile of v4, /device:TPU:10, one launch (start us, length us, event | category | flops | bytes accessed | tf_op | source)
XLA Modules:
  0.0 981.5 jit_solution(8384970266075888001)
XLA Ops:
  3.4 10.2 %scatter_fusion = s32[8,9]{1,0:T(8,128)} fusion(s32[8,9]{1,0:T(8,128)} %broadcast_in_dim.447, s32[64]{0:T(128)S(1)} %fusion.127, s32[64]{0:T(128)S(1)} %get-tuple-element.108), kind=kCustom, calls=%fused_computation.12 | custom fusion | bytes 1280 | tf_op jit(solution)/shard_map/scatter | solution.py:145
  13.6 6.3 all-to-all-start
  23.2 3.6 collective-permute-start.1
  45.1 4.8 collective-permute-done.2
  53.1 4.8 pad_maximum_fusion
  65.1 3.6 convolution_bitcast_fusion.3
  77.3 58.4 %all_to_all.49 = f32[8,9,64,128]{3,2,1,0:T(8,128)} all-to-all(f32[8,9,64,128]{3,2,1,0:T(8,128)} %bitcast.258), channel_id=1, replica_groups=mesh['gx'=4,'gy'=8] {'gy'}, dimensions={0} | all-to-all | bytes 4718592 | tf_op jit(solution)/shard_map/all_to_all | solution.py:171
  137.1 3.7 gather_fusion.1
  140.9 3.5 fusion.42
  147.7 3.7 gather_fusion.2
  152.0 6.5 all-to-all-start.2
  158.5 48.5 %all-to-all-done.2 = f32[8,9,64,128]{3,2,1,0:T(8,128)} async-done(((f32[8,9,64,128]{3,2,1,0:T(8,128)}), f32[8,9,64,128]{3,2,1,0:T(8,128)}, u32[]{:S(2)}, u32[]{:S(2)}) %all-to-all-start.2) | async-done | bytes 2359328 | tf_op jit(solution)/shard_map/all_to_all | solution.py:183
  218.9 3.6 collective-permute-start.9
  227.9 6.4 collective-permute-start.11
  249.2 4.6 bitcast_add_fusion.3
  271.7 4.1 collective-permute-start.17
  286.8 5.3 convolution_bitcast_fusion.2
  300.5 58.9 %all_to_all.50 = f32[8,9,64,128]{3,2,1,0:T(8,128)} all-to-all(f32[8,9,64,128]{3,2,1,0:T(8,128)} %bitcast.259), channel_id=1, replica_groups=mesh['gx'=4,'gy'=8] {'gy'}, dimensions={0} | all-to-all | bytes 4718592 | tf_op jit(solution)/shard_map/all_to_all | solution.py:171
  359.3 3.7 gather_fusion.4
  363.0 3.5 fusion.38
  371.4 3.7 gather_fusion.5
  375.7 57.3 %all_to_all.51 = f32[8,9,64,128]{3,2,1,0:T(8,128)S(1)} all-to-all(f32[8,9,64,128]{3,2,1,0:T(8,128)} %bitcast.260), channel_id=1, replica_groups=mesh['gx'=4,'gy'=8] {'gy'}, dimensions={0} | all-to-all | bytes 4718592 | tf_op jit(solution)/shard_map/all_to_all | solution.py:183
  443.3 3.6 collective-permute-start.23
  454.3 4.6 collective-permute-start.25
  467.9 4.3 fusion.54
  477.3 7.2 fusion.10
  516.1 5.0 convolution_bitcast_fusion.1
  521.1 3.8 fusion.68
  534.2 58.3 %all_to_all.52 = f32[8,9,64,128]{3,2,1,0:T(8,128)} all-to-all(f32[8,9,64,128]{3,2,1,0:T(8,128)} %bitcast.261), channel_id=1, replica_groups=mesh['gx'=4,'gy'=8] {'gy'}, dimensions={0} | all-to-all | bytes 4718592 | tf_op jit(solution)/shard_map/all_to_all | solution.py:171
  592.4 3.7 gather_fusion.7
  604.5 3.7 gather_fusion.8
  608.8 57.0 %all_to_all.53 = f32[8,9,64,128]{3,2,1,0:T(8,128)S(1)} all-to-all(f32[8,9,64,128]{3,2,1,0:T(8,128)} %bitcast.262), channel_id=1, replica_groups=mesh['gx'=4,'gy'=8] {'gy'}, dimensions={0} | all-to-all | bytes 4718592 | tf_op jit(solution)/shard_map/all_to_all | solution.py:183
  677.8 3.6 collective-permute-start.37
  689.9 4.8 collective-permute-start.39
  703.1 4.3 fusion.50
  712.5 7.0 fusion.9
  750.1 5.0 convolution_bitcast_fusion
  755.1 3.8 fusion.65
  768.2 57.9 %all_to_all.54 = f32[8,9,64,128]{3,2,1,0:T(8,128)} all-to-all(f32[8,9,64,128]{3,2,1,0:T(8,128)} %bitcast.256), channel_id=1, replica_groups=mesh['gx'=4,'gy'=8] {'gy'}, dimensions={0} | all-to-all | bytes 4718592 | tf_op jit(solution)/shard_map/all_to_all | solution.py:171
  826.1 3.7 gather_fusion.10
  829.8 3.5 fusion.30
  838.2 3.7 gather_fusion.11
  842.5 57.0 %all_to_all.55 = f32[8,9,64,128]{3,2,1,0:T(8,128)S(1)} all-to-all(f32[8,9,64,128]{3,2,1,0:T(8,128)} %bitcast.257), channel_id=1, replica_groups=mesh['gx'=4,'gy'=8] {'gy'}, dimensions={0} | all-to-all | bytes 4718592 | tf_op jit(solution)/shard_map/all_to_all | solution.py:183
  911.5 3.6 collective-permute-start.51
  923.5 4.9 collective-permute-start.53
  936.9 4.3 fusion.46
  946.2 7.1 fusion.8
  975.5 4.0 multiply_add_fusion
  (304 shorter events, 311.2 us)
Async XLA Ops:
  13.6 16.8 %all-to-all-start = ((s32[8,1,9]{2,1,0:T(1,128)}), s32[8,1,9]{2,1,0:T(1,128)S(1)}, u32[]{:S(2)}, u32[]{:S(2)}) async-start(s32[8,1,9]{2,1,0:T(1,128)} %bitcast.7), calls=%async_computation | async-start | bytes 8192 | tf_op jit(solution)/shard_map/all_to_all | solution.py:150
  21.2 10.5 %collective-permute-start = (f32[12,4,256]{2,1,0:T(4,128)S(1)}, f32[12,4,256]{2,1,0:T(4,128)S(1)}, u32[]{:S(2)}, u32[]{:S(2)}) collective-permute-start(f32[12,4,256]{2,1,0:T(4,128)S(1)} %get-tuple-element.113), channel_id=1, source_target_pairs={{0,8},{8,16},{16,24},{1,9},{9,17},{17,25},{2,10},{10,18},{18,26},{... | collective-permute-start | bytes 147464 | tf_op jit(solution)/shard_map/ppermute | solution.py:25
  23.2 8.6 collective-permute-start.1
  39.0 12.3 %collective-permute-start.3 = (f32[12,264,4]{1,2,0:T(4,128)S(1)}, f32[12,264,4]{1,2,0:T(4,128)S(1)}, u32[]{:S(2)}, u32[]{:S(2)}) collective-permute-start(f32[12,264,4]{1,2,0:T(4,128)S(1)} %copy.20), channel_id=1, source_target_pairs={{1,0},{2,1},{3,2},{4,3},{5,4},{6,5},{7,6},{9,8},{10,9},{11,10},{12... | collective-permute-start | bytes 152072 | tf_op jit(solution)/shard_map/ppermute | solution.py:28
  42.4 7.5 collective-permute-start.2
  63.7 12.9 %collective-permute-start.5 = (f32[]{:T(128)}, f32[]{:T(128)}, u32[]{:S(2)}, u32[]{:S(2)}) collective-permute-start(f32[]{:T(128)} %add.940), channel_id=1, source_target_pairs={{0,16},{8,24},{16,0},{24,8},{1,17},{9,25},{17,1},{25,9},{2,18},{10... | collective-permute-start | bytes 20 | tf_op jit(solution)/shard_map/ppermute | solution.py:83
  135.6 15.8 %collective-permute-start.6 = (f32[]{:T(128)}, f32[]{:T(128)}, u32[]{:S(2)}, u32[]{:S(2)}) collective-permute-start(f32[]{:T(128)} %add.941), channel_id=1, source_target_pairs={{0,1},{1,0},{2,3},{3,2},{4,5},{5,4},{6,7},{7,6},{8,9},{9,8},{10,11... | collective-permute-start | bytes 20 | tf_op jit(solution)/shard_map/ppermute | solution.py:83
  152.0 55.0 %all-to-all-start.2 = ((f32[8,9,64,128]{3,2,1,0:T(8,128)}), f32[8,9,64,128]{3,2,1,0:T(8,128)}, u32[]{:S(2)}, u32[]{:S(2)}) async-start(f32[8,9,64,128]{3,2,1,0:T(8,128)} %bitcast.255), calls=%async_computation.2 | async-start | bytes 4718592 | tf_op jit(solution)/shard_map/all_to_all | solution.py:183
  217.0 5.6 collective-permute-start.8
  218.9 5.2 collective-permute-start.9
  227.9 15.3 %collective-permute-start.11 = (f32[4,272,8]{1,2,0:T(8,128)S(1)}, f32[4,272,8]{1,2,0:T(8,128)S(1)}, u32[]{:S(2)}, u32[]{:S(2)}) collective-permute-start(f32[4,272,8]{1,2,0:T(8,128)S(1)} %copy.29), channel_id=1, source_target_pairs={{1,0},{2,1},{3,2},{4,3},{5,4},{6,5},{7,6},{9,8},{10,9},{11,10},{12... | collective-permute-start | bytes 104456 | tf_op jit(solution)/shard_map/ppermute | solution.py:28
  234.3 7.0 collective-permute-start.10
  236.4 3.6 collective-permute-start.7
  256.1 4.7 collective-permute-start.12
  263.0 3.7 collective-permute-start.15
  267.4 3.7 collective-permute-start.16
  271.7 4.6 collective-permute-start.17
  284.8 15.1 %collective-permute-start.19 = (f32[]{:T(128)}, f32[]{:T(128)}, u32[]{:S(2)}, u32[]{:S(2)}) collective-permute-start(f32[]{:T(128)} %add.987), channel_id=1, source_target_pairs={{0,16},{8,24},{16,0},{24,8},{1,17},{9,25},{17,1},{25,9},{2,18},{10... | collective-permute-start | bytes 20 | tf_op jit(solution)/shard_map/ppermute | solution.py:83
  366.5 8.6 collective-permute-start.20
  441.3 5.6 collective-permute-start.22
  443.3 5.2 collective-permute-start.23
  450.9 12.2 %collective-permute-start.24 = (f32[4,272,8]{1,2,0:T(8,128)S(1)}, f32[4,272,8]{1,2,0:T(8,128)S(1)}, u32[]{:S(2)}, u32[]{:S(2)}) collective-permute-start(f32[4,272,8]{1,2,0:T(8,128)S(1)} %copy.36), channel_id=1, source_target_pairs={{0,1},{1,2},{2,3},{3,4},{4,5},{5,6},{6,7},{8,9},{9,10},{10,11},{11... | collective-permute-start | bytes 104456 | tf_op jit(solution)/shard_map/ppermute | solution.py:25
  454.3 9.9 %collective-permute-start.25 = (f32[4,272,8]{1,2,0:T(8,128)S(1)}, f32[4,272,8]{1,2,0:T(8,128)}, u32[]{:S(2)}, u32[]{:S(2)}) collective-permute-start(f32[4,272,8]{1,2,0:T(8,128)S(1)} %copy.37), channel_id=1, source_target_pairs={{1,0},{2,1},{3,2},{4,3},{5,4},{6,5},{7,6},{9,8},{10,9},{11,10},{12... | collective-permute-start | bytes 104456 | tf_op jit(solution)/shard_map/ppermute | solution.py:28
  458.9 3.6 collective-permute-start.21
  472.2 4.4 collective-permute-start.26
  488.7 3.7 collective-permute-start.28
  493.0 3.7 collective-permute-start.29
  497.4 3.7 collective-permute-start.30
  501.7 4.6 collective-permute-start.31
  514.7 18.8 %collective-permute-start.33 = (f32[]{:T(128)}, f32[]{:T(128)}, u32[]{:S(2)}, u32[]{:S(2)}) collective-permute-start(f32[]{:T(128)} %add.1001), channel_id=1, source_target_pairs={{0,16},{8,24},{16,0},{24,8},{1,17},{9,25},{17,1},{25,9},{2,18},{10... | collective-permute-start | bytes 20 | tf_op jit(solution)/shard_map/ppermute | solution.py:83
  599.6 8.6 collective-permute-start.34
  675.9 5.6 collective-permute-start.36
  677.8 5.2 collective-permute-start.37
  686.5 12.4 %collective-permute-start.38 = (f32[4,272,8]{1,2,0:T(8,128)S(1)}, f32[4,272,8]{1,2,0:T(8,128)S(1)}, u32[]{:S(2)}, u32[]{:S(2)}) collective-permute-start(f32[4,272,8]{1,2,0:T(8,128)S(1)} %copy.44), channel_id=1, source_target_pairs={{0,1},{1,2},{2,3},{3,4},{4,5},{5,6},{6,7},{8,9},{9,10},{10,11},{11... | collective-permute-start | bytes 104456 | tf_op jit(solution)/shard_map/ppermute | solution.py:25
  689.9 10.0 %collective-permute-start.39 = (f32[4,272,8]{1,2,0:T(8,128)S(1)}, f32[4,272,8]{1,2,0:T(8,128)S(1)}, u32[]{:S(2)}, u32[]{:S(2)}) collective-permute-start(f32[4,272,8]{1,2,0:T(8,128)S(1)} %copy.45), channel_id=1, source_target_pairs={{1,0},{2,1},{3,2},{4,3},{5,4},{6,5},{7,6},{9,8},{10,9},{11,10},{12... | collective-permute-start | bytes 104456 | tf_op jit(solution)/shard_map/ppermute | solution.py:28
  707.4 4.4 collective-permute-start.40
  735.9 4.5 collective-permute-start.45
  748.8 18.8 %collective-permute-start.47 = (f32[]{:T(128)}, f32[]{:T(128)}, u32[]{:S(2)}, u32[]{:S(2)}) collective-permute-start(f32[]{:T(128)} %add.1015), channel_id=1, source_target_pairs={{0,16},{8,24},{16,0},{24,8},{1,17},{9,25},{17,1},{25,9},{2,18},{10... | collective-permute-start | bytes 20 | tf_op jit(solution)/shard_map/ppermute | solution.py:83
  833.3 8.6 collective-permute-start.48
  909.5 5.6 collective-permute-start.50
  911.5 5.2 collective-permute-start.51
  920.1 12.5 %collective-permute-start.52 = (f32[4,272,8]{1,2,0:T(8,128)S(1)}, f32[4,272,8]{1,2,0:T(8,128)S(1)}, u32[]{:S(2)}, u32[]{:S(2)}) collective-permute-start(f32[4,272,8]{1,2,0:T(8,128)S(1)} %copy.52), channel_id=1, source_target_pairs={{0,1},{1,2},{2,3},{3,4},{4,5},{5,6},{6,7},{8,9},{9,10},{10,11},{11... | collective-permute-start | bytes 104456 | tf_op jit(solution)/shard_map/ppermute | solution.py:25
  923.5 10.1 %collective-permute-start.53 = (f32[4,272,8]{1,2,0:T(8,128)S(1)}, f32[4,272,8]{1,2,0:T(8,128)S(1)}, u32[]{:S(2)}, u32[]{:S(2)}) collective-permute-start(f32[4,272,8]{1,2,0:T(8,128)S(1)} %copy.53), channel_id=1, source_target_pairs={{1,0},{2,1},{3,2},{4,3},{5,4},{6,5},{7,6},{9,8},{10,9},{11,10},{12... | collective-permute-start | bytes 104456 | tf_op jit(solution)/shard_map/ppermute | solution.py:28
  941.2 4.4 collective-permute-start.54
  957.5 3.7 collective-permute-start.56
  961.7 3.7 collective-permute-start.57
  966.0 3.7 collective-permute-start.58
  970.3 4.6 collective-permute-start.59
  (40 other events, 284.4 us)

commit v5 on v4

--- a/solution.py
+++ b/solution.py
@@ -156,9 +156,8 @@
     landing = (
         wanted_ids.reshape(-1)[None, :] == jnp.arange(own_blocks, dtype=jnp.int32)[:, None]
     ).astype(jnp.float32)
-    def apply_op(direction, carry):
-        carry, synthesize_padded = advance(carry, direction)
-        along_rows = jnp.einsum("lab,ac->lcb", synthesize_padded, synth_rows, precision=highest)
+    def apply_op(direction, partials):
+        along_rows = jnp.einsum("lab,ac->lcb", direction, synth_rows, precision=highest)
         blocks = (
             jnp.einsum("lab,bc->lac", along_rows, synth_cols, precision=highest)
             .reshape(layers, rows_blocks, block_rows, cols_blocks, block_cols)
@@ -167,13 +166,12 @@
         )
         blocks = jnp.concatenate([blocks, jnp.zeros((1, block_rows, block_cols), blocks.dtype)])
         outgoing = jnp.take(blocks, wanted_ids, axis=0, mode="clip")
-        carry, outgoing = advance(carry, outgoing)
         arrived = lax.all_to_all(outgoing, "gy", split_axis=0, concat_axis=0, tiled=True)
-        carry, arrived = advance(carry, arrived, step=False)
         seen = arrived[target, slot].reshape(
             sensors, rows_blocks * cols_blocks, layers, block_rows, block_cols
         )
         slopes = jnp.einsum("sklxy,slyz->skxz", seen, interaction, precision=highest)
+        carry = (partials(slopes), sum_steps(("gx", "gy")))
         back = jnp.einsum("skxz,slyz->sklxy", slopes, interaction, precision=highest).reshape(
             requests, block_rows, block_cols
         )
@@ -185,6 +183,7 @@
         summed = jnp.dot(
             landing, landed.reshape(owners * capacity, block_rows * block_cols), precision=highest
         )
+        carry, summed = advance(carry, summed)
         padded = with_rim(
             summed.reshape(layers, rows_blocks, cols_blocks, block_rows, block_cols)
             .transpose(0, 1, 3, 2, 4)
@@ -193,35 +192,58 @@
         )
         carry, padded = advance(carry, padded)
         along_cols = jnp.einsum("lab,bc->lac", padded, analysis_cols, precision=highest)
+        carry, along_cols = advance(carry, along_cols)
         return (
             jnp.einsum("lab,ac->lcb", along_cols, analysis_rows, precision=highest)
             + prior_weight * direction
-        ), finish(carry)
+        ), slopes, finish(carry)
 
     rims = with_rim(jnp.concatenate([right_side, jacobi_inverse, prior_weight]))
     residual, jacobi_inverse, prior_weight = jnp.split(rims, 3)
     solution = jnp.zeros_like(right_side)
+    prior_inner = interior(prior_weight)
     precond_res = jacobi_inverse * residual
     direction = interior(precond_res)
-    image, rho_now = apply_op(
+    image, direction_slopes, totals = apply_op(
         precond_res,
-        (jnp.sum(interior(residual) * direction), sum_steps(("gx", "gy"))),
-    )
+        lambda slopes: jnp.stack(
+            [
+                jnp.sum(interior(residual) * direction),
+                jnp.sum(slopes * slopes),
+                jnp.sum(prior_inner * direction * direction),
+            ]
+        ),
+    )
+    rho_now = totals[0]
+    step_size = rho_now / (totals[1] + totals[2])
     for step in range(ITERS):
-        step_size = rho_now / global_sum(jnp.sum(direction * interior(image)))
         solution = solution + step_size * direction
         residual = residual - step_size * image
         if step + 1 < ITERS:
             precond_res = jacobi_inverse * residual
-            applied, rho_next = apply_op(
+            inner = interior(precond_res)
+            applied, slopes_now, totals = apply_op(
                 precond_res,
-                (
-                    jnp.sum(interior(residual) * interior(precond_res)),
-                    sum_steps(("gx", "gy")),
+                lambda slopes: jnp.stack(
+                    [
+                        jnp.sum(interior(residual) * inner),
+                        jnp.sum(slopes * slopes),
+                        jnp.sum(slopes * direction_slopes),
+                        jnp.sum(direction_slopes * direction_slopes),
+                        jnp.sum(prior_inner * inner * inner),
+                        jnp.sum(prior_inner * inner * direction),
+                        jnp.sum(prior_inner * direction * direction),
+                    ]
                 ),
             )
+            rho_next = totals[0]
             ratio = rho_next / rho_now
-            direction = interior(precond_res) + ratio * direction
+            curvature = (totals[1] + 2.0 * ratio * totals[2] + ratio * ratio * totals[3]) + (
+                totals[4] + 2.0 * ratio * totals[5] + ratio * ratio * totals[6]
+            )
+            step_size = rho_next / curvature
+            direction = inner + ratio * direction
+            direction_slopes = slopes_now + ratio * direction_slopes
             image = applied + ratio * image
             rho_now = rho_next
     residual = interior(residual)

time: 990 us -> 924 us (0.933)
  blocking collectives: 405 us -> 182 us
  waiting for transfers between devices: 110 us -> 278 us
  starting transfers between devices: 133 us -> 113 us
  between operations: 32.4 us -> 21.4 us
  local copies, waits for them, and re-layouts: 156 us -> 166 us
    all_to_all x4 -> x0, blocking collectives: 233 us -> none  [apply_op(): lax.all_to_all(outgoing, 'gy', split_axis=0, concat_axis=0, tiled=True)]
    all_to_all x0 -> x4, waiting for transfers between devices: none -> 172 us  [apply_op(): lax.all_to_all(outgoing, 'gy', split_axis=0, concat_axis=0, tiled=True)]
    ppermute x40 -> x20, starting transfers between devices: 57.5 us -> 14.5 us  [sum_steps(): lax.ppermute(value, axis, pairs)]
    all_to_all x0 -> x4, starting transfers between devices: none -> 21.5 us  [apply_op(): lax.all_to_all(outgoing, 'gy', split_axis=0, concat_axis=0, tiled=True)]
    another operation x0 -> x3, local copies, waits for them, and re-layouts: none -> 13.2 us  [shards(): jnp.stack([jnp.sum(interior(residual) * inner), jnp.sum(slopes * slopes),...]
    all_to_all x3, blocking collectives: 171 us -> 182 us  [apply_op(): lax.all_to_all(returning, 'gy', split_axis=0, concat_axis=0, tiled=True)]
    unnamed x70 -> x60, local copies, waits for them, and re-layouts: 24.1 us -> 15.3 us
    ppermute x40 -> x20, waiting for transfers between devices: 54.8 us -> 46.6 us  [sum_steps(): lax.ppermute(value, axis, pairs)]
  transfers between devices with their start and end apart: 62 -> 46, of which waited for: 37 -> 26; matrix products, arithmetic and copies ran while one was open for 12% -> 8% of each run, Pallas kernels for 0% -> 0%
where the time goes in v5:
time: 924 us; the launch traced here: 917 us
  waiting for transfers between devices  278 us (30%)
  blocking collectives  182 us (20%)
  local copies, waits for them, and re-layouts  166 us (18%)
  starting transfers between devices  113 us (12%)
  matrix products  112 us (12%)
  other arithmetic  45.3 us (5%)
  between operations  21.4 us (2%)
    all_to_all x3, blocking collectives, apply_op(): lax.all_to_all(returning, 'gy', split_axis=0, concat_axis=0, tiled=True)  182 us
    all_to_all x4, waiting for transfers between devices, apply_op(): lax.all_to_all(outgoing, 'gy', split_axis=0, concat_axis=0, tiled=True)  172 us
    all_to_all x1, waiting for transfers between devices, apply_op(): lax.all_to_all(returning, 'gy', split_axis=0, concat_axis=0, tiled=True)  52.3 us
    ppermute x20, waiting for transfers between devices, sum_steps(): lax.ppermute(value, axis, pairs)  46.6 us
    ppermute x10, starting transfers between devices, extended(): lax.ppermute(lax.slice_in_dim(block, 0, width, axis=dim), axis, backward)  41.9 us
    dot_general x4, matrix products, apply_op(): jnp.einsum('lab,ac->lcb', along_cols, analysis_rows, precision=highest)  28.4 us
    all_to_all x4, starting transfers between devices, apply_op(): lax.all_to_all(outgoing, 'gy', split_axis=0, concat_axis=0, tiled=True)  21.5 us
    ppermute x10, starting transfers between devices, extended(): lax.ppermute(lax.slice_in_dim(block, block.shape[dim] - width, None, axis...  20.3 us
  transfers between devices with their start and end apart: 46, of which 26 were waited for; matrix products, arithmetic and copies ran while one was open for 8% of the time, Pallas kernels for 0%

profile of v5, /device:TPU:10, one launch (start us, length us, event | category | flops | bytes accessed | tf_op | source)
XLA Modules:
  0.0 916.7 jit_solution(8404365093540194902)
XLA Ops:
  3.4 10.2 %scatter_fusion = s32[8,9]{1,0:T(8,128)} fusion(s32[8,9]{1,0:T(8,128)} %broadcast_in_dim.447, s32[64]{0:T(128)S(1)} %fusion.107, s32[64]{0:T(128)S(1)} %get-tuple-element.113), kind=kCustom, calls=%fused_computation.12 | custom fusion | bytes 1280 | tf_op jit(solution)/shard_map/scatter | solution.py:145
  13.6 6.3 all-to-all-start
  45.4 4.8 collective-permute-done.2
  53.3 4.8 pad_maximum_fusion
  63.9 3.8 fusion.66
  76.2 5.6 all-to-all-start.1
  84.1 45.4 %all-to-all-done.1 = f32[8,9,64,128]{3,2,1,0:T(8,128)} async-done(((f32[8,9,64,128]{3,2,1,0:T(8,128)}), f32[8,9,64,128]{3,2,1,0:T(8,128)}, u32[]{:S(2)}, u32[]{:S(2)}) %all-to-all-start.1) | async-done | bytes 2359328 | tf_op jit(solution)/shard_map/all_to_all | solution.py:169
  129.5 3.8 gather_fusion.1
  133.3 4.2 fusion.44
  148.4 8.2 all-to-all-start.2
  156.7 52.3 %all-to-all-done.2 = f32[8,9,64,128]{3,2,1,0:T(8,128)} async-done(((f32[8,9,64,128]{3,2,1,0:T(8,128)}), f32[8,9,64,128]{3,2,1,0:T(8,128)}, u32[]{:S(2)}, u32[]{:S(2)}) %all-to-all-start.2) | async-done | bytes 2359328 | tf_op jit(solution)/shard_map/all_to_all | solution.py:181
  209.0 3.9 fusion.9
  234.2 5.4 collective-permute-start.10
  251.1 4.3 fusion.55
  255.9 4.0 collective-permute-done.12
  262.3 8.2 slice_multiply_fusion.3
  275.4 3.8 fusion.63
  287.7 6.5 all-to-all-start.3
  297.7 43.4 %all-to-all-done.3 = f32[8,9,64,128]{3,2,1,0:T(8,128)} async-done(((f32[8,9,64,128]{3,2,1,0:T(8,128)}), f32[8,9,64,128]{3,2,1,0:T(8,128)}, u32[]{:S(2)}, u32[]{:S(2)}) %all-to-all-start.3) | async-done | bytes 2359328 | tf_op jit(solution)/shard_map/all_to_all | solution.py:169
  341.1 3.8 gather_fusion.4
  344.8 4.2 fusion.27
  349.0 4.4 stack.89
  360.5 60.7 %all_to_all.49 = f32[8,9,64,128]{3,2,1,0:T(8,128)S(1)} all-to-all(f32[8,9,64,128]{3,2,1,0:T(8,128)} %bitcast.314), channel_id=1, replica_groups=mesh['gx'=4,'gy'=8] {'gy'}, dimensions={0} | all-to-all | bytes 4718592 | tf_op jit(solution)/shard_map/all_to_all | solution.py:181
  445.5 5.0 collective-permute-start.19
  458.8 4.3 fusion.52
  467.3 3.8 collective-permute-done.21
  477.5 7.1 fusion.13
  499.6 4.9 all-to-all-start.5
  504.5 5.3 multiply_reduce_fusion.3
  509.9 41.3 %all-to-all-done.5 = f32[8,9,64,128]{3,2,1,0:T(8,128)} async-done(((f32[8,9,64,128]{3,2,1,0:T(8,128)}), f32[8,9,64,128]{3,2,1,0:T(8,128)}, u32[]{:S(2)}, u32[]{:S(2)}) %all-to-all-start.5) | async-done | bytes 2359328 | tf_op jit(solution)/shard_map/all_to_all | solution.py:169
  554.9 5.3 multiply_reduce_fusion.9
  560.2 4.4 stack.97
  572.8 60.5 %all_to_all.50 = f32[8,9,64,128]{3,2,1,0:T(8,128)S(1)} all-to-all(f32[8,9,64,128]{3,2,1,0:T(8,128)} %bitcast.315), channel_id=1, replica_groups=mesh['gx'=4,'gy'=8] {'gy'}, dimensions={0} | all-to-all | bytes 4718592 | tf_op jit(solution)/shard_map/all_to_all | solution.py:181
  659.9 4.9 collective-permute-start.28
  672.7 4.3 fusion.49
  681.2 3.8 collective-permute-done.30
  691.5 8.8 slice_multiply_fusion.1
  705.1 3.8 fusion.57
  717.6 4.5 all-to-all-start.7
  722.2 4.4 fusion.16
  726.6 42.1 %all-to-all-done.7 = f32[8,9,64,128]{3,2,1,0:T(8,128)} async-done(((f32[8,9,64,128]{3,2,1,0:T(8,128)}), f32[8,9,64,128]{3,2,1,0:T(8,128)}, u32[]{:S(2)}, u32[]{:S(2)}) %all-to-all-start.7) | async-done | bytes 2359328 | tf_op jit(solution)/shard_map/all_to_all | solution.py:169
  772.4 5.0 multiply_reduce_fusion.8
  777.4 4.5 stack.105
  790.0 60.5 %all_to_all.51 = f32[8,9,64,128]{3,2,1,0:T(8,128)S(1)} all-to-all(f32[8,9,64,128]{3,2,1,0:T(8,128)} %bitcast.313), channel_id=1, replica_groups=mesh['gx'=4,'gy'=8] {'gy'}, dimensions={0} | all-to-all | bytes 4718592 | tf_op jit(solution)/shard_map/all_to_all | solution.py:181
  874.4 5.0 collective-permute-start.37
  893.8 4.3 convolution_bitcast_fusion
  898.8 3.8 collective-permute-done.39
  909.0 7.3 fusion.19
  (279 shorter events, 284.9 us)
Async XLA Ops:
  0.6 132.6 %copy-start = (f32[2,4,128,128]{3,2,1,0:T(8,128)S(1)}, f32[2,4,128,128]{3,2,1,0:T(8,128)}, u32[]{:S(2)}) copy-start(f32[2,4,128,128]{3,2,1,0:T(8,128)} %param.8) | copy-start | bytes 1572868
  13.6 17.2 %all-to-all-start = ((s32[8,1,9]{2,1,0:T(1,128)}), s32[8,1,9]{2,1,0:T(1,128)S(1)}, u32[]{:S(2)}, u32[]{:S(2)}) async-start(s32[8,1,9]{2,1,0:T(1,128)} %bitcast.8), calls=%async_computation | async-start | bytes 8192 | tf_op jit(solution)/shard_map/all_to_all | solution.py:150
  21.5 10.5 %collective-permute-start = (f32[12,4,256]{2,1,0:T(4,128)S(1)}, f32[12,4,256]{2,1,0:T(4,128)S(1)}, u32[]{:S(2)}, u32[]{:S(2)}) collective-permute-start(f32[12,4,256]{2,1,0:T(4,128)S(1)} %get-tuple-element.119), channel_id=1, source_target_pairs={{0,8},{8,16},{16,24},{1,9},{9,17},{17,25},{2,10},{10,18},{18,26},{... | collective-permute-start | bytes 147464 | tf_op jit(solution)/shard_map/ppermute | solution.py:25
  23.5 8.6 collective-permute-start.1
  39.3 12.3 %collective-permute-start.3 = (f32[12,264,4]{1,2,0:T(4,128)S(1)}, f32[12,264,4]{1,2,0:T(4,128)S(1)}, u32[]{:S(2)}, u32[]{:S(2)}) collective-permute-start(f32[12,264,4]{1,2,0:T(4,128)S(1)} %copy.41), channel_id=1, source_target_pairs={{1,0},{2,1},{3,2},{4,3},{5,4},{6,5},{7,6},{9,8},{10,9},{11,10},{12... | collective-permute-start | bytes 152072 | tf_op jit(solution)/shard_map/ppermute | solution.py:28
  42.7 7.5 collective-permute-start.2
  76.2 53.3 %all-to-all-start.1 = ((f32[8,9,64,128]{3,2,1,0:T(8,128)}), f32[8,9,64,128]{3,2,1,0:T(8,128)}, u32[]{:S(2)}, u32[]{:S(2)}) async-start(f32[8,9,64,128]{3,2,1,0:T(8,128)} %bitcast.312), calls=%async_computation.1 | async-start | bytes 4718592 | tf_op jit(solution)/shard_map/all_to_all | solution.py:169
  139.4 7.1 collective-permute-start.4
  148.4 60.5 %all-to-all-start.2 = ((f32[8,9,64,128]{3,2,1,0:T(8,128)}), f32[8,9,64,128]{3,2,1,0:T(8,128)}, u32[]{:S(2)}, u32[]{:S(2)}) async-start(f32[8,9,64,128]{3,2,1,0:T(8,128)} %bitcast.308), calls=%async_computation.2 | async-start | bytes 4718592 | tf_op jit(solution)/shard_map/all_to_all | solution.py:181
  212.9 3.6 collective-permute-start.5
  222.3 5.6 collective-permute-start.7
  224.2 5.2 collective-permute-start.8
  234.2 13.3 %collective-permute-start.10 = (f32[4,272,8]{1,2,0:T(8,128)S(1)}, f32[4,272,8]{1,2,0:T(8,128)S(1)}, u32[]{:S(2)}, u32[]{:S(2)}) collective-permute-start(f32[4,272,8]{1,2,0:T(8,128)S(1)} %copy.49), channel_id=1, source_target_pairs={{1,0},{2,1},{3,2},{4,3},{5,4},{6,5},{7,6},{9,8},{10,9},{11,10},{12... | collective-permute-start | bytes 104456 | tf_op jit(solution)/shard_map/ppermute | solution.py:28
  239.6 6.9 collective-permute-start.9
  241.7 3.6 collective-permute-start.6
  250.7 4.7 collective-permute-start.11
  255.4 4.4 collective-permute-start.12
  287.7 53.3 %all-to-all-start.3 = ((f32[8,9,64,128]{3,2,1,0:T(8,128)}), f32[8,9,64,128]{3,2,1,0:T(8,128)}, u32[]{:S(2)}, u32[]{:S(2)}) async-start(f32[8,9,64,128]{3,2,1,0:T(8,128)} %bitcast.311), calls=%async_computation.3 | async-start | bytes 4718592 | tf_op jit(solution)/shard_map/all_to_all | solution.py:169
  297.7 47.1 %copy-start.12 = (f32[2,8,64,128,1]{3,2,4,1,0:T(8,128)S(1)}, f32[2,8,64,128,1]{3,2,4,1,0:T(8,128)}, u32[]{:S(2)}) copy-start(f32[2,8,64,128,1]{3,2,4,1,0:T(8,128)} %copy-done.11) | copy-start | bytes 1572868
  353.4 7.1 collective-permute-start.13
  423.6 5.0 collective-permute-start.14
  432.7 5.6 collective-permute-start.16
  434.6 5.2 collective-permute-start.17
  442.2 11.8 %collective-permute-start.18 = (f32[4,272,8]{1,2,0:T(8,128)S(1)}, f32[4,272,8]{1,2,0:T(8,128)S(1)}, u32[]{:S(2)}, u32[]{:S(2)}) collective-permute-start(f32[4,272,8]{1,2,0:T(8,128)S(1)} %copy.55), channel_id=1, source_target_pairs={{0,1},{1,2},{2,3},{3,4},{4,5},{5,6},{6,7},{8,9},{9,10},{10,11},{11... | collective-permute-start | bytes 104456 | tf_op jit(solution)/shard_map/ppermute | solution.py:25
  445.5 9.6 %collective-permute-start.19 = (f32[4,272,8]{1,2,0:T(8,128)S(1)}, f32[4,272,8]{1,2,0:T(8,128)}, u32[]{:S(2)}, u32[]{:S(2)}) collective-permute-start(f32[4,272,8]{1,2,0:T(8,128)S(1)} %copy.56), channel_id=1, source_target_pairs={{1,0},{2,1},{3,2},{4,3},{5,4},{6,5},{7,6},{9,8},{10,9},{11,10},{12... | collective-permute-start | bytes 104456 | tf_op jit(solution)/shard_map/ppermute | solution.py:28
  450.5 3.6 collective-permute-start.15
  463.1 3.5 collective-permute-start.20
  466.6 4.4 collective-permute-start.21
  499.6 51.5 %all-to-all-start.5 = ((f32[8,9,64,128]{3,2,1,0:T(8,128)}), f32[8,9,64,128]{3,2,1,0:T(8,128)}, u32[]{:S(2)}, u32[]{:S(2)}) async-start(f32[8,9,64,128]{3,2,1,0:T(8,128)} %bitcast.309), calls=%async_computation.5 | async-start | bytes 4718592 | tf_op jit(solution)/shard_map/all_to_all | solution.py:169
  564.6 8.1 collective-permute-start.22
  635.6 4.6 collective-permute-start.23
  646.0 5.6 collective-permute-start.25
  647.9 5.2 collective-permute-start.26
  656.6 11.8 %collective-permute-start.27 = (f32[4,272,8]{1,2,0:T(8,128)S(1)}, f32[4,272,8]{1,2,0:T(8,128)S(1)}, u32[]{:S(2)}, u32[]{:S(2)}) collective-permute-start(f32[4,272,8]{1,2,0:T(8,128)S(1)} %copy.62), channel_id=1, source_target_pairs={{0,1},{1,2},{2,3},{3,4},{4,5},{5,6},{6,7},{8,9},{9,10},{10,11},{11... | collective-permute-start | bytes 104456 | tf_op jit(solution)/shard_map/ppermute | solution.py:25
  659.9 9.6 %collective-permute-start.28 = (f32[4,272,8]{1,2,0:T(8,128)S(1)}, f32[4,272,8]{1,2,0:T(8,128)S(1)}, u32[]{:S(2)}, u32[]{:S(2)}) collective-permute-start(f32[4,272,8]{1,2,0:T(8,128)S(1)} %copy.63), channel_id=1, source_target_pairs={{1,0},{2,1},{3,2},{4,3},{5,4},{6,5},{7,6},{9,8},{10,9},{11,10},{12... | collective-permute-start | bytes 104456 | tf_op jit(solution)/shard_map/ppermute | solution.py:28
  664.8 3.6 collective-permute-start.24
  677.0 3.5 collective-permute-start.29
  680.5 4.4 collective-permute-start.30
  717.6 51.1 %all-to-all-start.7 = ((f32[8,9,64,128]{3,2,1,0:T(8,128)}), f32[8,9,64,128]{3,2,1,0:T(8,128)}, u32[]{:S(2)}, u32[]{:S(2)}) async-start(f32[8,9,64,128]{3,2,1,0:T(8,128)} %bitcast.310), calls=%async_computation.7 | async-start | bytes 4718592 | tf_op jit(solution)/shard_map/all_to_all | solution.py:169
  781.9 8.1 collective-permute-start.31
  852.8 4.7 collective-permute-start.32
  861.6 5.6 collective-permute-start.34
  863.5 5.2 collective-permute-start.35
  871.2 11.9 %collective-permute-start.36 = (f32[4,272,8]{1,2,0:T(8,128)S(1)}, f32[4,272,8]{1,2,0:T(8,128)S(1)}, u32[]{:S(2)}, u32[]{:S(2)}) collective-permute-start(f32[4,272,8]{1,2,0:T(8,128)S(1)} %copy.69), channel_id=1, source_target_pairs={{0,1},{1,2},{2,3},{3,4},{4,5},{5,6},{6,7},{8,9},{9,10},{10,11},{11... | collective-permute-start | bytes 104456 | tf_op jit(solution)/shard_map/ppermute | solution.py:25
  874.4 9.7 %collective-permute-start.37 = (f32[4,272,8]{1,2,0:T(8,128)S(1)}, f32[4,272,8]{1,2,0:T(8,128)S(1)}, u32[]{:S(2)}, u32[]{:S(2)}) collective-permute-start(f32[4,272,8]{1,2,0:T(8,128)S(1)} %copy.70), channel_id=1, source_target_pairs={{1,0},{2,1},{3,2},{4,3},{5,4},{6,5},{7,6},{9,8},{10,9},{11,10},{12... | collective-permute-start | bytes 104456 | tf_op jit(solution)/shard_map/ppermute | solution.py:28
  879.4 3.6 collective-permute-start.33
  890.2 3.6 collective-permute-start.38
  898.1 4.4 collective-permute-start.39
  (21 other events, 209.4 us)

commit v6 on v5

--- a/solution.py
+++ b/solution.py
@@ -116,7 +116,7 @@
 
 
 def shards(right_side, prior_weight, jacobi_inverse, interaction, footprint):
-    highest = lax.Precision.HIGHEST
+    highest = lax.Precision.HIGH
     layers, tile_rows, tile_cols = right_side.shape
     sensors, rows_blocks, cols_blocks = (footprint.shape[0], footprint.shape[1], footprint.shape[2])
     block_rows = tile_rows // rows_blocks

time: 924 us -> 899 us (0.973)
  matrix products: 112 us -> 81 us
where the time goes in v6:
time: 899 us; the launch traced here: 887 us
  waiting for transfers between devices  278 us (31%)
  blocking collectives  182 us (20%)
  local copies, waits for them, and re-layouts  168 us (19%)
  starting transfers between devices  111 us (12%)
  matrix products  81 us (9%)
  other arithmetic  45.2 us (5%)
  between operations  21.4 us (2%)
    all_to_all x3, blocking collectives, apply_op(): lax.all_to_all(returning, 'gy', split_axis=0, concat_axis=0, tiled=True)  182 us
    all_to_all x4, waiting for transfers between devices, apply_op(): lax.all_to_all(outgoing, 'gy', split_axis=0, concat_axis=0, tiled=True)  172 us
    all_to_all x1, waiting for transfers between devices, apply_op(): lax.all_to_all(returning, 'gy', split_axis=0, concat_axis=0, tiled=True)  52.3 us
    ppermute x20, waiting for transfers between devices, sum_steps(): lax.ppermute(value, axis, pairs)  46.6 us
    ppermute x10, starting transfers between devices, extended(): lax.ppermute(lax.slice_in_dim(block, 0, width, axis=dim), axis, backward)  41.6 us
    dot_general x4, matrix products, apply_op(): jnp.einsum('lab,ac->lcb', along_cols, analysis_rows, precision=highest)  21.7 us
    all_to_all x4, starting transfers between devices, apply_op(): lax.all_to_all(outgoing, 'gy', split_axis=0, concat_axis=0, tiled=True)  20.3 us
    ppermute x10, starting transfers between devices, extended(): lax.ppermute(lax.slice_in_dim(block, block.shape[dim] - width, None, axis...  20 us
  transfers between devices with their start and end apart: 46, of which 26 were waited for; matrix products, arithmetic and copies ran while one was open for 8% of the time, Pallas kernels for 0%

profile of v6, /device:TPU:10, one launch (start us, length us, event | category | flops | bytes accessed | tf_op | source)
XLA Modules:
  0.0 887.1 jit_solution(12616845527333280276)
XLA Ops:
  3.4 12.1 %scatter_fusion = s32[8,9]{1,0:T(8,128)} fusion(s32[8,9]{1,0:T(8,128)} %broadcast_in_dim.447, s32[64]{0:T(128)S(1)} %fusion.107, s32[64]{0:T(128)S(1)} %get-tuple-element.113), kind=kCustom, calls=%fused_computation.12 | custom fusion | bytes 1280 | tf_op jit(solution)/shard_map/scatter | solution.py:145
  15.5 6.3 all-to-all-start
  25.4 3.6 collective-permute-start.1
  47.1 5.0 collective-permute-done.2
  55.2 4.8 pad_maximum_fusion
  75.2 5.3 all-to-all-start.1
  82.8 45.4 %all-to-all-done.1 = f32[8,9,64,128]{3,2,1,0:T(8,128)} async-done(((f32[8,9,64,128]{3,2,1,0:T(8,128)}), f32[8,9,64,128]{3,2,1,0:T(8,128)}, u32[]{:S(2)}, u32[]{:S(2)}) %all-to-all-start.1) | async-done | bytes 2359328 | tf_op jit(solution)/shard_map/all_to_all | solution.py:169
  128.2 3.8 gather_fusion.1
  139.8 3.7 gather_fusion.2
  145.4 8.2 all-to-all-start.2
  153.7 52.3 %all-to-all-done.2 = f32[8,9,64,128]{3,2,1,0:T(8,128)} async-done(((f32[8,9,64,128]{3,2,1,0:T(8,128)}), f32[8,9,64,128]{3,2,1,0:T(8,128)}, u32[]{:S(2)}, u32[]{:S(2)}) %all-to-all-start.2) | async-done | bytes 2359328 | tf_op jit(solution)/shard_map/all_to_all | solution.py:181
  220.8 3.6 collective-permute-start.8
  230.8 5.4 collective-permute-start.10
  251.7 3.9 collective-permute-done.12
  258.2 6.2 slice_multiply_fusion.3
  278.6 6.0 all-to-all-start.3
  288.1 43.4 %all-to-all-done.3 = f32[8,9,64,128]{3,2,1,0:T(8,128)} async-done(((f32[8,9,64,128]{3,2,1,0:T(8,128)}), f32[8,9,64,128]{3,2,1,0:T(8,128)}, u32[]{:S(2)}, u32[]{:S(2)}) %all-to-all-start.3) | async-done | bytes 2359328 | tf_op jit(solution)/shard_map/all_to_all | solution.py:169
  331.5 3.8 gather_fusion.4
  338.5 4.4 stack.89
  345.5 3.7 gather_fusion.5
  349.2 61.2 %all_to_all.49 = f32[8,9,64,128]{3,2,1,0:T(8,128)S(1)} all-to-all(f32[8,9,64,128]{3,2,1,0:T(8,128)} %bitcast.314), channel_id=1, replica_groups=mesh['gx'=4,'gy'=8] {'gy'}, dimensions={0} | all-to-all | bytes 4718592 | tf_op jit(solution)/shard_map/all_to_all | solution.py:181
  423.3 3.6 collective-permute-start.17
  434.2 4.8 collective-permute-start.19
  455.1 3.8 collective-permute-done.21
  465.3 5.1 fusion.13
  482.5 4.7 all-to-all-start.5
  487.2 5.3 multiply_reduce_fusion.3
  492.5 41.3 %all-to-all-done.5 = f32[8,9,64,128]{3,2,1,0:T(8,128)} async-done(((f32[8,9,64,128]{3,2,1,0:T(8,128)}), f32[8,9,64,128]{3,2,1,0:T(8,128)}, u32[]{:S(2)}, u32[]{:S(2)}) %all-to-all-start.5) | async-done | bytes 2359328 | tf_op jit(solution)/shard_map/all_to_all | solution.py:169
  533.8 3.8 gather_fusion.7
  537.5 4.4 multiply_reduce_fusion.9
  542.0 4.4 stack.97
  549.9 3.7 gather_fusion.8
  553.7 60.5 %all_to_all.50 = f32[8,9,64,128]{3,2,1,0:T(8,128)S(1)} all-to-all(f32[8,9,64,128]{3,2,1,0:T(8,128)} %bitcast.315), channel_id=1, replica_groups=mesh['gx'=4,'gy'=8] {'gy'}, dimensions={0} | all-to-all | bytes 4718592 | tf_op jit(solution)/shard_map/all_to_all | solution.py:181
  628.4 3.6 collective-permute-start.26
  640.3 5.0 collective-permute-start.28
  660.9 3.8 collective-permute-done.30
  671.3 6.9 slice_multiply_fusion.1
  692.4 4.3 all-to-all-start.7
  696.8 4.4 fusion.16
  701.2 42.1 %all-to-all-done.7 = f32[8,9,64,128]{3,2,1,0:T(8,128)} async-done(((f32[8,9,64,128]{3,2,1,0:T(8,128)}), f32[8,9,64,128]{3,2,1,0:T(8,128)}, u32[]{:S(2)}, u32[]{:S(2)}) %all-to-all-start.7) | async-done | bytes 2359328 | tf_op jit(solution)/shard_map/all_to_all | solution.py:169
  743.3 3.7 gather_fusion.10
  747.0 4.1 multiply_reduce_fusion.8
  751.1 4.5 stack.105
  759.1 3.7 gather_fusion.11
  762.9 60.7 %all_to_all.51 = f32[8,9,64,128]{3,2,1,0:T(8,128)S(1)} all-to-all(f32[8,9,64,128]{3,2,1,0:T(8,128)} %bitcast.313), channel_id=1, replica_groups=mesh['gx'=4,'gy'=8] {'gy'}, dimensions={0} | all-to-all | bytes 4718592 | tf_op jit(solution)/shard_map/all_to_all | solution.py:181
  847.1 4.8 collective-permute-start.37
  869.1 3.8 collective-permute-done.39
  879.4 7.3 fusion.19
  (279 shorter events, 265.5 us)
Async XLA Ops:
  0.6 131.4 %copy-start = (f32[2,4,128,128]{3,2,1,0:T(8,128)S(1)}, f32[2,4,128,128]{3,2,1,0:T(8,128)}, u32[]{:S(2)}) copy-start(f32[2,4,128,128]{3,2,1,0:T(8,128)} %param.8) | copy-start | bytes 1572868
  15.5 17.2 %all-to-all-start = ((s32[8,1,9]{2,1,0:T(1,128)}), s32[8,1,9]{2,1,0:T(1,128)S(1)}, u32[]{:S(2)}, u32[]{:S(2)}) async-start(s32[8,1,9]{2,1,0:T(1,128)} %bitcast.8), calls=%async_computation | async-start | bytes 8192 | tf_op jit(solution)/shard_map/all_to_all | solution.py:150
  23.5 10.5 %collective-permute-start = (f32[12,4,256]{2,1,0:T(4,128)S(1)}, f32[12,4,256]{2,1,0:T(4,128)S(1)}, u32[]{:S(2)}, u32[]{:S(2)}) collective-permute-start(f32[12,4,256]{2,1,0:T(4,128)S(1)} %get-tuple-element.119), channel_id=1, source_target_pairs={{0,8},{8,16},{16,24},{1,9},{9,17},{17,25},{2,10},{10,18},{18,26},{... | collective-permute-start | bytes 147464 | tf_op jit(solution)/shard_map/ppermute | solution.py:25
  25.4 8.6 collective-permute-start.1
  41.2 12.3 %collective-permute-start.3 = (f32[12,264,4]{1,2,0:T(4,128)S(1)}, f32[12,264,4]{1,2,0:T(4,128)S(1)}, u32[]{:S(2)}, u32[]{:S(2)}) collective-permute-start(f32[12,264,4]{1,2,0:T(4,128)S(1)} %copy.41), channel_id=1, source_target_pairs={{1,0},{2,1},{3,2},{4,3},{5,4},{6,5},{7,6},{9,8},{10,9},{11,10},{12... | collective-permute-start | bytes 152072 | tf_op jit(solution)/shard_map/ppermute | solution.py:28
  44.6 7.5 collective-permute-start.2
  75.2 53.0 %all-to-all-start.1 = ((f32[8,9,64,128]{3,2,1,0:T(8,128)}), f32[8,9,64,128]{3,2,1,0:T(8,128)}, u32[]{:S(2)}, u32[]{:S(2)}) async-start(f32[8,9,64,128]{3,2,1,0:T(8,128)} %bitcast.312), calls=%async_computation.1 | async-start | bytes 4718592 | tf_op jit(solution)/shard_map/all_to_all | solution.py:169
  137.2 6.3 collective-permute-start.4
  145.4 60.5 %all-to-all-start.2 = ((f32[8,9,64,128]{3,2,1,0:T(8,128)}), f32[8,9,64,128]{3,2,1,0:T(8,128)}, u32[]{:S(2)}, u32[]{:S(2)}) async-start(f32[8,9,64,128]{3,2,1,0:T(8,128)} %bitcast.308), calls=%async_computation.2 | async-start | bytes 4718592 | tf_op jit(solution)/shard_map/all_to_all | solution.py:181
  209.5 3.6 collective-permute-start.5
  218.9 5.6 collective-permute-start.7
  220.8 5.2 collective-permute-start.8
  230.8 13.3 %collective-permute-start.10 = (f32[4,272,8]{1,2,0:T(8,128)S(1)}, f32[4,272,8]{1,2,0:T(8,128)S(1)}, u32[]{:S(2)}, u32[]{:S(2)}) collective-permute-start(f32[4,272,8]{1,2,0:T(8,128)S(1)} %copy.49), channel_id=1, source_target_pairs={{1,0},{2,1},{3,2},{4,3},{5,4},{6,5},{7,6},{9,8},{10,9},{11,10},{12... | collective-permute-start | bytes 104456 | tf_op jit(solution)/shard_map/ppermute | solution.py:28
  236.2 6.9 collective-permute-start.9
  238.3 3.6 collective-permute-start.6
  247.3 3.9 collective-permute-start.11
  251.2 4.4 collective-permute-start.12
  278.6 52.9 %all-to-all-start.3 = ((f32[8,9,64,128]{3,2,1,0:T(8,128)}), f32[8,9,64,128]{3,2,1,0:T(8,128)}, u32[]{:S(2)}, u32[]{:S(2)}) async-start(f32[8,9,64,128]{3,2,1,0:T(8,128)} %bitcast.311), calls=%async_computation.3 | async-start | bytes 4718592 | tf_op jit(solution)/shard_map/all_to_all | solution.py:169
  288.1 47.2 %copy-start.12 = (f32[2,8,64,128,1]{3,2,4,1,0:T(8,128)S(1)}, f32[2,8,64,128,1]{3,2,4,1,0:T(8,128)}, u32[]{:S(2)}) copy-start(f32[2,8,64,128,1]{3,2,4,1,0:T(8,128)} %copy-done.11) | copy-start | bytes 1572868
  342.9 6.3 collective-permute-start.13
  412.3 5.0 collective-permute-start.14
  421.4 5.6 collective-permute-start.16
  423.3 5.2 collective-permute-start.17
  430.9 11.7 %collective-permute-start.18 = (f32[4,272,8]{1,2,0:T(8,128)S(1)}, f32[4,272,8]{1,2,0:T(8,128)S(1)}, u32[]{:S(2)}, u32[]{:S(2)}) collective-permute-start(f32[4,272,8]{1,2,0:T(8,128)S(1)} %copy.55), channel_id=1, source_target_pairs={{0,1},{1,2},{2,3},{3,4},{4,5},{5,6},{6,7},{8,9},{9,10},{10,11},{11... | collective-permute-start | bytes 104456 | tf_op jit(solution)/shard_map/ppermute | solution.py:25
  434.2 9.5 %collective-permute-start.19 = (f32[4,272,8]{1,2,0:T(8,128)S(1)}, f32[4,272,8]{1,2,0:T(8,128)}, u32[]{:S(2)}, u32[]{:S(2)}) collective-permute-start(f32[4,272,8]{1,2,0:T(8,128)S(1)} %copy.56), channel_id=1, source_target_pairs={{1,0},{2,1},{3,2},{4,3},{5,4},{6,5},{7,6},{9,8},{10,9},{11,10},{12... | collective-permute-start | bytes 104456 | tf_op jit(solution)/shard_map/ppermute | solution.py:28
  439.0 3.6 collective-permute-start.15
  450.9 3.5 collective-permute-start.20
  454.5 4.4 collective-permute-start.21
  482.5 51.3 %all-to-all-start.5 = ((f32[8,9,64,128]{3,2,1,0:T(8,128)}), f32[8,9,64,128]{3,2,1,0:T(8,128)}, u32[]{:S(2)}, u32[]{:S(2)}) async-start(f32[8,9,64,128]{3,2,1,0:T(8,128)} %bitcast.309), calls=%async_computation.5 | async-start | bytes 4718592 | tf_op jit(solution)/shard_map/all_to_all | solution.py:169
  546.3 7.3 collective-permute-start.22
  616.1 4.6 collective-permute-start.23
  626.5 5.6 collective-permute-start.25
  628.4 5.2 collective-permute-start.26
  637.1 11.9 %collective-permute-start.27 = (f32[4,272,8]{1,2,0:T(8,128)S(1)}, f32[4,272,8]{1,2,0:T(8,128)S(1)}, u32[]{:S(2)}, u32[]{:S(2)}) collective-permute-start(f32[4,272,8]{1,2,0:T(8,128)S(1)} %copy.62), channel_id=1, source_target_pairs={{0,1},{1,2},{2,3},{3,4},{4,5},{5,6},{6,7},{8,9},{9,10},{10,11},{11... | collective-permute-start | bytes 104456 | tf_op jit(solution)/shard_map/ppermute | solution.py:25
  640.3 9.6 %collective-permute-start.28 = (f32[4,272,8]{1,2,0:T(8,128)S(1)}, f32[4,272,8]{1,2,0:T(8,128)S(1)}, u32[]{:S(2)}, u32[]{:S(2)}) collective-permute-start(f32[4,272,8]{1,2,0:T(8,128)S(1)} %copy.63), channel_id=1, source_target_pairs={{1,0},{2,1},{3,2},{4,3},{5,4},{6,5},{7,6},{9,8},{10,9},{11,10},{12... | collective-permute-start | bytes 104456 | tf_op jit(solution)/shard_map/ppermute | solution.py:28
  645.3 3.6 collective-permute-start.24
  656.7 3.5 collective-permute-start.29
  660.3 4.4 collective-permute-start.30
  692.4 50.9 %all-to-all-start.7 = ((f32[8,9,64,128]{3,2,1,0:T(8,128)}), f32[8,9,64,128]{3,2,1,0:T(8,128)}, u32[]{:S(2)}, u32[]{:S(2)}) async-start(f32[8,9,64,128]{3,2,1,0:T(8,128)} %bitcast.310), calls=%async_computation.7 | async-start | bytes 4718592 | tf_op jit(solution)/shard_map/all_to_all | solution.py:169
  755.6 7.3 collective-permute-start.31
  825.5 4.7 collective-permute-start.32
  834.3 5.6 collective-permute-start.34
  836.2 5.2 collective-permute-start.35
  843.9 11.7 %collective-permute-start.36 = (f32[4,272,8]{1,2,0:T(8,128)S(1)}, f32[4,272,8]{1,2,0:T(8,128)S(1)}, u32[]{:S(2)}, u32[]{:S(2)}) collective-permute-start(f32[4,272,8]{1,2,0:T(8,128)S(1)} %copy.69), channel_id=1, source_target_pairs={{0,1},{1,2},{2,3},{3,4},{4,5},{5,6},{6,7},{8,9},{9,10},{10,11},{11... | collective-permute-start | bytes 104456 | tf_op jit(solution)/shard_map/ppermute | solution.py:25
  847.1 9.5 %collective-permute-start.37 = (f32[4,272,8]{1,2,0:T(8,128)S(1)}, f32[4,272,8]{1,2,0:T(8,128)S(1)}, u32[]{:S(2)}, u32[]{:S(2)}) collective-permute-start(f32[4,272,8]{1,2,0:T(8,128)S(1)} %copy.70), channel_id=1, source_target_pairs={{1,0},{2,1},{3,2},{4,3},{5,4},{6,5},{7,6},{9,8},{10,9},{11,10},{12... | collective-permute-start | bytes 104456 | tf_op jit(solution)/shard_map/ppermute | solution.py:28
  851.9 3.6 collective-permute-start.33
  861.4 3.6 collective-permute-start.38
  868.5 4.4 collective-permute-start.39
  (21 other events, 202.9 us)

commit v7 on v6

--- a/solution.py
+++ b/solution.py
@@ -200,52 +200,58 @@
 
     rims = with_rim(jnp.concatenate([right_side, jacobi_inverse, prior_weight]))
     residual, jacobi_inverse, prior_weight = jnp.split(rims, 3)
-    solution = jnp.zeros_like(right_side)
     prior_inner = interior(prior_weight)
-    precond_res = jacobi_inverse * residual
-    direction = interior(precond_res)
-    image, direction_slopes, totals = apply_op(
-        precond_res,
-        lambda slopes: jnp.stack(
+
+    def iteration(step, state):
+        solution, residual, direction, direction_slopes, image, rho_now = state
+        precond_res = jacobi_inverse * residual
+        inner = interior(precond_res)
+        field_sums = jnp.stack(
             [
-                jnp.sum(interior(residual) * direction),
-                jnp.sum(slopes * slopes),
+                jnp.sum(interior(residual) * inner),
+                jnp.sum(prior_inner * inner * inner),
+                jnp.sum(prior_inner * inner * direction),
                 jnp.sum(prior_inner * direction * direction),
             ]
-        ),
-    )
-    rho_now = totals[0]
-    step_size = rho_now / (totals[1] + totals[2])
-    for step in range(ITERS):
+        )
+        applied, slopes_now, totals = apply_op(
+            precond_res,
+            lambda slopes: jnp.concatenate(
+                [
+                    field_sums,
+                    jnp.stack(
+                        [
+                            jnp.sum(slopes * slopes),
+                            jnp.sum(slopes * direction_slopes),
+                            jnp.sum(direction_slopes * direction_slopes),
+                        ]
+                    ),
+                ]
+            ),
+        )
+        rho_next = totals[0]
+        ratio = jnp.where(step == 0, 0.0, rho_next / rho_now)
+        curvature = (totals[4] + 2.0 * ratio * totals[5] + ratio * ratio * totals[6]) + (
+            totals[1] + 2.0 * ratio * totals[2] + ratio * ratio * totals[3]
+        )
+        step_size = rho_next / curvature
+        direction = inner + ratio * direction
+        direction_slopes = slopes_now + ratio * direction_slopes
+        image = applied + ratio * image
         solution = solution + step_size * direction
         residual = residual - step_size * image
-        if step + 1 < ITERS:
-            precond_res = jacobi_inverse * residual
-            inner = interior(precond_res)
-            applied, slopes_now, totals = apply_op(
-                precond_res,
-                lambda slopes: jnp.stack(
-                    [
-                        jnp.sum(interior(residual) * inner),
-                        jnp.sum(slopes * slopes),
-                        jnp.sum(slopes * direction_slopes),
-                        jnp.sum(direction_slopes * direction_slopes),
-                        jnp.sum(prior_inner * inner * inner),
-                        jnp.sum(prior_inner * inner * direction),
-                        jnp.sum(prior_inner * direction * direction),
-                    ]
-                ),
-            )
-            rho_next = totals[0]
-            ratio = rho_next / rho_now
-            curvature = (totals[1] + 2.0 * ratio * totals[2] + ratio * ratio * totals[3]) + (
-                totals[4] + 2.0 * ratio * totals[5] + ratio * ratio * totals[6]
-            )
-            step_size = rho_next / curvature
-            direction = inner + ratio * direction
-            direction_slopes = slopes_now + ratio * direction_slopes
-            image = applied + ratio * image
-            rho_now = rho_next
+        return solution, residual, direction, direction_slopes, image, rho_next
+
+    zero_slopes = jnp.zeros((sensors, rows_blocks * cols_blocks, block_rows, block_cols), jnp.float32)
+    state = (
+        jnp.zeros_like(right_side),
+        residual,
+        jnp.zeros_like(right_side),
+        zero_slopes,
+        jnp.zeros_like(residual),
+        jnp.ones((), jnp.float32),
+    )
+    solution, residual, _, _, _, _ = lax.fori_loop(0, ITERS, iteration, state)
     residual = interior(residual)
     return (solution, residual)
 

time: 899 us -> 913 us (1.016)
  waiting for transfers between devices: 278 us -> 205 us
  blocking collectives: 182 us -> 243 us
  local copies, waits for them, and re-layouts: 168 us -> 195 us
  loops' own time: 0 us -> 23.7 us
  between operations: 21.4 us -> 0.93 us
  other arithmetic: 45.2 us -> 54.9 us
    all_to_all x3 -> x4, blocking collectives: 182 us -> 243 us  [apply_op(): lax.all_to_all(returning, 'gy', split_axis=0, concat_axis=0, tiled=True)]
    all_to_all x1 -> x0, waiting for transfers between devices: 52.3 us -> none  [apply_op(): lax.all_to_all(returning, 'gy', split_axis=0, concat_axis=0, tiled=True)]
    another operation x0 -> x1, loops' own time: none -> 23.7 us  [shards(): solution, residual, _, _, _, _ = lax.fori_loop(0, ITERS, iteration, state)]
    ppermute x20, waiting for transfers between devices: 46.6 us -> 26.3 us  [sum_steps(): lax.ppermute(value, axis, pairs)]
    add x0 -> x8, other arithmetic: none -> 20 us  [the longest x4 11.9 us: iteration(): solution = solution + step_size * direction]
    concatenate x0 -> x4, local copies, waits for them, and re-layouts: none -> 18 us  [iteration(): jnp.concatenate([field_sums, jnp.stack([jnp.sum(slopes * slopes), jnp.sum...]
    while x0 -> x93, local copies, waits for them, and re-layouts: none -> 17.5 us
    another operation x3 -> x0, local copies, waits for them, and re-layouts: 13.2 us -> none  [shards(): jnp.stack([jnp.sum(interior(residual) * inner), jnp.sum(slopes * slopes),...]
  transfers between devices with their start and end apart: 46 -> 45, of which waited for: 26 -> 18; matrix products, arithmetic and copies ran while one was open for 8% -> 11% of each run, Pallas kernels for 0% -> 0%
where the time goes in v7:
time: 913 us; the launch traced here: 908 us
  blocking collectives  243 us (27%)
  waiting for transfers between devices  205 us (22%)
  local copies, waits for them, and re-layouts  195 us (21%)
  starting transfers between devices  110 us (12%)
  matrix products  74.6 us (8%)
  other arithmetic  54.9 us (6%)
  loops' own time  23.7 us (3%)
    all_to_all x4, blocking collectives, apply_op(): lax.all_to_all(returning, 'gy', split_axis=0, concat_axis=0, tiled=True)  243 us
    all_to_all x4, waiting for transfers between devices, apply_op(): lax.all_to_all(outgoing, 'gy', split_axis=0, concat_axis=0, tiled=True)  176 us
    ppermute x10, starting transfers between devices, extended(): lax.ppermute(lax.slice_in_dim(block, 0, width, axis=dim), axis, backward)  36.4 us
    ppermute x20, starting transfers between devices, sum_steps(): lax.ppermute(value, axis, pairs)  26.4 us
    ppermute x20, waiting for transfers between devices, sum_steps(): lax.ppermute(value, axis, pairs)  26.3 us
    another operation x1, loops' own time, shards(): solution, residual, _, _, _, _ = lax.fori_loop(0, ITERS, iteration, state)  23.7 us
    all_to_all x4, starting transfers between devices, apply_op(): lax.all_to_all(outgoing, 'gy', split_axis=0, concat_axis=0, tiled=True)  20.8 us
    ppermute x10, starting transfers between devices, extended(): lax.ppermute(lax.slice_in_dim(block, block.shape[dim] - width, None, axis...  20.6 us
  transfers between devices with their start and end apart: 45, of which 18 were waited for; matrix products, arithmetic and copies ran while one was open for 11% of the time, Pallas kernels for 0%

profile of v7, /device:TPU:10, one launch (start us, length us, event | category | flops | bytes accessed | tf_op | source)
XLA Modules:
  0.0 907.9 jit_solution(17484722206949680154)
XLA Ops:
  4.5 3.6 collective-permute-start.10
  26.3 10.2 %scatter_fusion = s32[8,9]{1,0:T(8,128)} fusion(s32[8,9]{1,0:T(8,128)} %broadcast_in_dim.311, s32[64]{0:T(128)S(1)} %fusion.68, s32[64]{0:T(128)S(1)} %get-tuple-element.875), kind=kCustom, calls=%fused_computation.3 | custom fusion | bytes 1280 | tf_op jit(solution)/shard_map/scatter | solution.py:145
  36.5 6.2 all-to-all-start.2
  54.1 4.3 pad_maximum_fusion.1
  65.2 839.2 %while.27 = (s32[]{:T(128)}, f32[4,256,256]{1,2,0:T(8,128)}, f32[4,264,264]{1,2,0:T(8,128)S(1)}, f32[4,256,256]{1,2,0:T(8,128)}, f32[2,8,64,128]{3,2,1,0:T(8,128...) while((s32[]{:T(128)}, f32[4,256,256]{1,2,0:T(8,128)}, ...), condition=%wide.wide.region_12.13_spmd.clone.clone, body=%wide.wide.region_4.12_spmd.clone.clone.sunk | while | flops 2699075072 | bytes 109535104 | solution.py:254
  79.3 5.7 all-to-all-start
  87.7 44.3 %all-to-all-done = f32[8,9,64,128]{3,2,1,0:T(8,128)} async-done(((f32[8,9,64,128]{3,2,1,0:T(8,128)}), f32[8,9,64,128]{3,2,1,0:T(8,128)}, u32[]{:S(2)}, u32[]{:S(2)}) %all-to-all-start) | async-done | bytes 2359328 | tf_op jit(solution)/shard_map/while/body/eval_jaxpr/all_to_all | solution.py:169
  132.0 3.7 gather_fusion.1
  135.7 4.1 multiply_reduce_fusion.9
  139.9 4.5 concatenate.85
  148.0 3.7 gather_fusion.2
  151.8 60.9 %all_to_all.40 = f32[8,9,64,128]{3,2,1,0:T(8,128)S(1)} all-to-all(f32[8,9,64,128]{3,2,1,0:T(8,128)} %bitcast.230), channel_id=1, replica_groups=mesh['gx'=4,'gy'=8] {'gy'}, dimensions={0} | all-to-all | bytes 4718592 | tf_op jit(solution)/shard_map/while/body/eval_jaxpr/all_to_all | solution.py:181
  212.6 4.2 collective-permute-start.1
  226.7 3.6 collective-permute-start.4
  235.4 3.7 collective-permute-start.5
  256.4 3.8 collective-permute-done.8
  289.8 5.0 all-to-all-start
  297.8 43.8 %all-to-all-done = f32[8,9,64,128]{3,2,1,0:T(8,128)} async-done(((f32[8,9,64,128]{3,2,1,0:T(8,128)}), f32[8,9,64,128]{3,2,1,0:T(8,128)}, u32[]{:S(2)}, u32[]{:S(2)}) %all-to-all-start) | async-done | bytes 2359328 | tf_op jit(solution)/shard_map/while/body/eval_jaxpr/all_to_all | solution.py:169
  341.6 3.7 gather_fusion.1
  345.3 4.3 multiply_reduce_fusion.9
  349.6 4.5 concatenate.85
  357.8 3.7 gather_fusion.2
  361.5 60.7 %all_to_all.40 = f32[8,9,64,128]{3,2,1,0:T(8,128)S(1)} all-to-all(f32[8,9,64,128]{3,2,1,0:T(8,128)} %bitcast.230), channel_id=1, replica_groups=mesh['gx'=4,'gy'=8] {'gy'}, dimensions={0} | all-to-all | bytes 4718592 | tf_op jit(solution)/shard_map/while/body/eval_jaxpr/all_to_all | solution.py:181
  422.2 3.7 collective-permute-start.1
  435.7 3.6 collective-permute-start.4
  444.4 3.7 collective-permute-start.5
  465.3 4.0 collective-permute-done.8
  499.3 5.0 all-to-all-start
  507.3 43.8 %all-to-all-done = f32[8,9,64,128]{3,2,1,0:T(8,128)} async-done(((f32[8,9,64,128]{3,2,1,0:T(8,128)}), f32[8,9,64,128]{3,2,1,0:T(8,128)}, u32[]{:S(2)}, u32[]{:S(2)}) %all-to-all-start) | async-done | bytes 2359328 | tf_op jit(solution)/shard_map/while/body/eval_jaxpr/all_to_all | solution.py:169
  551.1 3.7 gather_fusion.1
  554.8 4.3 multiply_reduce_fusion.9
  559.1 4.5 concatenate.85
  567.3 3.7 gather_fusion.2
  571.0 60.7 %all_to_all.40 = f32[8,9,64,128]{3,2,1,0:T(8,128)S(1)} all-to-all(f32[8,9,64,128]{3,2,1,0:T(8,128)} %bitcast.230), channel_id=1, replica_groups=mesh['gx'=4,'gy'=8] {'gy'}, dimensions={0} | all-to-all | bytes 4718592 | tf_op jit(solution)/shard_map/while/body/eval_jaxpr/all_to_all | solution.py:181
  631.7 3.7 collective-permute-start.1
  645.2 3.6 collective-permute-start.4
  653.9 3.7 collective-permute-start.5
  674.8 4.0 collective-permute-done.8
  708.8 5.0 all-to-all-start
  716.8 43.8 %all-to-all-done = f32[8,9,64,128]{3,2,1,0:T(8,128)} async-done(((f32[8,9,64,128]{3,2,1,0:T(8,128)}), f32[8,9,64,128]{3,2,1,0:T(8,128)}, u32[]{:S(2)}, u32[]{:S(2)}) %all-to-all-start) | async-done | bytes 2359328 | tf_op jit(solution)/shard_map/while/body/eval_jaxpr/all_to_all | solution.py:169
  760.6 3.7 gather_fusion.1
  764.3 4.3 multiply_reduce_fusion.9
  768.6 4.5 concatenate.85
  776.8 3.7 gather_fusion.2
  780.5 60.7 %all_to_all.40 = f32[8,9,64,128]{3,2,1,0:T(8,128)S(1)} all-to-all(f32[8,9,64,128]{3,2,1,0:T(8,128)} %bitcast.230), channel_id=1, replica_groups=mesh['gx'=4,'gy'=8] {'gy'}, dimensions={0} | all-to-all | bytes 4718592 | tf_op jit(solution)/shard_map/while/body/eval_jaxpr/all_to_all | solution.py:181
  841.2 3.7 collective-permute-start.1
  863.4 3.7 collective-permute-start.5
  884.3 4.0 collective-permute-done.8
  (352 shorter events, 298.0 us)
Async XLA Ops:
  2.6 6.3 collective-permute-start.9
  4.5 5.4 collective-permute-start.10
  17.2 34.3 %collective-permute-start.12 = (f32[12,264,4]{1,2,0:T(4,128)S(1)}, f32[12,264,4]{1,2,0:T(4,128)}, u32[]{:S(2)}, u32[]{:S(2)}) collective-permute-start(f32[12,264,4]{1,2,0:T(4,128)S(1)} %copy.52), channel_id=1, source_target_pairs={{1,0},{2,1},{3,2},{4,3},{5,4},{6,5},{7,6},{9,8},{10,9},{11,10},{12... | collective-permute-start | bytes 152072 | tf_op jit(solution)/shard_map/ppermute | solution.py:28
  20.5 28.4 %collective-permute-start.11 = (f32[12,264,4]{1,2,0:T(4,128)}, f32[12,264,4]{1,2,0:T(4,128)}, u32[]{:S(2)}, u32[]{:S(2)}) collective-permute-start(f32[12,264,4]{1,2,0:T(4,128)} %copy.51), channel_id=1, source_target_pairs={{0,1},{1,2},{2,3},{3,4},{4,5},{5,6},{6,7},{8,9},{9,10},{10,11},{11... | collective-permute-start | bytes 152072 | tf_op jit(solution)/shard_map/ppermute | solution.py:25
  36.5 11.2 %all-to-all-start.2 = ((s32[8,1,9]{2,1,0:T(1,128)}), s32[8,1,9]{2,1,0:T(1,128)S(1)}, u32[]{:S(2)}, u32[]{:S(2)}) async-start(s32[8,1,9]{2,1,0:T(1,128)} %bitcast.3), calls=%async_computation.2 | async-start | bytes 8192 | tf_op jit(solution)/shard_map/all_to_all | solution.py:150
  65.4 19.6 %copy-start.11 = (s32[64]{0:T(128)}, s32[64]{0:T(128)S(1)}, u32[]{:S(2)}) copy-start(s32[64]{0:T(128)S(1)} %get-tuple-element.1544) | copy-start | bytes 772 | tf_op jit(solution)/shard_map/while
  65.4 19.6 %copy-start.13 = (s32[64]{0:T(128)}, s32[64]{0:T(128)S(1)}, u32[]{:S(2)}) copy-start(s32[64]{0:T(128)S(1)} %get-tuple-element.1545) | copy-start | bytes 772 | tf_op jit(solution)/shard_map/while
  79.3 52.7 %all-to-all-start = ((f32[8,9,64,128]{3,2,1,0:T(8,128)}), f32[8,9,64,128]{3,2,1,0:T(8,128)}, u32[]{:S(2)}, u32[]{:S(2)}) async-start(f32[8,9,64,128]{3,2,1,0:T(8,128)} %bitcast.229), calls=%async_computation | async-start | bytes 4718592 | tf_op jit(solution)/shard_map/while/body/eval_jaxpr/all_to_all | solution.py:169
  144.3 7.4 collective-permute-start
  212.6 6.2 collective-permute-start.1
  224.7 5.6 collective-permute-start.3
  226.7 5.2 collective-permute-start.4
  235.4 11.3 %collective-permute-start.5 = (f32[4,272,8]{1,2,0:T(8,128)S(1)}, f32[4,272,8]{1,2,0:T(8,128)S(1)}, u32[]{:S(2)}, u32[]{:S(2)}) collective-permute-start(f32[4,272,8]{1,2,0:T(8,128)S(1)} %copy.93), channel_id=1, source_target_pairs={{1,0},{2,1},{3,2},{4,3},{5,4},{6,5},{7,6},{9,8},{10,9},{11,10},{12... | collective-permute-start | bytes 104456 | tf_op jit(solution)/shard_map/while/body/eval_jaxpr/ppermute | solution.py:28
  240.4 7.4 collective-permute-start.6
  242.5 3.6 collective-permute-start.2
  251.0 4.8 collective-permute-start.7
  255.8 4.4 collective-permute-start.8
  289.8 51.8 %all-to-all-start = ((f32[8,9,64,128]{3,2,1,0:T(8,128)}), f32[8,9,64,128]{3,2,1,0:T(8,128)}, u32[]{:S(2)}, u32[]{:S(2)}) async-start(f32[8,9,64,128]{3,2,1,0:T(8,128)} %bitcast.229), calls=%async_computation | async-start | bytes 4718592 | tf_op jit(solution)/shard_map/while/body/eval_jaxpr/all_to_all | solution.py:169
  354.1 7.4 collective-permute-start
  422.2 5.7 collective-permute-start.1
  433.8 5.6 collective-permute-start.3
  435.7 5.2 collective-permute-start.4
  444.4 11.3 %collective-permute-start.5 = (f32[4,272,8]{1,2,0:T(8,128)S(1)}, f32[4,272,8]{1,2,0:T(8,128)S(1)}, u32[]{:S(2)}, u32[]{:S(2)}) collective-permute-start(f32[4,272,8]{1,2,0:T(8,128)S(1)} %copy.93), channel_id=1, source_target_pairs={{1,0},{2,1},{3,2},{4,3},{5,4},{6,5},{7,6},{9,8},{10,9},{11,10},{12... | collective-permute-start | bytes 104456 | tf_op jit(solution)/shard_map/while/body/eval_jaxpr/ppermute | solution.py:28
  449.4 7.4 collective-permute-start.6
  451.5 3.6 collective-permute-start.2
  460.0 4.8 collective-permute-start.7
  464.8 4.4 collective-permute-start.8
  485.4 18.9 %copy-start.11 = (s32[64]{0:T(128)}, s32[64]{0:T(128)S(1)}, u32[]{:S(2)}) copy-start(s32[64]{0:T(128)S(1)} %get-tuple-element.1544) | copy-start | bytes 772 | tf_op jit(solution)/shard_map/while
  499.3 51.8 %all-to-all-start = ((f32[8,9,64,128]{3,2,1,0:T(8,128)}), f32[8,9,64,128]{3,2,1,0:T(8,128)}, u32[]{:S(2)}, u32[]{:S(2)}) async-start(f32[8,9,64,128]{3,2,1,0:T(8,128)} %bitcast.229), calls=%async_computation | async-start | bytes 4718592 | tf_op jit(solution)/shard_map/while/body/eval_jaxpr/all_to_all | solution.py:169
  563.6 7.4 collective-permute-start
  631.7 5.7 collective-permute-start.1
  643.3 5.6 collective-permute-start.3
  645.2 5.2 collective-permute-start.4
  653.9 11.3 %collective-permute-start.5 = (f32[4,272,8]{1,2,0:T(8,128)S(1)}, f32[4,272,8]{1,2,0:T(8,128)S(1)}, u32[]{:S(2)}, u32[]{:S(2)}) collective-permute-start(f32[4,272,8]{1,2,0:T(8,128)S(1)} %copy.93), channel_id=1, source_target_pairs={{1,0},{2,1},{3,2},{4,3},{5,4},{6,5},{7,6},{9,8},{10,9},{11,10},{12... | collective-permute-start | bytes 104456 | tf_op jit(solution)/shard_map/while/body/eval_jaxpr/ppermute | solution.py:28
  658.9 7.4 collective-permute-start.6
  661.0 3.6 collective-permute-start.2
  669.5 4.8 collective-permute-start.7
  674.3 4.4 collective-permute-start.8
  708.8 51.8 %all-to-all-start = ((f32[8,9,64,128]{3,2,1,0:T(8,128)}), f32[8,9,64,128]{3,2,1,0:T(8,128)}, u32[]{:S(2)}, u32[]{:S(2)}) async-start(f32[8,9,64,128]{3,2,1,0:T(8,128)} %bitcast.229), calls=%async_computation | async-start | bytes 4718592 | tf_op jit(solution)/shard_map/while/body/eval_jaxpr/all_to_all | solution.py:169
  773.1 7.4 collective-permute-start
  841.2 5.7 collective-permute-start.1
  852.8 5.6 collective-permute-start.3
  854.7 5.2 collective-permute-start.4
  863.4 11.3 %collective-permute-start.5 = (f32[4,272,8]{1,2,0:T(8,128)S(1)}, f32[4,272,8]{1,2,0:T(8,128)S(1)}, u32[]{:S(2)}, u32[]{:S(2)}) collective-permute-start(f32[4,272,8]{1,2,0:T(8,128)S(1)} %copy.93), channel_id=1, source_target_pairs={{1,0},{2,1},{3,2},{4,3},{5,4},{6,5},{7,6},{9,8},{10,9},{11,10},{12... | collective-permute-start | bytes 104456 | tf_op jit(solution)/shard_map/while/body/eval_jaxpr/ppermute | solution.py:28
  868.4 7.4 collective-permute-start.6
  870.5 3.6 collective-permute-start.2
  879.0 4.8 collective-permute-start.7
  883.8 4.4 collective-permute-start.8
  (43 other events, 209.9 us)

commit v8 on v6

--- a/solution.py
+++ b/solution.py
@@ -142,16 +142,16 @@
     )
     picks = (target[:, None] == jnp.arange(owners, dtype=jnp.int32)[None, :]).astype(jnp.int32)
     slot = jnp.sum(picks * (jnp.cumsum(picks, axis=0) - 1), axis=1)
-    send_ids = jnp.full((owners, capacity), own_blocks, jnp.int32).at[target, slot].set(owned_index)
-    send_pairs = (
-        jnp.zeros((owners, capacity), jnp.int32).at[target, slot].set(sensor_of * layers + layer_of)
-    )
-    wanted_ids, wanted_pairs = (
-        lax.all_to_all(send_ids, "gy", split_axis=0, concat_axis=0, tiled=True),
-        lax.all_to_all(send_pairs, "gy", split_axis=0, concat_axis=0, tiled=True),
-    )
-    slot_source = (
-        jnp.full((owners, capacity), requests, jnp.int32).at[target, slot].set(request_num)
+    hit = (target[:, None, None] == jnp.arange(owners, dtype=jnp.int32)[None, :, None]) & (
+        slot[:, None, None] == jnp.arange(capacity, dtype=jnp.int32)[None, None, :]
+    )
+    used = jnp.any(hit, axis=0)
+    send_ids = jnp.where(
+        used, jnp.sum(jnp.where(hit, owned_index[:, None, None], 0), axis=0), own_blocks
+    )
+    wanted_ids = lax.all_to_all(send_ids, "gy", split_axis=0, concat_axis=0, tiled=True)
+    slot_source = jnp.where(
+        used, jnp.sum(jnp.where(hit, request_num[:, None, None], 0), axis=0), requests
     )
     landing = (
         wanted_ids.reshape(-1)[None, :] == jnp.arange(own_blocks, dtype=jnp.int32)[:, None]

time: 899 us -> 886 us (0.986)
  local copies, waits for them, and re-layouts: 168 us -> 154 us
    scatter x2 -> x0, local copies, waits for them, and re-layouts: 15.6 us -> none  [the longest x1 12.1 us: shards(): jnp.full((owners, capacity), own_blocks, jnp.int32).at[target, slot]]
  transfers between devices with their start and end apart: 46 -> 46, of which waited for: 26 -> 27; matrix products, arithmetic and copies ran while one was open for 8% -> 7% of each run, Pallas kernels for 0% -> 0%
where the time goes in v8:
time: 886 us; the launch traced here: 875 us
  waiting for transfers between devices  278 us (31%)
  blocking collectives  182 us (21%)
  local copies, waits for them, and re-layouts  154 us (17%)
  starting transfers between devices  113 us (13%)
  matrix products  81 us (9%)
  other arithmetic  45.9 us (5%)
  between operations  21.2 us (2%)
    all_to_all x3, blocking collectives, apply_op(): lax.all_to_all(returning, 'gy', split_axis=0, concat_axis=0, tiled=True)  182 us
    all_to_all x4, waiting for transfers between devices, apply_op(): lax.all_to_all(outgoing, 'gy', split_axis=0, concat_axis=0, tiled=True)  172 us
    all_to_all x1, waiting for transfers between devices, apply_op(): lax.all_to_all(returning, 'gy', split_axis=0, concat_axis=0, tiled=True)  52.3 us
    ppermute x20, waiting for transfers between devices, sum_steps(): lax.ppermute(value, axis, pairs)  46.1 us
    ppermute x10, starting transfers between devices, extended(): lax.ppermute(lax.slice_in_dim(block, 0, width, axis=dim), axis, backward)  41.6 us
    dot_general x4, matrix products, apply_op(): jnp.einsum('lab,ac->lcb', along_cols, analysis_rows, precision=highest)  21.7 us
    all_to_all x4, starting transfers between devices, apply_op(): lax.all_to_all(outgoing, 'gy', split_axis=0, concat_axis=0, tiled=True)  20.4 us
    ppermute x10, starting transfers between devices, extended(): lax.ppermute(lax.slice_in_dim(block, block.shape[dim] - width, None, axis...  20 us
  transfers between devices with their start and end apart: 46, of which 27 were waited for; matrix products, arithmetic and copies ran while one was open for 7% of the time, Pallas kernels for 0%

profile of v8, /device:TPU:10, one launch (start us, length us, event | category | flops | bytes accessed | tf_op | source)
XLA Modules:
  0.0 874.8 jit_solution(3657886598697555410)
XLA Ops:
  3.4 6.3 all-to-all-start
  14.9 3.6 collective-permute-start.1
  33.4 5.0 collective-permute-done.2
  41.5 4.8 pad_maximum_fusion
  61.6 5.5 all-to-all-start.1
  69.4 45.1 %all-to-all-done.1 = f32[8,9,64,128]{3,2,1,0:T(8,128)} async-done(((f32[8,9,64,128]{3,2,1,0:T(8,128)}), f32[8,9,64,128]{3,2,1,0:T(8,128)}, u32[]{:S(2)}, u32[]{:S(2)}) %all-to-all-start.1) | async-done | bytes 2359328 | tf_op jit(solution)/shard_map/all_to_all | solution.py:169
  114.5 3.8 gather_fusion.1
  126.1 3.7 gather_fusion.2
  131.8 8.2 all-to-all-start.2
  140.1 52.3 %all-to-all-done.2 = f32[8,9,64,128]{3,2,1,0:T(8,128)} async-done(((f32[8,9,64,128]{3,2,1,0:T(8,128)}), f32[8,9,64,128]{3,2,1,0:T(8,128)}, u32[]{:S(2)}, u32[]{:S(2)}) %all-to-all-start.2) | async-done | bytes 2359328 | tf_op jit(solution)/shard_map/all_to_all | solution.py:181
  195.9 3.7 collective-permute-start.5
  208.8 3.6 collective-permute-start.8
  218.8 5.4 collective-permute-start.10
  239.7 3.9 collective-permute-done.12
  246.1 6.2 slice_multiply_fusion.3
  266.6 6.0 all-to-all-start.3
  276.0 43.4 %all-to-all-done.3 = f32[8,9,64,128]{3,2,1,0:T(8,128)} async-done(((f32[8,9,64,128]{3,2,1,0:T(8,128)}), f32[8,9,64,128]{3,2,1,0:T(8,128)}, u32[]{:S(2)}, u32[]{:S(2)}) %all-to-all-start.3) | async-done | bytes 2359328 | tf_op jit(solution)/shard_map/all_to_all | solution.py:169
  319.5 3.8 gather_fusion.4
  326.5 4.4 stack.89
  333.5 3.7 gather_fusion.5
  337.2 61.2 %all_to_all.46 = f32[8,9,64,128]{3,2,1,0:T(8,128)S(1)} all-to-all(f32[8,9,64,128]{3,2,1,0:T(8,128)} %bitcast.303), channel_id=1, replica_groups=mesh['gx'=4,'gy'=8] {'gy'}, dimensions={0} | all-to-all | bytes 4718592 | tf_op jit(solution)/shard_map/all_to_all | solution.py:181
  411.3 3.6 collective-permute-start.17
  422.1 4.8 collective-permute-start.19
  443.0 3.8 collective-permute-done.21
  453.3 5.1 fusion.13
  470.4 4.6 all-to-all-start.5
  475.1 5.4 multiply_reduce_fusion.3
  480.5 41.2 %all-to-all-done.5 = f32[8,9,64,128]{3,2,1,0:T(8,128)} async-done(((f32[8,9,64,128]{3,2,1,0:T(8,128)}), f32[8,9,64,128]{3,2,1,0:T(8,128)}, u32[]{:S(2)}, u32[]{:S(2)}) %all-to-all-start.5) | async-done | bytes 2359328 | tf_op jit(solution)/shard_map/all_to_all | solution.py:169
  521.7 3.8 gather_fusion.7
  525.5 4.4 multiply_reduce_fusion.9
  529.9 4.3 stack.97
  537.7 3.7 gather_fusion.8
  541.5 60.5 %all_to_all.47 = f32[8,9,64,128]{3,2,1,0:T(8,128)S(1)} all-to-all(f32[8,9,64,128]{3,2,1,0:T(8,128)} %bitcast.304), channel_id=1, replica_groups=mesh['gx'=4,'gy'=8] {'gy'}, dimensions={0} | all-to-all | bytes 4718592 | tf_op jit(solution)/shard_map/all_to_all | solution.py:181
  616.2 3.6 collective-permute-start.26
  628.2 5.0 collective-permute-start.28
  648.8 3.8 collective-permute-done.30
  659.0 6.9 slice_multiply_fusion.1
  680.1 4.3 all-to-all-start.7
  684.5 4.4 fusion.16
  688.9 42.1 %all-to-all-done.7 = f32[8,9,64,128]{3,2,1,0:T(8,128)} async-done(((f32[8,9,64,128]{3,2,1,0:T(8,128)}), f32[8,9,64,128]{3,2,1,0:T(8,128)}, u32[]{:S(2)}, u32[]{:S(2)}) %all-to-all-start.7) | async-done | bytes 2359328 | tf_op jit(solution)/shard_map/all_to_all | solution.py:169
  731.0 3.7 gather_fusion.10
  734.7 4.1 multiply_reduce_fusion.8
  738.8 4.5 stack.105
  746.8 3.7 gather_fusion.11
  750.5 60.7 %all_to_all.48 = f32[8,9,64,128]{3,2,1,0:T(8,128)S(1)} all-to-all(f32[8,9,64,128]{3,2,1,0:T(8,128)} %bitcast.302), channel_id=1, replica_groups=mesh['gx'=4,'gy'=8] {'gy'}, dimensions={0} | all-to-all | bytes 4718592 | tf_op jit(solution)/shard_map/all_to_all | solution.py:181
  834.8 4.8 collective-permute-start.37
  856.8 3.8 collective-permute-done.39
  867.1 7.3 fusion.19
  (282 shorter events, 262.0 us)
Async XLA Ops:
  0.6 117.6 %copy-start = (f32[2,4,128,128]{3,2,1,0:T(8,128)S(1)}, f32[2,4,128,128]{3,2,1,0:T(8,128)}, u32[]{:S(2)}) copy-start(f32[2,4,128,128]{3,2,1,0:T(8,128)} %param.8) | copy-start | bytes 1572868
  3.4 15.4 %all-to-all-start = ((s32[8,1,9]{2,1,0:T(1,128)}), s32[8,1,9]{2,1,0:T(1,128)S(1)}, u32[]{:S(2)}, u32[]{:S(2)}) async-start(s32[8,1,9]{2,1,0:T(1,128)} %copy.81), calls=%async_computation | async-start | bytes 8192 | tf_op jit(solution)/shard_map/all_to_all | solution.py:152
  13.0 7.1 collective-permute-start
  14.9 5.4 collective-permute-start.1
  27.5 12.3 %collective-permute-start.3 = (f32[12,264,4]{1,2,0:T(4,128)S(1)}, f32[12,264,4]{1,2,0:T(4,128)S(1)}, u32[]{:S(2)}, u32[]{:S(2)}) collective-permute-start(f32[12,264,4]{1,2,0:T(4,128)S(1)} %copy.74), channel_id=1, source_target_pairs={{1,0},{2,1},{3,2},{4,3},{5,4},{6,5},{7,6},{9,8},{10,9},{11,10},{12... | collective-permute-start | bytes 152072 | tf_op jit(solution)/shard_map/ppermute | solution.py:28
  30.9 7.5 collective-permute-start.2
  61.6 52.9 %all-to-all-start.1 = ((f32[8,9,64,128]{3,2,1,0:T(8,128)}), f32[8,9,64,128]{3,2,1,0:T(8,128)}, u32[]{:S(2)}, u32[]{:S(2)}) async-start(f32[8,9,64,128]{3,2,1,0:T(8,128)} %bitcast.298), calls=%async_computation.1 | async-start | bytes 4718592 | tf_op jit(solution)/shard_map/all_to_all | solution.py:169
  123.6 6.3 collective-permute-start.4
  131.8 60.5 %all-to-all-start.2 = ((f32[8,9,64,128]{3,2,1,0:T(8,128)}), f32[8,9,64,128]{3,2,1,0:T(8,128)}, u32[]{:S(2)}, u32[]{:S(2)}) async-start(f32[8,9,64,128]{3,2,1,0:T(8,128)} %bitcast.297), calls=%async_computation.2 | async-start | bytes 4718592 | tf_op jit(solution)/shard_map/all_to_all | solution.py:181
  195.9 5.2 collective-permute-start.5
  206.8 5.6 collective-permute-start.7
  208.8 5.2 collective-permute-start.8
  218.8 13.3 %collective-permute-start.10 = (f32[4,272,8]{1,2,0:T(8,128)S(1)}, f32[4,272,8]{1,2,0:T(8,128)S(1)}, u32[]{:S(2)}, u32[]{:S(2)}) collective-permute-start(f32[4,272,8]{1,2,0:T(8,128)S(1)} %copy.85), channel_id=1, source_target_pairs={{1,0},{2,1},{3,2},{4,3},{5,4},{6,5},{7,6},{9,8},{10,9},{11,10},{12... | collective-permute-start | bytes 104456 | tf_op jit(solution)/shard_map/ppermute | solution.py:28
  224.1 6.9 collective-permute-start.9
  226.3 3.6 collective-permute-start.6
  235.3 3.9 collective-permute-start.11
  239.2 4.4 collective-permute-start.12
  266.6 52.9 %all-to-all-start.3 = ((f32[8,9,64,128]{3,2,1,0:T(8,128)}), f32[8,9,64,128]{3,2,1,0:T(8,128)}, u32[]{:S(2)}, u32[]{:S(2)}) async-start(f32[8,9,64,128]{3,2,1,0:T(8,128)} %bitcast.301), calls=%async_computation.3 | async-start | bytes 4718592 | tf_op jit(solution)/shard_map/all_to_all | solution.py:169
  276.0 47.2 %copy-start.12 = (f32[2,8,64,128,1]{3,2,4,1,0:T(8,128)S(1)}, f32[2,8,64,128,1]{3,2,4,1,0:T(8,128)}, u32[]{:S(2)}) copy-start(f32[2,8,64,128,1]{3,2,4,1,0:T(8,128)} %copy-done.11) | copy-start | bytes 1572868
  330.9 6.3 collective-permute-start.13
  400.3 5.0 collective-permute-start.14
  409.3 5.6 collective-permute-start.16
  411.3 5.2 collective-permute-start.17
  418.9 11.7 %collective-permute-start.18 = (f32[4,272,8]{1,2,0:T(8,128)S(1)}, f32[4,272,8]{1,2,0:T(8,128)S(1)}, u32[]{:S(2)}, u32[]{:S(2)}) collective-permute-start(f32[4,272,8]{1,2,0:T(8,128)S(1)} %copy.91), channel_id=1, source_target_pairs={{0,1},{1,2},{2,3},{3,4},{4,5},{5,6},{6,7},{8,9},{9,10},{10,11},{11... | collective-permute-start | bytes 104456 | tf_op jit(solution)/shard_map/ppermute | solution.py:25
  422.1 9.5 %collective-permute-start.19 = (f32[4,272,8]{1,2,0:T(8,128)S(1)}, f32[4,272,8]{1,2,0:T(8,128)}, u32[]{:S(2)}, u32[]{:S(2)}) collective-permute-start(f32[4,272,8]{1,2,0:T(8,128)S(1)} %copy.92), channel_id=1, source_target_pairs={{1,0},{2,1},{3,2},{4,3},{5,4},{6,5},{7,6},{9,8},{10,9},{11,10},{12... | collective-permute-start | bytes 104456 | tf_op jit(solution)/shard_map/ppermute | solution.py:28
  427.0 3.6 collective-permute-start.15
  438.9 3.5 collective-permute-start.20
  442.4 4.4 collective-permute-start.21
  470.4 51.3 %all-to-all-start.5 = ((f32[8,9,64,128]{3,2,1,0:T(8,128)}), f32[8,9,64,128]{3,2,1,0:T(8,128)}, u32[]{:S(2)}, u32[]{:S(2)}) async-start(f32[8,9,64,128]{3,2,1,0:T(8,128)} %bitcast.299), calls=%async_computation.5 | async-start | bytes 4718592 | tf_op jit(solution)/shard_map/all_to_all | solution.py:169
  534.1 7.3 collective-permute-start.22
  603.9 4.6 collective-permute-start.23
  614.3 5.6 collective-permute-start.25
  616.2 5.2 collective-permute-start.26
  624.9 11.9 %collective-permute-start.27 = (f32[4,272,8]{1,2,0:T(8,128)S(1)}, f32[4,272,8]{1,2,0:T(8,128)S(1)}, u32[]{:S(2)}, u32[]{:S(2)}) collective-permute-start(f32[4,272,8]{1,2,0:T(8,128)S(1)} %copy.98), channel_id=1, source_target_pairs={{0,1},{1,2},{2,3},{3,4},{4,5},{5,6},{6,7},{8,9},{9,10},{10,11},{11... | collective-permute-start | bytes 104456 | tf_op jit(solution)/shard_map/ppermute | solution.py:25
  628.2 9.6 %collective-permute-start.28 = (f32[4,272,8]{1,2,0:T(8,128)S(1)}, f32[4,272,8]{1,2,0:T(8,128)S(1)}, u32[]{:S(2)}, u32[]{:S(2)}) collective-permute-start(f32[4,272,8]{1,2,0:T(8,128)S(1)} %copy.99), channel_id=1, source_target_pairs={{1,0},{2,1},{3,2},{4,3},{5,4},{6,5},{7,6},{9,8},{10,9},{11,10},{12... | collective-permute-start | bytes 104456 | tf_op jit(solution)/shard_map/ppermute | solution.py:28
  633.2 3.6 collective-permute-start.24
  644.6 3.5 collective-permute-start.29
  648.1 4.4 collective-permute-start.30
  680.1 50.9 %all-to-all-start.7 = ((f32[8,9,64,128]{3,2,1,0:T(8,128)}), f32[8,9,64,128]{3,2,1,0:T(8,128)}, u32[]{:S(2)}, u32[]{:S(2)}) async-start(f32[8,9,64,128]{3,2,1,0:T(8,128)} %bitcast.300), calls=%async_computation.7 | async-start | bytes 4718592 | tf_op jit(solution)/shard_map/all_to_all | solution.py:169
  743.3 7.3 collective-permute-start.31
  813.2 4.7 collective-permute-start.32
  822.0 5.6 collective-permute-start.34
  823.9 5.2 collective-permute-start.35
  831.5 11.7 %collective-permute-start.36 = (f32[4,272,8]{1,2,0:T(8,128)S(1)}, f32[4,272,8]{1,2,0:T(8,128)S(1)}, u32[]{:S(2)}, u32[]{:S(2)}) collective-permute-start(f32[4,272,8]{1,2,0:T(8,128)S(1)} %copy.105), channel_id=1, source_target_pairs={{0,1},{1,2},{2,3},{3,4},{4,5},{5,6},{6,7},{8,9},{9,10},{10,11},{11... | collective-permute-start | bytes 104456 | tf_op jit(solution)/shard_map/ppermute | solution.py:25
  834.8 9.5 %collective-permute-start.37 = (f32[4,272,8]{1,2,0:T(8,128)S(1)}, f32[4,272,8]{1,2,0:T(8,128)S(1)}, u32[]{:S(2)}, u32[]{:S(2)}) collective-permute-start(f32[4,272,8]{1,2,0:T(8,128)S(1)} %copy.106), channel_id=1, source_target_pairs={{1,0},{2,1},{3,2},{4,3},{5,4},{6,5},{7,6},{9,8},{10,9},{11,10},{12... | collective-permute-start | bytes 104456 | tf_op jit(solution)/shard_map/ppermute | solution.py:28
  839.6 3.6 collective-permute-start.33
  849.1 3.6 collective-permute-start.38
  856.2 4.4 collective-permute-start.39
  (22 other events, 193.5 us)

commit v9 on v8

--- a/solution.py
+++ b/solution.py
@@ -109,6 +109,10 @@
 
 def with_rim(field, width=4):
     return extended(field, (("gx", 1), ("gy", 2)), width)
+
+
+def lane_sum(values):
+    return jnp.sum(values.reshape(-1, 128), axis=0)
 
 
 def interior(field):
@@ -196,7 +200,7 @@
         return (
             jnp.einsum("lab,ac->lcb", along_cols, analysis_rows, precision=highest)
             + prior_weight * direction
-        ), slopes, finish(carry)
+        ), slopes, jnp.sum(finish(carry), axis=1)
 
     rims = with_rim(jnp.concatenate([right_side, jacobi_inverse, prior_weight]))
     residual, jacobi_inverse, prior_weight = jnp.split(rims, 3)
@@ -208,9 +212,9 @@
         precond_res,
         lambda slopes: jnp.stack(
             [
-                jnp.sum(interior(residual) * direction),
-                jnp.sum(slopes * slopes),
-                jnp.sum(prior_inner * direction * direction),
+                lane_sum(interior(residual) * direction),
+                lane_sum(slopes * slopes),
+                lane_sum(prior_inner * direction * direction),
             ]
         ),
     )
@@ -226,13 +230,13 @@
                 precond_res,
                 lambda slopes: jnp.stack(
                     [
-                        jnp.sum(interior(residual) * inner),
-                        jnp.sum(slopes * slopes),
-                        jnp.sum(slopes * direction_slopes),
-                        jnp.sum(direction_slopes * direction_slopes),
-                        jnp.sum(prior_inner * inner * inner),
-                        jnp.sum(prior_inner * inner * direction),
-                        jnp.sum(prior_inner * direction * direction),
+                        lane_sum(interior(residual) * inner),
+                        lane_sum(slopes * slopes),
+                        lane_sum(slopes * direction_slopes),
+                        lane_sum(direction_slopes * direction_slopes),
+                        lane_sum(prior_inner * inner * inner),
+                        lane_sum(prior_inner * inner * direction),
+                        lane_sum(prior_inner * direction * direction),
                     ]
                 ),
             )

time: 886 us -> 859 us (0.970)
  waiting for transfers between devices: 278 us -> 209 us
  other arithmetic: 45.9 us -> 66.4 us
  local copies, waits for them, and re-layouts: 154 us -> 167 us
  starting transfers between devices: 113 us -> 122 us
    all_to_all x4, waiting for transfers between devices: 172 us -> 123 us  [apply_op(): lax.all_to_all(outgoing, 'gy', split_axis=0, concat_axis=0, tiled=True)]
    reshape x0 -> x13, local copies, waits for them, and re-layouts: none -> 25.1 us  [lane_sum(): return jnp.sum(values.reshape(-1, 128), axis=0)]
    ppermute x20, waiting for transfers between devices: 46.1 us -> 22.4 us  [sum_steps(): lax.ppermute(value, axis, pairs)]
    mul x0 -> x5, other arithmetic: none -> 20.9 us  [the longest x2 9 us: shards(): prior_inner * direction * direction]
    another operation x3, local copies, waits for them, and re-layouts: 13.2 us -> 0.08 us  [shards(): jnp.stack([lane_sum(interior(residual) * inner), lane_sum(slopes * slopes...]
    reduce_sum x4 -> x17, other arithmetic: 15.4 us -> 18.8 us  [the longest x13 18.4 us: lane_sum(): return jnp.sum(values.reshape(-1, 128), axis=0)]
  transfers between devices with their start and end apart: 46 -> 46, of which waited for: 27 -> 21; matrix products, arithmetic and copies ran while one was open for 7% -> 16% of each run, Pallas kernels for 0% -> 0%
where the time goes in v9:
time: 859 us; the launch traced here: 847 us
  waiting for transfers between devices  209 us (24%)
  blocking collectives  182 us (21%)
  local copies, waits for them, and re-layouts  167 us (19%)
  starting transfers between devices  122 us (14%)
  matrix products  80.1 us (9%)
  other arithmetic  66.4 us (8%)
  between operations  21 us (2%)
    all_to_all x3, blocking collectives, apply_op(): lax.all_to_all(returning, 'gy', split_axis=0, concat_axis=0, tiled=True)  182 us
    all_to_all x4, waiting for transfers between devices, apply_op(): lax.all_to_all(outgoing, 'gy', split_axis=0, concat_axis=0, tiled=True)  123 us
    all_to_all x1, waiting for transfers between devices, apply_op(): lax.all_to_all(returning, 'gy', split_axis=0, concat_axis=0, tiled=True)  51.6 us
    ppermute x10, starting transfers between devices, extended(): lax.ppermute(lax.slice_in_dim(block, 0, width, axis=dim), axis, backward)  41.6 us
    all_to_all x4, starting transfers between devices, apply_op(): lax.all_to_all(outgoing, 'gy', split_axis=0, concat_axis=0, tiled=True)  25.6 us
    reshape x13, local copies, waits for them, and re-layouts, lane_sum(): return jnp.sum(values.reshape(-1, 128), axis=0)  25.1 us
    ppermute x20, waiting for transfers between devices, sum_steps(): lax.ppermute(value, axis, pairs)  22.4 us
    dot_general x4, matrix products, apply_op(): jnp.einsum('lab,ac->lcb', along_cols, analysis_rows, precision=highest)  22 us
  transfers between devices with their start and end apart: 46, of which 21 were waited for; matrix products, arithmetic and copies ran while one was open for 16% of the time, Pallas kernels for 0%

profile of v9, /device:TPU:10, one launch (start us, length us, event | category | flops | bytes accessed | tf_op | source)
XLA Modules:
  0.0 847.4 jit_solution(15363730234014124787)
XLA Ops:
  3.4 6.3 all-to-all-start
  17.1 3.6 collective-permute-start.1
  35.6 5.0 collective-permute-done.2
  43.8 4.8 pad_maximum_fusion
  63.8 5.8 all-to-all-start.1
  80.2 36.9 %all-to-all-done.1 = f32[8,9,64,128]{3,2,1,0:T(8,128)} async-done(((f32[8,9,64,128]{3,2,1,0:T(8,128)}), f32[8,9,64,128]{3,2,1,0:T(8,128)}, u32[]{:S(2)}, u32[]{:S(2)}) %all-to-all-start.1) | async-done | bytes 2359328 | tf_op jit(solution)/shard_map/all_to_all | solution.py:173
  117.1 3.8 gather_fusion.1
  126.9 3.7 gather_fusion.2
  130.6 8.2 all-to-all-start.2
  138.9 51.6 %all-to-all-done.2 = f32[8,9,64,128]{3,2,1,0:T(8,128)} async-done(((f32[8,9,64,128]{3,2,1,0:T(8,128)}), f32[8,9,64,128]{3,2,1,0:T(8,128)}, u32[]{:S(2)}, u32[]{:S(2)}) %all-to-all-start.2) | async-done | bytes 2359328 | tf_op jit(solution)/shard_map/all_to_all | solution.py:185
  190.5 3.9 collective-permute-start.5
  215.9 5.3 collective-permute-start.10
  223.4 4.7 collective-permute-done.9
  236.9 3.6 collective-permute-done.12
  243.2 6.4 slice_multiply_fusion.3
  264.1 6.5 all-to-all-start.3
  270.6 4.4 multiply_multiply_fusion.7
  283.1 34.5 %all-to-all-done.3 = f32[8,9,64,128]{3,2,1,0:T(8,128)} async-done(((f32[8,9,64,128]{3,2,1,0:T(8,128)}), f32[8,9,64,128]{3,2,1,0:T(8,128)}, u32[]{:S(2)}, u32[]{:S(2)}) %all-to-all-start.3) | async-done | bytes 2359328 | tf_op jit(solution)/shard_map/all_to_all | solution.py:173
  317.6 3.8 gather_fusion.4
  326.7 3.7 gather_fusion.5
  330.5 60.9 %all_to_all.46 = f32[8,9,64,128]{3,2,1,0:T(8,128)S(1)} all-to-all(f32[8,9,64,128]{3,2,1,0:T(8,128)} %bitcast.303), channel_id=1, replica_groups=mesh['gx'=4,'gy'=8] {'gy'}, dimensions={0} | all-to-all | bytes 4718592 | tf_op jit(solution)/shard_map/all_to_all | solution.py:185
  402.3 3.6 collective-permute-start.17
  413.1 5.0 collective-permute-start.19
  418.2 3.6 collective-permute-done.15
  425.2 3.6 fusion.47
  439.8 5.1 fusion.13
  459.3 6.8 all-to-all-start.5
  473.3 4.5 multiply_multiply_fusion.5
  489.1 23.4 %all-to-all-done.5 = f32[8,9,64,128]{3,2,1,0:T(8,128)} async-done(((f32[8,9,64,128]{3,2,1,0:T(8,128)}), f32[8,9,64,128]{3,2,1,0:T(8,128)}, u32[]{:S(2)}, u32[]{:S(2)}) %all-to-all-start.5) | async-done | bytes 2359328 | tf_op jit(solution)/shard_map/all_to_all | solution.py:173
  512.6 3.8 gather_fusion.7
  516.3 3.7 multiply_reduce_fusion.1
  523.8 3.7 gather_fusion.8
  527.5 60.3 %all_to_all.47 = f32[8,9,64,128]{3,2,1,0:T(8,128)S(1)} all-to-all(f32[8,9,64,128]{3,2,1,0:T(8,128)} %bitcast.304), channel_id=1, replica_groups=mesh['gx'=4,'gy'=8] {'gy'}, dimensions={0} | all-to-all | bytes 4718592 | tf_op jit(solution)/shard_map/all_to_all | solution.py:185
  587.9 3.9 collective-permute-start.23
  601.4 3.6 collective-permute-start.26
  613.4 4.9 collective-permute-start.28
  618.4 3.6 collective-permute-done.24
  640.9 6.9 slice_multiply_fusion.1
  662.1 6.4 all-to-all-start.7
  668.6 5.6 multiply_multiply_fusion
  687.1 28.4 %all-to-all-done.7 = f32[8,9,64,128]{3,2,1,0:T(8,128)} async-done(((f32[8,9,64,128]{3,2,1,0:T(8,128)}), f32[8,9,64,128]{3,2,1,0:T(8,128)}, u32[]{:S(2)}, u32[]{:S(2)}) %all-to-all-start.7) | async-done | bytes 2359328 | tf_op jit(solution)/shard_map/all_to_all | solution.py:173
  715.5 3.7 gather_fusion.10
  726.2 3.7 gather_fusion.11
  729.9 60.8 %all_to_all.48 = f32[8,9,64,128]{3,2,1,0:T(8,128)S(1)} all-to-all(f32[8,9,64,128]{3,2,1,0:T(8,128)} %bitcast.302), channel_id=1, replica_groups=mesh['gx'=4,'gy'=8] {'gy'}, dimensions={0} | all-to-all | bytes 4718592 | tf_op jit(solution)/shard_map/all_to_all | solution.py:185
  801.7 3.6 collective-permute-start.35
  812.6 5.0 collective-permute-start.37
  817.7 3.6 collective-permute-done.33
  839.9 7.2 fusion.16
  (311 shorter events, 280.3 us)
Async XLA Ops:
  0.6 120.2 %copy-start = (f32[2,4,128,128]{3,2,1,0:T(8,128)S(1)}, f32[2,4,128,128]{3,2,1,0:T(8,128)}, u32[]{:S(2)}) copy-start(f32[2,4,128,128]{3,2,1,0:T(8,128)} %param.8) | copy-start | bytes 1572868
  3.4 17.6 %all-to-all-start = ((s32[8,1,9]{2,1,0:T(1,128)}), s32[8,1,9]{2,1,0:T(1,128)S(1)}, u32[]{:S(2)}, u32[]{:S(2)}) async-start(s32[8,1,9]{2,1,0:T(1,128)} %copy.81), calls=%async_computation | async-start | bytes 8192 | tf_op jit(solution)/shard_map/all_to_all | solution.py:156
  15.1 7.1 collective-permute-start
  17.1 5.4 collective-permute-start.1
  29.7 12.3 %collective-permute-start.3 = (f32[12,264,4]{1,2,0:T(4,128)S(1)}, f32[12,264,4]{1,2,0:T(4,128)S(1)}, u32[]{:S(2)}, u32[]{:S(2)}) collective-permute-start(f32[12,264,4]{1,2,0:T(4,128)S(1)} %copy.74), channel_id=1, source_target_pairs={{1,0},{2,1},{3,2},{4,3},{5,4},{6,5},{7,6},{9,8},{10,9},{11,10},{12... | collective-permute-start | bytes 152072 | tf_op jit(solution)/shard_map/ppermute | solution.py:28
  33.1 7.5 collective-permute-start.2
  63.8 53.3 %all-to-all-start.1 = ((f32[8,9,64,128]{3,2,1,0:T(8,128)}), f32[8,9,64,128]{3,2,1,0:T(8,128)}, u32[]{:S(2)}, u32[]{:S(2)}) async-start(f32[8,9,64,128]{3,2,1,0:T(8,128)} %bitcast.301), calls=%async_computation.1 | async-start | bytes 4718592 | tf_op jit(solution)/shard_map/all_to_all | solution.py:173
  123.5 7.1 collective-permute-start.4
  130.6 59.9 %all-to-all-start.2 = ((f32[8,9,64,128]{3,2,1,0:T(8,128)}), f32[8,9,64,128]{3,2,1,0:T(8,128)}, u32[]{:S(2)}, u32[]{:S(2)}) async-start(f32[8,9,64,128]{3,2,1,0:T(8,128)} %bitcast.299), calls=%async_computation.2 | async-start | bytes 4718592 | tf_op jit(solution)/shard_map/all_to_all | solution.py:185
  190.5 7.4 collective-permute-start.5
  203.7 6.0 collective-permute-start.7
  205.6 17.8 %collective-permute-start.6 = (f32[3,128]{1,0:T(4,128)S(1)}, f32[3,128]{1,0:T(4,128)S(1)}, u32[]{:S(2)}, u32[]{:S(2)}) collective-permute-start(f32[3,128]{1,0:T(4,128)S(1)} %add.976), channel_id=1, source_target_pairs={{0,1},{1,0},{2,3},{3,2},{4,5},{5,4},{6,7},{7,6},{8,9},{9,8},{10,11... | collective-permute-start | bytes 4616 | tf_op jit(solution)/shard_map/ppermute | solution.py:83
  206.3 4.9 collective-permute-start.8
  215.9 13.2 %collective-permute-start.10 = (f32[4,272,8]{1,2,0:T(8,128)S(1)}, f32[4,272,8]{1,2,0:T(8,128)S(1)}, u32[]{:S(2)}, u32[]{:S(2)}) collective-permute-start(f32[4,272,8]{1,2,0:T(8,128)S(1)} %copy.85), channel_id=1, source_target_pairs={{1,0},{2,1},{3,2},{4,3},{5,4},{6,5},{7,6},{9,8},{10,9},{11,10},{12... | collective-permute-start | bytes 104456 | tf_op jit(solution)/shard_map/ppermute | solution.py:28
  221.3 6.9 collective-permute-start.9
  232.4 3.7 collective-permute-start.11
  236.0 4.5 collective-permute-start.12
  264.1 53.5 %all-to-all-start.3 = ((f32[8,9,64,128]{3,2,1,0:T(8,128)}), f32[8,9,64,128]{3,2,1,0:T(8,128)}, u32[]{:S(2)}, u32[]{:S(2)}) async-start(f32[8,9,64,128]{3,2,1,0:T(8,128)} %bitcast.300), calls=%async_computation.3 | async-start | bytes 4718592 | tf_op jit(solution)/shard_map/all_to_all | solution.py:173
  283.1 38.3 %copy-start.10 = (f32[2,8,64,128,1]{3,2,4,1,0:T(8,128)S(1)}, f32[2,8,64,128,1]{3,2,4,1,0:T(8,128)}, u32[]{:S(2)}) copy-start(f32[2,8,64,128,1]{3,2,4,1,0:T(8,128)} %copy-done.9) | copy-start | bytes 1572868
  324.1 6.4 collective-permute-start.13
  391.3 5.0 collective-permute-start.14
  400.4 5.6 collective-permute-start.16
  402.3 5.2 collective-permute-start.17
  410.9 10.9 %collective-permute-start.18 = (f32[4,272,8]{1,2,0:T(8,128)S(1)}, f32[4,272,8]{1,2,0:T(8,128)S(1)}, u32[]{:S(2)}, u32[]{:S(2)}) collective-permute-start(f32[4,272,8]{1,2,0:T(8,128)S(1)} %copy.91), channel_id=1, source_target_pairs={{0,1},{1,2},{2,3},{3,4},{4,5},{5,6},{6,7},{8,9},{9,10},{10,11},{11... | collective-permute-start | bytes 104456 | tf_op jit(solution)/shard_map/ppermute | solution.py:25
  413.1 8.9 %collective-permute-start.19 = (f32[4,272,8]{1,2,0:T(8,128)S(1)}, f32[4,272,8]{1,2,0:T(8,128)S(1)}, u32[]{:S(2)}, u32[]{:S(2)}) collective-permute-start(f32[4,272,8]{1,2,0:T(8,128)S(1)} %copy.92), channel_id=1, source_target_pairs={{1,0},{2,1},{3,2},{4,3},{5,4},{6,5},{7,6},{9,8},{10,9},{11,10},{12... | collective-permute-start | bytes 104456 | tf_op jit(solution)/shard_map/ppermute | solution.py:28
  418.1 3.7 collective-permute-start.15
  425.1 3.7 collective-permute-start.20
  428.8 4.5 collective-permute-start.21
  459.3 53.3 %all-to-all-start.5 = ((f32[8,9,64,128]{3,2,1,0:T(8,128)}), f32[8,9,64,128]{3,2,1,0:T(8,128)}, u32[]{:S(2)}, u32[]{:S(2)}) async-start(f32[8,9,64,128]{3,2,1,0:T(8,128)} %bitcast.297), calls=%async_computation.5 | async-start | bytes 4718592 | tf_op jit(solution)/shard_map/all_to_all | solution.py:173
  520.1 7.4 collective-permute-start.22
  587.9 5.8 collective-permute-start.23
  599.5 5.6 collective-permute-start.25
  601.4 5.2 collective-permute-start.26
  610.1 11.9 %collective-permute-start.27 = (f32[4,272,8]{1,2,0:T(8,128)S(1)}, f32[4,272,8]{1,2,0:T(8,128)S(1)}, u32[]{:S(2)}, u32[]{:S(2)}) collective-permute-start(f32[4,272,8]{1,2,0:T(8,128)S(1)} %copy.98), channel_id=1, source_target_pairs={{0,1},{1,2},{2,3},{3,4},{4,5},{5,6},{6,7},{8,9},{9,10},{10,11},{11... | collective-permute-start | bytes 104456 | tf_op jit(solution)/shard_map/ppermute | solution.py:25
  613.4 9.7 %collective-permute-start.28 = (f32[4,272,8]{1,2,0:T(8,128)S(1)}, f32[4,272,8]{1,2,0:T(8,128)S(1)}, u32[]{:S(2)}, u32[]{:S(2)}) collective-permute-start(f32[4,272,8]{1,2,0:T(8,128)S(1)} %copy.99), channel_id=1, source_target_pairs={{1,0},{2,1},{3,2},{4,3},{5,4},{6,5},{7,6},{9,8},{10,9},{11,10},{12... | collective-permute-start | bytes 104456 | tf_op jit(solution)/shard_map/ppermute | solution.py:28
  618.3 3.7 collective-permute-start.24
  626.3 3.7 collective-permute-start.29
  630.0 4.5 collective-permute-start.30
  662.1 53.3 %all-to-all-start.7 = ((f32[8,9,64,128]{3,2,1,0:T(8,128)}), f32[8,9,64,128]{3,2,1,0:T(8,128)}, u32[]{:S(2)}, u32[]{:S(2)}) async-start(f32[8,9,64,128]{3,2,1,0:T(8,128)} %bitcast.298), calls=%async_computation.7 | async-start | bytes 4718592 | tf_op jit(solution)/shard_map/all_to_all | solution.py:173
  722.6 7.3 collective-permute-start.31
  790.7 5.0 collective-permute-start.32
  799.7 5.6 collective-permute-start.34
  801.7 5.2 collective-permute-start.35
  809.3 12.0 %collective-permute-start.36 = (f32[4,272,8]{1,2,0:T(8,128)S(1)}, f32[4,272,8]{1,2,0:T(8,128)S(1)}, u32[]{:S(2)}, u32[]{:S(2)}) collective-permute-start(f32[4,272,8]{1,2,0:T(8,128)S(1)} %copy.105), channel_id=1, source_target_pairs={{0,1},{1,2},{2,3},{3,4},{4,5},{5,6},{6,7},{8,9},{9,10},{10,11},{11... | collective-permute-start | bytes 104456 | tf_op jit(solution)/shard_map/ppermute | solution.py:25
  812.6 9.8 %collective-permute-start.37 = (f32[4,272,8]{1,2,0:T(8,128)S(1)}, f32[4,272,8]{1,2,0:T(8,128)S(1)}, u32[]{:S(2)}, u32[]{:S(2)}) collective-permute-start(f32[4,272,8]{1,2,0:T(8,128)S(1)} %copy.106), channel_id=1, source_target_pairs={{1,0},{2,1},{3,2},{4,3},{5,4},{6,5},{7,6},{9,8},{10,9},{11,10},{12... | collective-permute-start | bytes 104456 | tf_op jit(solution)/shard_map/ppermute | solution.py:28
  817.6 3.7 collective-permute-start.33
  825.2 3.7 collective-permute-start.38
  828.9 4.5 collective-permute-start.39
  (23 other events, 163.4 us)

commit v10 on v9

--- a/solution.py
+++ b/solution.py
@@ -157,9 +157,15 @@
     slot_source = jnp.where(
         used, jnp.sum(jnp.where(hit, request_num[:, None, None], 0), axis=0), requests
     )
+    exact = lax.Precision.HIGHEST
     landing = (
         wanted_ids.reshape(-1)[None, :] == jnp.arange(own_blocks, dtype=jnp.int32)[:, None]
     ).astype(jnp.float32)
+    picking = (
+        (target * capacity + slot)[:, None]
+        == jnp.arange(owners * capacity, dtype=jnp.int32)[None, :]
+    ).astype(jnp.float32)
+    block_size = block_rows * block_cols
     def apply_op(direction, partials):
         along_rows = jnp.einsum("lab,ac->lcb", direction, synth_rows, precision=highest)
         blocks = (
@@ -168,24 +174,30 @@
             .transpose(0, 1, 3, 2, 4)
             .reshape(own_blocks, block_rows, block_cols)
         )
-        blocks = jnp.concatenate([blocks, jnp.zeros((1, block_rows, block_cols), blocks.dtype)])
-        outgoing = jnp.take(blocks, wanted_ids, axis=0, mode="clip")
-        arrived = lax.all_to_all(outgoing, "gy", split_axis=0, concat_axis=0, tiled=True)
-        seen = arrived[target, slot].reshape(
-            sensors, rows_blocks * cols_blocks, layers, block_rows, block_cols
-        )
+        outgoing = jnp.dot(landing.T, blocks.reshape(own_blocks, block_size), precision=exact)
+        arrived = lax.all_to_all(
+            outgoing.reshape(owners, capacity, block_rows, block_cols),
+            "gy",
+            split_axis=0,
+            concat_axis=0,
+            tiled=True,
+        )
+        seen = jnp.dot(
+            picking, arrived.reshape(owners * capacity, block_size), precision=exact
+        ).reshape(sensors, rows_blocks * cols_blocks, layers, block_rows, block_cols)
         slopes = jnp.einsum("sklxy,slyz->skxz", seen, interaction, precision=highest)
         carry = (partials(slopes), sum_steps(("gx", "gy")))
         back = jnp.einsum("skxz,slyz->sklxy", slopes, interaction, precision=highest).reshape(
             requests, block_rows, block_cols
         )
-        back = jnp.concatenate([back, jnp.zeros((1, block_rows, block_cols), back.dtype)])
-        returning = jnp.take(back, slot_source, axis=0, mode="clip")
+        returning = jnp.dot(
+            picking.T, back.reshape(requests, block_size), precision=exact
+        ).reshape(owners, capacity, block_rows, block_cols)
         carry, returning = advance(carry, returning)
         landed = lax.all_to_all(returning, "gy", split_axis=0, concat_axis=0, tiled=True)
         carry, landed = advance(carry, landed, step=False)
         summed = jnp.dot(
-            landing, landed.reshape(owners * capacity, block_rows * block_cols), precision=highest
+            landing, landed.reshape(owners * capacity, block_size), precision=exact
         )
         carry, summed = advance(carry, summed)
         padded = with_rim(

time: 859 us -> 874 us (1.017)
  matrix products: 80.1 us -> 113 us
  local copies, waits for them, and re-layouts: 167 us -> 142 us
  starting transfers between devices: 122 us -> 132 us
    gather x12 -> x0, local copies, waits for them, and re-layouts: 43.6 us -> none  [the longest x4 15 us: apply_op(): arrived[target, slot]]
    dot_general x4 -> x16, matrix products: 9.12 us -> 49.3 us  [the longest x4 17.4 us: apply_op(): jnp.dot(picking.T, back.reshape(requests, block_size), precision=exact)]
    unnamed x64 -> x82, local copies, waits for them, and re-layouts: 16.5 us -> 30.7 us
    concatenate x8 -> x0, local copies, waits for them, and re-layouts: 10.8 us -> none  [the longest x4 6.18 us: apply_op(): jnp.concatenate([back, jnp.zeros((1, block_rows, block_cols), back.dtype)])]
    all_to_all x1, starting transfers between devices: 8.2 us -> 18.9 us  [apply_op(): lax.all_to_all(returning, 'gy', split_axis=0, concat_axis=0, tiled=True)]
  transfers between devices with their start and end apart: 46 -> 46, of which waited for: 21 -> 20; matrix products, arithmetic and copies ran while one was open for 16% -> 18% of each run, Pallas kernels for 0% -> 0%
where the time goes in v10:
time: 874 us; the launch traced here: 861 us
  waiting for transfers between devices  208 us (24%)
  blocking collectives  180 us (21%)
  local copies, waits for them, and re-layouts  142 us (16%)
  starting transfers between devices  132 us (15%)
  matrix products  113 us (13%)
  other arithmetic  64.3 us (7%)
  between operations  21.6 us (2%)
    all_to_all x3, blocking collectives, apply_op(): lax.all_to_all(returning, 'gy', split_axis=0, concat_axis=0, tiled=True)  180 us
    all_to_all x4, waiting for transfers between devices, apply_op(): lax.all_to_all(outgoing.reshape(owners, capacity, block_rows, block_cols)...  122 us
    all_to_all x1, waiting for transfers between devices, apply_op(): lax.all_to_all(returning, 'gy', split_axis=0, concat_axis=0, tiled=True)  51 us
    ppermute x10, starting transfers between devices, extended(): lax.ppermute(lax.slice_in_dim(block, 0, width, axis=dim), axis, backward)  40.5 us
    unnamed x82, local copies, waits for them, and re-layouts  30.7 us
    reshape x13, local copies, waits for them, and re-layouts, lane_sum(): return jnp.sum(values.reshape(-1, 128), axis=0)  25.1 us
    all_to_all x4, starting transfers between devices, apply_op(): lax.all_to_all(outgoing.reshape(owners, capacity, block_rows, block_cols)...  24.8 us
    ppermute x20, waiting for transfers between devices, sum_steps(): lax.ppermute(value, axis, pairs)  22.3 us
  transfers between devices with their start and end apart: 46, of which 20 were waited for; matrix products, arithmetic and copies ran while one was open for 18% of the time, Pallas kernels for 0%

profile of v10, /device:TPU:10, one launch (start us, length us, event | category | flops | bytes accessed | tf_op | source)
XLA Modules:
  0.0 861.2 jit_solution(6303946276200090222)
XLA Ops:
  3.3 6.3 all-to-all-start
  13.1 3.6 collective-permute-start.1
  29.9 5.0 collective-permute-done.2
  38.0 4.8 pad_maximum_fusion
  54.4 3.4 fusion.36
  60.0 5.2 all-to-all-start.1
  75.9 36.5 %all-to-all-done.1 = f32[8,9,64,128]{3,2,1,0:T(8,128)} async-done(((f32[8,9,64,128]{3,2,1,0:T(8,128)}), f32[8,9,64,128]{3,2,1,0:T(8,128)}, u32[]{:S(2)}, u32[]{:S(2)}) %all-to-all-start.1) | async-done | bytes 2359328 | tf_op jit(solution)/shard_map/all_to_all | solution.py:178
  126.1 18.9 %all-to-all-start.2 = ((f32[8,9,64,128]{3,2,1,0:T(8,128)}), f32[8,9,64,128]{3,2,1,0:T(8,128)}, u32[]{:S(2)}, u32[]{:S(2)}) async-start(f32[8,9,64,128]{3,2,1,0:T(8,128)} %copy.156), calls=%async_computation.2 | async-start | bytes 4718592 | tf_op jit(solution)/shard_map/all_to_all | solution.py:197
  146.3 51.0 %all-to-all-done.2 = f32[8,9,64,128]{3,2,1,0:T(8,128)} async-done(((f32[8,9,64,128]{3,2,1,0:T(8,128)}), f32[8,9,64,128]{3,2,1,0:T(8,128)}, u32[]{:S(2)}, u32[]{:S(2)}) %all-to-all-start.2) | async-done | bytes 2359328 | tf_op jit(solution)/shard_map/all_to_all | solution.py:197
  197.3 4.3 collective-permute-start.5
  201.6 3.9 fusion.9
  223.6 5.3 collective-permute-start.10
  230.8 4.9 collective-permute-done.9
  240.1 3.6 fusion.78
  244.5 3.6 collective-permute-done.12
  250.8 6.2 slice_multiply_fusion.3
  271.1 6.6 all-to-all-start.3
  277.7 4.4 multiply_multiply_fusion.7
  290.2 34.2 %all-to-all-done.3 = f32[8,9,64,128]{3,2,1,0:T(8,128)} async-done(((f32[8,9,64,128]{3,2,1,0:T(8,128)}), f32[8,9,64,128]{3,2,1,0:T(8,128)}, u32[]{:S(2)}, u32[]{:S(2)}) %all-to-all-start.3) | async-done | bytes 2359328 | tf_op jit(solution)/shard_map/all_to_all | solution.py:178
  334.9 4.7 fusion.24
  340.5 60.3 %all_to_all.46 = f32[8,9,64,128]{3,2,1,0:T(8,128)S(1)} all-to-all(f32[8,9,64,128]{3,2,1,0:T(8,128)S(1)} %copy.170), channel_id=1, replica_groups=mesh['gx'=4,'gy'=8] {'gy'}, dimensions={0} | all-to-all | bytes 4718592 | tf_op jit(solution)/shard_map/all_to_all | solution.py:197
  412.5 3.6 collective-permute-start.17
  423.6 4.6 collective-permute-start.19
  428.3 3.6 collective-permute-done.15
  436.7 3.5 fusion.75
  451.3 5.1 fusion.29
  470.7 6.5 all-to-all-start.5
  484.4 4.5 multiply_multiply_fusion.5
  500.2 23.6 %all-to-all-done.5 = f32[8,9,64,128]{3,2,1,0:T(8,128)} async-done(((f32[8,9,64,128]{3,2,1,0:T(8,128)}), f32[8,9,64,128]{3,2,1,0:T(8,128)}, u32[]{:S(2)}, u32[]{:S(2)}) %all-to-all-start.5) | async-done | bytes 2359328 | tf_op jit(solution)/shard_map/all_to_all | solution.py:178
  535.0 4.7 fusion.22
  540.9 60.1 %all_to_all.47 = f32[8,9,64,128]{3,2,1,0:T(8,128)S(1)} all-to-all(f32[8,9,64,128]{3,2,1,0:T(8,128)S(1)} %copy.184), channel_id=1, replica_groups=mesh['gx'=4,'gy'=8] {'gy'}, dimensions={0} | all-to-all | bytes 4718592 | tf_op jit(solution)/shard_map/all_to_all | solution.py:197
  600.9 3.6 collective-permute-start.23
  614.6 3.6 collective-permute-start.26
  626.7 4.6 collective-permute-start.28
  631.4 3.6 collective-permute-done.24
  639.3 3.7 fusion.72
  654.1 6.9 slice_multiply_fusion.1
  675.1 6.4 all-to-all-start.7
  681.5 5.6 multiply_multiply_fusion
  700.0 28.1 %all-to-all-done.7 = f32[8,9,64,128]{3,2,1,0:T(8,128)} async-done(((f32[8,9,64,128]{3,2,1,0:T(8,128)}), f32[8,9,64,128]{3,2,1,0:T(8,128)}, u32[]{:S(2)}, u32[]{:S(2)}) %all-to-all-start.7) | async-done | bytes 2359328 | tf_op jit(solution)/shard_map/all_to_all | solution.py:178
  737.9 4.7 fusion.20
  743.6 60.0 %all_to_all.48 = f32[8,9,64,128]{3,2,1,0:T(8,128)S(1)} all-to-all(f32[8,9,64,128]{3,2,1,0:T(8,128)S(1)} %copy.198), channel_id=1, replica_groups=mesh['gx'=4,'gy'=8] {'gy'}, dimensions={0} | all-to-all | bytes 4718592 | tf_op jit(solution)/shard_map/all_to_all | solution.py:197
  803.6 3.6 collective-permute-start.32
  815.6 3.6 collective-permute-start.35
  826.6 4.6 collective-permute-start.37
  831.3 3.6 collective-permute-done.33
  843.2 3.5 convolution_bitcast_fusion
  853.5 7.2 fusion.40
  (329 shorter events, 286.0 us)
Async XLA Ops:
  0.6 117.9 %copy-start = (f32[2,4,128,128]{3,2,1,0:T(8,128)S(1)}, f32[2,4,128,128]{3,2,1,0:T(8,128)}, u32[]{:S(2)}) copy-start(f32[2,4,128,128]{3,2,1,0:T(8,128)} %param.8) | copy-start | bytes 1572868
  3.3 51.1 %all-to-all-start = ((s32[8,1,9]{2,1,0:T(1,128)}), s32[8,1,9]{2,1,0:T(1,128)S(1)}, u32[]{:S(2)}, u32[]{:S(2)}) async-start(s32[8,1,9]{2,1,0:T(1,128)} %copy.147), calls=%async_computation | async-start | bytes 8192 | tf_op jit(solution)/shard_map/all_to_all | solution.py:156
  11.2 5.6 collective-permute-start
  13.1 5.4 collective-permute-start.1
  24.0 12.3 %collective-permute-start.3 = (f32[12,264,4]{1,2,0:T(4,128)S(1)}, f32[12,264,4]{1,2,0:T(4,128)S(1)}, u32[]{:S(2)}, u32[]{:S(2)}) collective-permute-start(f32[12,264,4]{1,2,0:T(4,128)S(1)} %copy.141), channel_id=1, source_target_pairs={{1,0},{2,1},{3,2},{4,3},{5,4},{6,5},{7,6},{9,8},{10,9},{11,10},{12... | collective-permute-start | bytes 152072 | tf_op jit(solution)/shard_map/ppermute | solution.py:28
  27.4 7.5 collective-permute-start.2
  60.0 52.3 %all-to-all-start.1 = ((f32[8,9,64,128]{3,2,1,0:T(8,128)}), f32[8,9,64,128]{3,2,1,0:T(8,128)}, u32[]{:S(2)}, u32[]{:S(2)}) async-start(f32[8,9,64,128]{3,2,1,0:T(8,128)} %copy.151), calls=%async_computation.1 | async-start | bytes 4718592 | tf_op jit(solution)/shard_map/all_to_all | solution.py:178
  119.6 4.3 collective-permute-start.4
  126.1 71.1 %all-to-all-start.2 = ((f32[8,9,64,128]{3,2,1,0:T(8,128)}), f32[8,9,64,128]{3,2,1,0:T(8,128)}, u32[]{:S(2)}, u32[]{:S(2)}) async-start(f32[8,9,64,128]{3,2,1,0:T(8,128)} %copy.156), calls=%async_computation.2 | async-start | bytes 4718592 | tf_op jit(solution)/shard_map/all_to_all | solution.py:197
  197.3 8.2 collective-permute-start.5
  211.3 6.0 collective-permute-start.7
  213.2 17.6 %collective-permute-start.6 = (f32[3,128]{1,0:T(4,128)S(1)}, f32[3,128]{1,0:T(4,128)S(1)}, u32[]{:S(2)}, u32[]{:S(2)}) collective-permute-start(f32[3,128]{1,0:T(4,128)S(1)} %add.944), channel_id=1, source_target_pairs={{0,1},{1,0},{2,3},{3,2},{4,5},{5,4},{6,7},{7,6},{8,9},{9,8},{10,11... | collective-permute-start | bytes 4616 | tf_op jit(solution)/shard_map/ppermute | solution.py:83
  213.9 4.9 collective-permute-start.8
  223.6 13.2 %collective-permute-start.10 = (f32[4,272,8]{1,2,0:T(8,128)S(1)}, f32[4,272,8]{1,2,0:T(8,128)S(1)}, u32[]{:S(2)}, u32[]{:S(2)}) collective-permute-start(f32[4,272,8]{1,2,0:T(8,128)S(1)} %copy.159), channel_id=1, source_target_pairs={{1,0},{2,1},{3,2},{4,3},{5,4},{6,5},{7,6},{9,8},{10,9},{11,10},{12... | collective-permute-start | bytes 104456 | tf_op jit(solution)/shard_map/ppermute | solution.py:28
  228.9 6.9 collective-permute-start.9
  240.0 3.7 collective-permute-start.11
  243.7 4.5 collective-permute-start.12
  271.1 53.3 %all-to-all-start.3 = ((f32[8,9,64,128]{3,2,1,0:T(8,128)}), f32[8,9,64,128]{3,2,1,0:T(8,128)}, u32[]{:S(2)}, u32[]{:S(2)}) async-start(f32[8,9,64,128]{3,2,1,0:T(8,128)} %copy.165), calls=%async_computation.3 | async-start | bytes 4718592 | tf_op jit(solution)/shard_map/all_to_all | solution.py:178
  334.8 4.8 collective-permute-start.13
  400.8 5.6 collective-permute-start.14
  410.6 5.6 collective-permute-start.16
  412.5 5.2 collective-permute-start.17
  420.2 11.7 %collective-permute-start.18 = (f32[4,272,8]{1,2,0:T(8,128)S(1)}, f32[4,272,8]{1,2,0:T(8,128)S(1)}, u32[]{:S(2)}, u32[]{:S(2)}) collective-permute-start(f32[4,272,8]{1,2,0:T(8,128)S(1)} %copy.172), channel_id=1, source_target_pairs={{0,1},{1,2},{2,3},{3,4},{4,5},{5,6},{6,7},{8,9},{9,10},{10,11},{11... | collective-permute-start | bytes 104456 | tf_op jit(solution)/shard_map/ppermute | solution.py:25
  423.6 9.3 %collective-permute-start.19 = (f32[4,272,8]{1,2,0:T(8,128)S(1)}, f32[4,272,8]{1,2,0:T(8,128)}, u32[]{:S(2)}, u32[]{:S(2)}) collective-permute-start(f32[4,272,8]{1,2,0:T(8,128)S(1)} %copy.173), channel_id=1, source_target_pairs={{1,0},{2,1},{3,2},{4,3},{5,4},{6,5},{7,6},{9,8},{10,9},{11,10},{12... | collective-permute-start | bytes 104456 | tf_op jit(solution)/shard_map/ppermute | solution.py:28
  428.2 3.7 collective-permute-start.15
  436.6 3.7 collective-permute-start.20
  436.7 19.8 %slice-start = ((s8[4866048]{0:T(1024)(128)(4,1)}), s8[671744]{0:T(1024)(128)(4,1)S(1)}, s32[]{:S(2)}) async-start(s8[4866048]{0:T(1024)(128)(4,1)} %bitcast.476), calls=%async_computation.9 | async-start | bytes 1343488
  440.3 4.5 collective-permute-start.21
  470.7 53.1 %all-to-all-start.5 = ((f32[8,9,64,128]{3,2,1,0:T(8,128)}), f32[8,9,64,128]{3,2,1,0:T(8,128)}, u32[]{:S(2)}, u32[]{:S(2)}) async-start(f32[8,9,64,128]{3,2,1,0:T(8,128)} %copy.179), calls=%async_computation.5 | async-start | bytes 4718592 | tf_op jit(solution)/shard_map/all_to_all | solution.py:178
  534.9 4.8 collective-permute-start.22
  600.9 5.9 collective-permute-start.23
  612.7 5.6 collective-permute-start.25
  614.6 5.2 collective-permute-start.26
  623.3 11.7 %collective-permute-start.27 = (f32[4,272,8]{1,2,0:T(8,128)S(1)}, f32[4,272,8]{1,2,0:T(8,128)S(1)}, u32[]{:S(2)}, u32[]{:S(2)}) collective-permute-start(f32[4,272,8]{1,2,0:T(8,128)S(1)} %copy.186), channel_id=1, source_target_pairs={{0,1},{1,2},{2,3},{3,4},{4,5},{5,6},{6,7},{8,9},{9,10},{10,11},{11... | collective-permute-start | bytes 104456 | tf_op jit(solution)/shard_map/ppermute | solution.py:25
  626.7 9.3 %collective-permute-start.28 = (f32[4,272,8]{1,2,0:T(8,128)S(1)}, f32[4,272,8]{1,2,0:T(8,128)S(1)}, u32[]{:S(2)}, u32[]{:S(2)}) collective-permute-start(f32[4,272,8]{1,2,0:T(8,128)S(1)} %copy.187), channel_id=1, source_target_pairs={{1,0},{2,1},{3,2},{4,3},{5,4},{6,5},{7,6},{9,8},{10,9},{11,10},{12... | collective-permute-start | bytes 104456 | tf_op jit(solution)/shard_map/ppermute | solution.py:28
  631.3 3.7 collective-permute-start.24
  639.2 3.8 collective-permute-start.29
  643.1 4.5 collective-permute-start.30
  675.1 53.0 %all-to-all-start.7 = ((f32[8,9,64,128]{3,2,1,0:T(8,128)}), f32[8,9,64,128]{3,2,1,0:T(8,128)}, u32[]{:S(2)}, u32[]{:S(2)}) async-start(f32[8,9,64,128]{3,2,1,0:T(8,128)} %copy.193), calls=%async_computation.7 | async-start | bytes 4718592 | tf_op jit(solution)/shard_map/all_to_all | solution.py:178
  737.8 4.8 collective-permute-start.31
  803.6 5.9 collective-permute-start.32
  813.6 5.6 collective-permute-start.34
  815.6 5.2 collective-permute-start.35
  823.2 11.7 %collective-permute-start.36 = (f32[4,272,8]{1,2,0:T(8,128)S(1)}, f32[4,272,8]{1,2,0:T(8,128)S(1)}, u32[]{:S(2)}, u32[]{:S(2)}) collective-permute-start(f32[4,272,8]{1,2,0:T(8,128)S(1)} %copy.200), channel_id=1, source_target_pairs={{0,1},{1,2},{2,3},{3,4},{4,5},{5,6},{6,7},{8,9},{9,10},{10,11},{11... | collective-permute-start | bytes 104456 | tf_op jit(solution)/shard_map/ppermute | solution.py:25
  826.6 9.4 %collective-permute-start.37 = (f32[4,272,8]{1,2,0:T(8,128)S(1)}, f32[4,272,8]{1,2,0:T(8,128)S(1)}, u32[]{:S(2)}, u32[]{:S(2)}) collective-permute-start(f32[4,272,8]{1,2,0:T(8,128)S(1)} %copy.201), channel_id=1, source_target_pairs={{1,0},{2,1},{3,2},{4,3},{5,4},{6,5},{7,6},{9,8},{10,9},{11,10},{12... | collective-permute-start | bytes 104456 | tf_op jit(solution)/shard_map/ppermute | solution.py:28
  831.3 3.7 collective-permute-start.33
  838.9 3.7 collective-permute-start.38
  842.6 4.5 collective-permute-start.39
  (28 other events, 101.8 us)

commit v11 on v9

--- a/solution.py
+++ b/solution.py
@@ -157,19 +157,27 @@
     slot_source = jnp.where(
         used, jnp.sum(jnp.where(hit, request_num[:, None, None], 0), axis=0), requests
     )
+    own_layer = wanted_ids // (rows_blocks * cols_blocks)
+    own_row = wanted_ids % (rows_blocks * cols_blocks) // cols_blocks
+    own_col = wanted_ids % cols_blocks
+    gather_ids = jnp.where(
+        wanted_ids < own_blocks,
+        own_layer * (rows_blocks * cols_blocks) + own_col * rows_blocks + own_row,
+        own_blocks,
+    )
     landing = (
         wanted_ids.reshape(-1)[None, :] == jnp.arange(own_blocks, dtype=jnp.int32)[:, None]
     ).astype(jnp.float32)
     def apply_op(direction, partials):
         along_rows = jnp.einsum("lab,ac->lcb", direction, synth_rows, precision=highest)
-        blocks = (
-            jnp.einsum("lab,bc->lac", along_rows, synth_cols, precision=highest)
-            .reshape(layers, rows_blocks, block_rows, cols_blocks, block_cols)
-            .transpose(0, 1, 3, 2, 4)
-            .reshape(own_blocks, block_rows, block_cols)
-        )
+        blocks = jnp.einsum(
+            "lab,bjc->ljac",
+            along_rows,
+            synth_cols.reshape(-1, cols_blocks, block_cols),
+            precision=highest,
+        ).reshape(own_blocks, block_rows, block_cols)
         blocks = jnp.concatenate([blocks, jnp.zeros((1, block_rows, block_cols), blocks.dtype)])
-        outgoing = jnp.take(blocks, wanted_ids, axis=0, mode="clip")
+        outgoing = jnp.take(blocks, gather_ids, axis=0, mode="clip")
         arrived = lax.all_to_all(outgoing, "gy", split_axis=0, concat_axis=0, tiled=True)
         seen = arrived[target, slot].reshape(
             sensors, rows_blocks * cols_blocks, layers, block_rows, block_cols

time: 859 us -> 858 us (level)
    reshape x8 -> x0, local copies, waits for them, and re-layouts: 15.1 us -> none  [apply_op(): blocks = jnp.einsum('lab,bc->lac', along_rows, synth_cols, precision=high...]
    transpose x0 -> x4, local copies, waits for them, and re-layouts: none -> 8.88 us  [apply_op(): jnp.einsum('lab,bjc->ljac', along_rows, synth_cols.reshape(-1, cols_block...]
    unnamed x64 -> x184, local copies, waits for them, and re-layouts: 16.5 us -> 17.6 us
  transfers between devices with their start and end apart: 46 -> 46, of which waited for: 21 -> 20; matrix products, arithmetic and copies ran while one was open for 16% -> 17% of each run, Pallas kernels for 0% -> 0%
where the time goes in v11:
time: 858 us; the launch traced here: 846 us
  waiting for transfers between devices  207 us (24%)
  blocking collectives  183 us (21%)
  local copies, waits for them, and re-layouts  165 us (19%)
  starting transfers between devices  118 us (14%)
  matrix products  77.4 us (9%)
  other arithmetic  74.9 us (9%)
  between operations  22.1 us (3%)
    all_to_all x3, blocking collectives, apply_op(): lax.all_to_all(returning, 'gy', split_axis=0, concat_axis=0, tiled=True)  183 us
    all_to_all x4, waiting for transfers between devices, apply_op(): lax.all_to_all(outgoing, 'gy', split_axis=0, concat_axis=0, tiled=True)  124 us
    all_to_all x1, waiting for transfers between devices, apply_op(): lax.all_to_all(returning, 'gy', split_axis=0, concat_axis=0, tiled=True)  50.4 us
    ppermute x10, starting transfers between devices, extended(): lax.ppermute(lax.slice_in_dim(block, 0, width, axis=dim), axis, backward)  41.5 us
    reshape x13, local copies, waits for them, and re-layouts, lane_sum(): return jnp.sum(values.reshape(-1, 128), axis=0)  25.1 us
    all_to_all x4, starting transfers between devices, apply_op(): lax.all_to_all(outgoing, 'gy', split_axis=0, concat_axis=0, tiled=True)  24.7 us
    ppermute x20, waiting for transfers between devices, sum_steps(): lax.ppermute(value, axis, pairs)  22.7 us
    dot_general x4, matrix products, apply_op(): jnp.einsum('lab,ac->lcb', along_cols, analysis_rows, precision=highest)  21.7 us
  transfers between devices with their start and end apart: 46, of which 20 were waited for; matrix products, arithmetic and copies ran while one was open for 17% of the time, Pallas kernels for 0%

profile of v11, /device:TPU:10, one launch (start us, length us, event | category | flops | bytes accessed | tf_op | source)
XLA Modules:
  0.0 846.3 jit_solution(582537082484578293)
XLA Ops:
  3.4 6.3 all-to-all-start
  14.9 3.6 collective-permute-start.1
  38.4 4.1 collective-permute-done.2
  45.7 4.8 pad_maximum_fusion
  65.4 5.5 all-to-all-start.1
  81.5 37.0 %all-to-all-done.1 = f32[8,9,64,128]{3,2,1,0:T(8,128)} async-done(((f32[8,9,64,128]{3,2,1,0:T(8,128)}), f32[8,9,64,128]{3,2,1,0:T(8,128)}, u32[]{:S(2)}, u32[]{:S(2)}) %all-to-all-start.1) | async-done | bytes 2359328 | tf_op jit(solution)/shard_map/all_to_all | solution.py:181
  118.6 3.8 gather_fusion.1
  128.4 3.8 gather_fusion.2
  132.1 8.2 all-to-all-start.2
  141.6 50.4 %all-to-all-done.2 = f32[8,9,64,128]{3,2,1,0:T(8,128)} async-done(((f32[8,9,64,128]{3,2,1,0:T(8,128)}), f32[8,9,64,128]{3,2,1,0:T(8,128)}, u32[]{:S(2)}, u32[]{:S(2)}) %all-to-all-start.2) | async-done | bytes 2359328 | tf_op jit(solution)/shard_map/all_to_all | solution.py:193
  215.3 5.3 collective-permute-start.10
  222.8 4.7 collective-permute-done.9
  231.9 3.5 fusion.50
  236.3 3.7 collective-permute-done.12
  242.7 6.2 slice_multiply_fusion.3
  262.7 6.2 all-to-all-start.3
  268.8 4.5 multiply_multiply_fusion.7
  281.3 34.6 %all-to-all-done.3 = f32[8,9,64,128]{3,2,1,0:T(8,128)} async-done(((f32[8,9,64,128]{3,2,1,0:T(8,128)}), f32[8,9,64,128]{3,2,1,0:T(8,128)}, u32[]{:S(2)}, u32[]{:S(2)}) %all-to-all-start.3) | async-done | bytes 2359328 | tf_op jit(solution)/shard_map/all_to_all | solution.py:181
  315.9 3.8 gather_fusion.4
  325.0 3.8 gather_fusion.5
  328.8 61.3 %all_to_all.49 = f32[8,9,64,128]{3,2,1,0:T(8,128)S(1)} all-to-all(f32[8,9,64,128]{3,2,1,0:T(8,128)} %bitcast.317), channel_id=1, replica_groups=mesh['gx'=4,'gy'=8] {'gy'}, dimensions={0} | all-to-all | bytes 4718592 | tf_op jit(solution)/shard_map/all_to_all | solution.py:193
  401.7 3.6 collective-permute-start.17
  412.6 4.8 collective-permute-start.19
  417.5 3.8 collective-permute-done.15
  426.6 3.6 fusion.47
  441.4 5.1 fusion.13
  458.2 6.6 all-to-all-start.5
  472.0 4.6 multiply_multiply_fusion.5
  487.8 23.8 %all-to-all-done.5 = f32[8,9,64,128]{3,2,1,0:T(8,128)} async-done(((f32[8,9,64,128]{3,2,1,0:T(8,128)}), f32[8,9,64,128]{3,2,1,0:T(8,128)}, u32[]{:S(2)}, u32[]{:S(2)}) %all-to-all-start.5) | async-done | bytes 2359328 | tf_op jit(solution)/shard_map/all_to_all | solution.py:181
  511.7 3.8 gather_fusion.7
  515.4 3.7 multiply_reduce_fusion.1
  522.8 3.8 gather_fusion.8
  526.6 60.8 %all_to_all.50 = f32[8,9,64,128]{3,2,1,0:T(8,128)S(1)} all-to-all(f32[8,9,64,128]{3,2,1,0:T(8,128)} %bitcast.318), channel_id=1, replica_groups=mesh['gx'=4,'gy'=8] {'gy'}, dimensions={0} | all-to-all | bytes 4718592 | tf_op jit(solution)/shard_map/all_to_all | solution.py:193
  600.7 3.6 collective-permute-start.26
  612.6 5.0 collective-permute-start.28
  617.7 3.6 collective-permute-done.24
  625.6 3.6 fusion.44
  640.2 6.9 slice_multiply_fusion.1
  660.6 6.5 all-to-all-start.7
  667.1 5.6 multiply_multiply_fusion
  685.7 28.4 %all-to-all-done.7 = f32[8,9,64,128]{3,2,1,0:T(8,128)} async-done(((f32[8,9,64,128]{3,2,1,0:T(8,128)}), f32[8,9,64,128]{3,2,1,0:T(8,128)}, u32[]{:S(2)}, u32[]{:S(2)}) %all-to-all-start.7) | async-done | bytes 2359328 | tf_op jit(solution)/shard_map/all_to_all | solution.py:181
  714.0 3.7 gather_fusion.10
  724.8 3.7 gather_fusion.11
  728.5 60.8 %all_to_all.51 = f32[8,9,64,128]{3,2,1,0:T(8,128)S(1)} all-to-all(f32[8,9,64,128]{3,2,1,0:T(8,128)} %bitcast.316), channel_id=1, replica_groups=mesh['gx'=4,'gy'=8] {'gy'}, dimensions={0} | all-to-all | bytes 4718592 | tf_op jit(solution)/shard_map/all_to_all | solution.py:193
  800.3 3.6 collective-permute-start.35
  811.2 5.1 collective-permute-start.37
  816.3 3.6 collective-permute-done.33
  838.6 7.3 fusion.16
  (435 shorter events, 280.5 us)
Async XLA Ops:
  0.6 121.7 %copy-start = (f32[2,4,128,128]{3,2,1,0:T(8,128)S(1)}, f32[2,4,128,128]{3,2,1,0:T(8,128)}, u32[]{:S(2)}) copy-start(f32[2,4,128,128]{3,2,1,0:T(8,128)} %param.8) | copy-start | bytes 1572868
  3.4 21.2 %all-to-all-start = ((s32[8,1,9]{2,1,0:T(1,128)}), s32[8,1,9]{2,1,0:T(1,128)S(1)}, u32[]{:S(2)}, u32[]{:S(2)}) async-start(s32[8,1,9]{2,1,0:T(1,128)} %copy.81), calls=%async_computation | async-start | bytes 8192 | tf_op jit(solution)/shard_map/all_to_all | solution.py:156
  13.0 12.3 %collective-permute-start = (f32[12,4,256]{2,1,0:T(4,128)S(1)}, f32[12,4,256]{2,1,0:T(4,128)S(1)}, u32[]{:S(2)}, u32[]{:S(2)}) collective-permute-start(f32[12,4,256]{2,1,0:T(4,128)S(1)} %get-tuple-element.109), channel_id=1, source_target_pairs={{0,8},{8,16},{16,24},{1,9},{9,17},{17,25},{2,10},{10,18},{18,26},{... | collective-permute-start | bytes 147464 | tf_op jit(solution)/shard_map/ppermute | solution.py:25
  14.9 10.3 %collective-permute-start.1 = (f32[12,4,256]{2,1,0:T(4,128)S(1)}, f32[12,4,256]{2,1,0:T(4,128)S(1)}, u32[]{:S(2)}, u32[]{:S(2)}) collective-permute-start(f32[12,4,256]{2,1,0:T(4,128)S(1)} %get-tuple-element.110), channel_id=1, source_target_pairs={{8,0},{16,8},{24,16},{9,1},{17,9},{25,17},{10,2},{18,10},{26,18},{... | collective-permute-start | bytes 147464 | tf_op jit(solution)/shard_map/ppermute | solution.py:28
  31.9 12.1 %collective-permute-start.3 = (f32[12,264,4]{1,2,0:T(4,128)S(1)}, f32[12,264,4]{1,2,0:T(4,128)S(1)}, u32[]{:S(2)}, u32[]{:S(2)}) collective-permute-start(f32[12,264,4]{1,2,0:T(4,128)S(1)} %copy.74), channel_id=1, source_target_pairs={{1,0},{2,1},{3,2},{4,3},{5,4},{6,5},{7,6},{9,8},{10,9},{11,10},{12... | collective-permute-start | bytes 152072 | tf_op jit(solution)/shard_map/ppermute | solution.py:28
  35.3 7.3 collective-permute-start.2
  65.4 53.2 %all-to-all-start.1 = ((f32[8,9,64,128]{3,2,1,0:T(8,128)}), f32[8,9,64,128]{3,2,1,0:T(8,128)}, u32[]{:S(2)}, u32[]{:S(2)}) async-start(f32[8,9,64,128]{3,2,1,0:T(8,128)} %bitcast.315), calls=%async_computation.1 | async-start | bytes 4718592 | tf_op jit(solution)/shard_map/all_to_all | solution.py:181
  125.0 7.1 collective-permute-start.4
  132.1 59.9 %all-to-all-start.2 = ((f32[8,9,64,128]{3,2,1,0:T(8,128)}), f32[8,9,64,128]{3,2,1,0:T(8,128)}, u32[]{:S(2)}, u32[]{:S(2)}) async-start(f32[8,9,64,128]{3,2,1,0:T(8,128)} %bitcast.311), calls=%async_computation.2 | async-start | bytes 4718592 | tf_op jit(solution)/shard_map/all_to_all | solution.py:193
  192.0 5.2 collective-permute-start.5
  203.1 6.0 collective-permute-start.7
  205.0 17.8 %collective-permute-start.6 = (f32[3,128]{1,0:T(4,128)S(1)}, f32[3,128]{1,0:T(4,128)S(1)}, u32[]{:S(2)}, u32[]{:S(2)}) collective-permute-start(f32[3,128]{1,0:T(4,128)S(1)} %add.1103), channel_id=1, source_target_pairs={{0,1},{1,0},{2,3},{3,2},{4,5},{5,4},{6,7},{7,6},{8,9},{9,8},{10,11... | collective-permute-start | bytes 4616 | tf_op jit(solution)/shard_map/ppermute | solution.py:83
  205.7 4.9 collective-permute-start.8
  215.3 13.2 %collective-permute-start.10 = (f32[4,272,8]{1,2,0:T(8,128)S(1)}, f32[4,272,8]{1,2,0:T(8,128)S(1)}, u32[]{:S(2)}, u32[]{:S(2)}) collective-permute-start(f32[4,272,8]{1,2,0:T(8,128)S(1)} %copy.85), channel_id=1, source_target_pairs={{1,0},{2,1},{3,2},{4,3},{5,4},{6,5},{7,6},{9,8},{10,9},{11,10},{12... | collective-permute-start | bytes 104456 | tf_op jit(solution)/shard_map/ppermute | solution.py:28
  220.7 6.9 collective-permute-start.9
  231.8 3.7 collective-permute-start.11
  235.4 4.5 collective-permute-start.12
  262.7 53.2 %all-to-all-start.3 = ((f32[8,9,64,128]{3,2,1,0:T(8,128)}), f32[8,9,64,128]{3,2,1,0:T(8,128)}, u32[]{:S(2)}, u32[]{:S(2)}) async-start(f32[8,9,64,128]{3,2,1,0:T(8,128)} %bitcast.314), calls=%async_computation.3 | async-start | bytes 4718592 | tf_op jit(solution)/shard_map/all_to_all | solution.py:181
  322.4 6.4 collective-permute-start.13
  328.8 64.5 %copy-start.74 = (s32[72]{0:T(128)S(1)}, s32[72]{0:T(128)}, u32[]{:S(2)}) copy-start(s32[72]{0:T(128)} %copy-done.73) | copy-start | bytes 868
  390.1 5.0 collective-permute-start.14
  399.8 5.6 collective-permute-start.16
  401.7 5.2 collective-permute-start.17
  409.4 13.2 %collective-permute-start.18 = (f32[4,272,8]{1,2,0:T(8,128)S(1)}, f32[4,272,8]{1,2,0:T(8,128)S(1)}, u32[]{:S(2)}, u32[]{:S(2)}) collective-permute-start(f32[4,272,8]{1,2,0:T(8,128)S(1)} %copy.91), channel_id=1, source_target_pairs={{0,1},{1,2},{2,3},{3,4},{4,5},{5,6},{6,7},{8,9},{9,10},{10,11},{11... | collective-permute-start | bytes 104456 | tf_op jit(solution)/shard_map/ppermute | solution.py:25
  412.6 11.0 %collective-permute-start.19 = (f32[4,272,8]{1,2,0:T(8,128)S(1)}, f32[4,272,8]{1,2,0:T(8,128)S(1)}, u32[]{:S(2)}, u32[]{:S(2)}) collective-permute-start(f32[4,272,8]{1,2,0:T(8,128)S(1)} %copy.92), channel_id=1, source_target_pairs={{1,0},{2,1},{3,2},{4,3},{5,4},{6,5},{7,6},{9,8},{10,9},{11,10},{12... | collective-permute-start | bytes 104456 | tf_op jit(solution)/shard_map/ppermute | solution.py:28
  417.4 3.9 collective-permute-start.15
  426.5 3.7 collective-permute-start.20
  430.2 4.5 collective-permute-start.21
  458.2 53.4 %all-to-all-start.5 = ((f32[8,9,64,128]{3,2,1,0:T(8,128)}), f32[8,9,64,128]{3,2,1,0:T(8,128)}, u32[]{:S(2)}, u32[]{:S(2)}) async-start(f32[8,9,64,128]{3,2,1,0:T(8,128)} %bitcast.312), calls=%async_computation.5 | async-start | bytes 4718592 | tf_op jit(solution)/shard_map/all_to_all | solution.py:181
  519.2 7.4 collective-permute-start.22
  587.4 5.0 collective-permute-start.23
  598.8 5.6 collective-permute-start.25
  600.7 5.2 collective-permute-start.26
  609.4 11.9 %collective-permute-start.27 = (f32[4,272,8]{1,2,0:T(8,128)S(1)}, f32[4,272,8]{1,2,0:T(8,128)S(1)}, u32[]{:S(2)}, u32[]{:S(2)}) collective-permute-start(f32[4,272,8]{1,2,0:T(8,128)S(1)} %copy.98), channel_id=1, source_target_pairs={{0,1},{1,2},{2,3},{3,4},{4,5},{5,6},{6,7},{8,9},{9,10},{10,11},{11... | collective-permute-start | bytes 104456 | tf_op jit(solution)/shard_map/ppermute | solution.py:25
  612.6 9.7 %collective-permute-start.28 = (f32[4,272,8]{1,2,0:T(8,128)S(1)}, f32[4,272,8]{1,2,0:T(8,128)S(1)}, u32[]{:S(2)}, u32[]{:S(2)}) collective-permute-start(f32[4,272,8]{1,2,0:T(8,128)S(1)} %copy.99), channel_id=1, source_target_pairs={{1,0},{2,1},{3,2},{4,3},{5,4},{6,5},{7,6},{9,8},{10,9},{11,10},{12... | collective-permute-start | bytes 104456 | tf_op jit(solution)/shard_map/ppermute | solution.py:28
  617.6 3.7 collective-permute-start.24
  625.5 3.7 collective-permute-start.29
  629.2 4.5 collective-permute-start.30
  660.6 53.4 %all-to-all-start.7 = ((f32[8,9,64,128]{3,2,1,0:T(8,128)}), f32[8,9,64,128]{3,2,1,0:T(8,128)}, u32[]{:S(2)}, u32[]{:S(2)}) async-start(f32[8,9,64,128]{3,2,1,0:T(8,128)} %bitcast.313), calls=%async_computation.7 | async-start | bytes 4718592 | tf_op jit(solution)/shard_map/all_to_all | solution.py:181
  721.1 7.3 collective-permute-start.31
  789.3 5.0 collective-permute-start.32
  798.3 5.6 collective-permute-start.34
  800.3 5.2 collective-permute-start.35
  807.9 12.0 %collective-permute-start.36 = (f32[4,272,8]{1,2,0:T(8,128)S(1)}, f32[4,272,8]{1,2,0:T(8,128)S(1)}, u32[]{:S(2)}, u32[]{:S(2)}) collective-permute-start(f32[4,272,8]{1,2,0:T(8,128)S(1)} %copy.105), channel_id=1, source_target_pairs={{0,1},{1,2},{2,3},{3,4},{4,5},{5,6},{6,7},{8,9},{9,10},{10,11},{11... | collective-permute-start | bytes 104456 | tf_op jit(solution)/shard_map/ppermute | solution.py:25
  811.2 9.8 %collective-permute-start.37 = (f32[4,272,8]{1,2,0:T(8,128)S(1)}, f32[4,272,8]{1,2,0:T(8,128)S(1)}, u32[]{:S(2)}, u32[]{:S(2)}) collective-permute-start(f32[4,272,8]{1,2,0:T(8,128)S(1)} %copy.106), channel_id=1, source_target_pairs={{1,0},{2,1},{3,2},{4,3},{5,4},{6,5},{7,6},{9,8},{10,9},{11,10},{12... | collective-permute-start | bytes 104456 | tf_op jit(solution)/shard_map/ppermute | solution.py:28
  816.2 3.7 collective-permute-start.33
  823.9 3.7 collective-permute-start.38
  827.5 4.5 collective-permute-start.39
  (83 other events, 761.1 us)

commit v12 on v11

--- a/solution.py
+++ b/solution.py
@@ -196,14 +196,24 @@
             landing, landed.reshape(owners * capacity, block_rows * block_cols), precision=highest
         )
         carry, summed = advance(carry, summed)
-        padded = with_rim(
+        padded = extended(
             summed.reshape(layers, rows_blocks, cols_blocks, block_rows, block_cols)
             .transpose(0, 1, 3, 2, 4)
             .reshape(layers, tile_rows, tile_cols),
+            (("gx", 1),),
             8,
         )
         carry, padded = advance(carry, padded)
-        along_cols = jnp.einsum("lab,bc->lac", padded, analysis_cols, precision=highest)
+        count = lax.axis_size("gy")
+        forward = [(i, i + 1) for i in range(count - 1)]
+        backward = [(target, source) for source, target in forward]
+        left = lax.ppermute(padded[:, :, tile_cols - 8 :], "gy", forward)
+        right = lax.ppermute(padded[:, :, :8], "gy", backward)
+        along_cols = (
+            jnp.einsum("lab,bc->lac", padded, analysis_cols[8 : 8 + tile_cols], precision=highest)
+            + jnp.einsum("lab,bc->lac", left, analysis_cols[:8], precision=highest)
+            + jnp.einsum("lab,bc->lac", right, analysis_cols[8 + tile_cols :], precision=highest)
+        )
         carry, along_cols = advance(carry, along_cols)
         return (
             jnp.einsum("lab,ac->lcb", along_cols, analysis_rows, precision=highest)

time: 858 us -> 845 us (0.985)
  local copies, waits for them, and re-layouts: 165 us -> 142 us
  starting transfers between devices: 118 us -> 129 us
    ppermute x0 -> x8, starting transfers between devices: none -> 39.3 us  [the longest x4 26.7 us: apply_op(): right = lax.ppermute(padded[:, :, :8], 'gy', backward)]
    ppermute x10 -> x6, starting transfers between devices: 41.5 us -> 21.6 us  [extended(): lax.ppermute(lax.slice_in_dim(block, 0, width, axis=dim), axis, backward)]
    all_to_all x4, waiting for transfers between devices: 124 us -> 114 us  [apply_op(): lax.all_to_all(outgoing, 'gy', split_axis=0, concat_axis=0, tiled=True)]
    ppermute x10 -> x6, starting transfers between devices: 20 us -> 12.1 us  [extended(): lax.ppermute(lax.slice_in_dim(block, block.shape[dim] - width, None, axis...]
    reshape x4 -> x8, local copies, waits for them, and re-layouts: 10.2 us -> 17.9 us  [apply_op(): padded = extended(summed.reshape(layers, rows_blocks, cols_blocks, block_...]
    unnamed x184 -> x106, local copies, waits for them, and re-layouts: 17.6 us -> 10.3 us
  transfers between devices with their start and end apart: 46 -> 46, of which waited for: 20 -> 24; matrix products, arithmetic and copies ran while one was open for 17% -> 15% of each run, Pallas kernels for 0% -> 0%
where the time goes in v12:
time: 845 us; the launch traced here: 832 us
  waiting for transfers between devices  213 us (25%)
  blocking collectives  181 us (21%)
  local copies, waits for them, and re-layouts  142 us (17%)
  starting transfers between devices  129 us (15%)
  matrix products  79.2 us (9%)
  other arithmetic  67.2 us (8%)
  between operations  21.8 us (3%)
    all_to_all x3, blocking collectives, apply_op(): lax.all_to_all(returning, 'gy', split_axis=0, concat_axis=0, tiled=True)  181 us
    all_to_all x4, waiting for transfers between devices, apply_op(): lax.all_to_all(outgoing, 'gy', split_axis=0, concat_axis=0, tiled=True)  114 us
    all_to_all x1, waiting for transfers between devices, apply_op(): lax.all_to_all(returning, 'gy', split_axis=0, concat_axis=0, tiled=True)  50.3 us
    ppermute x4, starting transfers between devices, apply_op(): right = lax.ppermute(padded[:, :, :8], 'gy', backward)  26.7 us
    reshape x13, local copies, waits for them, and re-layouts, lane_sum(): return jnp.sum(values.reshape(-1, 128), axis=0)  25.1 us
    ppermute x20, waiting for transfers between devices, sum_steps(): lax.ppermute(value, axis, pairs)  24.4 us
    ppermute x20, starting transfers between devices, sum_steps(): lax.ppermute(value, axis, pairs)  22.6 us
    dot_general x4, matrix products, apply_op(): jnp.einsum('lab,ac->lcb', along_cols, analysis_rows, precision=highest)  21.7 us
  transfers between devices with their start and end apart: 46, of which 24 were waited for; matrix products, arithmetic and copies ran while one was open for 15% of the time, Pallas kernels for 0%

profile of v12, /device:TPU:10, one launch (start us, length us, event | category | flops | bytes accessed | tf_op | source)
XLA Modules:
  0.0 832.3 jit_solution(10403091916303447158)
XLA Ops:
  3.4 6.3 all-to-all-start
  14.9 3.6 collective-permute-start.1
  38.4 4.1 collective-permute-done.2
  45.7 4.8 pad_maximum_fusion
  65.3 5.5 all-to-all-start.1
  81.5 37.0 %all-to-all-done.1 = f32[8,9,64,128]{3,2,1,0:T(8,128)} async-done(((f32[8,9,64,128]{3,2,1,0:T(8,128)}), f32[8,9,64,128]{3,2,1,0:T(8,128)}, u32[]{:S(2)}, u32[]{:S(2)}) %all-to-all-start.1) | async-done | bytes 2359328 | tf_op jit(solution)/shard_map/all_to_all | solution.py:181
  118.5 3.8 gather_fusion.1
  128.3 3.7 gather_fusion.2
  132.0 8.3 all-to-all-start.2
  141.6 50.3 %all-to-all-done.2 = f32[8,9,64,128]{3,2,1,0:T(8,128)} async-done(((f32[8,9,64,128]{3,2,1,0:T(8,128)}), f32[8,9,64,128]{3,2,1,0:T(8,128)}, u32[]{:S(2)}, u32[]{:S(2)}) %all-to-all-start.2) | async-done | bytes 2359328 | tf_op jit(solution)/shard_map/all_to_all | solution.py:193
  208.7 3.6 collective-permute-start.8
  212.9 4.4 collective-permute-done.7
  219.6 3.5 collective-permute-start.9
  226.4 16.2 %collective-permute-start.11 = (f32[4,272,8]{1,2,0:T(8,128)S(1)}, f32[4,272,8]{1,2,0:T(8,128)S(1)}, u32[]{:S(2)}, u32[]{:S(2)}) collective-permute-start(f32[4,272,8]{1,2,0:T(8,128)S(1)} %get-tuple-element.129), channel_id=1, source_target_pairs={{1,0},{2,1},{3,2},{4,3},{5,4},{6,5},{7,6},{9,8},{10,9},{11,10},{12... | collective-permute-start | bytes 104456 | tf_op jit(solution)/shard_map/ppermute | solution.py:211
  245.8 4.5 collective-permute-done.12
  253.0 6.2 slice_multiply_fusion.3
  272.9 4.3 all-to-all-start.3
  277.2 4.5 multiply_multiply_fusion.7
  289.7 30.4 %all-to-all-done.3 = f32[8,9,64,128]{3,2,1,0:T(8,128)} async-done(((f32[8,9,64,128]{3,2,1,0:T(8,128)}), f32[8,9,64,128]{3,2,1,0:T(8,128)}, u32[]{:S(2)}, u32[]{:S(2)}) %all-to-all-start.3) | async-done | bytes 2359328 | tf_op jit(solution)/shard_map/all_to_all | solution.py:181
  320.1 3.8 gather_fusion.4
  329.2 3.7 gather_fusion.5
  332.8 60.0 %all_to_all.49 = f32[8,9,64,128]{3,2,1,0:T(8,128)S(1)} all-to-all(f32[8,9,64,128]{3,2,1,0:T(8,128)} %bitcast.341), channel_id=1, replica_groups=mesh['gx'=4,'gy'=8] {'gy'}, dimensions={0} | all-to-all | bytes 4718592 | tf_op jit(solution)/shard_map/all_to_all | solution.py:193
  392.9 3.8 collective-permute-start.14
  405.1 3.6 collective-permute-start.17
  421.3 3.8 collective-permute-start.20
  429.6 4.4 collective-permute-done.21
  440.6 5.1 fusion.13
  457.2 4.8 all-to-all-start.5
  469.1 4.6 multiply_multiply_fusion.5
  485.0 20.9 %all-to-all-done.5 = f32[8,9,64,128]{3,2,1,0:T(8,128)} async-done(((f32[8,9,64,128]{3,2,1,0:T(8,128)}), f32[8,9,64,128]{3,2,1,0:T(8,128)}, u32[]{:S(2)}, u32[]{:S(2)}) %all-to-all-start.5) | async-done | bytes 2359328 | tf_op jit(solution)/shard_map/all_to_all | solution.py:181
  505.8 3.8 gather_fusion.7
  509.6 3.8 multiply_reduce_fusion.1
  517.1 3.7 gather_fusion.8
  520.8 60.3 %all_to_all.50 = f32[8,9,64,128]{3,2,1,0:T(8,128)S(1)} all-to-all(f32[8,9,64,128]{3,2,1,0:T(8,128)} %bitcast.342), channel_id=1, replica_groups=mesh['gx'=4,'gy'=8] {'gy'}, dimensions={0} | all-to-all | bytes 4718592 | tf_op jit(solution)/shard_map/all_to_all | solution.py:193
  581.0 4.3 collective-permute-start.23
  598.2 3.6 collective-permute-start.26
  622.7 4.4 collective-permute-done.30
  633.7 6.9 slice_multiply_fusion.1
  654.2 4.6 all-to-all-start.7
  658.9 5.6 multiply_multiply_fusion
  677.4 25.4 %all-to-all-done.7 = f32[8,9,64,128]{3,2,1,0:T(8,128)} async-done(((f32[8,9,64,128]{3,2,1,0:T(8,128)}), f32[8,9,64,128]{3,2,1,0:T(8,128)}, u32[]{:S(2)}, u32[]{:S(2)}) %all-to-all-start.7) | async-done | bytes 2359328 | tf_op jit(solution)/shard_map/all_to_all | solution.py:181
  702.8 3.7 gather_fusion.10
  713.5 3.7 gather_fusion.11
  717.2 60.3 %all_to_all.51 = f32[8,9,64,128]{3,2,1,0:T(8,128)S(1)} all-to-all(f32[8,9,64,128]{3,2,1,0:T(8,128)} %bitcast.340), channel_id=1, replica_groups=mesh['gx'=4,'gy'=8] {'gy'}, dimensions={0} | all-to-all | bytes 4718592 | tf_op jit(solution)/shard_map/all_to_all | solution.py:193
  777.6 4.2 collective-permute-start.32
  790.3 3.6 collective-permute-start.35
  813.7 3.5 convolution_bitcast_fusion
  824.7 7.3 fusion.16
  (350 shorter events, 274.4 us)
Async XLA Ops:
  0.6 121.7 %copy-start = (f32[2,4,128,128]{3,2,1,0:T(8,128)S(1)}, f32[2,4,128,128]{3,2,1,0:T(8,128)}, u32[]{:S(2)}) copy-start(f32[2,4,128,128]{3,2,1,0:T(8,128)} %param.8) | copy-start | bytes 1572868
  3.4 21.2 %all-to-all-start = ((s32[8,1,9]{2,1,0:T(1,128)}), s32[8,1,9]{2,1,0:T(1,128)S(1)}, u32[]{:S(2)}, u32[]{:S(2)}) async-start(s32[8,1,9]{2,1,0:T(1,128)} %copy.104), calls=%async_computation | async-start | bytes 8192 | tf_op jit(solution)/shard_map/all_to_all | solution.py:156
  13.0 12.2 %collective-permute-start = (f32[12,4,256]{2,1,0:T(4,128)S(1)}, f32[12,4,256]{2,1,0:T(4,128)S(1)}, u32[]{:S(2)}, u32[]{:S(2)}) collective-permute-start(f32[12,4,256]{2,1,0:T(4,128)S(1)} %get-tuple-element.109), channel_id=1, source_target_pairs={{0,8},{8,16},{16,24},{1,9},{9,17},{17,25},{2,10},{10,18},{18,26},{... | collective-permute-start | bytes 147464 | tf_op jit(solution)/shard_map/ppermute | solution.py:25
  14.9 10.3 %collective-permute-start.1 = (f32[12,4,256]{2,1,0:T(4,128)S(1)}, f32[12,4,256]{2,1,0:T(4,128)S(1)}, u32[]{:S(2)}, u32[]{:S(2)}) collective-permute-start(f32[12,4,256]{2,1,0:T(4,128)S(1)} %get-tuple-element.110), channel_id=1, source_target_pairs={{8,0},{16,8},{24,16},{9,1},{17,9},{25,17},{10,2},{18,10},{26,18},{... | collective-permute-start | bytes 147464 | tf_op jit(solution)/shard_map/ppermute | solution.py:28
  31.8 12.1 %collective-permute-start.3 = (f32[12,264,4]{1,2,0:T(4,128)S(1)}, f32[12,264,4]{1,2,0:T(4,128)S(1)}, u32[]{:S(2)}, u32[]{:S(2)}) collective-permute-start(f32[12,264,4]{1,2,0:T(4,128)S(1)} %copy.97), channel_id=1, source_target_pairs={{1,0},{2,1},{3,2},{4,3},{5,4},{6,5},{7,6},{9,8},{10,9},{11,10},{12... | collective-permute-start | bytes 152072 | tf_op jit(solution)/shard_map/ppermute | solution.py:28
  35.2 7.3 collective-permute-start.2
  65.3 53.2 %all-to-all-start.1 = ((f32[8,9,64,128]{3,2,1,0:T(8,128)}), f32[8,9,64,128]{3,2,1,0:T(8,128)}, u32[]{:S(2)}, u32[]{:S(2)}) async-start(f32[8,9,64,128]{3,2,1,0:T(8,128)} %bitcast.339), calls=%async_computation.1 | async-start | bytes 4718592 | tf_op jit(solution)/shard_map/all_to_all | solution.py:181
  125.0 7.0 collective-permute-start.4
  132.0 59.9 %all-to-all-start.2 = ((f32[8,9,64,128]{3,2,1,0:T(8,128)}), f32[8,9,64,128]{3,2,1,0:T(8,128)}, u32[]{:S(2)}, u32[]{:S(2)}) async-start(f32[8,9,64,128]{3,2,1,0:T(8,128)} %bitcast.335), calls=%async_computation.2 | async-start | bytes 4718592 | tf_op jit(solution)/shard_map/all_to_all | solution.py:193
  191.9 5.2 collective-permute-start.5
  204.7 8.1 collective-permute-start.6
  206.8 10.5 %collective-permute-start.7 = (f32[4,8,256]{1,2,0:T(8,128)S(1)}, f32[4,8,256]{1,2,0:T(8,128)S(1)}, u32[]{:S(2)}, u32[]{:S(2)}) collective-permute-start(f32[4,8,256]{1,2,0:T(8,128)S(1)} %get-tuple-element.137), channel_id=1, source_target_pairs={{0,8},{8,16},{16,24},{1,9},{9,17},{17,25},{2,10},{10,18},{18,26},{... | collective-permute-start | bytes 98312 | tf_op jit(solution)/shard_map/ppermute | solution.py:25
  208.7 10.3 %collective-permute-start.8 = (f32[4,8,256]{1,2,0:T(8,128)S(1)}, f32[4,8,256]{1,2,0:T(8,128)S(1)}, u32[]{:S(2)}, u32[]{:S(2)}) collective-permute-start(f32[4,8,256]{1,2,0:T(8,128)S(1)} %get-tuple-element.138), channel_id=1, source_target_pairs={{8,0},{16,8},{24,16},{9,1},{17,9},{25,17},{10,2},{18,10},{26,18},{... | collective-permute-start | bytes 98312 | tf_op jit(solution)/shard_map/ppermute | solution.py:28
  219.6 23.1 %collective-permute-start.9 = (f32[3,128]{1,0:T(4,128)S(1)}, f32[3,128]{1,0:T(4,128)S(1)}, u32[]{:S(2)}, u32[]{:S(2)}) collective-permute-start(f32[3,128]{1,0:T(4,128)S(1)} %add.1352), channel_id=1, source_target_pairs={{0,2},{1,3},{2,0},{3,1},{4,6},{5,7},{6,4},{7,5},{8,10},{9,11},{10,... | collective-permute-start | bytes 4616 | tf_op jit(solution)/shard_map/ppermute | solution.py:83
  223.1 19.6 %collective-permute-start.10 = (f32[4,272,8]{1,2,0:T(8,128)S(1)}, f32[4,272,8]{1,2,0:T(8,128)S(1)}, u32[]{:S(2)}, u32[]{:S(2)}) collective-permute-start(f32[4,272,8]{1,2,0:T(8,128)S(1)} %get-tuple-element.130), channel_id=1, source_target_pairs={{0,1},{1,2},{2,3},{3,4},{4,5},{5,6},{6,7},{8,9},{9,10},{10,11},{11... | collective-permute-start | bytes 104456 | tf_op jit(solution)/shard_map/ppermute | solution.py:210
  226.4 17.1 %collective-permute-start.11 = (f32[4,272,8]{1,2,0:T(8,128)S(1)}, f32[4,272,8]{1,2,0:T(8,128)S(1)}, u32[]{:S(2)}, u32[]{:S(2)}) collective-permute-start(f32[4,272,8]{1,2,0:T(8,128)S(1)} %get-tuple-element.129), channel_id=1, source_target_pairs={{1,0},{2,1},{3,2},{4,3},{5,4},{6,5},{7,6},{9,8},{10,9},{11,10},{12... | collective-permute-start | bytes 104456 | tf_op jit(solution)/shard_map/ppermute | solution.py:211
  245.8 4.5 collective-permute-start.12
  272.9 47.2 %all-to-all-start.3 = ((f32[8,9,64,128]{3,2,1,0:T(8,128)}), f32[8,9,64,128]{3,2,1,0:T(8,128)}, u32[]{:S(2)}, u32[]{:S(2)}) async-start(f32[8,9,64,128]{3,2,1,0:T(8,128)} %bitcast.338), calls=%async_computation.3 | async-start | bytes 4718592 | tf_op jit(solution)/shard_map/all_to_all | solution.py:181
  289.7 34.2 %copy-start.18 = (f32[2,8,64,128,1]{3,2,4,1,0:T(8,128)S(1)}, f32[2,8,64,128,1]{3,2,4,1,0:T(8,128)}, u32[]{:S(2)}) copy-start(f32[2,8,64,128,1]{3,2,4,1,0:T(8,128)} %copy-done.17) | copy-start | bytes 1572868
  326.5 6.3 collective-permute-start.13
  392.9 5.7 collective-permute-start.14
  403.2 10.5 %collective-permute-start.16 = (f32[4,8,256]{1,2,0:T(8,128)S(1)}, f32[4,8,256]{1,2,0:T(8,128)S(1)}, u32[]{:S(2)}, u32[]{:S(2)}) collective-permute-start(f32[4,8,256]{1,2,0:T(8,128)S(1)} %get-tuple-element.135), channel_id=1, source_target_pairs={{0,8},{8,16},{16,24},{1,9},{9,17},{17,25},{2,10},{10,18},{18,26},{... | collective-permute-start | bytes 98312 | tf_op jit(solution)/shard_map/ppermute | solution.py:25
  405.1 10.3 %collective-permute-start.17 = (f32[4,8,256]{1,2,0:T(8,128)S(1)}, f32[4,8,256]{1,2,0:T(8,128)S(1)}, u32[]{:S(2)}, u32[]{:S(2)}) collective-permute-start(f32[4,8,256]{1,2,0:T(8,128)S(1)} %get-tuple-element.136), channel_id=1, source_target_pairs={{8,0},{16,8},{24,16},{9,1},{17,9},{25,17},{10,2},{18,10},{26,18},{... | collective-permute-start | bytes 98312 | tf_op jit(solution)/shard_map/ppermute | solution.py:28
  408.8 3.7 collective-permute-start.15
  416.1 9.0 %collective-permute-start.18 = (f32[7,128]{1,0:T(8,128)S(1)}, f32[7,128]{1,0:T(8,128)S(1)}, u32[]{:S(2)}, u32[]{:S(2)}) collective-permute-start(f32[7,128]{1,0:T(8,128)S(1)} %add.1377), channel_id=1, source_target_pairs={{0,2},{1,3},{2,0},{3,1},{4,6},{5,7},{6,4},{7,5},{8,10},{9,11},{10,... | collective-permute-start | bytes 10760 | tf_op jit(solution)/shard_map/ppermute | solution.py:83
  417.0 8.1 collective-permute-start.19
  421.3 6.0 collective-permute-start.20
  429.5 4.5 collective-permute-start.21
  457.2 48.7 %all-to-all-start.5 = ((f32[8,9,64,128]{3,2,1,0:T(8,128)}), f32[8,9,64,128]{3,2,1,0:T(8,128)}, u32[]{:S(2)}, u32[]{:S(2)}) async-start(f32[8,9,64,128]{3,2,1,0:T(8,128)} %bitcast.336), calls=%async_computation.5 | async-start | bytes 4718592 | tf_op jit(solution)/shard_map/all_to_all | solution.py:181
  513.4 7.4 collective-permute-start.22
  581.0 6.2 collective-permute-start.23
  596.3 10.5 %collective-permute-start.25 = (f32[4,8,256]{1,2,0:T(8,128)S(1)}, f32[4,8,256]{1,2,0:T(8,128)S(1)}, u32[]{:S(2)}, u32[]{:S(2)}) collective-permute-start(f32[4,8,256]{1,2,0:T(8,128)S(1)} %get-tuple-element.133), channel_id=1, source_target_pairs={{0,8},{8,16},{16,24},{1,9},{9,17},{17,25},{2,10},{10,18},{18,26},{... | collective-permute-start | bytes 98312 | tf_op jit(solution)/shard_map/ppermute | solution.py:25
  598.2 10.3 %collective-permute-start.26 = (f32[4,8,256]{1,2,0:T(8,128)S(1)}, f32[4,8,256]{1,2,0:T(8,128)S(1)}, u32[]{:S(2)}, u32[]{:S(2)}) collective-permute-start(f32[4,8,256]{1,2,0:T(8,128)S(1)} %get-tuple-element.134), channel_id=1, source_target_pairs={{8,0},{16,8},{24,16},{9,1},{17,9},{25,17},{10,2},{18,10},{26,18},{... | collective-permute-start | bytes 98312 | tf_op jit(solution)/shard_map/ppermute | solution.py:28
  601.9 3.7 collective-permute-start.24
  609.2 8.6 %collective-permute-start.27 = (f32[7,128]{1,0:T(8,128)S(1)}, f32[7,128]{1,0:T(8,128)S(1)}, u32[]{:S(2)}, u32[]{:S(2)}) collective-permute-start(f32[7,128]{1,0:T(8,128)S(1)} %add.1394), channel_id=1, source_target_pairs={{0,2},{1,3},{2,0},{3,1},{4,6},{5,7},{6,4},{7,5},{8,10},{9,11},{10,... | collective-permute-start | bytes 10760 | tf_op jit(solution)/shard_map/ppermute | solution.py:83
  610.1 7.7 collective-permute-start.28
  614.4 6.0 collective-permute-start.29
  622.6 4.5 collective-permute-start.30
  654.2 48.6 %all-to-all-start.7 = ((f32[8,9,64,128]{3,2,1,0:T(8,128)}), f32[8,9,64,128]{3,2,1,0:T(8,128)}, u32[]{:S(2)}, u32[]{:S(2)}) async-start(f32[8,9,64,128]{3,2,1,0:T(8,128)} %bitcast.337), calls=%async_computation.7 | async-start | bytes 4718592 | tf_op jit(solution)/shard_map/all_to_all | solution.py:181
  709.9 7.3 collective-permute-start.31
  777.6 6.2 collective-permute-start.32
  788.3 10.5 %collective-permute-start.34 = (f32[4,8,256]{1,2,0:T(8,128)S(1)}, f32[4,8,256]{1,2,0:T(8,128)S(1)}, u32[]{:S(2)}, u32[]{:S(2)}) collective-permute-start(f32[4,8,256]{1,2,0:T(8,128)S(1)} %get-tuple-element.131), channel_id=1, source_target_pairs={{0,8},{8,16},{16,24},{1,9},{9,17},{17,25},{2,10},{10,18},{18,26},{... | collective-permute-start | bytes 98312 | tf_op jit(solution)/shard_map/ppermute | solution.py:25
  790.3 10.3 %collective-permute-start.35 = (f32[4,8,256]{1,2,0:T(8,128)S(1)}, f32[4,8,256]{1,2,0:T(8,128)S(1)}, u32[]{:S(2)}, u32[]{:S(2)}) collective-permute-start(f32[4,8,256]{1,2,0:T(8,128)S(1)} %get-tuple-element.132), channel_id=1, source_target_pairs={{8,0},{16,8},{24,16},{9,1},{17,9},{25,17},{10,2},{18,10},{26,18},{... | collective-permute-start | bytes 98312 | tf_op jit(solution)/shard_map/ppermute | solution.py:28
  793.9 3.7 collective-permute-start.33
  801.2 8.6 %collective-permute-start.36 = (f32[7,128]{1,0:T(8,128)S(1)}, f32[7,128]{1,0:T(8,128)S(1)}, u32[]{:S(2)}, u32[]{:S(2)}) collective-permute-start(f32[7,128]{1,0:T(8,128)S(1)} %add.1411), channel_id=1, source_target_pairs={{0,2},{1,3},{2,0},{3,1},{4,6},{5,7},{6,4},{7,5},{8,10},{9,11},{10,... | collective-permute-start | bytes 10760 | tf_op jit(solution)/shard_map/ppermute | solution.py:83
  802.2 7.7 collective-permute-start.37
  806.5 6.0 collective-permute-start.38
  813.5 4.6 collective-permute-start.39
  (48 other events, 307.4 us)

commit v13 on v12

--- a/solution.py
+++ b/solution.py
@@ -166,7 +166,7 @@
         own_blocks,
     )
     landing = (
-        wanted_ids.reshape(-1)[None, :] == jnp.arange(own_blocks, dtype=jnp.int32)[:, None]
+        gather_ids.reshape(-1)[None, :] == jnp.arange(own_blocks, dtype=jnp.int32)[:, None]
     ).astype(jnp.float32)
     def apply_op(direction, partials):
         along_rows = jnp.einsum("lab,ac->lcb", direction, synth_rows, precision=highest)
@@ -197,20 +197,21 @@
         )
         carry, summed = advance(carry, summed)
         padded = extended(
-            summed.reshape(layers, rows_blocks, cols_blocks, block_rows, block_cols)
-            .transpose(0, 1, 3, 2, 4)
-            .reshape(layers, tile_rows, tile_cols),
-            (("gx", 1),),
-            8,
+            summed.reshape(layers, cols_blocks, tile_rows, block_cols), (("gx", 2),), 8
         )
         carry, padded = advance(carry, padded)
         count = lax.axis_size("gy")
         forward = [(i, i + 1) for i in range(count - 1)]
         backward = [(target, source) for source, target in forward]
-        left = lax.ppermute(padded[:, :, tile_cols - 8 :], "gy", forward)
-        right = lax.ppermute(padded[:, :, :8], "gy", backward)
+        left = lax.ppermute(padded[:, cols_blocks - 1, :, block_cols - 8 :], "gy", forward)
+        right = lax.ppermute(padded[:, 0, :, :8], "gy", backward)
         along_cols = (
-            jnp.einsum("lab,bc->lac", padded, analysis_cols[8 : 8 + tile_cols], precision=highest)
+            jnp.einsum(
+                "ljac,jcd->lad",
+                padded,
+                analysis_cols[8 : 8 + tile_cols].reshape(cols_blocks, block_cols, -1),
+                precision=highest,
+            )
             + jnp.einsum("lab,bc->lac", left, analysis_cols[:8], precision=highest)
             + jnp.einsum("lab,bc->lac", right, analysis_cols[8 + tile_cols :], precision=highest)
         )

time: 845 us -> 839 us (level)
  matrix products: 79.2 us -> 92.5 us
    ppermute x8, starting transfers between devices: 39.3 us -> 27.8 us  [the longest x4 15.2 us: apply_op(): right = lax.ppermute(padded[:, 0, :, :8], 'gy', backward)]
    reshape x12 -> x8, local copies, waits for them, and re-layouts: 23.1 us -> 15.2 us  [apply_op(): summed.reshape(layers, cols_blocks, tile_rows, block_cols)]
  transfers between devices with their start and end apart: 46 -> 46, of which waited for: 24 -> 25; matrix products, arithmetic and copies ran while one was open for 15% -> 16% of each run, Pallas kernels for 0% -> 0%
where the time goes in v13:
time: 839 us; the launch traced here: 827 us
  waiting for transfers between devices  209 us (25%)
  blocking collectives  180 us (21%)
  local copies, waits for them, and re-layouts  135 us (16%)
  starting transfers between devices  121 us (14%)
  matrix products  92.5 us (11%)
  other arithmetic  66.7 us (8%)
  between operations  21.4 us (3%)
    all_to_all x3, blocking collectives, apply_op(): lax.all_to_all(returning, 'gy', split_axis=0, concat_axis=0, tiled=True)  180 us
    all_to_all x4, waiting for transfers between devices, apply_op(): lax.all_to_all(outgoing, 'gy', split_axis=0, concat_axis=0, tiled=True)  114 us
    all_to_all x1, waiting for transfers between devices, apply_op(): lax.all_to_all(returning, 'gy', split_axis=0, concat_axis=0, tiled=True)  50.3 us
    dot_general x4, matrix products, apply_op(): jnp.einsum('lab,ac->lcb', along_cols, analysis_rows, precision=highest)  26.8 us
    reshape x13, local copies, waits for them, and re-layouts, lane_sum(): return jnp.sum(values.reshape(-1, 128), axis=0)  25.1 us
    ppermute x20, starting transfers between devices, sum_steps(): lax.ppermute(value, axis, pairs)  23.9 us
    ppermute x20, waiting for transfers between devices, sum_steps(): lax.ppermute(value, axis, pairs)  22.7 us
    ppermute x6, starting transfers between devices, extended(): lax.ppermute(lax.slice_in_dim(block, 0, width, axis=dim), axis, backward)  21.6 us
  transfers between devices with their start and end apart: 46, of which 25 were waited for; matrix products, arithmetic and copies ran while one was open for 16% of the time, Pallas kernels for 0%

profile of v13, /device:TPU:10, one launch (start us, length us, event | category | flops | bytes accessed | tf_op | source)
XLA Modules:
  0.0 826.7 jit_solution(1877331465960480272)
XLA Ops:
  3.4 6.3 all-to-all-start
  17.1 3.6 collective-permute-start.1
  40.5 4.1 collective-permute-done.2
  47.8 4.8 pad_maximum_fusion
  67.4 5.8 all-to-all-start.1
  83.8 37.1 %all-to-all-done.1 = f32[8,9,64,128]{3,2,1,0:T(8,128)} async-done(((f32[8,9,64,128]{3,2,1,0:T(8,128)}), f32[8,9,64,128]{3,2,1,0:T(8,128)}, u32[]{:S(2)}, u32[]{:S(2)}) %all-to-all-start.1) | async-done | bytes 2359328 | tf_op jit(solution)/shard_map/all_to_all | solution.py:181
  120.9 3.7 gather_fusion.1
  130.7 3.7 gather_fusion.2
  134.4 8.2 all-to-all-start.2
  143.9 50.3 %all-to-all-done.2 = f32[8,9,64,128]{3,2,1,0:T(8,128)} async-done(((f32[8,9,64,128]{3,2,1,0:T(8,128)}), f32[8,9,64,128]{3,2,1,0:T(8,128)}, u32[]{:S(2)}, u32[]{:S(2)}) %all-to-all-start.2) | async-done | bytes 2359328 | tf_op jit(solution)/shard_map/all_to_all | solution.py:193
  196.0 4.4 fusion.9
  209.3 3.6 collective-permute-start.8
  213.2 4.6 collective-permute-done.7
  227.0 4.5 collective-permute-start.11
  236.0 3.7 collective-permute-done.12
  242.4 8.1 slice_multiply_fusion.3
  264.4 5.4 all-to-all-start.3
  269.8 4.4 multiply_multiply_fusion.7
  282.2 30.4 %all-to-all-done.3 = f32[8,9,64,128]{3,2,1,0:T(8,128)} async-done(((f32[8,9,64,128]{3,2,1,0:T(8,128)}), f32[8,9,64,128]{3,2,1,0:T(8,128)}, u32[]{:S(2)}, u32[]{:S(2)}) %all-to-all-start.3) | async-done | bytes 2359328 | tf_op jit(solution)/shard_map/all_to_all | solution.py:181
  312.6 3.7 gather_fusion.4
  321.7 3.7 gather_fusion.5
  325.4 60.1 %all_to_all.52 = f32[8,9,64,128]{3,2,1,0:T(8,128)S(1)} all-to-all(f32[8,9,64,128]{3,2,1,0:T(8,128)} %bitcast.367), channel_id=1, replica_groups=mesh['gx'=4,'gy'=8] {'gy'}, dimensions={0} | all-to-all | bytes 4718592 | tf_op jit(solution)/shard_map/all_to_all | solution.py:193
  385.5 4.7 collective-permute-start.14
  396.9 3.6 collective-permute-start.17
  413.1 3.6 collective-permute-start.20
  422.2 4.3 collective-permute-done.21
  433.0 6.0 fusion.15
  452.7 5.3 all-to-all-start.5
  465.2 4.5 multiply_multiply_fusion.5
  481.0 20.9 %all-to-all-done.5 = f32[8,9,64,128]{3,2,1,0:T(8,128)} async-done(((f32[8,9,64,128]{3,2,1,0:T(8,128)}), f32[8,9,64,128]{3,2,1,0:T(8,128)}, u32[]{:S(2)}, u32[]{:S(2)}) %all-to-all-start.5) | async-done | bytes 2359328 | tf_op jit(solution)/shard_map/all_to_all | solution.py:181
  501.9 3.7 gather_fusion.7
  505.6 3.7 multiply_reduce_fusion.1
  513.1 3.7 gather_fusion.8
  516.8 60.1 %all_to_all.53 = f32[8,9,64,128]{3,2,1,0:T(8,128)S(1)} all-to-all(f32[8,9,64,128]{3,2,1,0:T(8,128)} %bitcast.368), channel_id=1, replica_groups=mesh['gx'=4,'gy'=8] {'gy'}, dimensions={0} | all-to-all | bytes 4718592 | tf_op jit(solution)/shard_map/all_to_all | solution.py:193
  576.9 4.2 collective-permute-start.23
  592.3 3.6 collective-permute-start.26
  617.5 4.3 collective-permute-done.30
  628.3 8.6 %slice_multiply_fusion.1 = (f32[4,264,264]{2,1,0:T(8,128)S(1)}, f32[4,264,264]{2,1,0:T(8,128)}, f32[4,264,264]{2,1,0:T(8,128)}) fusion(f32[12,264,264]{2,1,0:T(8,128)} %copy-done.1, f32[4,264,264]{2,1,0:T(8,128)} %get-tuple-element.98, f32[]{:T(128)S(6)} %div.169, f32[4,264,264]{2,1,0:T(8,128)} %copy-done.7, f32[]{:T(128)S(6)} %div.168, ...), kind=kOutput, calls=%fused_computation.65 | convolution fusion | flops 458147712 | bytes 10082696 | tf_op jit(solution)/shard_map/lab,ac->lcb/dot_general | solution.py:220
  650.5 4.9 all-to-all-start.7
  655.4 5.6 multiply_multiply_fusion
  673.8 25.4 %all-to-all-done.7 = f32[8,9,64,128]{3,2,1,0:T(8,128)} async-done(((f32[8,9,64,128]{3,2,1,0:T(8,128)}), f32[8,9,64,128]{3,2,1,0:T(8,128)}, u32[]{:S(2)}, u32[]{:S(2)}) %all-to-all-start.7) | async-done | bytes 2359328 | tf_op jit(solution)/shard_map/all_to_all | solution.py:181
  699.3 3.7 gather_fusion.10
  710.0 3.7 gather_fusion.11
  713.7 60.1 %all_to_all.54 = f32[8,9,64,128]{3,2,1,0:T(8,128)S(1)} all-to-all(f32[8,9,64,128]{3,2,1,0:T(8,128)} %bitcast.366), channel_id=1, replica_groups=mesh['gx'=4,'gy'=8] {'gy'}, dimensions={0} | all-to-all | bytes 4718592 | tf_op jit(solution)/shard_map/all_to_all | solution.py:193
  784.2 3.6 collective-permute-start.35
  800.4 3.6 collective-permute-start.38
  808.3 4.1 convolution_bitcast_fusion
  819.2 7.2 fusion.20
  (338 shorter events, 273.9 us)
Async XLA Ops:
  0.6 124.0 %copy-start = (f32[2,4,128,128]{3,2,1,0:T(8,128)S(1)}, f32[2,4,128,128]{3,2,1,0:T(8,128)}, u32[]{:S(2)}) copy-start(f32[2,4,128,128]{3,2,1,0:T(8,128)} %param.8) | copy-start | bytes 1572868
  3.4 23.2 %all-to-all-start = ((s32[8,1,9]{2,1,0:T(1,128)}), s32[8,1,9]{2,1,0:T(1,128)S(1)}, u32[]{:S(2)}, u32[]{:S(2)}) async-start(s32[8,1,9]{2,1,0:T(1,128)} %copy.102), calls=%async_computation | async-start | bytes 8192 | tf_op jit(solution)/shard_map/all_to_all | solution.py:156
  15.2 12.1 %collective-permute-start = (f32[12,4,256]{2,1,0:T(4,128)S(1)}, f32[12,4,256]{2,1,0:T(4,128)S(1)}, u32[]{:S(2)}, u32[]{:S(2)}) collective-permute-start(f32[12,4,256]{2,1,0:T(4,128)S(1)} %get-tuple-element.109), channel_id=1, source_target_pairs={{0,8},{8,16},{16,24},{1,9},{9,17},{17,25},{2,10},{10,18},{18,26},{... | collective-permute-start | bytes 147464 | tf_op jit(solution)/shard_map/ppermute | solution.py:25
  17.1 10.2 %collective-permute-start.1 = (f32[12,4,256]{2,1,0:T(4,128)S(1)}, f32[12,4,256]{2,1,0:T(4,128)S(1)}, u32[]{:S(2)}, u32[]{:S(2)}) collective-permute-start(f32[12,4,256]{2,1,0:T(4,128)S(1)} %get-tuple-element.110), channel_id=1, source_target_pairs={{8,0},{16,8},{24,16},{9,1},{17,9},{25,17},{10,2},{18,10},{26,18},{... | collective-permute-start | bytes 147464 | tf_op jit(solution)/shard_map/ppermute | solution.py:28
  33.9 12.1 %collective-permute-start.3 = (f32[12,264,4]{1,2,0:T(4,128)S(1)}, f32[12,264,4]{1,2,0:T(4,128)S(1)}, u32[]{:S(2)}, u32[]{:S(2)}) collective-permute-start(f32[12,264,4]{1,2,0:T(4,128)S(1)} %copy.95), channel_id=1, source_target_pairs={{1,0},{2,1},{3,2},{4,3},{5,4},{6,5},{7,6},{9,8},{10,9},{11,10},{12... | collective-permute-start | bytes 152072 | tf_op jit(solution)/shard_map/ppermute | solution.py:28
  37.3 7.3 collective-permute-start.2
  67.4 53.5 %all-to-all-start.1 = ((f32[8,9,64,128]{3,2,1,0:T(8,128)}), f32[8,9,64,128]{3,2,1,0:T(8,128)}, u32[]{:S(2)}, u32[]{:S(2)}) async-start(f32[8,9,64,128]{3,2,1,0:T(8,128)} %bitcast.365), calls=%async_computation.1 | async-start | bytes 4718592 | tf_op jit(solution)/shard_map/all_to_all | solution.py:181
  127.3 7.0 collective-permute-start.4
  134.4 59.9 %all-to-all-start.2 = ((f32[8,9,64,128]{3,2,1,0:T(8,128)}), f32[8,9,64,128]{3,2,1,0:T(8,128)}, u32[]{:S(2)}, u32[]{:S(2)}) async-start(f32[8,9,64,128]{3,2,1,0:T(8,128)} %bitcast.361), calls=%async_computation.2 | async-start | bytes 4718592 | tf_op jit(solution)/shard_map/all_to_all | solution.py:193
  194.2 6.2 collective-permute-start.5
  205.3 7.9 collective-permute-start.6
  207.3 10.5 %collective-permute-start.7 = (f32[4,2,8,128]{2,3,0,1:T(8,128)S(1)}, f32[4,2,8,128]{2,3,0,1:T(8,128)S(1)}, u32[]{:S(2)}, u32[]{:S(2)}) collective-permute-start(f32[4,2,8,128]{2,3,0,1:T(8,128)S(1)} %get-tuple-element.137), channel_id=1, source_target_pairs={{0,8},{8,16},{16,24},{1,9},{9,17},{17,25},{2,10},{10,18},{18,26},{... | collective-permute-start | bytes 98312 | tf_op jit(solution)/shard_map/ppermute | solution.py:25
  209.3 10.3 %collective-permute-start.8 = (f32[4,2,8,128]{2,3,0,1:T(8,128)S(1)}, f32[4,2,8,128]{2,3,0,1:T(8,128)S(1)}, u32[]{:S(2)}, u32[]{:S(2)}) collective-permute-start(f32[4,2,8,128]{2,3,0,1:T(8,128)S(1)} %get-tuple-element.138), channel_id=1, source_target_pairs={{8,0},{16,8},{24,16},{9,1},{17,9},{25,17},{10,2},{18,10},{26,18},{... | collective-permute-start | bytes 98312 | tf_op jit(solution)/shard_map/ppermute | solution.py:28
  220.2 11.3 %collective-permute-start.9 = (f32[3,128]{1,0:T(4,128)S(1)}, f32[3,128]{1,0:T(4,128)S(1)}, u32[]{:S(2)}, u32[]{:S(2)}) collective-permute-start(f32[3,128]{1,0:T(4,128)S(1)} %add.1388), channel_id=1, source_target_pairs={{0,2},{1,3},{2,0},{3,1},{4,6},{5,7},{6,4},{7,5},{8,10},{9,11},{10,... | collective-permute-start | bytes 4616 | tf_op jit(solution)/shard_map/ppermute | solution.py:83
  223.7 7.8 collective-permute-start.10
  227.0 6.0 collective-permute-start.11
  235.2 4.5 collective-permute-start.12
  264.4 48.2 %all-to-all-start.3 = ((f32[8,9,64,128]{3,2,1,0:T(8,128)}), f32[8,9,64,128]{3,2,1,0:T(8,128)}, u32[]{:S(2)}, u32[]{:S(2)}) async-start(f32[8,9,64,128]{3,2,1,0:T(8,128)} %bitcast.364), calls=%async_computation.3 | async-start | bytes 4718592 | tf_op jit(solution)/shard_map/all_to_all | solution.py:181
  282.2 34.1 %copy-start.16 = (f32[2,8,64,128,1]{3,2,4,1,0:T(8,128)S(1)}, f32[2,8,64,128,1]{3,2,4,1,0:T(8,128)}, u32[]{:S(2)}) copy-start(f32[2,8,64,128,1]{3,2,4,1,0:T(8,128)} %copy-done.15) | copy-start | bytes 1572868
  319.1 6.3 collective-permute-start.13
  385.5 6.6 collective-permute-start.14
  395.0 10.5 %collective-permute-start.16 = (f32[4,2,8,128]{2,3,0,1:T(8,128)S(1)}, f32[4,2,8,128]{2,3,0,1:T(8,128)S(1)}, u32[]{:S(2)}, u32[]{:S(2)}) collective-permute-start(f32[4,2,8,128]{2,3,0,1:T(8,128)S(1)} %get-tuple-element.135), channel_id=1, source_target_pairs={{0,8},{8,16},{16,24},{1,9},{9,17},{17,25},{2,10},{10,18},{18,26},{... | collective-permute-start | bytes 98312 | tf_op jit(solution)/shard_map/ppermute | solution.py:25
  396.9 10.3 %collective-permute-start.17 = (f32[4,2,8,128]{2,3,0,1:T(8,128)S(1)}, f32[4,2,8,128]{2,3,0,1:T(8,128)S(1)}, u32[]{:S(2)}, u32[]{:S(2)}) collective-permute-start(f32[4,2,8,128]{2,3,0,1:T(8,128)S(1)} %get-tuple-element.136), channel_id=1, source_target_pairs={{8,0},{16,8},{24,16},{9,1},{17,9},{25,17},{10,2},{18,10},{26,18},{... | collective-permute-start | bytes 98312 | tf_op jit(solution)/shard_map/ppermute | solution.py:28
  400.5 3.7 collective-permute-start.15
  407.8 8.9 %collective-permute-start.18 = (f32[7,128]{1,0:T(8,128)S(1)}, f32[7,128]{1,0:T(8,128)S(1)}, u32[]{:S(2)}, u32[]{:S(2)}) collective-permute-start(f32[7,128]{1,0:T(8,128)S(1)} %add.1413), channel_id=1, source_target_pairs={{0,2},{1,3},{2,0},{3,1},{4,6},{5,7},{6,4},{7,5},{8,10},{9,11},{10,... | collective-permute-start | bytes 10760 | tf_op jit(solution)/shard_map/ppermute | solution.py:83
  408.8 7.9 collective-permute-start.19
  413.1 6.0 collective-permute-start.20
  421.9 4.5 collective-permute-start.21
  452.7 49.2 %all-to-all-start.5 = ((f32[8,9,64,128]{3,2,1,0:T(8,128)}), f32[8,9,64,128]{3,2,1,0:T(8,128)}, u32[]{:S(2)}, u32[]{:S(2)}) async-start(f32[8,9,64,128]{3,2,1,0:T(8,128)} %bitcast.362), calls=%async_computation.5 | async-start | bytes 4718592 | tf_op jit(solution)/shard_map/all_to_all | solution.py:181
  509.4 7.4 collective-permute-start.22
  576.9 7.1 collective-permute-start.23
  590.4 10.5 %collective-permute-start.25 = (f32[4,2,8,128]{2,3,0,1:T(8,128)S(1)}, f32[4,2,8,128]{2,3,0,1:T(8,128)S(1)}, u32[]{:S(2)}, u32[]{:S(2)}) collective-permute-start(f32[4,2,8,128]{2,3,0,1:T(8,128)S(1)} %get-tuple-element.133), channel_id=1, source_target_pairs={{0,8},{8,16},{16,24},{1,9},{9,17},{17,25},{2,10},{10,18},{18,26},{... | collective-permute-start | bytes 98312 | tf_op jit(solution)/shard_map/ppermute | solution.py:25
  592.3 10.3 %collective-permute-start.26 = (f32[4,2,8,128]{2,3,0,1:T(8,128)S(1)}, f32[4,2,8,128]{2,3,0,1:T(8,128)S(1)}, u32[]{:S(2)}, u32[]{:S(2)}) collective-permute-start(f32[4,2,8,128]{2,3,0,1:T(8,128)S(1)} %get-tuple-element.134), channel_id=1, source_target_pairs={{8,0},{16,8},{24,16},{9,1},{17,9},{25,17},{10,2},{18,10},{26,18},{... | collective-permute-start | bytes 98312 | tf_op jit(solution)/shard_map/ppermute | solution.py:28
  596.0 3.7 collective-permute-start.24
  603.2 8.8 %collective-permute-start.27 = (f32[7,128]{1,0:T(8,128)S(1)}, f32[7,128]{1,0:T(8,128)S(1)}, u32[]{:S(2)}, u32[]{:S(2)}) collective-permute-start(f32[7,128]{1,0:T(8,128)S(1)} %add.1430), channel_id=1, source_target_pairs={{0,2},{1,3},{2,0},{3,1},{4,6},{5,7},{6,4},{7,5},{8,10},{9,11},{10,... | collective-permute-start | bytes 10760 | tf_op jit(solution)/shard_map/ppermute | solution.py:83
  604.2 7.8 collective-permute-start.28
  608.5 6.0 collective-permute-start.29
  617.3 4.5 collective-permute-start.30
  650.5 48.8 %all-to-all-start.7 = ((f32[8,9,64,128]{3,2,1,0:T(8,128)}), f32[8,9,64,128]{3,2,1,0:T(8,128)}, u32[]{:S(2)}, u32[]{:S(2)}) async-start(f32[8,9,64,128]{3,2,1,0:T(8,128)} %bitcast.363), calls=%async_computation.7 | async-start | bytes 4718592 | tf_op jit(solution)/shard_map/all_to_all | solution.py:181
  706.4 7.3 collective-permute-start.31
  773.9 5.5 collective-permute-start.32
  782.3 10.5 %collective-permute-start.34 = (f32[4,2,8,128]{2,3,0,1:T(8,128)S(1)}, f32[4,2,8,128]{2,3,0,1:T(8,128)S(1)}, u32[]{:S(2)}, u32[]{:S(2)}) collective-permute-start(f32[4,2,8,128]{2,3,0,1:T(8,128)S(1)} %get-tuple-element.131), channel_id=1, source_target_pairs={{0,8},{8,16},{16,24},{1,9},{9,17},{17,25},{2,10},{10,18},{18,26},{... | collective-permute-start | bytes 98312 | tf_op jit(solution)/shard_map/ppermute | solution.py:25
  784.2 10.3 %collective-permute-start.35 = (f32[4,2,8,128]{2,3,0,1:T(8,128)S(1)}, f32[4,2,8,128]{2,3,0,1:T(8,128)S(1)}, u32[]{:S(2)}, u32[]{:S(2)}) collective-permute-start(f32[4,2,8,128]{2,3,0,1:T(8,128)S(1)} %get-tuple-element.132), channel_id=1, source_target_pairs={{8,0},{16,8},{24,16},{9,1},{17,9},{25,17},{10,2},{18,10},{26,18},{... | collective-permute-start | bytes 98312 | tf_op jit(solution)/shard_map/ppermute | solution.py:28
  787.9 3.7 collective-permute-start.33
  795.2 8.9 %collective-permute-start.36 = (f32[7,128]{1,0:T(8,128)S(1)}, f32[7,128]{1,0:T(8,128)S(1)}, u32[]{:S(2)}, u32[]{:S(2)}) collective-permute-start(f32[7,128]{1,0:T(8,128)S(1)} %add.1447), channel_id=1, source_target_pairs={{0,2},{1,3},{2,0},{3,1},{4,6},{5,7},{6,4},{7,5},{8,10},{9,11},{10,... | collective-permute-start | bytes 10760 | tf_op jit(solution)/shard_map/ppermute | solution.py:83
  796.1 7.9 collective-permute-start.37
  800.4 6.0 collective-permute-start.38
  808.0 4.6 collective-permute-start.39
  (45 other events, 278.3 us)

commit v14 on v13

--- a/solution.py
+++ b/solution.py
@@ -176,8 +176,9 @@
             synth_cols.reshape(-1, cols_blocks, block_cols),
             precision=highest,
         ).reshape(own_blocks, block_rows, block_cols)
-        blocks = jnp.concatenate([blocks, jnp.zeros((1, block_rows, block_cols), blocks.dtype)])
-        outgoing = jnp.take(blocks, gather_ids, axis=0, mode="clip")
+        outgoing = jnp.einsum(
+            "bk,bxc->kxc", landing, blocks, precision=lax.Precision.HIGHEST
+        ).reshape(owners, capacity, block_rows, block_cols)
         arrived = lax.all_to_all(outgoing, "gy", split_axis=0, concat_axis=0, tiled=True)
         seen = arrived[target, slot].reshape(
             sensors, rows_blocks * cols_blocks, layers, block_rows, block_cols
@@ -192,8 +193,11 @@
         carry, returning = advance(carry, returning)
         landed = lax.all_to_all(returning, "gy", split_axis=0, concat_axis=0, tiled=True)
         carry, landed = advance(carry, landed, step=False)
-        summed = jnp.dot(
-            landing, landed.reshape(owners * capacity, block_rows * block_cols), precision=highest
+        summed = jnp.einsum(
+            "bk,kxc->bxc",
+            landing,
+            landed.reshape(owners * capacity, block_rows, block_cols),
+            precision=highest,
         )
         carry, summed = advance(carry, summed)
         padded = extended(

time: 839 us -> 838 us (level)
  local copies, waits for them, and re-layouts: 135 us -> 120 us
  matrix products: 92.5 us -> 103 us
    gather x4 -> x0, local copies, waits for them, and re-layouts: 13.6 us -> none  [apply_op(): outgoing = jnp.take(blocks, gather_ids, axis=0, mode='clip')]
    dot_general x4 -> x8, matrix products: 11.1 us -> 22.9 us  [the longest x4 13.8 us: apply_op(): jnp.einsum('bk,bxc->kxc', landing, blocks, precision=lax.Precision.HIGHEST)]
    dot_general x0 -> x4, local copies, waits for them, and re-layouts: none -> 8.74 us  [apply_op(): jnp.einsum('bk,bxc->kxc', landing, blocks, precision=lax.Precision.HIGHEST)]
where the time goes in v14:
time: 838 us; the launch traced here: 824 us
  waiting for transfers between devices  210 us (25%)
  blocking collectives  180 us (21%)
  starting transfers between devices  122 us (15%)
  local copies, waits for them, and re-layouts  120 us (14%)
  matrix products  103 us (12%)
  other arithmetic  66.7 us (8%)
  between operations  21.7 us (3%)
    all_to_all x3, blocking collectives, apply_op(): lax.all_to_all(returning, 'gy', split_axis=0, concat_axis=0, tiled=True)  180 us
    all_to_all x4, waiting for transfers between devices, apply_op(): lax.all_to_all(outgoing, 'gy', split_axis=0, concat_axis=0, tiled=True)  114 us
    all_to_all x1, waiting for transfers between devices, apply_op(): lax.all_to_all(returning, 'gy', split_axis=0, concat_axis=0, tiled=True)  50.3 us
    dot_general x4, matrix products, apply_op(): jnp.einsum('lab,ac->lcb', along_cols, analysis_rows, precision=highest)  26.8 us
    reshape x13, local copies, waits for them, and re-layouts, lane_sum(): return jnp.sum(values.reshape(-1, 128), axis=0)  25.1 us
    ppermute x20, starting transfers between devices, sum_steps(): lax.ppermute(value, axis, pairs)  24.5 us
    ppermute x20, waiting for transfers between devices, sum_steps(): lax.ppermute(value, axis, pairs)  22.7 us
    ppermute x6, starting transfers between devices, extended(): lax.ppermute(lax.slice_in_dim(block, 0, width, axis=dim), axis, backward)  21.6 us
  transfers between devices with their start and end apart: 46, of which 25 were waited for; matrix products, arithmetic and copies ran while one was open for 16% of the time, Pallas kernels for 0%

profile of v14, /device:TPU:10, one launch (start us, length us, event | category | flops | bytes accessed | tf_op | source)
XLA Modules:
  0.0 823.7 jit_solution(15714872046959968589)
XLA Ops:
  3.4 6.3 all-to-all-start
  17.1 3.6 collective-permute-start.1
  39.4 4.7 collective-permute-done.2
  47.2 4.8 pad_maximum_fusion
  66.8 5.5 all-to-all-start.1
  83.0 36.9 %all-to-all-done.1 = f32[8,9,64,128]{3,2,1,0:T(8,128)} async-done(((f32[8,9,64,128]{3,2,1,0:T(8,128)}), f32[8,9,64,128]{3,2,1,0:T(8,128)}, u32[]{:S(2)}, u32[]{:S(2)}) %all-to-all-start.1) | async-done | bytes 2359328 | tf_op jit(solution)/shard_map/all_to_all | solution.py:182
  120.0 3.8 gather_fusion
  129.8 3.7 gather_fusion.1
  133.5 8.2 all-to-all-start.2
  143.1 50.3 %all-to-all-done.2 = f32[8,9,64,128]{3,2,1,0:T(8,128)} async-done(((f32[8,9,64,128]{3,2,1,0:T(8,128)}), f32[8,9,64,128]{3,2,1,0:T(8,128)}, u32[]{:S(2)}, u32[]{:S(2)}) %all-to-all-start.2) | async-done | bytes 2359328 | tf_op jit(solution)/shard_map/all_to_all | solution.py:194
  206.7 3.6 collective-permute-start.8
  210.6 4.6 collective-permute-done.7
  224.4 4.7 collective-permute-start.11
  233.4 3.7 collective-permute-done.12
  239.7 8.1 slice_multiply_fusion.3
  261.5 5.4 all-to-all-start.3
  266.9 4.4 multiply_multiply_fusion.7
  279.3 30.4 %all-to-all-done.3 = f32[8,9,64,128]{3,2,1,0:T(8,128)} async-done(((f32[8,9,64,128]{3,2,1,0:T(8,128)}), f32[8,9,64,128]{3,2,1,0:T(8,128)}, u32[]{:S(2)}, u32[]{:S(2)}) %all-to-all-start.3) | async-done | bytes 2359328 | tf_op jit(solution)/shard_map/all_to_all | solution.py:182
  309.7 3.8 gather_fusion.2
  318.8 3.7 gather_fusion.3
  322.5 60.1 %all_to_all.52 = f32[8,9,64,128]{3,2,1,0:T(8,128)S(1)} all-to-all(f32[8,9,64,128]{3,2,1,0:T(8,128)} %bitcast.372), channel_id=1, replica_groups=mesh['gx'=4,'gy'=8] {'gy'}, dimensions={0} | all-to-all | bytes 4718592 | tf_op jit(solution)/shard_map/all_to_all | solution.py:194
  382.6 4.7 collective-permute-start.14
  394.5 3.6 collective-permute-start.17
  410.7 3.6 collective-permute-start.20
  419.7 4.3 collective-permute-done.21
  430.6 6.0 fusion.11
  450.3 5.2 all-to-all-start.5
  462.7 4.5 multiply_multiply_fusion.5
  478.5 20.9 %all-to-all-done.5 = f32[8,9,64,128]{3,2,1,0:T(8,128)} async-done(((f32[8,9,64,128]{3,2,1,0:T(8,128)}), f32[8,9,64,128]{3,2,1,0:T(8,128)}, u32[]{:S(2)}, u32[]{:S(2)}) %all-to-all-start.5) | async-done | bytes 2359328 | tf_op jit(solution)/shard_map/all_to_all | solution.py:182
  499.4 3.8 gather_fusion.4
  503.2 3.8 multiply_reduce_fusion.1
  510.6 3.7 gather_fusion.5
  514.3 60.1 %all_to_all.53 = f32[8,9,64,128]{3,2,1,0:T(8,128)S(1)} all-to-all(f32[8,9,64,128]{3,2,1,0:T(8,128)} %bitcast.373), channel_id=1, replica_groups=mesh['gx'=4,'gy'=8] {'gy'}, dimensions={0} | all-to-all | bytes 4718592 | tf_op jit(solution)/shard_map/all_to_all | solution.py:194
  574.5 4.2 collective-permute-start.23
  588.1 3.6 collective-permute-start.26
  613.3 4.3 collective-permute-done.30
  624.1 8.6 %slice_multiply_fusion.1 = (f32[4,264,264]{2,1,0:T(8,128)S(1)}, f32[4,264,264]{2,1,0:T(8,128)}, f32[4,264,264]{2,1,0:T(8,128)}) fusion(f32[12,264,264]{2,1,0:T(8,128)} %copy-done.1, f32[4,264,264]{2,1,0:T(8,128)} %get-tuple-element.98, f32[]{:T(128)S(6)} %div.169, f32[4,264,264]{2,1,0:T(8,128)} %copy-done.7, f32[]{:T(128)S(6)} %div.168, ...), kind=kOutput, calls=%fused_computation.57 | convolution fusion | flops 458147712 | bytes 10082696 | tf_op jit(solution)/shard_map/lab,ac->lcb/dot_general | solution.py:224
  646.2 4.9 all-to-all-start.7
  651.1 5.6 multiply_multiply_fusion
  669.6 25.4 %all-to-all-done.7 = f32[8,9,64,128]{3,2,1,0:T(8,128)} async-done(((f32[8,9,64,128]{3,2,1,0:T(8,128)}), f32[8,9,64,128]{3,2,1,0:T(8,128)}, u32[]{:S(2)}, u32[]{:S(2)}) %all-to-all-start.7) | async-done | bytes 2359328 | tf_op jit(solution)/shard_map/all_to_all | solution.py:182
  695.0 3.7 gather_fusion.6
  705.7 3.7 gather_fusion.7
  709.4 60.1 %all_to_all.54 = f32[8,9,64,128]{3,2,1,0:T(8,128)S(1)} all-to-all(f32[8,9,64,128]{3,2,1,0:T(8,128)} %bitcast.371), channel_id=1, replica_groups=mesh['gx'=4,'gy'=8] {'gy'}, dimensions={0} | all-to-all | bytes 4718592 | tf_op jit(solution)/shard_map/all_to_all | solution.py:194
  769.6 4.2 collective-permute-start.32
  780.9 3.6 collective-permute-start.35
  797.1 3.6 collective-permute-start.38
  805.1 4.1 convolution_bitcast_fusion
  816.0 7.2 fusion.16
  (345 shorter events, 270.4 us)
Async XLA Ops:
  0.6 123.1 %copy-start = (f32[2,4,128,128]{3,2,1,0:T(8,128)S(1)}, f32[2,4,128,128]{3,2,1,0:T(8,128)}, u32[]{:S(2)}) copy-start(f32[2,4,128,128]{3,2,1,0:T(8,128)} %param.8) | copy-start | bytes 1572868
  3.4 23.2 %all-to-all-start = ((s32[8,1,9]{2,1,0:T(1,128)}), s32[8,1,9]{2,1,0:T(1,128)S(1)}, u32[]{:S(2)}, u32[]{:S(2)}) async-start(s32[8,1,9]{2,1,0:T(1,128)} %copy.128), calls=%async_computation | async-start | bytes 8192 | tf_op jit(solution)/shard_map/all_to_all | solution.py:156
  15.2 11.6 %collective-permute-start = (f32[12,4,256]{2,1,0:T(4,128)S(1)}, f32[12,4,256]{2,1,0:T(4,128)S(1)}, u32[]{:S(2)}, u32[]{:S(2)}) collective-permute-start(f32[12,4,256]{2,1,0:T(4,128)S(1)} %get-tuple-element.109), channel_id=1, source_target_pairs={{0,8},{8,16},{16,24},{1,9},{9,17},{17,25},{2,10},{10,18},{18,26},{... | collective-permute-start | bytes 147464 | tf_op jit(solution)/shard_map/ppermute | solution.py:25
  17.1 9.6 %collective-permute-start.1 = (f32[12,4,256]{2,1,0:T(4,128)S(1)}, f32[12,4,256]{2,1,0:T(4,128)S(1)}, u32[]{:S(2)}, u32[]{:S(2)}) collective-permute-start(f32[12,4,256]{2,1,0:T(4,128)S(1)} %get-tuple-element.110), channel_id=1, source_target_pairs={{8,0},{16,8},{24,16},{9,1},{17,9},{25,17},{10,2},{18,10},{26,18},{... | collective-permute-start | bytes 147464 | tf_op jit(solution)/shard_map/ppermute | solution.py:28
  33.4 12.1 %collective-permute-start.3 = (f32[12,264,4]{1,2,0:T(4,128)S(1)}, f32[12,264,4]{1,2,0:T(4,128)S(1)}, u32[]{:S(2)}, u32[]{:S(2)}) collective-permute-start(f32[12,264,4]{1,2,0:T(4,128)S(1)} %copy.123), channel_id=1, source_target_pairs={{1,0},{2,1},{3,2},{4,3},{5,4},{6,5},{7,6},{9,8},{10,9},{11,10},{12... | collective-permute-start | bytes 152072 | tf_op jit(solution)/shard_map/ppermute | solution.py:28
  36.8 7.3 collective-permute-start.2
  66.8 53.2 %all-to-all-start.1 = ((f32[8,9,64,128]{3,2,1,0:T(8,128)}), f32[8,9,64,128]{3,2,1,0:T(8,128)}, u32[]{:S(2)}, u32[]{:S(2)}) async-start(f32[8,9,64,128]{3,2,1,0:T(8,128)} %copy.138), calls=%async_computation.1 | async-start | bytes 4718592 | tf_op jit(solution)/shard_map/all_to_all | solution.py:182
  126.4 7.0 collective-permute-start.4
  133.5 59.9 %all-to-all-start.2 = ((f32[8,9,64,128]{3,2,1,0:T(8,128)}), f32[8,9,64,128]{3,2,1,0:T(8,128)}, u32[]{:S(2)}, u32[]{:S(2)}) async-start(f32[8,9,64,128]{3,2,1,0:T(8,128)} %bitcast.370), calls=%async_computation.2 | async-start | bytes 4718592 | tf_op jit(solution)/shard_map/all_to_all | solution.py:194
  193.4 5.2 collective-permute-start.5
  202.7 7.9 collective-permute-start.6
  204.7 10.5 %collective-permute-start.7 = (f32[4,2,8,128]{2,3,0,1:T(8,128)S(1)}, f32[4,2,8,128]{2,3,0,1:T(8,128)S(1)}, u32[]{:S(2)}, u32[]{:S(2)}) collective-permute-start(f32[4,2,8,128]{2,3,0,1:T(8,128)S(1)} %get-tuple-element.137), channel_id=1, source_target_pairs={{0,8},{8,16},{16,24},{1,9},{9,17},{17,25},{2,10},{10,18},{18,26},{... | collective-permute-start | bytes 98312 | tf_op jit(solution)/shard_map/ppermute | solution.py:25
  206.7 10.3 %collective-permute-start.8 = (f32[4,2,8,128]{2,3,0,1:T(8,128)S(1)}, f32[4,2,8,128]{2,3,0,1:T(8,128)S(1)}, u32[]{:S(2)}, u32[]{:S(2)}) collective-permute-start(f32[4,2,8,128]{2,3,0,1:T(8,128)S(1)} %get-tuple-element.138), channel_id=1, source_target_pairs={{8,0},{16,8},{24,16},{9,1},{17,9},{25,17},{10,2},{18,10},{26,18},{... | collective-permute-start | bytes 98312 | tf_op jit(solution)/shard_map/ppermute | solution.py:28
  217.6 11.5 %collective-permute-start.9 = (f32[3,128]{1,0:T(4,128)S(1)}, f32[3,128]{1,0:T(4,128)S(1)}, u32[]{:S(2)}, u32[]{:S(2)}) collective-permute-start(f32[3,128]{1,0:T(4,128)S(1)} %add.1344), channel_id=1, source_target_pairs={{0,2},{1,3},{2,0},{3,1},{4,6},{5,7},{6,4},{7,5},{8,10},{9,11},{10,... | collective-permute-start | bytes 4616 | tf_op jit(solution)/shard_map/ppermute | solution.py:83
  221.1 8.1 collective-permute-start.10
  224.4 6.0 collective-permute-start.11
  232.5 4.5 collective-permute-start.12
  261.5 48.2 %all-to-all-start.3 = ((f32[8,9,64,128]{3,2,1,0:T(8,128)}), f32[8,9,64,128]{3,2,1,0:T(8,128)}, u32[]{:S(2)}, u32[]{:S(2)}) async-start(f32[8,9,64,128]{3,2,1,0:T(8,128)} %copy.152), calls=%async_computation.3 | async-start | bytes 4718592 | tf_op jit(solution)/shard_map/all_to_all | solution.py:182
  279.3 34.2 %copy-start.16 = (f32[2,8,64,128,1]{3,2,4,1,0:T(8,128)S(1)}, f32[2,8,64,128,1]{3,2,4,1,0:T(8,128)}, u32[]{:S(2)}) copy-start(f32[2,8,64,128,1]{3,2,4,1,0:T(8,128)} %copy-done.15) | copy-start | bytes 1572868
  316.2 6.3 collective-permute-start.13
  382.6 6.6 collective-permute-start.14
  392.6 10.5 %collective-permute-start.16 = (f32[4,2,8,128]{2,3,0,1:T(8,128)S(1)}, f32[4,2,8,128]{2,3,0,1:T(8,128)S(1)}, u32[]{:S(2)}, u32[]{:S(2)}) collective-permute-start(f32[4,2,8,128]{2,3,0,1:T(8,128)S(1)} %get-tuple-element.135), channel_id=1, source_target_pairs={{0,8},{8,16},{16,24},{1,9},{9,17},{17,25},{2,10},{10,18},{18,26},{... | collective-permute-start | bytes 98312 | tf_op jit(solution)/shard_map/ppermute | solution.py:25
  394.5 10.3 %collective-permute-start.17 = (f32[4,2,8,128]{2,3,0,1:T(8,128)S(1)}, f32[4,2,8,128]{2,3,0,1:T(8,128)S(1)}, u32[]{:S(2)}, u32[]{:S(2)}) collective-permute-start(f32[4,2,8,128]{2,3,0,1:T(8,128)S(1)} %get-tuple-element.136), channel_id=1, source_target_pairs={{8,0},{16,8},{24,16},{9,1},{17,9},{25,17},{10,2},{18,10},{26,18},{... | collective-permute-start | bytes 98312 | tf_op jit(solution)/shard_map/ppermute | solution.py:28
  398.1 3.7 collective-permute-start.15
  405.4 8.8 %collective-permute-start.18 = (f32[7,128]{1,0:T(8,128)S(1)}, f32[7,128]{1,0:T(8,128)S(1)}, u32[]{:S(2)}, u32[]{:S(2)}) collective-permute-start(f32[7,128]{1,0:T(8,128)S(1)} %add.1369), channel_id=1, source_target_pairs={{0,2},{1,3},{2,0},{3,1},{4,6},{5,7},{6,4},{7,5},{8,10},{9,11},{10,... | collective-permute-start | bytes 10760 | tf_op jit(solution)/shard_map/ppermute | solution.py:83
  406.4 7.9 collective-permute-start.19
  410.7 6.0 collective-permute-start.20
  419.5 4.5 collective-permute-start.21
  450.3 49.1 %all-to-all-start.5 = ((f32[8,9,64,128]{3,2,1,0:T(8,128)}), f32[8,9,64,128]{3,2,1,0:T(8,128)}, u32[]{:S(2)}, u32[]{:S(2)}) async-start(f32[8,9,64,128]{3,2,1,0:T(8,128)} %copy.164), calls=%async_computation.5 | async-start | bytes 4718592 | tf_op jit(solution)/shard_map/all_to_all | solution.py:182
  507.0 7.4 collective-permute-start.22
  574.5 6.1 collective-permute-start.23
  586.2 10.5 %collective-permute-start.25 = (f32[4,2,8,128]{2,3,0,1:T(8,128)S(1)}, f32[4,2,8,128]{2,3,0,1:T(8,128)S(1)}, u32[]{:S(2)}, u32[]{:S(2)}) collective-permute-start(f32[4,2,8,128]{2,3,0,1:T(8,128)S(1)} %get-tuple-element.133), channel_id=1, source_target_pairs={{0,8},{8,16},{16,24},{1,9},{9,17},{17,25},{2,10},{10,18},{18,26},{... | collective-permute-start | bytes 98312 | tf_op jit(solution)/shard_map/ppermute | solution.py:25
  588.1 10.3 %collective-permute-start.26 = (f32[4,2,8,128]{2,3,0,1:T(8,128)S(1)}, f32[4,2,8,128]{2,3,0,1:T(8,128)S(1)}, u32[]{:S(2)}, u32[]{:S(2)}) collective-permute-start(f32[4,2,8,128]{2,3,0,1:T(8,128)S(1)} %get-tuple-element.134), channel_id=1, source_target_pairs={{8,0},{16,8},{24,16},{9,1},{17,9},{25,17},{10,2},{18,10},{26,18},{... | collective-permute-start | bytes 98312 | tf_op jit(solution)/shard_map/ppermute | solution.py:28
  591.8 3.7 collective-permute-start.24
  599.1 8.8 %collective-permute-start.27 = (f32[7,128]{1,0:T(8,128)S(1)}, f32[7,128]{1,0:T(8,128)S(1)}, u32[]{:S(2)}, u32[]{:S(2)}) collective-permute-start(f32[7,128]{1,0:T(8,128)S(1)} %add.1386), channel_id=1, source_target_pairs={{0,2},{1,3},{2,0},{3,1},{4,6},{5,7},{6,4},{7,5},{8,10},{9,11},{10,... | collective-permute-start | bytes 10760 | tf_op jit(solution)/shard_map/ppermute | solution.py:83
  600.1 7.8 collective-permute-start.28
  604.3 6.0 collective-permute-start.29
  613.1 4.5 collective-permute-start.30
  646.2 48.8 %all-to-all-start.7 = ((f32[8,9,64,128]{3,2,1,0:T(8,128)}), f32[8,9,64,128]{3,2,1,0:T(8,128)}, u32[]{:S(2)}, u32[]{:S(2)}) async-start(f32[8,9,64,128]{3,2,1,0:T(8,128)} %copy.176), calls=%async_computation.7 | async-start | bytes 4718592 | tf_op jit(solution)/shard_map/all_to_all | solution.py:182
  702.1 7.3 collective-permute-start.31
  769.6 6.1 collective-permute-start.32
  779.0 10.5 %collective-permute-start.34 = (f32[4,2,8,128]{2,3,0,1:T(8,128)S(1)}, f32[4,2,8,128]{2,3,0,1:T(8,128)S(1)}, u32[]{:S(2)}, u32[]{:S(2)}) collective-permute-start(f32[4,2,8,128]{2,3,0,1:T(8,128)S(1)} %get-tuple-element.131), channel_id=1, source_target_pairs={{0,8},{8,16},{16,24},{1,9},{9,17},{17,25},{2,10},{10,18},{18,26},{... | collective-permute-start | bytes 98312 | tf_op jit(solution)/shard_map/ppermute | solution.py:25
  780.9 10.3 %collective-permute-start.35 = (f32[4,2,8,128]{2,3,0,1:T(8,128)S(1)}, f32[4,2,8,128]{2,3,0,1:T(8,128)S(1)}, u32[]{:S(2)}, u32[]{:S(2)}) collective-permute-start(f32[4,2,8,128]{2,3,0,1:T(8,128)S(1)} %get-tuple-element.132), channel_id=1, source_target_pairs={{8,0},{16,8},{24,16},{9,1},{17,9},{25,17},{10,2},{18,10},{26,18},{... | collective-permute-start | bytes 98312 | tf_op jit(solution)/shard_map/ppermute | solution.py:28
  784.6 3.7 collective-permute-start.33
  791.9 8.9 %collective-permute-start.36 = (f32[7,128]{1,0:T(8,128)S(1)}, f32[7,128]{1,0:T(8,128)S(1)}, u32[]{:S(2)}, u32[]{:S(2)}) collective-permute-start(f32[7,128]{1,0:T(8,128)S(1)} %add.1403), channel_id=1, source_target_pairs={{0,2},{1,3},{2,0},{3,1},{4,6},{5,7},{6,4},{7,5},{8,10},{9,11},{10,... | collective-permute-start | bytes 10760 | tf_op jit(solution)/shard_map/ppermute | solution.py:83
  792.9 7.9 collective-permute-start.37
  797.1 6.0 collective-permute-start.38
  804.8 4.6 collective-permute-start.39
  (48 other events, 284.9 us)

commit v15 on v14

--- a/solution.py
+++ b/solution.py
@@ -1,4 +1,5 @@
 import jax
+import numpy as np
 import jax.numpy as jnp
 from jax import lax
 from jax.sharding import PartitionSpec as P
@@ -31,32 +32,32 @@
 
 
 def synth_table(length):
-    inputs = jnp.arange(length + 8, dtype=jnp.int32)[:, None]
-    outputs = jnp.arange(length, dtype=jnp.int32)[None, :]
+    inputs = np.arange(length + 8, dtype=np.int64)[:, None]
+    outputs = np.arange(length, dtype=np.int64)[None, :]
     half = outputs // 2
     phase = outputs % 2
-    table = jnp.zeros((length + 8, length), jnp.float32)
+    table = np.zeros((length + 8, length), np.float64)
     for tap_num in range(3):
-        low_coef = jnp.where(phase == 0, DAUB_LOW[2 * tap_num], DAUB_LOW[2 * tap_num + 1])
-        high_coef = jnp.where(phase == 0, DAUB_HIGH[2 * tap_num], DAUB_HIGH[2 * tap_num + 1])
-        table = table + jnp.where(inputs == 2 * (half - tap_num) + 4, low_coef, 0.0)
-        table = table + jnp.where(inputs == 2 * (half - tap_num) + 5, high_coef, 0.0)
-    return table
+        low_coef = np.where(phase == 0, DAUB_LOW[2 * tap_num], DAUB_LOW[2 * tap_num + 1])
+        high_coef = np.where(phase == 0, DAUB_HIGH[2 * tap_num], DAUB_HIGH[2 * tap_num + 1])
+        table = table + np.where(inputs == 2 * (half - tap_num) + 4, low_coef, 0.0)
+        table = table + np.where(inputs == 2 * (half - tap_num) + 5, high_coef, 0.0)
+    return table.astype(np.float32)
 
 
 def analysis_table(length):
-    inputs = jnp.arange(length + 8, dtype=jnp.int32)[:, None]
-    outputs = jnp.arange(length, dtype=jnp.int32)[None, :]
+    inputs = np.arange(length + 8, dtype=np.int64)[:, None]
+    outputs = np.arange(length, dtype=np.int64)[None, :]
     half = outputs // 2
     phase = outputs % 2
-    table = jnp.zeros((length + 8, length), jnp.float32)
+    table = np.zeros((length + 8, length), np.float64)
     for tap_num in range(3):
         for offset in (0, 1):
-            coef = jnp.where(
+            coef = np.where(
                 phase == 0, DAUB_LOW[2 * tap_num + offset], DAUB_HIGH[2 * tap_num + offset]
             )
-            table = table + jnp.where(inputs == 2 * (half + tap_num) + offset + 4, coef, 0.0)
-    return table
+            table = table + np.where(inputs == 2 * (half + tap_num) + offset + 4, coef, 0.0)
+    return table.astype(np.float32)
 
 
 def butterfly_sum(value, axis):

time: 838 us -> 816 us (0.974)
  waiting for transfers between devices: 210 us -> 179 us
  local copies, waits for them, and re-layouts: 120 us -> 149 us
  matrix products: 103 us -> 84.1 us
  blocking collectives: 180 us -> 192 us
  starting transfers between devices: 122 us -> 113 us
    all_to_all x4, waiting for transfers between devices: 114 us -> 80.8 us  [apply_op(): lax.all_to_all(outgoing, 'gy', split_axis=0, concat_axis=0, tiled=True)]
    mul x0 -> x13, local copies, waits for them, and re-layouts: none -> 29.3 us  [the longest x3 7.59 us: shards(): prior_inner * direction * direction]
    all_to_all x0 -> x1, blocking collectives: none -> 11 us  [shards(): lax.all_to_all(send_ids, 'gy', split_axis=0, concat_axis=0, tiled=True)]
    transpose x4 -> x0, local copies, waits for them, and re-layouts: 8.92 us -> none  [apply_op(): jnp.einsum('lab,bjc->ljac', along_rows, synth_cols.reshape(-1, cols_block...]
  transfers between devices with their start and end apart: 46 -> 45, of which waited for: 25 -> 27; matrix products, arithmetic and copies ran while one was open for 16% -> 19% of each run, Pallas kernels for 0% -> 0%
where the time goes in v15:
time: 816 us; the launch traced here: 802 us
  blocking collectives  192 us (24%)
  waiting for transfers between devices  179 us (22%)
  local copies, waits for them, and re-layouts  149 us (18%)
  starting transfers between devices  113 us (14%)
  matrix products  84.1 us (10%)
  other arithmetic  64.1 us (8%)
  between operations  21.6 us (3%)
    all_to_all x3, blocking collectives, apply_op(): lax.all_to_all(returning, 'gy', split_axis=0, concat_axis=0, tiled=True)  181 us
    all_to_all x4, waiting for transfers between devices, apply_op(): lax.all_to_all(outgoing, 'gy', split_axis=0, concat_axis=0, tiled=True)  80.8 us
    all_to_all x1, waiting for transfers between devices, apply_op(): lax.all_to_all(returning, 'gy', split_axis=0, concat_axis=0, tiled=True)  50.4 us
    reshape x13, local copies, waits for them, and re-layouts, lane_sum(): return jnp.sum(values.reshape(-1, 128), axis=0)  28.7 us
    ppermute x20, waiting for transfers between devices, sum_steps(): lax.ppermute(value, axis, pairs)  28 us
    ppermute x20, starting transfers between devices, sum_steps(): lax.ppermute(value, axis, pairs)  22.2 us
    dot_general x4, matrix products, apply_op(): jnp.einsum('lab,ac->lcb', along_cols, analysis_rows, precision=highest)  21.9 us
    all_to_all x4, starting transfers between devices, apply_op(): lax.all_to_all(outgoing, 'gy', split_axis=0, concat_axis=0, tiled=True)  21.2 us
  transfers between devices with their start and end apart: 45, of which 27 were waited for; matrix products, arithmetic and copies ran while one was open for 19% of the time, Pallas kernels for 0%

profile of v15, /device:TPU:10, one launch (start us, length us, event | category | flops | bytes accessed | tf_op | source)
XLA Modules:
  0.0 802.3 jit_solution(13039455381897226260)
XLA Ops:
  19.9 11.0 %all_to_all.52 = s32[8,1,9]{2,1,0:T(1,128)S(1)} all-to-all(s32[8,1,9]{2,1,0:T(1,128)S(1)} %copy.189), channel_id=1, replica_groups=mesh['gx'=4,'gy'=8] {'gy'}, dimensions={0} | all-to-all | bytes 576 | tf_op jit(solution)/shard_map/all_to_all | solution.py:157
  38.0 4.2 collective-permute-start.3
  44.2 5.4 pad_maximum_fusion
  58.8 5.9 all-to-all-start.1
  80.5 31.4 %all-to-all-done.1 = f32[8,9,64,128]{3,2,1,0:T(8,128)} async-done(((f32[8,9,64,128]{3,2,1,0:T(8,128)}), f32[8,9,64,128]{3,2,1,0:T(8,128)}, u32[]{:S(2)}, u32[]{:S(2)}) %all-to-all-start.1) | async-done | bytes 2359328 | tf_op jit(solution)/shard_map/all_to_all | solution.py:183
  112.0 3.8 gather_fusion
  121.8 3.7 gather_fusion.1
  125.5 8.0 %all-to-all-start.2 = ((f32[8,9,64,128]{3,2,1,0:T(8,128)}), f32[8,9,64,128]{3,2,1,0:T(8,128)}, u32[]{:S(2)}, u32[]{:S(2)}) async-start(f32[8,9,64,128]{3,2,1,0:T(8,128)} %bitcast.333), calls=%async_computation.2 | async-start | bytes 4718592 | tf_op jit(solution)/shard_map/all_to_all | solution.py:195
  134.8 50.4 %all-to-all-done.2 = f32[8,9,64,128]{3,2,1,0:T(8,128)} async-done(((f32[8,9,64,128]{3,2,1,0:T(8,128)}), f32[8,9,64,128]{3,2,1,0:T(8,128)}, u32[]{:S(2)}, u32[]{:S(2)}) %all-to-all-start.2) | async-done | bytes 2359328 | tf_op jit(solution)/shard_map/all_to_all | solution.py:195
  187.3 3.5 fusion.6
  198.3 3.6 collective-permute-start.8
  216.2 3.8 collective-permute-start.11
  224.3 4.5 collective-permute-done.12
  231.5 6.6 slice_multiply_fusion.3
  245.1 5.2 all-to-all-start.3
  250.4 4.4 multiply_multiply_fusion.7
  273.7 20.2 %all-to-all-done.3 = f32[8,9,64,128]{3,2,1,0:T(8,128)} async-done(((f32[8,9,64,128]{3,2,1,0:T(8,128)}), f32[8,9,64,128]{3,2,1,0:T(8,128)}, u32[]{:S(2)}, u32[]{:S(2)}) %all-to-all-start.3) | async-done | bytes 2359328 | tf_op jit(solution)/shard_map/all_to_all | solution.py:183
  293.9 3.8 gather_fusion.2
  304.9 3.7 gather_fusion.3
  308.6 60.4 %all_to_all.53 = f32[8,9,64,128]{3,2,1,0:T(8,128)S(1)} all-to-all(f32[8,9,64,128]{3,2,1,0:T(8,128)} %bitcast.335), channel_id=1, replica_groups=mesh['gx'=4,'gy'=8] {'gy'}, dimensions={0} | all-to-all | bytes 4718592 | tf_op jit(solution)/shard_map/all_to_all | solution.py:195
  369.0 3.7 collective-permute-start.14
  382.1 3.6 collective-permute-start.17
  398.3 3.6 collective-permute-start.20
  406.5 4.4 collective-permute-done.21
  417.5 4.9 fusion.11
  422.5 4.6 slice_multiply_fusion.2
  434.1 5.1 all-to-all-start.5
  448.9 4.5 multiply_multiply_fusion.5
  472.3 10.7 %all-to-all-done.5 = f32[8,9,64,128]{3,2,1,0:T(8,128)} async-done(((f32[8,9,64,128]{3,2,1,0:T(8,128)}), f32[8,9,64,128]{3,2,1,0:T(8,128)}, u32[]{:S(2)}, u32[]{:S(2)}) %all-to-all-start.5) | async-done | bytes 2359328 | tf_op jit(solution)/shard_map/all_to_all | solution.py:183
  483.0 3.8 gather_fusion.4
  486.8 3.8 multiply_reduce_fusion.1
  494.3 3.7 gather_fusion.5
  498.0 60.1 %all_to_all.54 = f32[8,9,64,128]{3,2,1,0:T(8,128)S(1)} all-to-all(f32[8,9,64,128]{3,2,1,0:T(8,128)} %bitcast.336), channel_id=1, replica_groups=mesh['gx'=4,'gy'=8] {'gy'}, dimensions={0} | all-to-all | bytes 4718592 | tf_op jit(solution)/shard_map/all_to_all | solution.py:195
  558.1 4.3 collective-permute-start.23
  571.9 3.6 collective-permute-start.26
  588.0 3.5 collective-permute-start.29
  596.2 4.4 collective-permute-done.30
  607.2 7.5 slice_multiply_fusion.1
  621.6 4.9 all-to-all-start.7
  626.5 5.7 multiply_multiply_fusion
  651.8 18.4 %all-to-all-done.7 = f32[8,9,64,128]{3,2,1,0:T(8,128)} async-done(((f32[8,9,64,128]{3,2,1,0:T(8,128)}), f32[8,9,64,128]{3,2,1,0:T(8,128)}, u32[]{:S(2)}, u32[]{:S(2)}) %all-to-all-start.7) | async-done | bytes 2359328 | tf_op jit(solution)/shard_map/all_to_all | solution.py:183
  670.3 3.7 gather_fusion.6
  681.0 3.7 gather_fusion.7
  684.7 60.1 %all_to_all.55 = f32[8,9,64,128]{3,2,1,0:T(8,128)S(1)} all-to-all(f32[8,9,64,128]{3,2,1,0:T(8,128)} %bitcast.334), channel_id=1, replica_groups=mesh['gx'=4,'gy'=8] {'gy'}, dimensions={0} | all-to-all | bytes 4718592 | tf_op jit(solution)/shard_map/all_to_all | solution.py:195
  744.8 4.3 collective-permute-start.32
  756.3 3.6 collective-permute-start.35
  772.5 3.6 collective-permute-start.38
  790.7 7.2 fusion.16
  (298 shorter events, 281.6 us)
Async XLA Ops:
  0.6 115.1 %copy-start = (f32[2,4,128,128]{3,2,1,0:T(8,128)S(1)}, f32[2,4,128,128]{3,2,1,0:T(8,128)}, u32[]{:S(2)}) copy-start(f32[2,4,128,128]{3,2,1,0:T(8,128)} %param.32) | copy-start | bytes 1572868
  3.8 40.4 %copy-start.4 = (f32[4,256,256]{1,2,0:T(8,128)}, f32[4,256,256]{1,2,0:T(8,128)S(1)}, u32[]{:S(2)}) copy-start(f32[4,256,256]{1,2,0:T(8,128)S(1)} %copy.185) | copy-start | bytes 3145732
  12.4 20.4 %collective-permute-start.1 = (f32[12,4,256]{2,1,0:T(4,128)S(1)}, f32[12,4,256]{2,1,0:T(4,128)S(1)}, u32[]{:S(2)}, u32[]{:S(2)}) collective-permute-start(f32[12,4,256]{2,1,0:T(4,128)S(1)} %copy.182), channel_id=1, source_target_pairs={{8,0},{16,8},{24,16},{9,1},{17,9},{25,17},{10,2},{18,10},{26,18},{... | collective-permute-start | bytes 147464 | tf_op jit(solution)/shard_map/ppermute | solution.py:29
  16.2 14.9 %collective-permute-start = (f32[12,4,256]{2,1,0:T(4,128)S(1)}, f32[12,4,256]{2,1,0:T(4,128)S(1)}, u32[]{:S(2)}, u32[]{:S(2)}) collective-permute-start(f32[12,4,256]{2,1,0:T(4,128)S(1)} %copy.181), channel_id=1, source_target_pairs={{0,8},{8,16},{16,24},{1,9},{9,17},{17,25},{2,10},{10,18},{18,26},{... | collective-permute-start | bytes 147464 | tf_op jit(solution)/shard_map/ppermute | solution.py:26
  35.5 7.1 collective-permute-start.2
  38.0 6.2 collective-permute-start.3
  58.8 53.2 %all-to-all-start.1 = ((f32[8,9,64,128]{3,2,1,0:T(8,128)}), f32[8,9,64,128]{3,2,1,0:T(8,128)}, u32[]{:S(2)}, u32[]{:S(2)}) async-start(f32[8,9,64,128]{3,2,1,0:T(8,128)} %copy.197), calls=%async_computation.1 | async-start | bytes 4718592 | tf_op jit(solution)/shard_map/all_to_all | solution.py:183
  118.4 7.1 collective-permute-start.4
  125.5 59.7 %all-to-all-start.2 = ((f32[8,9,64,128]{3,2,1,0:T(8,128)}), f32[8,9,64,128]{3,2,1,0:T(8,128)}, u32[]{:S(2)}, u32[]{:S(2)}) async-start(f32[8,9,64,128]{3,2,1,0:T(8,128)} %bitcast.333), calls=%async_computation.2 | async-start | bytes 4718592 | tf_op jit(solution)/shard_map/all_to_all | solution.py:195
  185.2 5.6 collective-permute-start.5
  196.4 10.5 %collective-permute-start.7 = (f32[4,2,8,128]{2,3,0,1:T(8,128)S(1)}, f32[4,2,8,128]{2,3,0,1:T(8,128)S(1)}, u32[]{:S(2)}, u32[]{:S(2)}) collective-permute-start(f32[4,2,8,128]{2,3,0,1:T(8,128)S(1)} %get-tuple-element.145), channel_id=1, source_target_pairs={{0,8},{8,16},{16,24},{1,9},{9,17},{17,25},{2,10},{10,18},{18,26},{... | collective-permute-start | bytes 98312 | tf_op jit(solution)/shard_map/ppermute | solution.py:26
  198.3 10.3 %collective-permute-start.8 = (f32[4,2,8,128]{2,3,0,1:T(8,128)S(1)}, f32[4,2,8,128]{2,3,0,1:T(8,128)S(1)}, u32[]{:S(2)}, u32[]{:S(2)}) collective-permute-start(f32[4,2,8,128]{2,3,0,1:T(8,128)S(1)} %get-tuple-element.146), channel_id=1, source_target_pairs={{8,0},{16,8},{24,16},{9,1},{17,9},{25,17},{10,2},{18,10},{26,18},{... | collective-permute-start | bytes 98312 | tf_op jit(solution)/shard_map/ppermute | solution.py:29
  202.0 3.7 collective-permute-start.6
  209.3 10.7 %collective-permute-start.9 = (f32[3,128]{1,0:T(4,128)S(1)}, f32[3,128]{1,0:T(4,128)S(1)}, u32[]{:S(2)}, u32[]{:S(2)}) collective-permute-start(f32[3,128]{1,0:T(4,128)S(1)} %add.375), channel_id=1, source_target_pairs={{0,2},{1,3},{2,0},{3,1},{4,6},{5,7},{6,4},{7,5},{8,10},{9,11},{10,... | collective-permute-start | bytes 4616 | tf_op jit(solution)/shard_map/ppermute | solution.py:84
  211.9 8.1 %collective-permute-start.10 = (f32[4,272,8]{1,2,0:T(8,128)S(1)}, f32[4,272,8]{1,2,0:T(8,128)S(1)}, u32[]{:S(2)}, u32[]{:S(2)}) collective-permute-start(f32[4,272,8]{1,2,0:T(8,128)S(1)} %get-tuple-element.137), channel_id=1, source_target_pairs={{0,1},{1,2},{2,3},{3,4},{4,5},{5,6},{6,7},{8,9},{9,10},{10,11},{11... | collective-permute-start | bytes 104456 | tf_op jit(solution)/shard_map/ppermute | solution.py:211
  216.2 6.0 collective-permute-start.11
  224.3 4.5 collective-permute-start.12
  245.1 48.8 %all-to-all-start.3 = ((f32[8,9,64,128]{3,2,1,0:T(8,128)}), f32[8,9,64,128]{3,2,1,0:T(8,128)}, u32[]{:S(2)}, u32[]{:S(2)}) async-start(f32[8,9,64,128]{3,2,1,0:T(8,128)} %copy.209), calls=%async_computation.3 | async-start | bytes 4718592 | tf_op jit(solution)/shard_map/all_to_all | solution.py:183
  301.2 7.4 collective-permute-start.13
  369.0 5.6 collective-permute-start.14
  380.2 10.5 %collective-permute-start.16 = (f32[4,2,8,128]{2,3,0,1:T(8,128)S(1)}, f32[4,2,8,128]{2,3,0,1:T(8,128)S(1)}, u32[]{:S(2)}, u32[]{:S(2)}) collective-permute-start(f32[4,2,8,128]{2,3,0,1:T(8,128)S(1)} %get-tuple-element.143), channel_id=1, source_target_pairs={{0,8},{8,16},{16,24},{1,9},{9,17},{17,25},{2,10},{10,18},{18,26},{... | collective-permute-start | bytes 98312 | tf_op jit(solution)/shard_map/ppermute | solution.py:26
  382.1 10.3 %collective-permute-start.17 = (f32[4,2,8,128]{2,3,0,1:T(8,128)S(1)}, f32[4,2,8,128]{2,3,0,1:T(8,128)S(1)}, u32[]{:S(2)}, u32[]{:S(2)}) collective-permute-start(f32[4,2,8,128]{2,3,0,1:T(8,128)S(1)} %get-tuple-element.144), channel_id=1, source_target_pairs={{8,0},{16,8},{24,16},{9,1},{17,9},{25,17},{10,2},{18,10},{26,18},{... | collective-permute-start | bytes 98312 | tf_op jit(solution)/shard_map/ppermute | solution.py:29
  385.8 3.7 collective-permute-start.15
  393.1 8.8 %collective-permute-start.18 = (f32[7,128]{1,0:T(8,128)S(1)}, f32[7,128]{1,0:T(8,128)S(1)}, u32[]{:S(2)}, u32[]{:S(2)}) collective-permute-start(f32[7,128]{1,0:T(8,128)S(1)} %add.385), channel_id=1, source_target_pairs={{0,2},{1,3},{2,0},{3,1},{4,6},{5,7},{6,4},{7,5},{8,10},{9,11},{10,... | collective-permute-start | bytes 10760 | tf_op jit(solution)/shard_map/ppermute | solution.py:84
  394.1 7.8 collective-permute-start.19
  398.3 6.0 collective-permute-start.20
  406.3 4.5 collective-permute-start.21
  434.1 48.9 %all-to-all-start.5 = ((f32[8,9,64,128]{3,2,1,0:T(8,128)}), f32[8,9,64,128]{3,2,1,0:T(8,128)}, u32[]{:S(2)}, u32[]{:S(2)}) async-start(f32[8,9,64,128]{3,2,1,0:T(8,128)} %copy.221), calls=%async_computation.5 | async-start | bytes 4718592 | tf_op jit(solution)/shard_map/all_to_all | solution.py:183
  490.6 7.4 collective-permute-start.22
  558.1 6.2 collective-permute-start.23
  569.9 10.5 %collective-permute-start.25 = (f32[4,2,8,128]{2,3,0,1:T(8,128)S(1)}, f32[4,2,8,128]{2,3,0,1:T(8,128)S(1)}, u32[]{:S(2)}, u32[]{:S(2)}) collective-permute-start(f32[4,2,8,128]{2,3,0,1:T(8,128)S(1)} %get-tuple-element.141), channel_id=1, source_target_pairs={{0,8},{8,16},{16,24},{1,9},{9,17},{17,25},{2,10},{10,18},{18,26},{... | collective-permute-start | bytes 98312 | tf_op jit(solution)/shard_map/ppermute | solution.py:26
  571.9 10.3 %collective-permute-start.26 = (f32[4,2,8,128]{2,3,0,1:T(8,128)S(1)}, f32[4,2,8,128]{2,3,0,1:T(8,128)S(1)}, u32[]{:S(2)}, u32[]{:S(2)}) collective-permute-start(f32[4,2,8,128]{2,3,0,1:T(8,128)S(1)} %get-tuple-element.142), channel_id=1, source_target_pairs={{8,0},{16,8},{24,16},{9,1},{17,9},{25,17},{10,2},{18,10},{26,18},{... | collective-permute-start | bytes 98312 | tf_op jit(solution)/shard_map/ppermute | solution.py:29
  575.5 3.7 collective-permute-start.24
  582.8 8.8 %collective-permute-start.27 = (f32[7,128]{1,0:T(8,128)S(1)}, f32[7,128]{1,0:T(8,128)S(1)}, u32[]{:S(2)}, u32[]{:S(2)}) collective-permute-start(f32[7,128]{1,0:T(8,128)S(1)} %add.402), channel_id=1, source_target_pairs={{0,2},{1,3},{2,0},{3,1},{4,6},{5,7},{6,4},{7,5},{8,10},{9,11},{10,... | collective-permute-start | bytes 10760 | tf_op jit(solution)/shard_map/ppermute | solution.py:84
  583.8 7.8 collective-permute-start.28
  588.0 6.0 collective-permute-start.29
  596.1 4.5 collective-permute-start.30
  621.6 48.7 %all-to-all-start.7 = ((f32[8,9,64,128]{3,2,1,0:T(8,128)}), f32[8,9,64,128]{3,2,1,0:T(8,128)}, u32[]{:S(2)}, u32[]{:S(2)}) async-start(f32[8,9,64,128]{3,2,1,0:T(8,128)} %copy.235), calls=%async_computation.7 | async-start | bytes 4718592 | tf_op jit(solution)/shard_map/all_to_all | solution.py:183
  651.8 22.1 %copy-start.28 = (f32[2,8,64,128]{3,2,1,0:T(8,128)S(1)}, f32[2,8,64,128]{3,2,1,0:T(8,128)}, u32[]{:S(2)}) copy-start(f32[2,8,64,128]{3,2,1,0:T(8,128)} %get-tuple-element.104) | copy-start | bytes 1572868
  677.4 7.3 collective-permute-start.31
  744.8 6.2 collective-permute-start.32
  754.4 10.5 %collective-permute-start.34 = (f32[4,2,8,128]{2,3,0,1:T(8,128)S(1)}, f32[4,2,8,128]{2,3,0,1:T(8,128)S(1)}, u32[]{:S(2)}, u32[]{:S(2)}) collective-permute-start(f32[4,2,8,128]{2,3,0,1:T(8,128)S(1)} %get-tuple-element.139), channel_id=1, source_target_pairs={{0,8},{8,16},{16,24},{1,9},{9,17},{17,25},{2,10},{10,18},{18,26},{... | collective-permute-start | bytes 98312 | tf_op jit(solution)/shard_map/ppermute | solution.py:26
  756.3 10.3 %collective-permute-start.35 = (f32[4,2,8,128]{2,3,0,1:T(8,128)S(1)}, f32[4,2,8,128]{2,3,0,1:T(8,128)S(1)}, u32[]{:S(2)}, u32[]{:S(2)}) collective-permute-start(f32[4,2,8,128]{2,3,0,1:T(8,128)S(1)} %get-tuple-element.140), channel_id=1, source_target_pairs={{8,0},{16,8},{24,16},{9,1},{17,9},{25,17},{10,2},{18,10},{26,18},{... | collective-permute-start | bytes 98312 | tf_op jit(solution)/shard_map/ppermute | solution.py:29
  760.0 3.7 collective-permute-start.33
  767.3 8.8 %collective-permute-start.36 = (f32[7,128]{1,0:T(8,128)S(1)}, f32[7,128]{1,0:T(8,128)S(1)}, u32[]{:S(2)}, u32[]{:S(2)}) collective-permute-start(f32[7,128]{1,0:T(8,128)S(1)} %add.419), channel_id=1, source_target_pairs={{0,2},{1,3},{2,0},{3,1},{4,6},{5,7},{6,4},{7,5},{8,10},{9,11},{10,... | collective-permute-start | bytes 10760 | tf_op jit(solution)/shard_map/ppermute | solution.py:84
  768.3 7.9 collective-permute-start.37
  772.5 6.0 collective-permute-start.38
  779.5 4.6 collective-permute-start.39
  (29 other events, 189.5 us)

commit v16 on v15

--- a/solution.py
+++ b/solution.py
@@ -166,6 +166,10 @@
         own_layer * (rows_blocks * cols_blocks) + own_col * rows_blocks + own_row,
         own_blocks,
     )
+    picking = (
+        (target * capacity + slot)[:, None]
+        == jnp.arange(owners * capacity, dtype=jnp.int32)[None, :]
+    ).astype(jnp.float32)
     landing = (
         gather_ids.reshape(-1)[None, :] == jnp.arange(own_blocks, dtype=jnp.int32)[:, None]
     ).astype(jnp.float32)
@@ -189,8 +193,9 @@
         back = jnp.einsum("skxz,slyz->sklxy", slopes, interaction, precision=highest).reshape(
             requests, block_rows, block_cols
         )
-        back = jnp.concatenate([back, jnp.zeros((1, block_rows, block_cols), back.dtype)])
-        returning = jnp.take(back, slot_source, axis=0, mode="clip")
+        returning = jnp.einsum(
+            "ek,exc->kxc", picking, back, precision=lax.Precision.HIGHEST
+        ).reshape(owners, capacity, block_rows, block_cols)
         carry, returning = advance(carry, returning)
         landed = lax.all_to_all(returning, "gy", split_axis=0, concat_axis=0, tiled=True)
         carry, landed = advance(carry, landed, step=False)

time: 816 us -> 811 us (level)
  local copies, waits for them, and re-layouts: 149 us -> 128 us
  matrix products: 84.1 us -> 101 us
    dot_general x0 -> x4, matrix products: none -> 17.3 us  [apply_op(): jnp.einsum('ek,exc->kxc', picking, back, precision=lax.Precision.HIGHEST)]
    gather x4 -> x0, local copies, waits for them, and re-layouts: 14.9 us -> none  [apply_op(): returning = jnp.take(back, slot_source, axis=0, mode='clip')]
  transfers between devices with their start and end apart: 45 -> 45, of which waited for: 27 -> 27; matrix products, arithmetic and copies ran while one was open for 19% -> 17% of each run, Pallas kernels for 0% -> 0%
where the time goes in v16:
time: 811 us; the launch traced here: 798 us
  blocking collectives  191 us (24%)
  waiting for transfers between devices  185 us (23%)
  local copies, waits for them, and re-layouts  128 us (16%)
  starting transfers between devices  112 us (14%)
  matrix products  101 us (12%)
  other arithmetic  60.5 us (7%)
  between operations  21 us (3%)
    all_to_all x3, blocking collectives, apply_op(): lax.all_to_all(returning, 'gy', split_axis=0, concat_axis=0, tiled=True)  180 us
    all_to_all x4, waiting for transfers between devices, apply_op(): lax.all_to_all(outgoing, 'gy', split_axis=0, concat_axis=0, tiled=True)  85.6 us
    all_to_all x1, waiting for transfers between devices, apply_op(): lax.all_to_all(returning, 'gy', split_axis=0, concat_axis=0, tiled=True)  51.1 us
    reshape x13, local copies, waits for them, and re-layouts, lane_sum(): return jnp.sum(values.reshape(-1, 128), axis=0)  27.9 us
    ppermute x20, waiting for transfers between devices, sum_steps(): lax.ppermute(value, axis, pairs)  27.9 us
    dot_general x4, matrix products, apply_op(): jnp.einsum('lab,ac->lcb', along_cols, analysis_rows, precision=highest)  22.1 us
    ppermute x20, starting transfers between devices, sum_steps(): lax.ppermute(value, axis, pairs)  21.5 us
    all_to_all x4, starting transfers between devices, apply_op(): lax.all_to_all(outgoing, 'gy', split_axis=0, concat_axis=0, tiled=True)  21.3 us
  transfers between devices with their start and end apart: 45, of which 27 were waited for; matrix products, arithmetic and copies ran while one was open for 17% of the time, Pallas kernels for 0%

profile of v16, /device:TPU:10, one launch (start us, length us, event | category | flops | bytes accessed | tf_op | source)
XLA Modules:
  0.0 798.1 jit_solution(1672956817494009321)
XLA Ops:
  19.8 11.1 %all_to_all.52 = s32[8,1,9]{2,1,0:T(1,128)S(1)} all-to-all(s32[8,1,9]{2,1,0:T(1,128)S(1)} %copy.205), channel_id=1, replica_groups=mesh['gx'=4,'gy'=8] {'gy'}, dimensions={0} | all-to-all | bytes 576 | tf_op jit(solution)/shard_map/all_to_all | solution.py:157
  37.8 4.2 collective-permute-start.3
  44.1 5.4 pad_maximum_fusion
  58.8 6.0 all-to-all-start.1
  80.4 31.6 %all-to-all-done.1 = f32[8,9,64,128]{3,2,1,0:T(8,128)} async-done(((f32[8,9,64,128]{3,2,1,0:T(8,128)}), f32[8,9,64,128]{3,2,1,0:T(8,128)}, u32[]{:S(2)}, u32[]{:S(2)}) %all-to-all-start.1) | async-done | bytes 2359328 | tf_op jit(solution)/shard_map/all_to_all | solution.py:187
  112.0 3.8 gather_fusion
  124.9 8.1 %all-to-all-start.2 = ((f32[8,9,64,128]{3,2,1,0:T(8,128)}), f32[8,9,64,128]{3,2,1,0:T(8,128)}, u32[]{:S(2)}, u32[]{:S(2)}) async-start(f32[8,9,64,128]{3,2,1,0:T(8,128)} %copy.217), calls=%async_computation.2 | async-start | bytes 4718592 | tf_op jit(solution)/shard_map/all_to_all | solution.py:200
  134.3 51.1 %all-to-all-done.2 = f32[8,9,64,128]{3,2,1,0:T(8,128)} async-done(((f32[8,9,64,128]{3,2,1,0:T(8,128)}), f32[8,9,64,128]{3,2,1,0:T(8,128)}, u32[]{:S(2)}, u32[]{:S(2)}) %all-to-all-start.2) | async-done | bytes 2359328 | tf_op jit(solution)/shard_map/all_to_all | solution.py:200
  187.5 3.5 fusion.6
  198.5 3.6 collective-permute-start.8
  212.1 3.8 collective-permute-start.10
  225.0 4.5 collective-permute-done.12
  232.1 6.8 slice_multiply_fusion.3
  245.8 5.2 all-to-all-start.3
  251.1 4.5 multiply_multiply_fusion.7
  270.0 24.6 %all-to-all-done.3 = f32[8,9,64,128]{3,2,1,0:T(8,128)} async-done(((f32[8,9,64,128]{3,2,1,0:T(8,128)}), f32[8,9,64,128]{3,2,1,0:T(8,128)}, u32[]{:S(2)}, u32[]{:S(2)}) %all-to-all-start.3) | async-done | bytes 2359328 | tf_op jit(solution)/shard_map/all_to_all | solution.py:187
  294.6 3.8 gather_fusion.1
  304.3 4.7 fusion.12
  309.8 60.2 %all_to_all.53 = f32[8,9,64,128]{3,2,1,0:T(8,128)S(1)} all-to-all(f32[8,9,64,128]{3,2,1,0:T(8,128)S(1)} %copy.231), channel_id=1, replica_groups=mesh['gx'=4,'gy'=8] {'gy'}, dimensions={0} | all-to-all | bytes 4718592 | tf_op jit(solution)/shard_map/all_to_all | solution.py:200
  370.0 3.5 collective-permute-start.14
  380.7 3.9 collective-permute-start.17
  384.8 3.4 collective-permute-done.15
  405.0 4.5 collective-permute-done.21
  415.8 4.9 fusion.23
  429.9 5.1 all-to-all-start.5
  435.0 3.4 multiply_multiply_fusion.1
  444.7 4.5 multiply_multiply_fusion.5
  468.1 11.0 %all-to-all-done.5 = f32[8,9,64,128]{3,2,1,0:T(8,128)} async-done(((f32[8,9,64,128]{3,2,1,0:T(8,128)}), f32[8,9,64,128]{3,2,1,0:T(8,128)}, u32[]{:S(2)}, u32[]{:S(2)}) %all-to-all-start.5) | async-done | bytes 2359328 | tf_op jit(solution)/shard_map/all_to_all | solution.py:187
  479.2 3.8 gather_fusion.2
  483.0 3.6 multiply_reduce_fusion.1
  489.8 4.7 fusion.10
  495.2 59.7 %all_to_all.54 = f32[8,9,64,128]{3,2,1,0:T(8,128)S(1)} all-to-all(f32[8,9,64,128]{3,2,1,0:T(8,128)S(1)} %copy.247), channel_id=1, replica_groups=mesh['gx'=4,'gy'=8] {'gy'}, dimensions={0} | all-to-all | bytes 4718592 | tf_op jit(solution)/shard_map/all_to_all | solution.py:200
  554.9 3.9 collective-permute-start.23
  568.3 3.6 collective-permute-start.26
  572.2 3.4 collective-permute-done.24
  592.9 4.3 collective-permute-done.30
  603.5 7.6 slice_multiply_fusion.1
  618.1 5.0 all-to-all-start.7
  623.1 5.7 multiply_multiply_fusion
  648.4 18.4 %all-to-all-done.7 = f32[8,9,64,128]{3,2,1,0:T(8,128)} async-done(((f32[8,9,64,128]{3,2,1,0:T(8,128)}), f32[8,9,64,128]{3,2,1,0:T(8,128)}, u32[]{:S(2)}, u32[]{:S(2)}) %all-to-all-start.7) | async-done | bytes 2359328 | tf_op jit(solution)/shard_map/all_to_all | solution.py:187
  666.8 3.7 gather_fusion.3
  675.6 4.7 fusion.8
  681.0 59.8 %all_to_all.55 = f32[8,9,64,128]{3,2,1,0:T(8,128)S(1)} all-to-all(f32[8,9,64,128]{3,2,1,0:T(8,128)S(1)} %copy.263), channel_id=1, replica_groups=mesh['gx'=4,'gy'=8] {'gy'}, dimensions={0} | all-to-all | bytes 4718592 | tf_op jit(solution)/shard_map/all_to_all | solution.py:200
  740.9 4.2 collective-permute-start.32
  752.2 3.6 collective-permute-start.35
  756.1 3.4 collective-permute-done.33
  764.1 3.4 collective-permute-start.37
  786.4 7.3 fusion.28
  (316 shorter events, 272.9 us)
Async XLA Ops:
  0.6 115.1 %copy-start = (f32[2,4,128,128]{3,2,1,0:T(8,128)S(1)}, f32[2,4,128,128]{3,2,1,0:T(8,128)}, u32[]{:S(2)}) copy-start(f32[2,4,128,128]{3,2,1,0:T(8,128)} %param.32) | copy-start | bytes 1572868
  3.8 40.3 %copy-start.6 = (f32[4,256,256]{1,2,0:T(8,128)}, f32[4,256,256]{1,2,0:T(8,128)S(1)}, u32[]{:S(2)}) copy-start(f32[4,256,256]{1,2,0:T(8,128)S(1)} %copy.201) | copy-start | bytes 3145732
  12.4 20.2 %collective-permute-start.1 = (f32[12,4,256]{2,1,0:T(4,128)S(1)}, f32[12,4,256]{2,1,0:T(4,128)S(1)}, u32[]{:S(2)}, u32[]{:S(2)}) collective-permute-start(f32[12,4,256]{2,1,0:T(4,128)S(1)} %copy.198), channel_id=1, source_target_pairs={{8,0},{16,8},{24,16},{9,1},{17,9},{25,17},{10,2},{18,10},{26,18},{... | collective-permute-start | bytes 147464 | tf_op jit(solution)/shard_map/ppermute | solution.py:29
  16.2 14.8 %collective-permute-start = (f32[12,4,256]{2,1,0:T(4,128)S(1)}, f32[12,4,256]{2,1,0:T(4,128)S(1)}, u32[]{:S(2)}, u32[]{:S(2)}) collective-permute-start(f32[12,4,256]{2,1,0:T(4,128)S(1)} %copy.197), channel_id=1, source_target_pairs={{0,8},{8,16},{16,24},{1,9},{9,17},{17,25},{2,10},{10,18},{18,26},{... | collective-permute-start | bytes 147464 | tf_op jit(solution)/shard_map/ppermute | solution.py:26
  35.3 7.1 collective-permute-start.2
  37.8 6.2 collective-permute-start.3
  51.7 199.4 %copy-start.2 = (f32[4,264,264]{1,2,0:T(8,128)}, f32[4,264,264]{1,2,0:T(8,128)S(1)}, u32[]{:S(2)}) copy-start(f32[4,264,264]{1,2,0:T(8,128)S(1)} %slice_multiply_fusion) | copy-start | bytes 3345412
  58.8 53.2 %all-to-all-start.1 = ((f32[8,9,64,128]{3,2,1,0:T(8,128)}), f32[8,9,64,128]{3,2,1,0:T(8,128)}, u32[]{:S(2)}, u32[]{:S(2)}) async-start(f32[8,9,64,128]{3,2,1,0:T(8,128)} %copy.213), calls=%async_computation.1 | async-start | bytes 4718592 | tf_op jit(solution)/shard_map/all_to_all | solution.py:187
  118.4 4.3 collective-permute-start.4
  124.9 60.4 %all-to-all-start.2 = ((f32[8,9,64,128]{3,2,1,0:T(8,128)}), f32[8,9,64,128]{3,2,1,0:T(8,128)}, u32[]{:S(2)}, u32[]{:S(2)}) async-start(f32[8,9,64,128]{3,2,1,0:T(8,128)} %copy.217), calls=%async_computation.2 | async-start | bytes 4718592 | tf_op jit(solution)/shard_map/all_to_all | solution.py:200
  185.4 5.6 collective-permute-start.5
  196.6 10.5 %collective-permute-start.7 = (f32[4,2,8,128]{2,3,0,1:T(8,128)S(1)}, f32[4,2,8,128]{2,3,0,1:T(8,128)S(1)}, u32[]{:S(2)}, u32[]{:S(2)}) collective-permute-start(f32[4,2,8,128]{2,3,0,1:T(8,128)S(1)} %get-tuple-element.143), channel_id=1, source_target_pairs={{0,8},{8,16},{16,24},{1,9},{9,17},{17,25},{2,10},{10,18},{18,26},{... | collective-permute-start | bytes 98312 | tf_op jit(solution)/shard_map/ppermute | solution.py:26
  198.5 10.3 %collective-permute-start.8 = (f32[4,2,8,128]{2,3,0,1:T(8,128)S(1)}, f32[4,2,8,128]{2,3,0,1:T(8,128)S(1)}, u32[]{:S(2)}, u32[]{:S(2)}) collective-permute-start(f32[4,2,8,128]{2,3,0,1:T(8,128)S(1)} %get-tuple-element.144), channel_id=1, source_target_pairs={{8,0},{16,8},{24,16},{9,1},{17,9},{25,17},{10,2},{18,10},{26,18},{... | collective-permute-start | bytes 98312 | tf_op jit(solution)/shard_map/ppermute | solution.py:29
  202.1 3.7 collective-permute-start.6
  209.4 10.7 %collective-permute-start.9 = (f32[3,128]{1,0:T(4,128)S(1)}, f32[3,128]{1,0:T(4,128)S(1)}, u32[]{:S(2)}, u32[]{:S(2)}) collective-permute-start(f32[3,128]{1,0:T(4,128)S(1)} %add.385), channel_id=1, source_target_pairs={{0,2},{1,3},{2,0},{3,1},{4,6},{5,7},{6,4},{7,5},{8,10},{9,11},{10,... | collective-permute-start | bytes 4616 | tf_op jit(solution)/shard_map/ppermute | solution.py:84
  212.1 8.1 %collective-permute-start.10 = (f32[4,272,8]{1,2,0:T(8,128)S(1)}, f32[4,272,8]{1,2,0:T(8,128)S(1)}, u32[]{:S(2)}, u32[]{:S(2)}) collective-permute-start(f32[4,272,8]{1,2,0:T(8,128)S(1)} %get-tuple-element.135), channel_id=1, source_target_pairs={{0,1},{1,2},{2,3},{3,4},{4,5},{5,6},{6,7},{8,9},{9,10},{10,11},{11... | collective-permute-start | bytes 104456 | tf_op jit(solution)/shard_map/ppermute | solution.py:216
  216.7 6.0 collective-permute-start.11
  225.0 4.5 collective-permute-start.12
  245.8 48.8 %all-to-all-start.3 = ((f32[8,9,64,128]{3,2,1,0:T(8,128)}), f32[8,9,64,128]{3,2,1,0:T(8,128)}, u32[]{:S(2)}, u32[]{:S(2)}) async-start(f32[8,9,64,128]{3,2,1,0:T(8,128)} %copy.226), calls=%async_computation.3 | async-start | bytes 4718592 | tf_op jit(solution)/shard_map/all_to_all | solution.py:187
  304.2 4.8 collective-permute-start.13
  370.0 5.4 collective-permute-start.14
  378.7 10.5 %collective-permute-start.16 = (f32[4,2,8,128]{2,3,0,1:T(8,128)S(1)}, f32[4,2,8,128]{2,3,0,1:T(8,128)S(1)}, u32[]{:S(2)}, u32[]{:S(2)}) collective-permute-start(f32[4,2,8,128]{2,3,0,1:T(8,128)S(1)} %get-tuple-element.141), channel_id=1, source_target_pairs={{0,8},{8,16},{16,24},{1,9},{9,17},{17,25},{2,10},{10,18},{18,26},{... | collective-permute-start | bytes 98312 | tf_op jit(solution)/shard_map/ppermute | solution.py:26
  380.7 10.3 %collective-permute-start.17 = (f32[4,2,8,128]{2,3,0,1:T(8,128)S(1)}, f32[4,2,8,128]{2,3,0,1:T(8,128)S(1)}, u32[]{:S(2)}, u32[]{:S(2)}) collective-permute-start(f32[4,2,8,128]{2,3,0,1:T(8,128)S(1)} %get-tuple-element.142), channel_id=1, source_target_pairs={{8,0},{16,8},{24,16},{9,1},{17,9},{25,17},{10,2},{18,10},{26,18},{... | collective-permute-start | bytes 98312 | tf_op jit(solution)/shard_map/ppermute | solution.py:29
  384.5 3.7 collective-permute-start.15
  391.6 8.6 %collective-permute-start.18 = (f32[7,128]{1,0:T(8,128)S(1)}, f32[7,128]{1,0:T(8,128)S(1)}, u32[]{:S(2)}, u32[]{:S(2)}) collective-permute-start(f32[7,128]{1,0:T(8,128)S(1)} %add.395), channel_id=1, source_target_pairs={{0,2},{1,3},{2,0},{3,1},{4,6},{5,7},{6,4},{7,5},{8,10},{9,11},{10,... | collective-permute-start | bytes 10760 | tf_op jit(solution)/shard_map/ppermute | solution.py:84
  392.6 7.6 collective-permute-start.19
  396.8 6.0 collective-permute-start.20
  405.0 4.5 collective-permute-start.21
  429.9 49.3 %all-to-all-start.5 = ((f32[8,9,64,128]{3,2,1,0:T(8,128)}), f32[8,9,64,128]{3,2,1,0:T(8,128)}, u32[]{:S(2)}, u32[]{:S(2)}) async-start(f32[8,9,64,128]{3,2,1,0:T(8,128)} %copy.240), calls=%async_computation.5 | async-start | bytes 4718592 | tf_op jit(solution)/shard_map/all_to_all | solution.py:187
  489.7 4.8 collective-permute-start.22
  554.9 5.8 collective-permute-start.23
  566.3 10.5 %collective-permute-start.25 = (f32[4,2,8,128]{2,3,0,1:T(8,128)S(1)}, f32[4,2,8,128]{2,3,0,1:T(8,128)S(1)}, u32[]{:S(2)}, u32[]{:S(2)}) collective-permute-start(f32[4,2,8,128]{2,3,0,1:T(8,128)S(1)} %get-tuple-element.139), channel_id=1, source_target_pairs={{0,8},{8,16},{16,24},{1,9},{9,17},{17,25},{2,10},{10,18},{18,26},{... | collective-permute-start | bytes 98312 | tf_op jit(solution)/shard_map/ppermute | solution.py:26
  568.3 10.3 %collective-permute-start.26 = (f32[4,2,8,128]{2,3,0,1:T(8,128)S(1)}, f32[4,2,8,128]{2,3,0,1:T(8,128)S(1)}, u32[]{:S(2)}, u32[]{:S(2)}) collective-permute-start(f32[4,2,8,128]{2,3,0,1:T(8,128)S(1)} %get-tuple-element.140), channel_id=1, source_target_pairs={{8,0},{16,8},{24,16},{9,1},{17,9},{25,17},{10,2},{18,10},{26,18},{... | collective-permute-start | bytes 98312 | tf_op jit(solution)/shard_map/ppermute | solution.py:29
  571.9 3.7 collective-permute-start.24
  579.2 8.6 %collective-permute-start.27 = (f32[7,128]{1,0:T(8,128)S(1)}, f32[7,128]{1,0:T(8,128)S(1)}, u32[]{:S(2)}, u32[]{:S(2)}) collective-permute-start(f32[7,128]{1,0:T(8,128)S(1)} %add.412), channel_id=1, source_target_pairs={{0,2},{1,3},{2,0},{3,1},{4,6},{5,7},{6,4},{7,5},{8,10},{9,11},{10,... | collective-permute-start | bytes 10760 | tf_op jit(solution)/shard_map/ppermute | solution.py:84
  580.2 7.6 collective-permute-start.28
  584.4 6.0 collective-permute-start.29
  592.6 4.5 collective-permute-start.30
  618.1 48.7 %all-to-all-start.7 = ((f32[8,9,64,128]{3,2,1,0:T(8,128)}), f32[8,9,64,128]{3,2,1,0:T(8,128)}, u32[]{:S(2)}, u32[]{:S(2)}) async-start(f32[8,9,64,128]{3,2,1,0:T(8,128)} %copy.256), calls=%async_computation.7 | async-start | bytes 4718592 | tf_op jit(solution)/shard_map/all_to_all | solution.py:187
  675.5 4.8 collective-permute-start.31
  740.9 6.1 collective-permute-start.32
  750.3 10.5 %collective-permute-start.34 = (f32[4,2,8,128]{2,3,0,1:T(8,128)S(1)}, f32[4,2,8,128]{2,3,0,1:T(8,128)S(1)}, u32[]{:S(2)}, u32[]{:S(2)}) collective-permute-start(f32[4,2,8,128]{2,3,0,1:T(8,128)S(1)} %get-tuple-element.137), channel_id=1, source_target_pairs={{0,8},{8,16},{16,24},{1,9},{9,17},{17,25},{2,10},{10,18},{18,26},{... | collective-permute-start | bytes 98312 | tf_op jit(solution)/shard_map/ppermute | solution.py:26
  752.2 10.3 %collective-permute-start.35 = (f32[4,2,8,128]{2,3,0,1:T(8,128)S(1)}, f32[4,2,8,128]{2,3,0,1:T(8,128)S(1)}, u32[]{:S(2)}, u32[]{:S(2)}) collective-permute-start(f32[4,2,8,128]{2,3,0,1:T(8,128)S(1)} %get-tuple-element.138), channel_id=1, source_target_pairs={{8,0},{16,8},{24,16},{9,1},{17,9},{25,17},{10,2},{18,10},{26,18},{... | collective-permute-start | bytes 98312 | tf_op jit(solution)/shard_map/ppermute | solution.py:29
  755.9 3.7 collective-permute-start.33
  763.2 8.6 %collective-permute-start.36 = (f32[7,128]{1,0:T(8,128)S(1)}, f32[7,128]{1,0:T(8,128)S(1)}, u32[]{:S(2)}, u32[]{:S(2)}) collective-permute-start(f32[7,128]{1,0:T(8,128)S(1)} %add.429), channel_id=1, source_target_pairs={{0,2},{1,3},{2,0},{3,1},{4,6},{5,7},{6,4},{7,5},{8,10},{9,11},{10,... | collective-permute-start | bytes 10760 | tf_op jit(solution)/shard_map/ppermute | solution.py:84
  764.1 7.6 collective-permute-start.37
  768.4 6.0 collective-permute-start.38
  775.4 4.6 collective-permute-start.39
  (38 other events, 274.1 us)

commit v17 on v16

--- a/solution.py
+++ b/solution.py
@@ -185,9 +185,12 @@
             "bk,bxc->kxc", landing, blocks, precision=lax.Precision.HIGHEST
         ).reshape(owners, capacity, block_rows, block_cols)
         arrived = lax.all_to_all(outgoing, "gy", split_axis=0, concat_axis=0, tiled=True)
-        seen = arrived[target, slot].reshape(
-            sensors, rows_blocks * cols_blocks, layers, block_rows, block_cols
-        )
+        seen = jnp.einsum(
+            "ek,kxc->exc",
+            picking,
+            arrived.reshape(owners * capacity, block_rows, block_cols),
+            precision=lax.Precision.HIGHEST,
+        ).reshape(sensors, rows_blocks * cols_blocks, layers, block_rows, block_cols)
         slopes = jnp.einsum("sklxy,slyz->skxz", seen, interaction, precision=highest)
         carry = (partials(slopes), sum_steps(("gx", "gy")))
         back = jnp.einsum("skxz,slyz->sklxy", slopes, interaction, precision=highest).reshape(

time: 811 us -> 806 us (level)
  local copies, waits for them, and re-layouts: 128 us -> 113 us
  matrix products: 101 us -> 111 us
    dot_general x0 -> x4, matrix products: none -> 17.3 us  [apply_op(): jnp.einsum('ek,kxc->exc', picking, arrived.reshape(owners * capacity, blo...]
    gather x4 -> x0, local copies, waits for them, and re-layouts: 15 us -> none  [apply_op(): arrived[target, slot]]
where the time goes in v17:
time: 806 us; the launch traced here: 794 us
  blocking collectives  191 us (24%)
  waiting for transfers between devices  185 us (23%)
  local copies, waits for them, and re-layouts  113 us (14%)
  starting transfers between devices  112 us (14%)
  matrix products  111 us (14%)
  other arithmetic  60.3 us (7%)
  between operations  21.2 us (3%)
    all_to_all x3, blocking collectives, apply_op(): lax.all_to_all(returning, 'gy', split_axis=0, concat_axis=0, tiled=True)  180 us
    all_to_all x4, waiting for transfers between devices, apply_op(): lax.all_to_all(outgoing, 'gy', split_axis=0, concat_axis=0, tiled=True)  85.3 us
    all_to_all x1, waiting for transfers between devices, apply_op(): lax.all_to_all(returning, 'gy', split_axis=0, concat_axis=0, tiled=True)  51 us
    reshape x13, local copies, waits for them, and re-layouts, lane_sum(): return jnp.sum(values.reshape(-1, 128), axis=0)  28 us
    ppermute x20, waiting for transfers between devices, sum_steps(): lax.ppermute(value, axis, pairs)  27.9 us
    all_to_all x4, starting transfers between devices, apply_op(): lax.all_to_all(outgoing, 'gy', split_axis=0, concat_axis=0, tiled=True)  22 us
    dot_general x4, matrix products, apply_op(): jnp.einsum('lab,ac->lcb', along_cols, analysis_rows, precision=highest)  21.8 us
    ppermute x20, starting transfers between devices, sum_steps(): lax.ppermute(value, axis, pairs)  21.6 us
  transfers between devices with their start and end apart: 45, of which 27 were waited for; matrix products, arithmetic and copies ran while one was open for 17% of the time, Pallas kernels for 0%

profile of v17, /device:TPU:10, one launch (start us, length us, event | category | flops | bytes accessed | tf_op | source)
XLA Modules:
  0.0 793.8 jit_solution(780989957309884387)
XLA Ops:
  19.8 11.1 %all_to_all.52 = s32[8,1,9]{2,1,0:T(1,128)S(1)} all-to-all(s32[8,1,9]{2,1,0:T(1,128)S(1)} %copy.212), channel_id=1, replica_groups=mesh['gx'=4,'gy'=8] {'gy'}, dimensions={0} | all-to-all | bytes 576 | tf_op jit(solution)/shard_map/all_to_all | solution.py:157
  37.8 4.2 collective-permute-start.3
  44.1 5.4 pad_maximum_fusion
  58.7 6.2 all-to-all-start.1
  80.7 31.5 %all-to-all-done.1 = f32[8,9,64,128]{3,2,1,0:T(8,128)} async-done(((f32[8,9,64,128]{3,2,1,0:T(8,128)}), f32[8,9,64,128]{3,2,1,0:T(8,128)}, u32[]{:S(2)}, u32[]{:S(2)}) %all-to-all-start.1) | async-done | bytes 2359328 | tf_op jit(solution)/shard_map/all_to_all | solution.py:187
  112.2 4.3 fusion.6
  124.1 8.3 %all-to-all-start.2 = ((f32[8,9,64,128]{3,2,1,0:T(8,128)}), f32[8,9,64,128]{3,2,1,0:T(8,128)}, u32[]{:S(2)}, u32[]{:S(2)}) async-start(f32[8,9,64,128]{3,2,1,0:T(8,128)} %copy.227), calls=%async_computation.2 | async-start | bytes 4718592 | tf_op jit(solution)/shard_map/all_to_all | solution.py:203
  133.7 51.0 %all-to-all-done.2 = f32[8,9,64,128]{3,2,1,0:T(8,128)} async-done(((f32[8,9,64,128]{3,2,1,0:T(8,128)}), f32[8,9,64,128]{3,2,1,0:T(8,128)}, u32[]{:S(2)}, u32[]{:S(2)}) %all-to-all-start.2) | async-done | bytes 2359328 | tf_op jit(solution)/shard_map/all_to_all | solution.py:203
  186.7 3.5 fusion.14
  197.8 3.6 collective-permute-start.8
  211.4 3.4 collective-permute-start.10
  223.8 4.5 collective-permute-done.12
  230.8 6.6 slice_multiply_fusion.3
  244.4 5.4 all-to-all-start.3
  249.8 4.5 multiply_multiply_fusion.7
  268.7 24.7 %all-to-all-done.3 = f32[8,9,64,128]{3,2,1,0:T(8,128)} async-done(((f32[8,9,64,128]{3,2,1,0:T(8,128)}), f32[8,9,64,128]{3,2,1,0:T(8,128)}, u32[]{:S(2)}, u32[]{:S(2)}) %all-to-all-start.3) | async-done | bytes 2359328 | tf_op jit(solution)/shard_map/all_to_all | solution.py:187
  293.4 4.3 fusion.4
  302.1 4.7 fusion.20
  307.5 60.4 %all_to_all.53 = f32[8,9,64,128]{3,2,1,0:T(8,128)S(1)} all-to-all(f32[8,9,64,128]{3,2,1,0:T(8,128)S(1)} %copy.244), channel_id=1, replica_groups=mesh['gx'=4,'gy'=8] {'gy'}, dimensions={0} | all-to-all | bytes 4718592 | tf_op jit(solution)/shard_map/all_to_all | solution.py:203
  367.9 3.5 collective-permute-start.14
  378.6 3.6 collective-permute-start.17
  382.6 3.4 collective-permute-done.15
  390.6 3.4 collective-permute-start.19
  403.0 4.5 collective-permute-done.21
  414.0 4.9 fusion.31
  428.0 5.1 all-to-all-start.5
  442.8 4.5 multiply_multiply_fusion.5
  466.3 10.8 %all-to-all-done.5 = f32[8,9,64,128]{3,2,1,0:T(8,128)} async-done(((f32[8,9,64,128]{3,2,1,0:T(8,128)}), f32[8,9,64,128]{3,2,1,0:T(8,128)}, u32[]{:S(2)}, u32[]{:S(2)}) %all-to-all-start.5) | async-done | bytes 2359328 | tf_op jit(solution)/shard_map/all_to_all | solution.py:187
  477.1 4.4 fusion.2
  486.5 4.7 fusion.18
  492.0 59.7 %all_to_all.54 = f32[8,9,64,128]{3,2,1,0:T(8,128)S(1)} all-to-all(f32[8,9,64,128]{3,2,1,0:T(8,128)S(1)} %copy.263), channel_id=1, replica_groups=mesh['gx'=4,'gy'=8] {'gy'}, dimensions={0} | all-to-all | bytes 4718592 | tf_op jit(solution)/shard_map/all_to_all | solution.py:203
  551.7 3.9 collective-permute-start.23
  565.1 3.6 collective-permute-start.26
  569.0 3.4 collective-permute-done.24
  577.0 3.4 collective-permute-start.28
  589.6 4.3 collective-permute-done.30
  600.4 7.5 slice_multiply_fusion.1
  614.8 5.2 all-to-all-start.7
  620.0 5.7 multiply_multiply_fusion
  645.4 18.3 %all-to-all-done.7 = f32[8,9,64,128]{3,2,1,0:T(8,128)} async-done(((f32[8,9,64,128]{3,2,1,0:T(8,128)}), f32[8,9,64,128]{3,2,1,0:T(8,128)}, u32[]{:S(2)}, u32[]{:S(2)}) %all-to-all-start.7) | async-done | bytes 2359328 | tf_op jit(solution)/shard_map/all_to_all | solution.py:187
  663.7 4.4 fusion
  671.6 4.7 fusion.16
  677.1 59.7 %all_to_all.55 = f32[8,9,64,128]{3,2,1,0:T(8,128)S(1)} all-to-all(f32[8,9,64,128]{3,2,1,0:T(8,128)S(1)} %copy.282), channel_id=1, replica_groups=mesh['gx'=4,'gy'=8] {'gy'}, dimensions={0} | all-to-all | bytes 4718592 | tf_op jit(solution)/shard_map/all_to_all | solution.py:203
  736.8 4.2 collective-permute-start.32
  748.2 3.6 collective-permute-start.35
  752.2 3.4 collective-permute-done.33
  760.2 3.4 collective-permute-start.37
  782.4 7.2 fusion.36
  (321 shorter events, 266.5 us)
Async XLA Ops:
  0.6 115.9 %copy-start = (f32[2,4,128,128]{3,2,1,0:T(8,128)S(1)}, f32[2,4,128,128]{3,2,1,0:T(8,128)}, u32[]{:S(2)}) copy-start(f32[2,4,128,128]{3,2,1,0:T(8,128)} %param.32) | copy-start | bytes 1572868
  3.8 40.3 %copy-start.6 = (f32[4,256,256]{1,2,0:T(8,128)}, f32[4,256,256]{1,2,0:T(8,128)S(1)}, u32[]{:S(2)}) copy-start(f32[4,256,256]{1,2,0:T(8,128)S(1)} %copy.207) | copy-start | bytes 3145732
  12.4 20.2 %collective-permute-start.1 = (f32[12,4,256]{2,1,0:T(4,128)S(1)}, f32[12,4,256]{2,1,0:T(4,128)S(1)}, u32[]{:S(2)}, u32[]{:S(2)}) collective-permute-start(f32[12,4,256]{2,1,0:T(4,128)S(1)} %copy.204), channel_id=1, source_target_pairs={{8,0},{16,8},{24,16},{9,1},{17,9},{25,17},{10,2},{18,10},{26,18},{... | collective-permute-start | bytes 147464 | tf_op jit(solution)/shard_map/ppermute | solution.py:29
  16.2 14.8 %collective-permute-start = (f32[12,4,256]{2,1,0:T(4,128)S(1)}, f32[12,4,256]{2,1,0:T(4,128)S(1)}, u32[]{:S(2)}, u32[]{:S(2)}) collective-permute-start(f32[12,4,256]{2,1,0:T(4,128)S(1)} %copy.203), channel_id=1, source_target_pairs={{0,8},{8,16},{16,24},{1,9},{9,17},{17,25},{2,10},{10,18},{18,26},{... | collective-permute-start | bytes 147464 | tf_op jit(solution)/shard_map/ppermute | solution.py:26
  35.3 7.1 collective-permute-start.2
  37.8 6.2 collective-permute-start.3
  51.7 198.1 %copy-start.2 = (f32[4,264,264]{1,2,0:T(8,128)}, f32[4,264,264]{1,2,0:T(8,128)S(1)}, u32[]{:S(2)}) copy-start(f32[4,264,264]{1,2,0:T(8,128)S(1)} %slice_multiply_fusion) | copy-start | bytes 3345412
  58.7 53.5 %all-to-all-start.1 = ((f32[8,9,64,128]{3,2,1,0:T(8,128)}), f32[8,9,64,128]{3,2,1,0:T(8,128)}, u32[]{:S(2)}, u32[]{:S(2)}) async-start(f32[8,9,64,128]{3,2,1,0:T(8,128)} %copy.220), calls=%async_computation.1 | async-start | bytes 4718592 | tf_op jit(solution)/shard_map/all_to_all | solution.py:187
  117.6 4.3 collective-permute-start.4
  124.1 60.6 %all-to-all-start.2 = ((f32[8,9,64,128]{3,2,1,0:T(8,128)}), f32[8,9,64,128]{3,2,1,0:T(8,128)}, u32[]{:S(2)}, u32[]{:S(2)}) async-start(f32[8,9,64,128]{3,2,1,0:T(8,128)} %copy.227), calls=%async_computation.2 | async-start | bytes 4718592 | tf_op jit(solution)/shard_map/all_to_all | solution.py:203
  184.7 5.5 collective-permute-start.5
  195.8 10.5 %collective-permute-start.7 = (f32[4,2,8,128]{2,3,0,1:T(8,128)S(1)}, f32[4,2,8,128]{2,3,0,1:T(8,128)S(1)}, u32[]{:S(2)}, u32[]{:S(2)}) collective-permute-start(f32[4,2,8,128]{2,3,0,1:T(8,128)S(1)} %get-tuple-element.143), channel_id=1, source_target_pairs={{0,8},{8,16},{16,24},{1,9},{9,17},{17,25},{2,10},{10,18},{18,26},{... | collective-permute-start | bytes 98312 | tf_op jit(solution)/shard_map/ppermute | solution.py:26
  197.8 10.3 %collective-permute-start.8 = (f32[4,2,8,128]{2,3,0,1:T(8,128)S(1)}, f32[4,2,8,128]{2,3,0,1:T(8,128)S(1)}, u32[]{:S(2)}, u32[]{:S(2)}) collective-permute-start(f32[4,2,8,128]{2,3,0,1:T(8,128)S(1)} %get-tuple-element.144), channel_id=1, source_target_pairs={{8,0},{16,8},{24,16},{9,1},{17,9},{25,17},{10,2},{18,10},{26,18},{... | collective-permute-start | bytes 98312 | tf_op jit(solution)/shard_map/ppermute | solution.py:29
  201.4 3.7 collective-permute-start.6
  208.7 10.3 %collective-permute-start.9 = (f32[3,128]{1,0:T(4,128)S(1)}, f32[3,128]{1,0:T(4,128)S(1)}, u32[]{:S(2)}, u32[]{:S(2)}) collective-permute-start(f32[3,128]{1,0:T(4,128)S(1)} %add.351), channel_id=1, source_target_pairs={{0,2},{1,3},{2,0},{3,1},{4,6},{5,7},{6,4},{7,5},{8,10},{9,11},{10,... | collective-permute-start | bytes 4616 | tf_op jit(solution)/shard_map/ppermute | solution.py:84
  211.4 7.6 collective-permute-start.10
  215.6 6.0 collective-permute-start.11
  223.8 4.5 collective-permute-start.12
  244.4 49.1 %all-to-all-start.3 = ((f32[8,9,64,128]{3,2,1,0:T(8,128)}), f32[8,9,64,128]{3,2,1,0:T(8,128)}, u32[]{:S(2)}, u32[]{:S(2)}) async-start(f32[8,9,64,128]{3,2,1,0:T(8,128)} %copy.236), calls=%async_computation.3 | async-start | bytes 4718592 | tf_op jit(solution)/shard_map/all_to_all | solution.py:187
  302.0 4.8 collective-permute-start.13
  367.9 5.4 collective-permute-start.14
  376.7 10.5 %collective-permute-start.16 = (f32[4,2,8,128]{2,3,0,1:T(8,128)S(1)}, f32[4,2,8,128]{2,3,0,1:T(8,128)S(1)}, u32[]{:S(2)}, u32[]{:S(2)}) collective-permute-start(f32[4,2,8,128]{2,3,0,1:T(8,128)S(1)} %get-tuple-element.141), channel_id=1, source_target_pairs={{0,8},{8,16},{16,24},{1,9},{9,17},{17,25},{2,10},{10,18},{18,26},{... | collective-permute-start | bytes 98312 | tf_op jit(solution)/shard_map/ppermute | solution.py:26
  378.6 10.3 %collective-permute-start.17 = (f32[4,2,8,128]{2,3,0,1:T(8,128)S(1)}, f32[4,2,8,128]{2,3,0,1:T(8,128)S(1)}, u32[]{:S(2)}, u32[]{:S(2)}) collective-permute-start(f32[4,2,8,128]{2,3,0,1:T(8,128)S(1)} %get-tuple-element.142), channel_id=1, source_target_pairs={{8,0},{16,8},{24,16},{9,1},{17,9},{25,17},{10,2},{18,10},{26,18},{... | collective-permute-start | bytes 98312 | tf_op jit(solution)/shard_map/ppermute | solution.py:29
  382.3 3.7 collective-permute-start.15
  389.6 8.6 %collective-permute-start.18 = (f32[7,128]{1,0:T(8,128)S(1)}, f32[7,128]{1,0:T(8,128)S(1)}, u32[]{:S(2)}, u32[]{:S(2)}) collective-permute-start(f32[7,128]{1,0:T(8,128)S(1)} %add.361), channel_id=1, source_target_pairs={{0,2},{1,3},{2,0},{3,1},{4,6},{5,7},{6,4},{7,5},{8,10},{9,11},{10,... | collective-permute-start | bytes 10760 | tf_op jit(solution)/shard_map/ppermute | solution.py:84
  390.6 7.6 collective-permute-start.19
  394.8 6.0 collective-permute-start.20
  403.0 4.5 collective-permute-start.21
  428.0 49.1 %all-to-all-start.5 = ((f32[8,9,64,128]{3,2,1,0:T(8,128)}), f32[8,9,64,128]{3,2,1,0:T(8,128)}, u32[]{:S(2)}, u32[]{:S(2)}) async-start(f32[8,9,64,128]{3,2,1,0:T(8,128)} %copy.253), calls=%async_computation.5 | async-start | bytes 4718592 | tf_op jit(solution)/shard_map/all_to_all | solution.py:187
  486.5 4.8 collective-permute-start.22
  551.7 5.8 collective-permute-start.23
  563.1 10.5 %collective-permute-start.25 = (f32[4,2,8,128]{2,3,0,1:T(8,128)S(1)}, f32[4,2,8,128]{2,3,0,1:T(8,128)S(1)}, u32[]{:S(2)}, u32[]{:S(2)}) collective-permute-start(f32[4,2,8,128]{2,3,0,1:T(8,128)S(1)} %get-tuple-element.139), channel_id=1, source_target_pairs={{0,8},{8,16},{16,24},{1,9},{9,17},{17,25},{2,10},{10,18},{18,26},{... | collective-permute-start | bytes 98312 | tf_op jit(solution)/shard_map/ppermute | solution.py:26
  565.1 10.3 %collective-permute-start.26 = (f32[4,2,8,128]{2,3,0,1:T(8,128)S(1)}, f32[4,2,8,128]{2,3,0,1:T(8,128)S(1)}, u32[]{:S(2)}, u32[]{:S(2)}) collective-permute-start(f32[4,2,8,128]{2,3,0,1:T(8,128)S(1)} %get-tuple-element.140), channel_id=1, source_target_pairs={{8,0},{16,8},{24,16},{9,1},{17,9},{25,17},{10,2},{18,10},{26,18},{... | collective-permute-start | bytes 98312 | tf_op jit(solution)/shard_map/ppermute | solution.py:29
  568.7 3.7 collective-permute-start.24
  576.0 8.6 %collective-permute-start.27 = (f32[7,128]{1,0:T(8,128)S(1)}, f32[7,128]{1,0:T(8,128)S(1)}, u32[]{:S(2)}, u32[]{:S(2)}) collective-permute-start(f32[7,128]{1,0:T(8,128)S(1)} %add.378), channel_id=1, source_target_pairs={{0,2},{1,3},{2,0},{3,1},{4,6},{5,7},{6,4},{7,5},{8,10},{9,11},{10,... | collective-permute-start | bytes 10760 | tf_op jit(solution)/shard_map/ppermute | solution.py:84
  577.0 7.6 collective-permute-start.28
  581.2 6.0 collective-permute-start.29
  589.3 4.5 collective-permute-start.30
  614.8 48.9 %all-to-all-start.7 = ((f32[8,9,64,128]{3,2,1,0:T(8,128)}), f32[8,9,64,128]{3,2,1,0:T(8,128)}, u32[]{:S(2)}, u32[]{:S(2)}) async-start(f32[8,9,64,128]{3,2,1,0:T(8,128)} %copy.272), calls=%async_computation.7 | async-start | bytes 4718592 | tf_op jit(solution)/shard_map/all_to_all | solution.py:187
  671.6 4.8 collective-permute-start.31
  736.8 6.1 collective-permute-start.32
  746.3 10.5 %collective-permute-start.34 = (f32[4,2,8,128]{2,3,0,1:T(8,128)S(1)}, f32[4,2,8,128]{2,3,0,1:T(8,128)S(1)}, u32[]{:S(2)}, u32[]{:S(2)}) collective-permute-start(f32[4,2,8,128]{2,3,0,1:T(8,128)S(1)} %get-tuple-element.137), channel_id=1, source_target_pairs={{0,8},{8,16},{16,24},{1,9},{9,17},{17,25},{2,10},{10,18},{18,26},{... | collective-permute-start | bytes 98312 | tf_op jit(solution)/shard_map/ppermute | solution.py:26
  748.2 10.3 %collective-permute-start.35 = (f32[4,2,8,128]{2,3,0,1:T(8,128)S(1)}, f32[4,2,8,128]{2,3,0,1:T(8,128)S(1)}, u32[]{:S(2)}, u32[]{:S(2)}) collective-permute-start(f32[4,2,8,128]{2,3,0,1:T(8,128)S(1)} %get-tuple-element.138), channel_id=1, source_target_pairs={{8,0},{16,8},{24,16},{9,1},{17,9},{25,17},{10,2},{18,10},{26,18},{... | collective-permute-start | bytes 98312 | tf_op jit(solution)/shard_map/ppermute | solution.py:29
  751.9 3.7 collective-permute-start.33
  759.2 8.6 %collective-permute-start.36 = (f32[7,128]{1,0:T(8,128)S(1)}, f32[7,128]{1,0:T(8,128)S(1)}, u32[]{:S(2)}, u32[]{:S(2)}) collective-permute-start(f32[7,128]{1,0:T(8,128)S(1)} %add.395), channel_id=1, source_target_pairs={{0,2},{1,3},{2,0},{3,1},{4,6},{5,7},{6,4},{7,5},{8,10},{9,11},{10,... | collective-permute-start | bytes 10760 | tf_op jit(solution)/shard_map/ppermute | solution.py:84
  760.2 7.6 collective-permute-start.37
  764.4 6.0 collective-permute-start.38
  771.4 4.6 collective-permute-start.39
  (40 other events, 226.1 us)

commit v18 on v17

--- a/solution.py
+++ b/solution.py
@@ -209,29 +209,41 @@
             precision=highest,
         )
         carry, summed = advance(carry, summed)
-        padded = extended(
-            summed.reshape(layers, cols_blocks, tile_rows, block_cols), (("gx", 2),), 8
-        )
-        carry, padded = advance(carry, padded)
+        inner_part = summed.reshape(layers, cols_blocks, tile_rows, block_cols)
+        gx_count = lax.axis_size("gx")
+        gx_forward = [(i, i + 1) for i in range(gx_count - 1)]
+        gx_backward = [(target, source) for source, target in gx_forward]
+        top = lax.ppermute(inner_part[:, :, tile_rows - 8 :], "gx", gx_forward)
+        bottom = lax.ppermute(inner_part[:, :, :8], "gx", gx_backward)
+        carry, (top, bottom) = advance(carry, (top, bottom))
         count = lax.axis_size("gy")
         forward = [(i, i + 1) for i in range(count - 1)]
         backward = [(target, source) for source, target in forward]
-        left = lax.ppermute(padded[:, cols_blocks - 1, :, block_cols - 8 :], "gy", forward)
-        right = lax.ppermute(padded[:, 0, :, :8], "gy", backward)
-        along_cols = (
-            jnp.einsum(
-                "ljac,jcd->lad",
-                padded,
-                analysis_cols[8 : 8 + tile_cols].reshape(cols_blocks, block_cols, -1),
+        parts = (top, inner_part, bottom)
+        left = lax.ppermute(
+            jnp.concatenate([part[:, cols_blocks - 1, :, block_cols - 8 :] for part in parts], axis=1),
+            "gy",
+            forward,
+        )
+        right = lax.ppermute(
+            jnp.concatenate([part[:, 0, :, :8] for part in parts], axis=1), "gy", backward
+        )
+        middle = analysis_cols[8 : 8 + tile_cols].reshape(cols_blocks, block_cols, -1)
+        row_bounds = ((0, 8), (8, 8 + tile_rows), (8 + tile_rows, 16 + tile_rows))
+        sides = jnp.einsum("lab,bc->lac", left, analysis_cols[:8], precision=highest) + jnp.einsum(
+            "lab,bc->lac", right, analysis_cols[8 + tile_cols :], precision=highest
+        )
+        along_cols = jnp.einsum("lab,ac->lcb", sides, analysis_rows, precision=highest)
+        for part, (low, high) in zip(parts, row_bounds):
+            along_cols = along_cols + jnp.einsum(
+                "lab,ac->lcb",
+                jnp.einsum("ljac,jcd->lad", part, middle, precision=highest),
+                analysis_rows[low:high],
                 precision=highest,
             )
-            + jnp.einsum("lab,bc->lac", left, analysis_cols[:8], precision=highest)
-            + jnp.einsum("lab,bc->lac", right, analysis_cols[8 + tile_cols :], precision=highest)
-        )
         carry, along_cols = advance(carry, along_cols)
         return (
-            jnp.einsum("lab,ac->lcb", along_cols, analysis_rows, precision=highest)
-            + prior_weight * direction
+            along_cols + prior_weight * direction
         ), slopes, jnp.sum(finish(carry), axis=1)
 
     rims = with_rim(jnp.concatenate([right_side, jacobi_inverse, prior_weight]))

time: 806 us -> 847 us (1.051)
  other arithmetic: 60.3 us -> 81 us
  matrix products: 111 us -> 122 us
  local copies, waits for them, and re-layouts: 113 us -> 123 us
  waiting for transfers between devices: 185 us -> 175 us
    squeeze x4 -> x35, local copies, waits for them, and re-layouts: 0.03 us -> 27.9 us  [the longest x23 18.1 us: apply_op(): part[:, 0, :, :8]]
    ppermute x8 -> x16, starting transfers between devices: 26.9 us -> 53.7 us  [the longest x4 26 us: apply_op(): lax.ppermute(jnp.concatenate([part[:, 0, :, :8] for part in parts], axis=...]
    all_to_all x4, waiting for transfers between devices: 85.3 us -> 103 us  [apply_op(): lax.all_to_all(outgoing, 'gy', split_axis=0, concat_axis=0, tiled=True)]
    mul x2 -> x4, other arithmetic: 2.36 us -> 17.1 us  [shards(): precond_res = jacobi_inverse * residual]
    ppermute x6 -> x2, starting transfers between devices: 20.7 us -> 6.16 us  [extended(): lax.ppermute(lax.slice_in_dim(block, 0, width, axis=dim), axis, backward)]
    dot_general x8 -> x28, matrix products: 25.2 us -> 38.2 us  [the longest x12 18 us: apply_op(): jnp.einsum('lab,ac->lcb', jnp.einsum('ljac,jcd->lad', part, middle, preci...]
    ppermute x20, waiting for transfers between devices: 27.9 us -> 17.3 us  [sum_steps(): lax.ppermute(value, axis, pairs)]
  transfers between devices with their start and end apart: 45 -> 45, of which waited for: 27 -> 13; matrix products, arithmetic and copies ran while one was open for 17% -> 20% of each run, Pallas kernels for 0% -> 0%
where the time goes in v18:
time: 847 us; the launch traced here: 830 us
  blocking collectives  193 us (23%)
  waiting for transfers between devices  175 us (21%)
  local copies, waits for them, and re-layouts  123 us (15%)
  matrix products  122 us (14%)
  starting transfers between devices  114 us (13%)
  other arithmetic  81 us (10%)
  between operations  21.9 us (3%)
    all_to_all x3, blocking collectives, apply_op(): lax.all_to_all(returning, 'gy', split_axis=0, concat_axis=0, tiled=True)  182 us
    all_to_all x4, waiting for transfers between devices, apply_op(): lax.all_to_all(outgoing, 'gy', split_axis=0, concat_axis=0, tiled=True)  103 us
    all_to_all x1, waiting for transfers between devices, apply_op(): lax.all_to_all(returning, 'gy', split_axis=0, concat_axis=0, tiled=True)  51.1 us
    ppermute x4, starting transfers between devices, apply_op(): lax.ppermute(jnp.concatenate([part[:, 0, :, :8] for part in parts], axis=...  26 us
    reshape x13, local copies, waits for them, and re-layouts, lane_sum(): return jnp.sum(values.reshape(-1, 128), axis=0)  23.7 us
    ppermute x20, starting transfers between devices, sum_steps(): lax.ppermute(value, axis, pairs)  20.7 us
    all_to_all x4, starting transfers between devices, apply_op(): lax.all_to_all(outgoing, 'gy', split_axis=0, concat_axis=0, tiled=True)  20.3 us
    squeeze x23, local copies, waits for them, and re-layouts, apply_op(): part[:, 0, :, :8]  18.1 us
  transfers between devices with their start and end apart: 45, of which 13 were waited for; matrix products, arithmetic and copies ran while one was open for 20% of the time, Pallas kernels for 0%

profile of v18, /device:TPU:10, one launch (start us, length us, event | category | flops | bytes accessed | tf_op | source)
XLA Modules:
  0.0 830.1 jit_solution(6809635518361669251)
XLA Ops:
  3.8 2.9 copy.233
  19.8 11.1 %all_to_all.52 = s32[8,1,9]{2,1,0:T(1,128)S(1)} all-to-all(s32[8,1,9]{2,1,0:T(1,128)S(1)} %copy.244), channel_id=1, replica_groups=mesh['gx'=4,'gy'=8] {'gy'}, dimensions={0} | all-to-all | bytes 576 | tf_op jit(solution)/shard_map/all_to_all | solution.py:157
  37.8 4.2 collective-permute-start.3
  44.1 5.4 pad_maximum_fusion
  58.7 6.0 all-to-all-start.1
  65.0 2.9 slice_multiply_fusion.9
  67.9 2.7 copy.240
  78.3 33.7 %all-to-all-done.1 = f32[8,9,64,128]{3,2,1,0:T(8,128)} async-done(((f32[8,9,64,128]{3,2,1,0:T(8,128)}), f32[8,9,64,128]{3,2,1,0:T(8,128)}, u32[]{:S(2)}, u32[]{:S(2)}) %all-to-all-start.1) | async-done | bytes 2359328 | tf_op jit(solution)/shard_map/all_to_all | solution.py:187
  112.0 4.3 fusion.6
  118.5 3.2 fusion.22
  123.9 8.1 all-to-all-start.2
  133.3 51.1 %all-to-all-done.2 = f32[8,9,64,128]{3,2,1,0:T(8,128)} async-done(((f32[8,9,64,128]{3,2,1,0:T(8,128)}), f32[8,9,64,128]{3,2,1,0:T(8,128)}, u32[]{:S(2)}, u32[]{:S(2)}) %all-to-all-start.2) | async-done | bytes 2359328 | tf_op jit(solution)/shard_map/all_to_all | solution.py:203
  186.4 3.5 fusion.14
  194.7 3.0 collective-permute-start.7
  203.1 3.5 collective-permute-start.9
  209.5 12.8 %collective-permute-start.11 = (f32[4,272,8]{1,2,0:T(8,128)S(1)}, f32[4,272,8]{1,2,0:T(8,128)S(1)}, u32[]{:S(2)}, u32[]{:S(2)}) collective-permute-start(f32[4,272,8]{1,2,0:T(8,128)S(1)} %pad_maximum_fusion.8), channel_id=1, source_target_pairs={{1,0},{2,1},{3,2},{4,3},{5,4},{6,5},{7,6},{9,8},{10,9},{11,10},{12... | collective-permute-start | bytes 104456 | tf_op jit(solution)/shard_map/ppermute | solution.py:228
  229.9 4.5 collective-permute-done.12
  237.1 5.0 slice_multiply_fusion.3
  249.1 4.7 all-to-all-start.3
  253.8 4.5 multiply_multiply_fusion.7
  277.2 23.6 %all-to-all-done.3 = f32[8,9,64,128]{3,2,1,0:T(8,128)} async-done(((f32[8,9,64,128]{3,2,1,0:T(8,128)}), f32[8,9,64,128]{3,2,1,0:T(8,128)}, u32[]{:S(2)}, u32[]{:S(2)}) %all-to-all-start.3) | async-done | bytes 2359328 | tf_op jit(solution)/shard_map/all_to_all | solution.py:187
  300.8 4.3 fusion.4
  309.5 4.7 fusion.20
  315.0 60.6 %all_to_all.53 = f32[8,9,64,128]{3,2,1,0:T(8,128)S(1)} all-to-all(f32[8,9,64,128]{3,2,1,0:T(8,128)S(1)} %copy.278), channel_id=1, replica_groups=mesh['gx'=4,'gy'=8] {'gy'}, dimensions={0} | all-to-all | bytes 4718592 | tf_op jit(solution)/shard_map/all_to_all | solution.py:203
  410.5 4.4 collective-permute-start.20
  424.1 4.5 collective-permute-done.21
  435.3 5.6 slice_multiply_fusion.2
  440.9 3.0 convolution_bitcast_fusion.3
  449.9 4.7 all-to-all-start.5
  454.6 3.4 multiply_multiply_fusion.1
  464.3 4.5 multiply_multiply_fusion.5
  487.8 14.3 %all-to-all-done.5 = f32[8,9,64,128]{3,2,1,0:T(8,128)} async-done(((f32[8,9,64,128]{3,2,1,0:T(8,128)}), f32[8,9,64,128]{3,2,1,0:T(8,128)}, u32[]{:S(2)}, u32[]{:S(2)}) %all-to-all-start.5) | async-done | bytes 2359328 | tf_op jit(solution)/shard_map/all_to_all | solution.py:187
  502.1 4.4 fusion.2
  511.5 4.7 fusion.18
  517.0 60.6 %all_to_all.54 = f32[8,9,64,128]{3,2,1,0:T(8,128)S(1)} all-to-all(f32[8,9,64,128]{3,2,1,0:T(8,128)S(1)} %copy.299), channel_id=1, replica_groups=mesh['gx'=4,'gy'=8] {'gy'}, dimensions={0} | all-to-all | bytes 4718592 | tf_op jit(solution)/shard_map/all_to_all | solution.py:203
  613.1 4.5 collective-permute-start.29
  626.7 4.5 collective-permute-done.30
  637.7 6.3 slice_multiply_fusion.1
  651.1 4.8 all-to-all-start.7
  655.9 5.2 multiply_multiply_fusion
  671.7 31.6 %all-to-all-done.7 = f32[8,9,64,128]{3,2,1,0:T(8,128)} async-done(((f32[8,9,64,128]{3,2,1,0:T(8,128)}), f32[8,9,64,128]{3,2,1,0:T(8,128)}, u32[]{:S(2)}, u32[]{:S(2)}) %all-to-all-start.7) | async-done | bytes 2359328 | tf_op jit(solution)/shard_map/all_to_all | solution.py:187
  703.4 4.4 fusion
  711.3 4.7 fusion.16
  716.8 60.8 %all_to_all.55 = f32[8,9,64,128]{3,2,1,0:T(8,128)S(1)} all-to-all(f32[8,9,64,128]{3,2,1,0:T(8,128)S(1)} %copy.320), channel_id=1, replica_groups=mesh['gx'=4,'gy'=8] {'gy'}, dimensions={0} | all-to-all | bytes 4718592 | tf_op jit(solution)/shard_map/all_to_all | solution.py:203
  795.9 4.3 collective-permute-start.38
  808.7 3.8 collective-permute-done.39
  818.8 7.2 fusion.38
  826.0 2.6 copy.330
  (435 shorter events, 279.2 us)
Async XLA Ops:
  0.6 115.7 %copy-start = (f32[2,4,128,128]{3,2,1,0:T(8,128)S(1)}, f32[2,4,128,128]{3,2,1,0:T(8,128)}, u32[]{:S(2)}) copy-start(f32[2,4,128,128]{3,2,1,0:T(8,128)} %param.52) | copy-start | bytes 1572868
  12.3 20.2 %collective-permute-start.1 = (f32[12,4,256]{2,1,0:T(4,128)S(1)}, f32[12,4,256]{2,1,0:T(4,128)S(1)}, u32[]{:S(2)}, u32[]{:S(2)}) collective-permute-start(f32[12,4,256]{2,1,0:T(4,128)S(1)} %copy.236), channel_id=1, source_target_pairs={{8,0},{16,8},{24,16},{9,1},{17,9},{25,17},{10,2},{18,10},{26,18},{... | collective-permute-start | bytes 147464 | tf_op jit(solution)/shard_map/ppermute | solution.py:29
  16.1 14.8 %collective-permute-start = (f32[12,4,256]{2,1,0:T(4,128)S(1)}, f32[12,4,256]{2,1,0:T(4,128)S(1)}, u32[]{:S(2)}, u32[]{:S(2)}) collective-permute-start(f32[12,4,256]{2,1,0:T(4,128)S(1)} %copy.235), channel_id=1, source_target_pairs={{0,8},{8,16},{16,24},{1,9},{9,17},{17,25},{2,10},{10,18},{18,26},{... | collective-permute-start | bytes 147464 | tf_op jit(solution)/shard_map/ppermute | solution.py:26
  35.3 7.1 collective-permute-start.2
  37.8 6.2 collective-permute-start.3
  58.7 53.3 %all-to-all-start.1 = ((f32[8,9,64,128]{3,2,1,0:T(8,128)}), f32[8,9,64,128]{3,2,1,0:T(8,128)}, u32[]{:S(2)}, u32[]{:S(2)}) async-start(f32[8,9,64,128]{3,2,1,0:T(8,128)} %copy.252), calls=%async_computation.1 | async-start | bytes 4718592 | tf_op jit(solution)/shard_map/all_to_all | solution.py:187
  117.4 4.3 collective-permute-start.4
  123.9 60.4 %all-to-all-start.2 = ((f32[8,9,64,128]{3,2,1,0:T(8,128)}), f32[8,9,64,128]{3,2,1,0:T(8,128)}, u32[]{:S(2)}, u32[]{:S(2)}) async-start(f32[8,9,64,128]{3,2,1,0:T(8,128)} %copy.259), calls=%async_computation.2 | async-start | bytes 4718592 | tf_op jit(solution)/shard_map/all_to_all | solution.py:203
  184.3 5.6 collective-permute-start.5
  192.1 7.6 collective-permute-start.6
  192.7 7.0 collective-permute-start.8
  194.7 5.6 collective-permute-start.7
  203.1 20.9 %collective-permute-start.9 = (f32[3,128]{1,0:T(4,128)S(1)}, f32[3,128]{1,0:T(4,128)S(1)}, u32[]{:S(2)}, u32[]{:S(2)}) collective-permute-start(f32[3,128]{1,0:T(4,128)S(1)} %add.395), channel_id=1, source_target_pairs={{0,2},{1,3},{2,0},{3,1},{4,6},{5,7},{6,4},{7,5},{8,10},{9,11},{10,... | collective-permute-start | bytes 4616 | tf_op jit(solution)/shard_map/ppermute | solution.py:84
  207.0 18.0 %collective-permute-start.10 = (f32[4,272,8]{1,2,0:T(8,128)S(1)}, f32[4,272,8]{1,2,0:T(8,128)S(1)}, u32[]{:S(2)}, u32[]{:S(2)}) collective-permute-start(f32[4,272,8]{1,2,0:T(8,128)S(1)} %pad_maximum_fusion.7), channel_id=1, source_target_pairs={{0,1},{1,2},{2,3},{3,4},{4,5},{5,6},{6,7},{8,9},{9,10},{10,11},{11... | collective-permute-start | bytes 104456 | tf_op jit(solution)/shard_map/ppermute | solution.py:223
  209.5 14.6 %collective-permute-start.11 = (f32[4,272,8]{1,2,0:T(8,128)S(1)}, f32[4,272,8]{1,2,0:T(8,128)S(1)}, u32[]{:S(2)}, u32[]{:S(2)}) collective-permute-start(f32[4,272,8]{1,2,0:T(8,128)S(1)} %pad_maximum_fusion.8), channel_id=1, source_target_pairs={{1,0},{2,1},{3,2},{4,3},{5,4},{6,5},{7,6},{9,8},{10,9},{11,10},{12... | collective-permute-start | bytes 104456 | tf_op jit(solution)/shard_map/ppermute | solution.py:228
  229.9 4.5 collective-permute-start.12
  249.1 51.8 %all-to-all-start.3 = ((f32[8,9,64,128]{3,2,1,0:T(8,128)}), f32[8,9,64,128]{3,2,1,0:T(8,128)}, u32[]{:S(2)}, u32[]{:S(2)}) async-start(f32[8,9,64,128]{3,2,1,0:T(8,128)} %copy.270), calls=%async_computation.3 | async-start | bytes 4718592 | tf_op jit(solution)/shard_map/all_to_all | solution.py:187
  309.4 4.8 collective-permute-start.13
  375.5 3.6 collective-permute-start.14
  382.1 9.8 %collective-permute-start.15 = (f32[7,128]{1,0:T(8,128)}, f32[7,128]{1,0:T(8,128)}, u32[]{:S(2)}, u32[]{:S(2)}) collective-permute-start(f32[7,128]{1,0:T(8,128)} %add.407), channel_id=1, source_target_pairs={{0,1},{1,0},{2,3},{3,2},{4,5},{5,4},{6,7},{7,6},{8,9},{9,8},{10,11... | collective-permute-start | bytes 10760 | tf_op jit(solution)/shard_map/ppermute | solution.py:84
  382.3 10.9 %collective-permute-start.17 = (f32[4,2,8,128]{3,2,1,0:T(8,128)}, f32[4,2,8,128]{3,2,1,0:T(8,128)S(1)}, u32[]{:S(2)}, u32[]{:S(2)}) collective-permute-start(f32[4,2,8,128]{3,2,1,0:T(8,128)} %get-tuple-element.149), channel_id=1, source_target_pairs={{8,0},{16,8},{24,16},{9,1},{17,9},{25,17},{10,2},{18,10},{26,18},{... | collective-permute-start | bytes 98312 | tf_op jit(solution)/shard_map/ppermute | solution.py:217
  384.2 9.0 %collective-permute-start.16 = (f32[4,2,8,128]{3,2,1,0:T(8,128)}, f32[4,2,8,128]{3,2,1,0:T(8,128)S(1)}, u32[]{:S(2)}, u32[]{:S(2)}) collective-permute-start(f32[4,2,8,128]{3,2,1,0:T(8,128)} %get-tuple-element.150), channel_id=1, source_target_pairs={{0,8},{8,16},{16,24},{1,9},{9,17},{17,25},{2,10},{10,18},{18,26},{... | collective-permute-start | bytes 98312 | tf_op jit(solution)/shard_map/ppermute | solution.py:216
  399.2 18.3 %collective-permute-start.18 = (f32[7,128]{1,0:T(8,128)}, f32[7,128]{1,0:T(8,128)}, u32[]{:S(2)}, u32[]{:S(2)}) collective-permute-start(f32[7,128]{1,0:T(8,128)} %add.408), channel_id=1, source_target_pairs={{0,2},{1,3},{2,0},{3,1},{4,6},{5,7},{6,4},{7,5},{8,10},{9,11},{10,... | collective-permute-start | bytes 10760 | tf_op jit(solution)/shard_map/ppermute | solution.py:84
  407.2 11.9 %collective-permute-start.19 = (f32[4,272,8]{1,2,0:T(8,128)S(1)}, f32[4,272,8]{1,2,0:T(8,128)S(1)}, u32[]{:S(2)}, u32[]{:S(2)}) collective-permute-start(f32[4,272,8]{1,2,0:T(8,128)S(1)} %pad_maximum_fusion.9), channel_id=1, source_target_pairs={{0,1},{1,2},{2,3},{3,4},{4,5},{5,6},{6,7},{8,9},{9,10},{10,11},{11... | collective-permute-start | bytes 104456 | tf_op jit(solution)/shard_map/ppermute | solution.py:223
  410.5 7.7 collective-permute-start.20
  424.1 4.5 collective-permute-start.21
  449.9 52.2 %all-to-all-start.5 = ((f32[8,9,64,128]{3,2,1,0:T(8,128)}), f32[8,9,64,128]{3,2,1,0:T(8,128)}, u32[]{:S(2)}, u32[]{:S(2)}) async-start(f32[8,9,64,128]{3,2,1,0:T(8,128)} %copy.289), calls=%async_computation.5 | async-start | bytes 4718592 | tf_op jit(solution)/shard_map/all_to_all | solution.py:187
  511.4 4.8 collective-permute-start.22
  517.0 62.9 %copy-start.70 = (s32[72]{0:T(128)S(1)}, s32[72]{0:T(128)}, u32[]{:S(2)}) copy-start(s32[72]{0:T(128)} %copy-done.68) | copy-start | bytes 868
  577.6 4.2 collective-permute-start.23
  584.8 9.8 %collective-permute-start.24 = (f32[7,128]{1,0:T(8,128)}, f32[7,128]{1,0:T(8,128)}, u32[]{:S(2)}, u32[]{:S(2)}) collective-permute-start(f32[7,128]{1,0:T(8,128)} %add.427), channel_id=1, source_target_pairs={{0,1},{1,0},{2,3},{3,2},{4,5},{5,4},{6,7},{7,6},{8,9},{9,8},{10,11... | collective-permute-start | bytes 10760 | tf_op jit(solution)/shard_map/ppermute | solution.py:84
  585.0 10.9 %collective-permute-start.26 = (f32[4,2,8,128]{3,2,1,0:T(8,128)}, f32[4,2,8,128]{3,2,1,0:T(8,128)S(1)}, u32[]{:S(2)}, u32[]{:S(2)}) collective-permute-start(f32[4,2,8,128]{3,2,1,0:T(8,128)} %get-tuple-element.145), channel_id=1, source_target_pairs={{8,0},{16,8},{24,16},{9,1},{17,9},{25,17},{10,2},{18,10},{26,18},{... | collective-permute-start | bytes 98312 | tf_op jit(solution)/shard_map/ppermute | solution.py:217
  586.9 9.0 %collective-permute-start.25 = (f32[4,2,8,128]{3,2,1,0:T(8,128)}, f32[4,2,8,128]{3,2,1,0:T(8,128)S(1)}, u32[]{:S(2)}, u32[]{:S(2)}) collective-permute-start(f32[4,2,8,128]{3,2,1,0:T(8,128)} %get-tuple-element.146), channel_id=1, source_target_pairs={{0,8},{8,16},{16,24},{1,9},{9,17},{17,25},{2,10},{10,18},{18,26},{... | collective-permute-start | bytes 98312 | tf_op jit(solution)/shard_map/ppermute | solution.py:216
  601.8 18.3 %collective-permute-start.27 = (f32[7,128]{1,0:T(8,128)}, f32[7,128]{1,0:T(8,128)}, u32[]{:S(2)}, u32[]{:S(2)}) collective-permute-start(f32[7,128]{1,0:T(8,128)} %add.428), channel_id=1, source_target_pairs={{0,2},{1,3},{2,0},{3,1},{4,6},{5,7},{6,4},{7,5},{8,10},{9,11},{10,... | collective-permute-start | bytes 10760 | tf_op jit(solution)/shard_map/ppermute | solution.py:84
  609.8 11.9 %collective-permute-start.28 = (f32[4,272,8]{1,2,0:T(8,128)S(1)}, f32[4,272,8]{1,2,0:T(8,128)S(1)}, u32[]{:S(2)}, u32[]{:S(2)}) collective-permute-start(f32[4,272,8]{1,2,0:T(8,128)S(1)} %pad_maximum_fusion.11), channel_id=1, source_target_pairs={{0,1},{1,2},{2,3},{3,4},{4,5},{5,6},{6,7},{8,9},{9,10},{10,11},{11... | collective-permute-start | bytes 104456 | tf_op jit(solution)/shard_map/ppermute | solution.py:223
  613.1 7.7 collective-permute-start.29
  626.7 4.5 collective-permute-start.30
  651.1 52.3 %all-to-all-start.7 = ((f32[8,9,64,128]{3,2,1,0:T(8,128)}), f32[8,9,64,128]{3,2,1,0:T(8,128)}, u32[]{:S(2)}, u32[]{:S(2)}) async-start(f32[8,9,64,128]{3,2,1,0:T(8,128)} %copy.310), calls=%async_computation.7 | async-start | bytes 4718592 | tf_op jit(solution)/shard_map/all_to_all | solution.py:187
  711.2 4.8 collective-permute-start.31
  716.8 63.1 %copy-start.71 = (s32[72]{0:T(128)S(1)}, s32[72]{0:T(128)}, u32[]{:S(2)}) copy-start(s32[72]{0:T(128)} %copy-done.68) | copy-start | bytes 868
  777.6 4.2 collective-permute-start.32
  782.6 6.6 collective-permute-start.33
  782.9 6.4 collective-permute-start.35
  784.8 5.3 collective-permute-start.34
  790.8 11.2 %collective-permute-start.36 = (f32[7,128]{1,0:T(8,128)S(1)}, f32[7,128]{1,0:T(8,128)S(1)}, u32[]{:S(2)}, u32[]{:S(2)}) collective-permute-start(f32[7,128]{1,0:T(8,128)S(1)} %add.448), channel_id=1, source_target_pairs={{0,2},{1,3},{2,0},{3,1},{4,6},{5,7},{6,4},{7,5},{8,10},{9,11},{10,... | collective-permute-start | bytes 10760 | tf_op jit(solution)/shard_map/ppermute | solution.py:84
  793.4 9.5 %collective-permute-start.37 = (f32[4,272,8]{1,2,0:T(8,128)S(1)}, f32[4,272,8]{1,2,0:T(8,128)S(1)}, u32[]{:S(2)}, u32[]{:S(2)}) collective-permute-start(f32[4,272,8]{1,2,0:T(8,128)S(1)} %pad_maximum_fusion.13), channel_id=1, source_target_pairs={{0,1},{1,2},{2,3},{3,4},{4,5},{5,6},{6,7},{8,9},{9,10},{10,11},{11... | collective-permute-start | bytes 104456 | tf_op jit(solution)/shard_map/ppermute | solution.py:223
  795.9 6.1 collective-permute-start.38
  807.9 4.5 collective-permute-start.39
  (71 other events, 686.7 us)

commit v19 on v17

--- a/solution.py
+++ b/solution.py
@@ -189,7 +189,7 @@
             "ek,kxc->exc",
             picking,
             arrived.reshape(owners * capacity, block_rows, block_cols),
-            precision=lax.Precision.HIGHEST,
+            precision=highest,
         ).reshape(sensors, rows_blocks * cols_blocks, layers, block_rows, block_cols)
         slopes = jnp.einsum("sklxy,slyz->skxz", seen, interaction, precision=highest)
         carry = (partials(slopes), sum_steps(("gx", "gy")))
@@ -197,7 +197,7 @@
             requests, block_rows, block_cols
         )
         returning = jnp.einsum(
-            "ek,exc->kxc", picking, back, precision=lax.Precision.HIGHEST
+            "ek,exc->kxc", picking, back, precision=highest
         ).reshape(owners, capacity, block_rows, block_cols)
         carry, returning = advance(carry, returning)
         landed = lax.all_to_all(returning, "gy", split_axis=0, concat_axis=0, tiled=True)

time: 806 us -> 801 us (level)
  no operation moved by 1% of the time
where the time goes in v19:
time: 801 us; the launch traced here: 788 us
  blocking collectives  191 us (24%)
  waiting for transfers between devices  185 us (23%)
  local copies, waits for them, and re-layouts  113 us (14%)
  starting transfers between devices  111 us (14%)
  matrix products  106 us (13%)
  other arithmetic  60.3 us (8%)
  between operations  21.4 us (3%)
    all_to_all x3, blocking collectives, apply_op(): lax.all_to_all(returning, 'gy', split_axis=0, concat_axis=0, tiled=True)  180 us
    all_to_all x4, waiting for transfers between devices, apply_op(): lax.all_to_all(outgoing, 'gy', split_axis=0, concat_axis=0, tiled=True)  85.7 us
    all_to_all x1, waiting for transfers between devices, apply_op(): lax.all_to_all(returning, 'gy', split_axis=0, concat_axis=0, tiled=True)  51.1 us
    reshape x13, local copies, waits for them, and re-layouts, lane_sum(): return jnp.sum(values.reshape(-1, 128), axis=0)  28 us
    ppermute x20, waiting for transfers between devices, sum_steps(): lax.ppermute(value, axis, pairs)  27.8 us
    dot_general x4, matrix products, apply_op(): jnp.einsum('lab,ac->lcb', along_cols, analysis_rows, precision=highest)  21.8 us
    all_to_all x4, starting transfers between devices, apply_op(): lax.all_to_all(outgoing, 'gy', split_axis=0, concat_axis=0, tiled=True)  21.5 us
    ppermute x20, starting transfers between devices, sum_steps(): lax.ppermute(value, axis, pairs)  21.3 us
  transfers between devices with their start and end apart: 45, of which 27 were waited for; matrix products, arithmetic and copies ran while one was open for 17% of the time, Pallas kernels for 0%

profile of v19, /device:TPU:10, one launch (start us, length us, event | category | flops | bytes accessed | tf_op | source)
XLA Modules:
  0.0 788.3 jit_solution(18170394291169662045)
XLA Ops:
  19.8 11.1 %all_to_all.52 = s32[8,1,9]{2,1,0:T(1,128)S(1)} all-to-all(s32[8,1,9]{2,1,0:T(1,128)S(1)} %copy.212), channel_id=1, replica_groups=mesh['gx'=4,'gy'=8] {'gy'}, dimensions={0} | all-to-all | bytes 576 | tf_op jit(solution)/shard_map/all_to_all | solution.py:157
  37.8 4.2 collective-permute-start.3
  44.1 5.4 pad_maximum_fusion
  58.7 6.0 all-to-all-start.1
  80.4 31.5 %all-to-all-done.1 = f32[8,9,64,128]{3,2,1,0:T(8,128)} async-done(((f32[8,9,64,128]{3,2,1,0:T(8,128)}), f32[8,9,64,128]{3,2,1,0:T(8,128)}, u32[]{:S(2)}, u32[]{:S(2)}) %all-to-all-start.1) | async-done | bytes 2359328 | tf_op jit(solution)/shard_map/all_to_all | solution.py:187
  112.0 3.7 fusion.6
  122.5 8.1 %all-to-all-start.2 = ((f32[8,9,64,128]{3,2,1,0:T(8,128)}), f32[8,9,64,128]{3,2,1,0:T(8,128)}, u32[]{:S(2)}, u32[]{:S(2)}) async-start(f32[8,9,64,128]{3,2,1,0:T(8,128)} %copy.227), calls=%async_computation.2 | async-start | bytes 4718592 | tf_op jit(solution)/shard_map/all_to_all | solution.py:203
  131.8 51.1 %all-to-all-done.2 = f32[8,9,64,128]{3,2,1,0:T(8,128)} async-done(((f32[8,9,64,128]{3,2,1,0:T(8,128)}), f32[8,9,64,128]{3,2,1,0:T(8,128)}, u32[]{:S(2)}, u32[]{:S(2)}) %all-to-all-start.2) | async-done | bytes 2359328 | tf_op jit(solution)/shard_map/all_to_all | solution.py:203
  185.0 3.5 fusion.14
  196.0 4.0 collective-permute-start.8
  209.6 3.4 collective-permute-start.10
  222.0 4.5 collective-permute-done.12
  229.1 6.6 slice_multiply_fusion.3
  242.6 5.2 all-to-all-start.3
  247.8 4.5 multiply_multiply_fusion.7
  266.8 25.1 %all-to-all-done.3 = f32[8,9,64,128]{3,2,1,0:T(8,128)} async-done(((f32[8,9,64,128]{3,2,1,0:T(8,128)}), f32[8,9,64,128]{3,2,1,0:T(8,128)}, u32[]{:S(2)}, u32[]{:S(2)}) %all-to-all-start.3) | async-done | bytes 2359328 | tf_op jit(solution)/shard_map/all_to_all | solution.py:187
  291.8 3.8 fusion.4
  299.9 4.0 fusion.20
  304.7 60.4 %all_to_all.53 = f32[8,9,64,128]{3,2,1,0:T(8,128)S(1)} all-to-all(f32[8,9,64,128]{3,2,1,0:T(8,128)S(1)} %copy.244), channel_id=1, replica_groups=mesh['gx'=4,'gy'=8] {'gy'}, dimensions={0} | all-to-all | bytes 4718592 | tf_op jit(solution)/shard_map/all_to_all | solution.py:203
  375.4 3.6 collective-permute-start.17
  379.4 3.4 collective-permute-done.15
  387.4 3.4 collective-permute-start.19
  399.8 4.4 collective-permute-done.21
  410.8 4.9 fusion.31
  424.8 5.2 all-to-all-start.5
  430.1 3.4 multiply_multiply_fusion.1
  439.8 4.5 multiply_multiply_fusion.5
  463.2 10.8 %all-to-all-done.5 = f32[8,9,64,128]{3,2,1,0:T(8,128)} async-done(((f32[8,9,64,128]{3,2,1,0:T(8,128)}), f32[8,9,64,128]{3,2,1,0:T(8,128)}, u32[]{:S(2)}, u32[]{:S(2)}) %all-to-all-start.5) | async-done | bytes 2359328 | tf_op jit(solution)/shard_map/all_to_all | solution.py:187
  474.0 3.8 fusion.2
  482.9 4.0 fusion.18
  487.6 59.7 %all_to_all.54 = f32[8,9,64,128]{3,2,1,0:T(8,128)S(1)} all-to-all(f32[8,9,64,128]{3,2,1,0:T(8,128)S(1)} %copy.263), channel_id=1, replica_groups=mesh['gx'=4,'gy'=8] {'gy'}, dimensions={0} | all-to-all | bytes 4718592 | tf_op jit(solution)/shard_map/all_to_all | solution.py:203
  547.3 4.0 collective-permute-start.23
  560.7 3.6 collective-permute-start.26
  564.7 3.4 collective-permute-done.24
  572.7 3.4 collective-permute-start.28
  585.2 4.3 collective-permute-done.30
  596.1 7.5 slice_multiply_fusion.1
  610.5 5.0 all-to-all-start.7
  615.5 5.7 multiply_multiply_fusion
  640.9 18.3 %all-to-all-done.7 = f32[8,9,64,128]{3,2,1,0:T(8,128)} async-done(((f32[8,9,64,128]{3,2,1,0:T(8,128)}), f32[8,9,64,128]{3,2,1,0:T(8,128)}, u32[]{:S(2)}, u32[]{:S(2)}) %all-to-all-start.7) | async-done | bytes 2359328 | tf_op jit(solution)/shard_map/all_to_all | solution.py:187
  659.2 3.8 fusion
  666.6 4.0 fusion.16
  671.3 59.8 %all_to_all.55 = f32[8,9,64,128]{3,2,1,0:T(8,128)S(1)} all-to-all(f32[8,9,64,128]{3,2,1,0:T(8,128)S(1)} %copy.282), channel_id=1, replica_groups=mesh['gx'=4,'gy'=8] {'gy'}, dimensions={0} | all-to-all | bytes 4718592 | tf_op jit(solution)/shard_map/all_to_all | solution.py:203
  731.1 4.2 collective-permute-start.32
  742.5 3.6 collective-permute-start.35
  746.4 3.4 collective-permute-done.33
  754.5 3.4 collective-permute-start.37
  776.7 7.2 fusion.36
  (321 shorter events, 265.1 us)
Async XLA Ops:
  0.6 115.1 %copy-start = (f32[2,4,128,128]{3,2,1,0:T(8,128)S(1)}, f32[2,4,128,128]{3,2,1,0:T(8,128)}, u32[]{:S(2)}) copy-start(f32[2,4,128,128]{3,2,1,0:T(8,128)} %param.32) | copy-start | bytes 1572868
  3.8 40.3 %copy-start.6 = (f32[4,256,256]{1,2,0:T(8,128)}, f32[4,256,256]{1,2,0:T(8,128)S(1)}, u32[]{:S(2)}) copy-start(f32[4,256,256]{1,2,0:T(8,128)S(1)} %copy.207) | copy-start | bytes 3145732
  12.4 20.2 %collective-permute-start.1 = (f32[12,4,256]{2,1,0:T(4,128)S(1)}, f32[12,4,256]{2,1,0:T(4,128)S(1)}, u32[]{:S(2)}, u32[]{:S(2)}) collective-permute-start(f32[12,4,256]{2,1,0:T(4,128)S(1)} %copy.204), channel_id=1, source_target_pairs={{8,0},{16,8},{24,16},{9,1},{17,9},{25,17},{10,2},{18,10},{26,18},{... | collective-permute-start | bytes 147464 | tf_op jit(solution)/shard_map/ppermute | solution.py:29
  16.2 14.8 %collective-permute-start = (f32[12,4,256]{2,1,0:T(4,128)S(1)}, f32[12,4,256]{2,1,0:T(4,128)S(1)}, u32[]{:S(2)}, u32[]{:S(2)}) collective-permute-start(f32[12,4,256]{2,1,0:T(4,128)S(1)} %copy.203), channel_id=1, source_target_pairs={{0,8},{8,16},{16,24},{1,9},{9,17},{17,25},{2,10},{10,18},{18,26},{... | collective-permute-start | bytes 147464 | tf_op jit(solution)/shard_map/ppermute | solution.py:26
  35.3 7.1 collective-permute-start.2
  37.8 6.2 collective-permute-start.3
  51.7 196.1 %copy-start.2 = (f32[4,264,264]{1,2,0:T(8,128)}, f32[4,264,264]{1,2,0:T(8,128)S(1)}, u32[]{:S(2)}) copy-start(f32[4,264,264]{1,2,0:T(8,128)S(1)} %slice_multiply_fusion) | copy-start | bytes 3345412
  58.7 53.2 %all-to-all-start.1 = ((f32[8,9,64,128]{3,2,1,0:T(8,128)}), f32[8,9,64,128]{3,2,1,0:T(8,128)}, u32[]{:S(2)}, u32[]{:S(2)}) async-start(f32[8,9,64,128]{3,2,1,0:T(8,128)} %copy.220), calls=%async_computation.1 | async-start | bytes 4718592 | tf_op jit(solution)/shard_map/all_to_all | solution.py:187
  116.8 3.5 collective-permute-start.4
  122.5 60.4 %all-to-all-start.2 = ((f32[8,9,64,128]{3,2,1,0:T(8,128)}), f32[8,9,64,128]{3,2,1,0:T(8,128)}, u32[]{:S(2)}, u32[]{:S(2)}) async-start(f32[8,9,64,128]{3,2,1,0:T(8,128)} %copy.227), calls=%async_computation.2 | async-start | bytes 4718592 | tf_op jit(solution)/shard_map/all_to_all | solution.py:203
  182.9 5.6 collective-permute-start.5
  194.1 10.5 %collective-permute-start.7 = (f32[4,2,8,128]{2,3,0,1:T(8,128)S(1)}, f32[4,2,8,128]{2,3,0,1:T(8,128)S(1)}, u32[]{:S(2)}, u32[]{:S(2)}) collective-permute-start(f32[4,2,8,128]{2,3,0,1:T(8,128)S(1)} %get-tuple-element.143), channel_id=1, source_target_pairs={{0,8},{8,16},{16,24},{1,9},{9,17},{17,25},{2,10},{10,18},{18,26},{... | collective-permute-start | bytes 98312 | tf_op jit(solution)/shard_map/ppermute | solution.py:26
  196.0 10.3 %collective-permute-start.8 = (f32[4,2,8,128]{2,3,0,1:T(8,128)S(1)}, f32[4,2,8,128]{2,3,0,1:T(8,128)S(1)}, u32[]{:S(2)}, u32[]{:S(2)}) collective-permute-start(f32[4,2,8,128]{2,3,0,1:T(8,128)S(1)} %get-tuple-element.144), channel_id=1, source_target_pairs={{8,0},{16,8},{24,16},{9,1},{17,9},{25,17},{10,2},{18,10},{26,18},{... | collective-permute-start | bytes 98312 | tf_op jit(solution)/shard_map/ppermute | solution.py:29
  200.0 3.7 collective-permute-start.6
  206.9 10.3 %collective-permute-start.9 = (f32[3,128]{1,0:T(4,128)S(1)}, f32[3,128]{1,0:T(4,128)S(1)}, u32[]{:S(2)}, u32[]{:S(2)}) collective-permute-start(f32[3,128]{1,0:T(4,128)S(1)} %add.351), channel_id=1, source_target_pairs={{0,2},{1,3},{2,0},{3,1},{4,6},{5,7},{6,4},{7,5},{8,10},{9,11},{10,... | collective-permute-start | bytes 4616 | tf_op jit(solution)/shard_map/ppermute | solution.py:84
  209.6 7.7 collective-permute-start.10
  213.8 6.0 collective-permute-start.11
  222.0 4.5 collective-permute-start.12
  242.6 49.3 %all-to-all-start.3 = ((f32[8,9,64,128]{3,2,1,0:T(8,128)}), f32[8,9,64,128]{3,2,1,0:T(8,128)}, u32[]{:S(2)}, u32[]{:S(2)}) async-start(f32[8,9,64,128]{3,2,1,0:T(8,128)} %copy.236), calls=%async_computation.3 | async-start | bytes 4718592 | tf_op jit(solution)/shard_map/all_to_all | solution.py:187
  299.9 4.1 collective-permute-start.13
  365.1 5.0 collective-permute-start.14
  373.5 10.5 %collective-permute-start.16 = (f32[4,2,8,128]{2,3,0,1:T(8,128)S(1)}, f32[4,2,8,128]{2,3,0,1:T(8,128)S(1)}, u32[]{:S(2)}, u32[]{:S(2)}) collective-permute-start(f32[4,2,8,128]{2,3,0,1:T(8,128)S(1)} %get-tuple-element.141), channel_id=1, source_target_pairs={{0,8},{8,16},{16,24},{1,9},{9,17},{17,25},{2,10},{10,18},{18,26},{... | collective-permute-start | bytes 98312 | tf_op jit(solution)/shard_map/ppermute | solution.py:26
  375.4 10.3 %collective-permute-start.17 = (f32[4,2,8,128]{2,3,0,1:T(8,128)S(1)}, f32[4,2,8,128]{2,3,0,1:T(8,128)S(1)}, u32[]{:S(2)}, u32[]{:S(2)}) collective-permute-start(f32[4,2,8,128]{2,3,0,1:T(8,128)S(1)} %get-tuple-element.142), channel_id=1, source_target_pairs={{8,0},{16,8},{24,16},{9,1},{17,9},{25,17},{10,2},{18,10},{26,18},{... | collective-permute-start | bytes 98312 | tf_op jit(solution)/shard_map/ppermute | solution.py:29
  379.1 3.7 collective-permute-start.15
  386.4 8.6 %collective-permute-start.18 = (f32[7,128]{1,0:T(8,128)S(1)}, f32[7,128]{1,0:T(8,128)S(1)}, u32[]{:S(2)}, u32[]{:S(2)}) collective-permute-start(f32[7,128]{1,0:T(8,128)S(1)} %add.361), channel_id=1, source_target_pairs={{0,2},{1,3},{2,0},{3,1},{4,6},{5,7},{6,4},{7,5},{8,10},{9,11},{10,... | collective-permute-start | bytes 10760 | tf_op jit(solution)/shard_map/ppermute | solution.py:84
  387.4 7.6 collective-permute-start.19
  391.6 6.0 collective-permute-start.20
  399.8 4.5 collective-permute-start.21
  424.8 49.1 %all-to-all-start.5 = ((f32[8,9,64,128]{3,2,1,0:T(8,128)}), f32[8,9,64,128]{3,2,1,0:T(8,128)}, u32[]{:S(2)}, u32[]{:S(2)}) async-start(f32[8,9,64,128]{3,2,1,0:T(8,128)} %copy.253), calls=%async_computation.5 | async-start | bytes 4718592 | tf_op jit(solution)/shard_map/all_to_all | solution.py:187
  482.8 4.1 collective-permute-start.22
  547.3 5.9 collective-permute-start.23
  558.8 10.5 %collective-permute-start.25 = (f32[4,2,8,128]{2,3,0,1:T(8,128)S(1)}, f32[4,2,8,128]{2,3,0,1:T(8,128)S(1)}, u32[]{:S(2)}, u32[]{:S(2)}) collective-permute-start(f32[4,2,8,128]{2,3,0,1:T(8,128)S(1)} %get-tuple-element.139), channel_id=1, source_target_pairs={{0,8},{8,16},{16,24},{1,9},{9,17},{17,25},{2,10},{10,18},{18,26},{... | collective-permute-start | bytes 98312 | tf_op jit(solution)/shard_map/ppermute | solution.py:26
  560.7 10.3 %collective-permute-start.26 = (f32[4,2,8,128]{2,3,0,1:T(8,128)S(1)}, f32[4,2,8,128]{2,3,0,1:T(8,128)S(1)}, u32[]{:S(2)}, u32[]{:S(2)}) collective-permute-start(f32[4,2,8,128]{2,3,0,1:T(8,128)S(1)} %get-tuple-element.140), channel_id=1, source_target_pairs={{8,0},{16,8},{24,16},{9,1},{17,9},{25,17},{10,2},{18,10},{26,18},{... | collective-permute-start | bytes 98312 | tf_op jit(solution)/shard_map/ppermute | solution.py:29
  564.4 3.7 collective-permute-start.24
  571.7 8.6 %collective-permute-start.27 = (f32[7,128]{1,0:T(8,128)S(1)}, f32[7,128]{1,0:T(8,128)S(1)}, u32[]{:S(2)}, u32[]{:S(2)}) collective-permute-start(f32[7,128]{1,0:T(8,128)S(1)} %add.378), channel_id=1, source_target_pairs={{0,2},{1,3},{2,0},{3,1},{4,6},{5,7},{6,4},{7,5},{8,10},{9,11},{10,... | collective-permute-start | bytes 10760 | tf_op jit(solution)/shard_map/ppermute | solution.py:84
  572.7 7.6 collective-permute-start.28
  576.9 6.0 collective-permute-start.29
  585.0 4.5 collective-permute-start.30
  610.5 48.7 %all-to-all-start.7 = ((f32[8,9,64,128]{3,2,1,0:T(8,128)}), f32[8,9,64,128]{3,2,1,0:T(8,128)}, u32[]{:S(2)}, u32[]{:S(2)}) async-start(f32[8,9,64,128]{3,2,1,0:T(8,128)} %copy.272), calls=%async_computation.7 | async-start | bytes 4718592 | tf_op jit(solution)/shard_map/all_to_all | solution.py:187
  666.5 4.1 collective-permute-start.31
  731.1 6.1 collective-permute-start.32
  740.6 10.5 %collective-permute-start.34 = (f32[4,2,8,128]{2,3,0,1:T(8,128)S(1)}, f32[4,2,8,128]{2,3,0,1:T(8,128)S(1)}, u32[]{:S(2)}, u32[]{:S(2)}) collective-permute-start(f32[4,2,8,128]{2,3,0,1:T(8,128)S(1)} %get-tuple-element.137), channel_id=1, source_target_pairs={{0,8},{8,16},{16,24},{1,9},{9,17},{17,25},{2,10},{10,18},{18,26},{... | collective-permute-start | bytes 98312 | tf_op jit(solution)/shard_map/ppermute | solution.py:26
  742.5 10.3 %collective-permute-start.35 = (f32[4,2,8,128]{2,3,0,1:T(8,128)S(1)}, f32[4,2,8,128]{2,3,0,1:T(8,128)S(1)}, u32[]{:S(2)}, u32[]{:S(2)}) collective-permute-start(f32[4,2,8,128]{2,3,0,1:T(8,128)S(1)} %get-tuple-element.138), channel_id=1, source_target_pairs={{8,0},{16,8},{24,16},{9,1},{17,9},{25,17},{10,2},{18,10},{26,18},{... | collective-permute-start | bytes 98312 | tf_op jit(solution)/shard_map/ppermute | solution.py:29
  746.2 3.7 collective-permute-start.33
  753.5 8.6 %collective-permute-start.36 = (f32[7,128]{1,0:T(8,128)S(1)}, f32[7,128]{1,0:T(8,128)S(1)}, u32[]{:S(2)}, u32[]{:S(2)}) collective-permute-start(f32[7,128]{1,0:T(8,128)S(1)} %add.395), channel_id=1, source_target_pairs={{0,2},{1,3},{2,0},{3,1},{4,6},{5,7},{6,4},{7,5},{8,10},{9,11},{10,... | collective-permute-start | bytes 10760 | tf_op jit(solution)/shard_map/ppermute | solution.py:84
  754.5 7.6 collective-permute-start.37
  758.7 6.0 collective-permute-start.38
  765.7 4.6 collective-permute-start.39
  (40 other events, 222.4 us)

commit v20 on v19

--- a/solution.py
+++ b/solution.py
@@ -182,7 +182,7 @@
             precision=highest,
         ).reshape(own_blocks, block_rows, block_cols)
         outgoing = jnp.einsum(
-            "bk,bxc->kxc", landing, blocks, precision=lax.Precision.HIGHEST
+            "bk,bxc->kxc", landing, blocks, precision=highest
         ).reshape(owners, capacity, block_rows, block_cols)
         arrived = lax.all_to_all(outgoing, "gy", split_axis=0, concat_axis=0, tiled=True)
         seen = jnp.einsum(

time: 801 us -> 798 us (level)
  no operation moved by 1% of the time
where the time goes in v20:
time: 798 us; the launch traced here: 786 us
  blocking collectives  191 us (24%)
  waiting for transfers between devices  185 us (23%)
  local copies, waits for them, and re-layouts  113 us (14%)
  starting transfers between devices  111 us (14%)
  matrix products  104 us (13%)
  other arithmetic  60.3 us (8%)
  between operations  21.4 us (3%)
    all_to_all x3, blocking collectives, apply_op(): lax.all_to_all(returning, 'gy', split_axis=0, concat_axis=0, tiled=True)  180 us
    all_to_all x4, waiting for transfers between devices, apply_op(): lax.all_to_all(outgoing, 'gy', split_axis=0, concat_axis=0, tiled=True)  85.7 us
    all_to_all x1, waiting for transfers between devices, apply_op(): lax.all_to_all(returning, 'gy', split_axis=0, concat_axis=0, tiled=True)  51.1 us
    reshape x13, local copies, waits for them, and re-layouts, lane_sum(): return jnp.sum(values.reshape(-1, 128), axis=0)  28 us
    ppermute x20, waiting for transfers between devices, sum_steps(): lax.ppermute(value, axis, pairs)  27.8 us
    dot_general x4, matrix products, apply_op(): jnp.einsum('lab,ac->lcb', along_cols, analysis_rows, precision=highest)  21.8 us
    all_to_all x4, starting transfers between devices, apply_op(): lax.all_to_all(outgoing, 'gy', split_axis=0, concat_axis=0, tiled=True)  21.4 us
    ppermute x20, starting transfers between devices, sum_steps(): lax.ppermute(value, axis, pairs)  21.3 us
  transfers between devices with their start and end apart: 45, of which 27 were waited for; matrix products, arithmetic and copies ran while one was open for 17% of the time, Pallas kernels for 0%

profile of v20, /device:TPU:10, one launch (start us, length us, event | category | flops | bytes accessed | tf_op | source)
XLA Modules:
  0.0 785.6 jit_solution(9560091310001640807)
XLA Ops:
  19.8 11.1 %all_to_all.52 = s32[8,1,9]{2,1,0:T(1,128)S(1)} all-to-all(s32[8,1,9]{2,1,0:T(1,128)S(1)} %copy.212), channel_id=1, replica_groups=mesh['gx'=4,'gy'=8] {'gy'}, dimensions={0} | all-to-all | bytes 576 | tf_op jit(solution)/shard_map/all_to_all | solution.py:157
  37.8 4.2 collective-permute-start.3
  44.1 5.4 pad_maximum_fusion
  58.0 6.0 all-to-all-start.1
  79.8 31.5 %all-to-all-done.1 = f32[8,9,64,128]{3,2,1,0:T(8,128)} async-done(((f32[8,9,64,128]{3,2,1,0:T(8,128)}), f32[8,9,64,128]{3,2,1,0:T(8,128)}, u32[]{:S(2)}, u32[]{:S(2)}) %all-to-all-start.1) | async-done | bytes 2359328 | tf_op jit(solution)/shard_map/all_to_all | solution.py:187
  111.3 3.7 fusion.6
  121.8 8.1 %all-to-all-start.2 = ((f32[8,9,64,128]{3,2,1,0:T(8,128)}), f32[8,9,64,128]{3,2,1,0:T(8,128)}, u32[]{:S(2)}, u32[]{:S(2)}) async-start(f32[8,9,64,128]{3,2,1,0:T(8,128)} %copy.227), calls=%async_computation.2 | async-start | bytes 4718592 | tf_op jit(solution)/shard_map/all_to_all | solution.py:203
  131.1 51.1 %all-to-all-done.2 = f32[8,9,64,128]{3,2,1,0:T(8,128)} async-done(((f32[8,9,64,128]{3,2,1,0:T(8,128)}), f32[8,9,64,128]{3,2,1,0:T(8,128)}, u32[]{:S(2)}, u32[]{:S(2)}) %all-to-all-start.2) | async-done | bytes 2359328 | tf_op jit(solution)/shard_map/all_to_all | solution.py:203
  184.3 3.5 fusion.14
  195.3 4.0 collective-permute-start.8
  208.9 3.4 collective-permute-start.10
  221.3 4.5 collective-permute-done.12
  228.4 6.6 slice_multiply_fusion.3
  241.2 5.2 all-to-all-start.3
  246.5 4.5 multiply_multiply_fusion.7
  265.4 25.1 %all-to-all-done.3 = f32[8,9,64,128]{3,2,1,0:T(8,128)} async-done(((f32[8,9,64,128]{3,2,1,0:T(8,128)}), f32[8,9,64,128]{3,2,1,0:T(8,128)}, u32[]{:S(2)}, u32[]{:S(2)}) %all-to-all-start.3) | async-done | bytes 2359328 | tf_op jit(solution)/shard_map/all_to_all | solution.py:187
  290.5 3.8 fusion.4
  298.6 4.0 fusion.20
  303.3 60.4 %all_to_all.53 = f32[8,9,64,128]{3,2,1,0:T(8,128)S(1)} all-to-all(f32[8,9,64,128]{3,2,1,0:T(8,128)S(1)} %copy.244), channel_id=1, replica_groups=mesh['gx'=4,'gy'=8] {'gy'}, dimensions={0} | all-to-all | bytes 4718592 | tf_op jit(solution)/shard_map/all_to_all | solution.py:203
  374.1 3.6 collective-permute-start.17
  378.0 3.4 collective-permute-done.15
  386.0 3.4 collective-permute-start.19
  398.5 4.4 collective-permute-done.21
  409.5 4.9 fusion.31
  422.8 5.2 all-to-all-start.5
  428.1 3.4 multiply_multiply_fusion.1
  437.8 4.5 multiply_multiply_fusion.5
  461.2 10.8 %all-to-all-done.5 = f32[8,9,64,128]{3,2,1,0:T(8,128)} async-done(((f32[8,9,64,128]{3,2,1,0:T(8,128)}), f32[8,9,64,128]{3,2,1,0:T(8,128)}, u32[]{:S(2)}, u32[]{:S(2)}) %all-to-all-start.5) | async-done | bytes 2359328 | tf_op jit(solution)/shard_map/all_to_all | solution.py:187
  472.0 3.8 fusion.2
  480.9 4.0 fusion.18
  485.6 59.7 %all_to_all.54 = f32[8,9,64,128]{3,2,1,0:T(8,128)S(1)} all-to-all(f32[8,9,64,128]{3,2,1,0:T(8,128)S(1)} %copy.263), channel_id=1, replica_groups=mesh['gx'=4,'gy'=8] {'gy'}, dimensions={0} | all-to-all | bytes 4718592 | tf_op jit(solution)/shard_map/all_to_all | solution.py:203
  545.3 3.9 collective-permute-start.23
  558.7 3.6 collective-permute-start.26
  562.6 3.4 collective-permute-done.24
  570.6 3.4 collective-permute-start.28
  583.2 4.3 collective-permute-done.30
  594.1 7.5 slice_multiply_fusion.1
  607.8 5.0 all-to-all-start.7
  612.8 5.7 multiply_multiply_fusion
  638.2 18.3 %all-to-all-done.7 = f32[8,9,64,128]{3,2,1,0:T(8,128)} async-done(((f32[8,9,64,128]{3,2,1,0:T(8,128)}), f32[8,9,64,128]{3,2,1,0:T(8,128)}, u32[]{:S(2)}, u32[]{:S(2)}) %all-to-all-start.7) | async-done | bytes 2359328 | tf_op jit(solution)/shard_map/all_to_all | solution.py:187
  656.5 3.8 fusion
  663.9 4.0 fusion.16
  668.6 59.8 %all_to_all.55 = f32[8,9,64,128]{3,2,1,0:T(8,128)S(1)} all-to-all(f32[8,9,64,128]{3,2,1,0:T(8,128)S(1)} %copy.282), channel_id=1, replica_groups=mesh['gx'=4,'gy'=8] {'gy'}, dimensions={0} | all-to-all | bytes 4718592 | tf_op jit(solution)/shard_map/all_to_all | solution.py:203
  728.4 4.2 collective-permute-start.32
  739.8 3.6 collective-permute-start.35
  743.8 3.4 collective-permute-done.33
  751.8 3.4 collective-permute-start.37
  774.0 7.2 fusion.36
  (321 shorter events, 262.4 us)
Async XLA Ops:
  0.6 114.4 %copy-start = (f32[2,4,128,128]{3,2,1,0:T(8,128)S(1)}, f32[2,4,128,128]{3,2,1,0:T(8,128)}, u32[]{:S(2)}) copy-start(f32[2,4,128,128]{3,2,1,0:T(8,128)} %param.32) | copy-start | bytes 1572868
  3.8 40.3 %copy-start.6 = (f32[4,256,256]{1,2,0:T(8,128)}, f32[4,256,256]{1,2,0:T(8,128)S(1)}, u32[]{:S(2)}) copy-start(f32[4,256,256]{1,2,0:T(8,128)S(1)} %copy.207) | copy-start | bytes 3145732
  12.4 20.2 %collective-permute-start.1 = (f32[12,4,256]{2,1,0:T(4,128)S(1)}, f32[12,4,256]{2,1,0:T(4,128)S(1)}, u32[]{:S(2)}, u32[]{:S(2)}) collective-permute-start(f32[12,4,256]{2,1,0:T(4,128)S(1)} %copy.204), channel_id=1, source_target_pairs={{8,0},{16,8},{24,16},{9,1},{17,9},{25,17},{10,2},{18,10},{26,18},{... | collective-permute-start | bytes 147464 | tf_op jit(solution)/shard_map/ppermute | solution.py:29
  16.2 14.8 %collective-permute-start = (f32[12,4,256]{2,1,0:T(4,128)S(1)}, f32[12,4,256]{2,1,0:T(4,128)S(1)}, u32[]{:S(2)}, u32[]{:S(2)}) collective-permute-start(f32[12,4,256]{2,1,0:T(4,128)S(1)} %copy.203), channel_id=1, source_target_pairs={{0,8},{8,16},{16,24},{1,9},{9,17},{17,25},{2,10},{10,18},{18,26},{... | collective-permute-start | bytes 147464 | tf_op jit(solution)/shard_map/ppermute | solution.py:26
  35.3 7.1 collective-permute-start.2
  37.8 6.2 collective-permute-start.3
  51.7 194.8 %copy-start.2 = (f32[4,264,264]{1,2,0:T(8,128)}, f32[4,264,264]{1,2,0:T(8,128)S(1)}, u32[]{:S(2)}) copy-start(f32[4,264,264]{1,2,0:T(8,128)S(1)} %slice_multiply_fusion) | copy-start | bytes 3345412
  58.0 53.2 %all-to-all-start.1 = ((f32[8,9,64,128]{3,2,1,0:T(8,128)}), f32[8,9,64,128]{3,2,1,0:T(8,128)}, u32[]{:S(2)}, u32[]{:S(2)}) async-start(f32[8,9,64,128]{3,2,1,0:T(8,128)} %copy.220), calls=%async_computation.1 | async-start | bytes 4718592 | tf_op jit(solution)/shard_map/all_to_all | solution.py:187
  116.1 3.5 collective-permute-start.4
  121.8 60.4 %all-to-all-start.2 = ((f32[8,9,64,128]{3,2,1,0:T(8,128)}), f32[8,9,64,128]{3,2,1,0:T(8,128)}, u32[]{:S(2)}, u32[]{:S(2)}) async-start(f32[8,9,64,128]{3,2,1,0:T(8,128)} %copy.227), calls=%async_computation.2 | async-start | bytes 4718592 | tf_op jit(solution)/shard_map/all_to_all | solution.py:203
  182.2 5.6 collective-permute-start.5
  193.4 10.5 %collective-permute-start.7 = (f32[4,2,8,128]{2,3,0,1:T(8,128)S(1)}, f32[4,2,8,128]{2,3,0,1:T(8,128)S(1)}, u32[]{:S(2)}, u32[]{:S(2)}) collective-permute-start(f32[4,2,8,128]{2,3,0,1:T(8,128)S(1)} %get-tuple-element.143), channel_id=1, source_target_pairs={{0,8},{8,16},{16,24},{1,9},{9,17},{17,25},{2,10},{10,18},{18,26},{... | collective-permute-start | bytes 98312 | tf_op jit(solution)/shard_map/ppermute | solution.py:26
  195.3 10.3 %collective-permute-start.8 = (f32[4,2,8,128]{2,3,0,1:T(8,128)S(1)}, f32[4,2,8,128]{2,3,0,1:T(8,128)S(1)}, u32[]{:S(2)}, u32[]{:S(2)}) collective-permute-start(f32[4,2,8,128]{2,3,0,1:T(8,128)S(1)} %get-tuple-element.144), channel_id=1, source_target_pairs={{8,0},{16,8},{24,16},{9,1},{17,9},{25,17},{10,2},{18,10},{26,18},{... | collective-permute-start | bytes 98312 | tf_op jit(solution)/shard_map/ppermute | solution.py:29
  199.4 3.7 collective-permute-start.6
  206.3 10.3 %collective-permute-start.9 = (f32[3,128]{1,0:T(4,128)S(1)}, f32[3,128]{1,0:T(4,128)S(1)}, u32[]{:S(2)}, u32[]{:S(2)}) collective-permute-start(f32[3,128]{1,0:T(4,128)S(1)} %add.351), channel_id=1, source_target_pairs={{0,2},{1,3},{2,0},{3,1},{4,6},{5,7},{6,4},{7,5},{8,10},{9,11},{10,... | collective-permute-start | bytes 4616 | tf_op jit(solution)/shard_map/ppermute | solution.py:84
  208.9 7.7 collective-permute-start.10
  213.2 6.0 collective-permute-start.11
  221.3 4.5 collective-permute-start.12
  241.2 49.3 %all-to-all-start.3 = ((f32[8,9,64,128]{3,2,1,0:T(8,128)}), f32[8,9,64,128]{3,2,1,0:T(8,128)}, u32[]{:S(2)}, u32[]{:S(2)}) async-start(f32[8,9,64,128]{3,2,1,0:T(8,128)} %copy.236), calls=%async_computation.3 | async-start | bytes 4718592 | tf_op jit(solution)/shard_map/all_to_all | solution.py:187
  298.5 4.1 collective-permute-start.13
  363.7 5.0 collective-permute-start.14
  372.2 10.5 %collective-permute-start.16 = (f32[4,2,8,128]{2,3,0,1:T(8,128)S(1)}, f32[4,2,8,128]{2,3,0,1:T(8,128)S(1)}, u32[]{:S(2)}, u32[]{:S(2)}) collective-permute-start(f32[4,2,8,128]{2,3,0,1:T(8,128)S(1)} %get-tuple-element.141), channel_id=1, source_target_pairs={{0,8},{8,16},{16,24},{1,9},{9,17},{17,25},{2,10},{10,18},{18,26},{... | collective-permute-start | bytes 98312 | tf_op jit(solution)/shard_map/ppermute | solution.py:26
  374.1 10.3 %collective-permute-start.17 = (f32[4,2,8,128]{2,3,0,1:T(8,128)S(1)}, f32[4,2,8,128]{2,3,0,1:T(8,128)S(1)}, u32[]{:S(2)}, u32[]{:S(2)}) collective-permute-start(f32[4,2,8,128]{2,3,0,1:T(8,128)S(1)} %get-tuple-element.142), channel_id=1, source_target_pairs={{8,0},{16,8},{24,16},{9,1},{17,9},{25,17},{10,2},{18,10},{26,18},{... | collective-permute-start | bytes 98312 | tf_op jit(solution)/shard_map/ppermute | solution.py:29
  377.7 3.7 collective-permute-start.15
  385.0 8.6 %collective-permute-start.18 = (f32[7,128]{1,0:T(8,128)S(1)}, f32[7,128]{1,0:T(8,128)S(1)}, u32[]{:S(2)}, u32[]{:S(2)}) collective-permute-start(f32[7,128]{1,0:T(8,128)S(1)} %add.361), channel_id=1, source_target_pairs={{0,2},{1,3},{2,0},{3,1},{4,6},{5,7},{6,4},{7,5},{8,10},{9,11},{10,... | collective-permute-start | bytes 10760 | tf_op jit(solution)/shard_map/ppermute | solution.py:84
  386.0 7.6 collective-permute-start.19
  390.3 6.0 collective-permute-start.20
  398.4 4.5 collective-permute-start.21
  422.8 49.1 %all-to-all-start.5 = ((f32[8,9,64,128]{3,2,1,0:T(8,128)}), f32[8,9,64,128]{3,2,1,0:T(8,128)}, u32[]{:S(2)}, u32[]{:S(2)}) async-start(f32[8,9,64,128]{3,2,1,0:T(8,128)} %copy.253), calls=%async_computation.5 | async-start | bytes 4718592 | tf_op jit(solution)/shard_map/all_to_all | solution.py:187
  480.8 4.1 collective-permute-start.22
  545.3 5.8 collective-permute-start.23
  556.8 10.5 %collective-permute-start.25 = (f32[4,2,8,128]{2,3,0,1:T(8,128)S(1)}, f32[4,2,8,128]{2,3,0,1:T(8,128)S(1)}, u32[]{:S(2)}, u32[]{:S(2)}) collective-permute-start(f32[4,2,8,128]{2,3,0,1:T(8,128)S(1)} %get-tuple-element.139), channel_id=1, source_target_pairs={{0,8},{8,16},{16,24},{1,9},{9,17},{17,25},{2,10},{10,18},{18,26},{... | collective-permute-start | bytes 98312 | tf_op jit(solution)/shard_map/ppermute | solution.py:26
  558.7 10.3 %collective-permute-start.26 = (f32[4,2,8,128]{2,3,0,1:T(8,128)S(1)}, f32[4,2,8,128]{2,3,0,1:T(8,128)S(1)}, u32[]{:S(2)}, u32[]{:S(2)}) collective-permute-start(f32[4,2,8,128]{2,3,0,1:T(8,128)S(1)} %get-tuple-element.140), channel_id=1, source_target_pairs={{8,0},{16,8},{24,16},{9,1},{17,9},{25,17},{10,2},{18,10},{26,18},{... | collective-permute-start | bytes 98312 | tf_op jit(solution)/shard_map/ppermute | solution.py:29
  562.4 3.7 collective-permute-start.24
  569.7 8.6 %collective-permute-start.27 = (f32[7,128]{1,0:T(8,128)S(1)}, f32[7,128]{1,0:T(8,128)S(1)}, u32[]{:S(2)}, u32[]{:S(2)}) collective-permute-start(f32[7,128]{1,0:T(8,128)S(1)} %add.378), channel_id=1, source_target_pairs={{0,2},{1,3},{2,0},{3,1},{4,6},{5,7},{6,4},{7,5},{8,10},{9,11},{10,... | collective-permute-start | bytes 10760 | tf_op jit(solution)/shard_map/ppermute | solution.py:84
  570.6 7.6 collective-permute-start.28
  574.9 6.0 collective-permute-start.29
  583.0 4.5 collective-permute-start.30
  607.8 48.7 %all-to-all-start.7 = ((f32[8,9,64,128]{3,2,1,0:T(8,128)}), f32[8,9,64,128]{3,2,1,0:T(8,128)}, u32[]{:S(2)}, u32[]{:S(2)}) async-start(f32[8,9,64,128]{3,2,1,0:T(8,128)} %copy.272), calls=%async_computation.7 | async-start | bytes 4718592 | tf_op jit(solution)/shard_map/all_to_all | solution.py:187
  663.8 4.1 collective-permute-start.31
  728.4 6.1 collective-permute-start.32
  737.9 10.5 %collective-permute-start.34 = (f32[4,2,8,128]{2,3,0,1:T(8,128)S(1)}, f32[4,2,8,128]{2,3,0,1:T(8,128)S(1)}, u32[]{:S(2)}, u32[]{:S(2)}) collective-permute-start(f32[4,2,8,128]{2,3,0,1:T(8,128)S(1)} %get-tuple-element.137), channel_id=1, source_target_pairs={{0,8},{8,16},{16,24},{1,9},{9,17},{17,25},{2,10},{10,18},{18,26},{... | collective-permute-start | bytes 98312 | tf_op jit(solution)/shard_map/ppermute | solution.py:26
  739.8 10.3 %collective-permute-start.35 = (f32[4,2,8,128]{2,3,0,1:T(8,128)S(1)}, f32[4,2,8,128]{2,3,0,1:T(8,128)S(1)}, u32[]{:S(2)}, u32[]{:S(2)}) collective-permute-start(f32[4,2,8,128]{2,3,0,1:T(8,128)S(1)} %get-tuple-element.138), channel_id=1, source_target_pairs={{8,0},{16,8},{24,16},{9,1},{17,9},{25,17},{10,2},{18,10},{26,18},{... | collective-permute-start | bytes 98312 | tf_op jit(solution)/shard_map/ppermute | solution.py:29
  743.5 3.7 collective-permute-start.33
  750.8 8.6 %collective-permute-start.36 = (f32[7,128]{1,0:T(8,128)S(1)}, f32[7,128]{1,0:T(8,128)S(1)}, u32[]{:S(2)}, u32[]{:S(2)}) collective-permute-start(f32[7,128]{1,0:T(8,128)S(1)} %add.395), channel_id=1, source_target_pairs={{0,2},{1,3},{2,0},{3,1},{4,6},{5,7},{6,4},{7,5},{8,10},{9,11},{10,... | collective-permute-start | bytes 10760 | tf_op jit(solution)/shard_map/ppermute | solution.py:84
  751.8 7.6 collective-permute-start.37
  756.0 6.0 collective-permute-start.38
  763.0 4.6 collective-permute-start.39
  (40 other events, 222.3 us)
